TPU v7x, 256 devices: a whole 4x4x8 slice. The times are simulated.
256 devices in a mesh: section: 16 (over x, z_lo), expert: 16 (over y, z_hi, core).
Axes of the slice: x: 4, y: 4, z: 8 (z_hi: 2, z_lo: 4; z = z_hi * 4 + z_lo), core: 2. Of those that a mesh axis runs over, the one named last changes fastest.
Arguments:
- stream: bfloat16 [16, 256, 4096], P('section', 'expert'), may hold values from -6 to 6
- queries: bfloat16 [16, 256, 4096], P('section', None, 'expert'), may hold values from -6 to 6
- keyvals: bfloat16 [16, 4096, 512], P('section', 'expert'), may hold values from -6 to 6
- w_out: bfloat16 [16, 4096, 4096], P('section', 'expert'), may hold values from -0.5 to 0.5
- norm_gain: float32 [16, 4096], P('section'), may hold values from 0.5 to 1.5
- w_gate: bfloat16 [16, 4096, 6144], P('section', None, 'expert'), may hold values from -0.09375 to 0.09375
- w_up: bfloat16 [16, 4096, 6144], P('section', None, 'expert'), may hold values from -0.09375 to 0.09375
- w_down: bfloat16 [16, 6144, 4096], P('section', 'expert'), may hold values from -0.3125 to 0.3125
- routes: int32 [16, 256, 2], P('section'), may hold values from 0 to 3, all different within a row; in each aligned block of 16 rows (0 to 15, 16 to 31, ..., all dimensions but the last counted through in order) at most 12 rows name the same one
- gate_scores: float32 [16, 256, 2], P('section'), may hold values from 0.05 to 20
Outputs:
- passed: bfloat16 [16, 256, 4096], P('section', 'expert')
Inputs may be any that keep to these rules, and one draw needn't show every extreme that they name: `routes`: each row names 2 different experts. In each aligned block of 16 rows (the tokens of one device) no expert is named by more than 12 rows.
All inputs are finite; a program needn't handle non-finite values.
Results may differ from a plain program's by a relative error of at most 0.02.
Values may be sent and summed in bfloat16 or wider, within the bound.
No kernel may reach another device: no remote copies, remote signals or barrier semaphores. Data moves between devices by JAX's collectives and lax.ppermute only.
A program may use at most 64 MiB of HBM per device.

v0:
```python
import math

import jax
import jax.numpy as jnp
from jax import lax
from jax.sharding import PartitionSpec as P

HD = 128
FF = 1536
QHEADS = 32
KVHEADS = 2
CTX = 4096
MB = 256


def shifted(block, axis, distance):
    devices = range(lax.axis_size(axis))
    route = [((i - distance) % len(devices), i) for i in devices]
    return lax.ppermute(block, axis, route)


def body(stream, queries, keyvals, w_out, norm_gain, w_gate, w_up, w_down, routes, gate_scores):
    my_index = lax.axis_index("expert")
    devices = lax.axis_size("expert")
    tok_rows = stream.shape[1]
    residual = stream[0]
    query_all = queries[0]
    proj_out = w_out[0]
    gain = norm_gain[0]
    gate_w = w_gate[0]
    up_w = w_up[0]
    down_w = w_down[0]
    heads_here = query_all.shape[1] // HD
    group = QHEADS // KVHEADS
    scale = 1.0 / math.sqrt(HD)
    query_pos = CTX - MB + jnp.arange(MB, dtype=jnp.int32)
    piece = lax.all_gather(keyvals[0], "expert", axis=0, tiled=True)
    tops = jnp.full((heads_here, MB), -1e30, jnp.float32)
    totals = jnp.zeros((heads_here, MB), jnp.float32)
    sums = jnp.zeros((heads_here, MB, HD), jnp.float32)
    key_pos = jnp.arange(piece.shape[0], dtype=jnp.int32)
    visible = key_pos[None, :] <= query_pos[:, None]
    new_tops = []
    new_totals = []
    new_sums = []
    for head in range(heads_here):
        column = (my_index * heads_here + head) // group * (2 * HD)
        keys = lax.dynamic_slice_in_dim(piece, column, HD, 1)
        values = lax.dynamic_slice_in_dim(piece, column + HD, HD, 1)
        query = query_all[:, head * HD : (head + 1) * HD]
        score = (
            lax.dot_general(
                query, keys, (((1,), (1,)), ((), ())), preferred_element_type=jnp.float32
            )
            * scale
        )
        top_new = jnp.maximum(tops[head], jnp.max(jnp.where(visible, score, -1e30), axis=1))
        weight = jnp.where(visible, jnp.exp(score - top_new[:, None]), 0.0)
        factor = jnp.exp(tops[head] - top_new)
        new_tops.append(top_new)
        new_totals.append(totals[head] * factor + jnp.sum(weight, axis=1))
        new_sums.append(
            sums[head] * factor[:, None]
            + jnp.dot(weight.astype(jnp.bfloat16), values, preferred_element_type=jnp.float32)
        )
    totals = jnp.stack(new_totals)
    sums = jnp.stack(new_sums)
    heads = (sums / totals[:, :, None]).astype(jnp.bfloat16)
    heads = jnp.transpose(heads, (1, 0, 2)).reshape(MB, heads_here * HD)
    attended = lax.psum_scatter(
        jnp.dot(heads, proj_out, preferred_element_type=jnp.float32).astype(jnp.bfloat16),
        "expert",
        scatter_dimension=0,
        tiled=True,
    ).astype(jnp.float32)
    middle = residual.astype(jnp.float32) + attended
    normed = (
        middle * lax.rsqrt(jnp.mean(middle * middle, axis=1, keepdims=True) + 1e-06) * gain
    ).astype(jnp.bfloat16)
    split = FF // gate_w.shape[1]
    experts_count = devices // split
    chosen = lax.dynamic_slice_in_dim(routes[0], my_index * tok_rows, tok_rows, 0)
    scores_in = lax.dynamic_slice_in_dim(gate_scores[0], my_index * tok_rows, tok_rows, 0)
    onehot = chosen[:, :, None] == jnp.arange(experts_count, dtype=jnp.int32)[None, None, :]
    share = jnp.sum(jnp.where(onehot, scores_in[:, :, None], 0.0), axis=1) / jnp.sum(
        scores_in, axis=1, keepdims=True
    )
    share_dev = jnp.repeat(share, split, axis=1)
    outgoing_rows = jnp.broadcast_to(normed[None], (devices, tok_rows, normed.shape[1]))
    rows = lax.all_to_all(outgoing_rows, "expert", split_axis=0, concat_axis=0, tiled=True)
    flat = rows.reshape(-1, rows.shape[-1])
    gate = jnp.dot(flat, gate_w, preferred_element_type=jnp.float32)
    upper = jnp.dot(flat, up_w, preferred_element_type=jnp.float32)
    activated = (jax.nn.silu(gate) * upper).astype(jnp.bfloat16)
    computed = (
        jnp.dot(activated, down_w, preferred_element_type=jnp.float32)
        .astype(jnp.bfloat16)
        .reshape(rows.shape)
    )
    picked = lax.all_to_all(computed, "expert", split_axis=0, concat_axis=0, tiled=True)
    mixed = jnp.einsum(
        "td,dtk->tk", share_dev, picked.astype(jnp.float32), precision=lax.Precision.HIGHEST
    )
    layer_out = (middle + mixed).astype(jnp.bfloat16)
    return shifted(layer_out[None], "section", 1)


def solution(mesh):
    return jax.shard_map(
        body,
        mesh=mesh,
        in_specs=(
            P("section", "expert", None),
            P("section", None, "expert"),
            P("section", "expert", None),
            P("section", "expert", None),
            P("section", None),
            P("section", None, "expert"),
            P("section", None, "expert"),
            P("section", "expert", None),
            P("section", None, None),
            P("section", None, None),
        ),
        out_specs=P("section", "expert", None),
        check_vma=False,
    )
```

profile of v0, /device:TPU:32, one launch (start us, length us, event | category | flops | bytes accessed | tf_op | source)
XLA Modules:
  0.0 325.2 jit_solution(16367630738279816033)
XLA Ops:
  6.5 0.0 copy-start
  6.5 0.0 copy-start.10
  6.5 0.0 all-gather.3.cloned.1.call-start
  6.5 0.7 all-gather.3.cloned.1.call-update
  7.3 0.0 reduce-scatter.2.cloned.1.call-start
  7.4 81.5 %all-gather.3.cloned.1.call-done = bf16[1,4096,512]{2,1,0:T(8,128)(2,1)} async-done(((bf16[1,256,512]{2,1,0:T(8,128)(2,1)}), bf16[1,4096,512]{2,1,0:T(8,128)(2,1)}) %all-gather.3.cloned.1.call-update) | async-done | bytes 4194320 | tf_op jit(solution)/shard_map/all_gather | solution.py:37
  88.8 0.0 copy-start.8
  88.8 2.3 select_reduce_fusion.1
  91.1 0.0 copy-done.10
  91.1 0.2 copy-done.8
  91.4 1.7 fusion.2
  93.1 1.1 fusion.4
  94.2 1.0 fusion.27
  95.2 0.0 copy-start.1
  95.2 1.0 fusion.33
  96.2 0.0 copy-start.3
  96.2 0.0 copy-start.5
  96.3 0.5 copy-done.1
  96.8 2.1 convolution_convert_fusion.1
  98.9 0.0 reduce-scatter.2.cloned.1.call-update
  98.9 82.8 %reduce-scatter.2.cloned.1.call-done = bf16[16,4096]{1,0:T(8,128)(2,1)} async-done(((bf16[256,4096]{1,0:T(8,128)(2,1)}), bf16[16,4096]{1,0:T(8,128)(2,1)}) %reduce-scatter.2.cloned.1.call-update) | async-done | bytes 131088 | tf_op jit(solution)/shard_map/reduce_scatter | solution.py:70
  181.7 0.0 copy-done.3
  181.7 0.0 copy-start.9
  181.7 1.2 multiply_reduce_fusion
  183.0 0.0 copy-done.5
  183.0 1.0 multiply_convert_fusion
  184.0 0.2 broadcast_in_dim.53
  184.2 58.2 %all_to_all.10 = bf16[16,16,4096]{2,1,0:T(8,128)(2,1)S(1)} all-to-all(bf16[16,16,4096]{2,1,0:T(8,128)(2,1)S(1)} %broadcast_in_dim.53), channel_id=1, replica_groups=mesh['section'=16,'expert'=16] {'expert'}, dimensions={0} | all-to-all | bytes 4194304 | tf_op jit(solution)/shard_map/all_to_all | solution.py:90
  242.4 0.0 copy-start.2
  242.4 1.3 copy-done.2
  243.7 0.0 copy-done.9
  243.7 2.0 fusion.9
  245.7 0.0 copy-done
  245.7 6.3 %convolution_convert_fusion = bf16[256,4096]{1,0:T(8,128)(2,1)} fusion(bf16[1,384,4096]{2,1,0:T(8,128)(2,1)S(1)} %copy-done, bf16[256,4096]{1,0:T(8,128)(2,1)} %bitcast.77, bf16[1,4096,384]{2,1,0:T(8,128)(2,1)} %param.16, f32[256,384]{1,0:T(8,128)} %fusion.9), kind=kOutput, calls=%fused_computation.4 | convolution fusion | flops 1612251136 | bytes 10878976 | tf_op jit(solution)/shard_map/dot_general | solution.py:96
  252.1 0.0 copy-start.6
  252.1 0.0 copy-start.7
  252.1 0.0 copy-start.4
  252.1 4.8 %all-to-all-start.1 = ((bf16[16,16,4096]{2,1,0:T(8,128)(2,1)}), bf16[16,16,4096]{2,1,0:T(8,128)(2,1)}, u32[]{:S(2)}, u32[]{:S(2)}) async-start(bf16[16,16,4096]{2,1,0:T(8,128)(2,1)} %bitcast.75), calls=%async_computation.2 | async-start | bytes 4194304 | tf_op jit(solution)/shard_map/all_to_all | solution.py:100
  256.8 0.0 copy-done.6
  256.8 0.1 fusion.62
  256.9 0.0 copy-done.7
  256.9 0.1 fusion.61
  257.0 0.1 copy.15
  257.1 50.3 %all-to-all-done.1 = bf16[16,16,4096]{2,1,0:T(8,128)(2,1)} async-done(((bf16[16,16,4096]{2,1,0:T(8,128)(2,1)}), bf16[16,16,4096]{2,1,0:T(8,128)(2,1)}, u32[]{:S(2)}, u32[]{:S(2)}) %all-to-all-start.1) | async-done | bytes 2097184 | tf_op jit(solution)/shard_map/all_to_all | solution.py:100
  307.5 4.6 %fusion.12 = f32[16,1,4096]{2,1,0:T(1,128)S(1)} fusion(f32[16,16,1]{1,2,0:T(1,128)S(1)} %copy.15, bf16[16,16,4096]{2,1,0:T(8,128)(2,1)} %all-to-all-done.1), kind=kOutput, calls=%fused_computation.21 | convolution fusion | flops 12582912 | bytes 2360320 | tf_op jit(solution)/shard_map/td,dtk->tk/dot_general | solution.py:101
  312.0 0.0 copy-done.4
  312.1 0.2 fusion.54
  312.2 0.1 collective-permute-start
  312.3 5.4 %collective-permute-done = bf16[1,16,4096]{2,1,0:T(8,128)(2,1)S(1)} collective-permute-done((bf16[1,16,4096]{2,1,0:T(8,128)(2,1)S(1)}, bf16[1,16,4096]{2,1,0:T(8,128)(2,1)S(1)}, u32[]{:S(2)}, u32[]{:S(2)}) %collective-permute-start) | collective-permute-done | bytes 131104 | tf_op jit(solution)/shard_map/ppermute | solution.py:19
  317.7 0.7 copy.24
  (10 shorter events, 0.1 us)
Async XLA Ops:
  6.5 239.2 %copy-start = (bf16[1,384,4096]{2,1,0:T(8,128)(2,1)S(1)}, bf16[1,384,4096]{2,1,0:T(8,128)(2,1)}, u32[]{:S(2)}) copy-start(bf16[1,384,4096]{2,1,0:T(8,128)(2,1)} %param.17) | copy-start | bytes 9437188
  6.5 84.6 %copy-start.10 = (bf16[1,256,256]{2,1,0:T(8,128)(2,1)S(1)}, bf16[1,256,256]{2,1,0:T(8,128)(2,1)}, u32[]{:S(2)}) copy-start(bf16[1,256,256]{2,1,0:T(8,128)(2,1)} %param.11) | copy-start | bytes 393220
  6.5 82.3 %all-gather.3.cloned.1.call-start = ((), (), s32[]{:S(2)}) async-start(), calls=%async_computation.4 | async-start | bytes 4456448 | tf_op jit(solution)/shard_map/all_gather | solution.py:37
  7.3 174.5 %reduce-scatter.2.cloned.1.call-start = ((), (), s32[]{:S(2)}) async-start(), calls=%async_computation.3 | async-start | bytes 2228224 | tf_op jit(solution)/shard_map/reduce_scatter | solution.py:70
  88.8 2.5 copy-start.8
  95.2 1.6 copy-start.1
  96.2 85.5 %copy-start.3 = (bf16[1,16,4096]{2,1,0:T(8,128)(2,1)S(1)}, bf16[1,16,4096]{2,1,0:T(8,128)(2,1)}, u32[]{:S(2)}) copy-start(bf16[1,16,4096]{2,1,0:T(8,128)(2,1)} %param.10) | copy-start | bytes 393220
  96.2 86.7 %copy-start.5 = (f32[1,4096]{1,0:T(1,128)S(1)}, f32[1,4096]{1,0:T(1,128)}, u32[]{:S(2)}) copy-start(f32[1,4096]{1,0:T(1,128)} %param.14) | copy-start | bytes 49156
  181.7 61.9 %copy-start.9 = (bf16[1,4096,384]{2,1,0:T(8,128)(2,1)S(1)}, bf16[1,4096,384]{2,1,0:T(8,128)(2,1)}, u32[]{:S(2)}) copy-start(bf16[1,4096,384]{2,1,0:T(8,128)(2,1)} %param.15) | copy-start | bytes 9437188
  242.4 1.3 copy-start.2
  252.1 4.8 %copy-start.6 = (f32[1,256,2]{1,2,0:T(2,128)S(1)}, f32[1,256,2]{1,2,0:T(2,128)}, u32[]{:S(2)}) copy-start(f32[1,256,2]{1,2,0:T(2,128)} %param.19) | copy-start | bytes 6148
  252.1 4.9 %copy-start.7 = (s32[1,256,2]{1,2,0:T(2,128)S(1)}, s32[1,256,2]{1,2,0:T(2,128)}, u32[]{:S(2)}) copy-start(s32[1,256,2]{1,2,0:T(2,128)} %param.18) | copy-start | bytes 6148
  252.1 60.0 %copy-start.4 = (bf16[16,4096]{1,0:T(8,128)(2,1)S(1)}, bf16[16,4096]{1,0:T(8,128)(2,1)}, u32[]{:S(2)}) copy-start(bf16[16,4096]{1,0:T(8,128)(2,1)} %reduce-scatter.2.cloned.1.call-done) | copy-start | bytes 393220
  252.1 55.4 %all-to-all-start.1 = ((bf16[16,16,4096]{2,1,0:T(8,128)(2,1)}), bf16[16,16,4096]{2,1,0:T(8,128)(2,1)}, u32[]{:S(2)}, u32[]{:S(2)}) async-start(bf16[16,16,4096]{2,1,0:T(8,128)(2,1)} %bitcast.75), calls=%async_computation.2 | async-start | bytes 4194304 | tf_op jit(solution)/shard_map/all_to_all | solution.py:100
  312.2 5.5 %collective-permute-start = (bf16[1,16,4096]{2,1,0:T(8,128)(2,1)S(1)}, bf16[1,16,4096]{2,1,0:T(8,128)(2,1)S(1)}, u32[]{:S(2)}, u32[]{:S(2)}) collective-permute-start(bf16[1,16,4096]{2,1,0:T(8,128)(2,1)S(1)} %fusion.54), channel_id=1, source_target_pairs={{240,0},{0,16},{16,32},{32,48},{48,64},{64,80},{80,96},{96,112},{1... | collective-permute-start | bytes 393224 | tf_op jit(solution)/shard_map/ppermute | solution.py:19
Sparse Core Ops, SparseCore 0:
  10.0 78.7 all-gather.2
  99.0 82.6 reduce-scatter.1
where the time goes:
time: 326 us; the launch traced here: 325 us
  waiting for transfers between devices  221 us (68%)
  blocking collectives  58.2 us (18%)
  matrix products  21 us (6%)
  between operations  13.6 us (4%)
  starting transfers between devices  4.88 us (1%)
  other arithmetic  3.66 us (1%)
    reduce_scatter x1, waiting for transfers between devices, body(): lax.psum_scatter(jnp.dot(heads, proj_out, preferred_element_type=jnp.floa...  82.8 us
    all_gather x1, waiting for transfers between devices, body(): piece = lax.all_gather(keyvals[0], 'expert', axis=0, tiled=True)  81.5 us
    all_to_all x1, blocking collectives, body(): lax.all_to_all(outgoing_rows, 'expert', split_axis=0, concat_axis=0, tile...  58.2 us
    all_to_all x1, waiting for transfers between devices, body(): lax.all_to_all(computed, 'expert', split_axis=0, concat_axis=0, tiled=True)  50.3 us
  transfers between devices with their start and end apart: 4, of which 4 were waited for; matrix products, arithmetic and copies ran while one was open for 0% of the time, Pallas kernels for 0%

commit v1 on v0

v1 whole, which is shorter than its diff:
```python
import math

import jax
import jax.numpy as jnp
from jax import lax
from jax.sharding import Mesh
from jax.sharding import PartitionSpec as P

HD = 128
FF = 1536
QHEADS = 32
KVHEADS = 2
CTX = 4096
MB = 256
CAP = 12
EXPERT_AXES = ("y", "zh", "core")


def shifted(block, axis, distance):
    devices = range(lax.axis_size(axis))
    route = [((i - distance) % len(devices), i) for i in devices]
    return lax.ppermute(block, axis, route)


def swap(block, axis):
    return lax.ppermute(block, axis, [(0, 1), (1, 0)])


def body(stream, queries, keyvals, w_out, norm_gain, w_gate, w_up, w_down, routes, gate_scores):
    ny = lax.axis_size("y")
    nz = lax.axis_size("zh")
    nc = lax.axis_size("core")
    yi = lax.axis_index("y")
    zi = lax.axis_index("zh")
    ci = lax.axis_index("core")
    my_index = (yi * nz + zi) * nc + ci
    devices = ny * nz * nc
    tok_rows = stream.shape[1]
    residual = stream[0]
    query_all = queries[0]
    proj_out = w_out[0]
    gain = norm_gain[0]
    gate_w = w_gate[0]
    up_w = w_up[0]
    down_w = w_down[0]
    heads_here = query_all.shape[1] // HD
    group = QHEADS // KVHEADS
    scale = 1.0 / math.sqrt(HD)
    block = keyvals.shape[1]

    kv = keyvals[0].reshape(block, KVHEADS, 2 * HD)
    rows_per_y = nz * nc * heads_here
    head_of_y = [y * rows_per_y // group for y in range(ny)]
    send_kv = jnp.stack([kv[:, h] for h in head_of_y])
    kv_y = lax.all_to_all(send_kv, "y", 0, 0, tiled=True)
    kv_z = jnp.stack([kv_y, swap(kv_y, "zh")])
    kv_c = jnp.stack([kv_z, swap(kv_z, "core")])
    piece = kv_c.reshape(-1, 2 * HD)
    src_c = jnp.where(jnp.arange(2) == 0, ci, 1 - ci)[:, None, None]
    src_z = jnp.where(jnp.arange(2) == 0, zi, 1 - zi)[None, :, None]
    src_y = jnp.arange(ny)[None, None, :]
    src_block = (src_y * nz + src_z) * nc + src_c
    key_pos = (src_block[..., None] * block + jnp.arange(block)[None, None, None, :]).reshape(-1)
    query_pos = CTX - MB + jnp.arange(MB, dtype=jnp.int32)
    visible = key_pos[None, :] <= query_pos[:, None]

    keys = piece[:, :HD]
    values = piece[:, HD:]
    query = query_all.reshape(MB, heads_here, HD).transpose(1, 0, 2)
    score = jnp.einsum("hqd,kd->hqk", query, keys, preferred_element_type=jnp.float32) * scale
    top = jnp.max(jnp.where(visible[None], score, -1e30), axis=2, keepdims=True)
    weight = jnp.where(visible[None], jnp.exp(score - top), 0.0)
    total = jnp.sum(weight, axis=2, keepdims=True)
    summed = jnp.einsum(
        "hqk,kd->hqd", weight.astype(jnp.bfloat16), values, preferred_element_type=jnp.float32
    )
    heads = (summed / total).astype(jnp.bfloat16)
    heads = heads.transpose(1, 0, 2).reshape(MB, heads_here * HD)
    head_terms = jnp.dot(heads, proj_out, preferred_element_type=jnp.float32).astype(jnp.bfloat16)

    terms = head_terms.reshape(ny, nz, nc, tok_rows, -1)
    keep_c = lax.dynamic_index_in_dim(terms, ci, 2, keepdims=False)
    give_c = lax.dynamic_index_in_dim(terms, 1 - ci, 2, keepdims=False)
    part_c = keep_c.astype(jnp.float32) + swap(give_c, "core").astype(jnp.float32)
    part_y = lax.all_to_all(part_c.astype(jnp.bfloat16), "y", 0, 0, tiled=True)
    part_y = jnp.sum(part_y.astype(jnp.float32), axis=0)
    keep_z = lax.dynamic_index_in_dim(part_y, zi, 0, keepdims=False)
    give_z = lax.dynamic_index_in_dim(part_y, 1 - zi, 0, keepdims=False)
    attended = keep_z + swap(give_z.astype(jnp.bfloat16), "zh").astype(jnp.float32)

    middle = residual.astype(jnp.float32) + attended
    normed = (
        middle * lax.rsqrt(jnp.mean(middle * middle, axis=1, keepdims=True) + 1e-06) * gain
    ).astype(jnp.bfloat16)

    split = FF // gate_w.shape[1]
    experts_count = devices // split
    chosen = lax.dynamic_slice_in_dim(routes[0], my_index * tok_rows, tok_rows, 0)
    scores_in = lax.dynamic_slice_in_dim(gate_scores[0], my_index * tok_rows, tok_rows, 0)
    onehot = chosen[:, :, None] == jnp.arange(experts_count, dtype=jnp.int32)[None, None, :]
    share = jnp.sum(jnp.where(onehot, scores_in[:, :, None], 0.0), axis=1) / jnp.sum(
        scores_in, axis=1, keepdims=True
    )
    routed = jnp.any(onehot, axis=1)
    slot = jnp.cumsum(routed.astype(jnp.int32), axis=0) - 1
    select = routed[None] & (slot[None] == jnp.arange(CAP)[:, None, None])
    select = select.transpose(2, 0, 1)
    dispatch = jnp.einsum(
        "xjt,td->xjd", select.astype(jnp.bfloat16), normed, preferred_element_type=jnp.float32
    ).astype(jnp.bfloat16)

    rows_y = lax.all_to_all(dispatch, "y", 0, 0, tiled=True)
    rows_z = jnp.stack([rows_y, swap(rows_y, "zh")])
    rows_c = jnp.stack([rows_z, swap(rows_z, "core")])
    flat = rows_c.reshape(-1, rows_c.shape[-1])
    gate = jnp.dot(flat, gate_w, preferred_element_type=jnp.float32)
    upper = jnp.dot(flat, up_w, preferred_element_type=jnp.float32)
    activated = (jax.nn.silu(gate) * upper).astype(jnp.bfloat16)
    computed = (
        jnp.dot(activated, down_w, preferred_element_type=jnp.float32)
        .astype(jnp.bfloat16)
        .reshape(rows_c.shape)
    )

    back_c = computed[0].astype(jnp.float32) + swap(computed[1], "core").astype(jnp.float32)
    back_c = back_c.astype(jnp.bfloat16)
    back_z = back_c[0].astype(jnp.float32) + swap(back_c[1], "zh").astype(jnp.float32)
    picked = lax.all_to_all(back_z.astype(jnp.bfloat16), "y", 0, 0, tiled=True)
    combine = select.transpose(2, 0, 1).astype(jnp.float32) * share[:, :, None]
    mixed = jnp.einsum(
        "txj,xjd->td", combine, picked.astype(jnp.float32), precision=lax.Precision.HIGHEST
    )
    layer_out = (middle + mixed).astype(jnp.bfloat16)
    return shifted(layer_out[None], "section", 1)


def solution(mesh):
    sizes = (mesh.shape["section"], 4, 2, 2)
    sub = Mesh(mesh.devices.reshape(sizes), ("section",) + EXPERT_AXES)
    ex = EXPERT_AXES
    return jax.shard_map(
        body,
        mesh=sub,
        in_specs=(
            P("section", ex, None),
            P("section", None, ex),
            P("section", ex, None),
            P("section", ex, None),
            P("section", None),
            P("section", None, ex),
            P("section", None, ex),
            P("section", ex, None),
            P("section", None, None),
            P("section", None, None),
        ),
        out_specs=P("section", ex, None),
        check_vma=False,
    )
```

time: 326 us -> 240 us (0.74)
  waiting for transfers between devices: 221 us -> 110 us
  blocking collectives: 58.2 us -> 10.6 us
  starting transfers between devices: 4.88 us -> 41.4 us
  other arithmetic: 3.66 us -> 33.8 us
  local copies, waits for them, and re-layouts: 3.1 us -> 19.9 us
  between operations: 13.6 us -> 0.24 us
    reduce_scatter x1 -> x0, waiting for transfers between devices: 82.8 us -> none  [body(): lax.psum_scatter(jnp.dot(heads, proj_out, preferred_element_type=jnp.floa...]
    all_gather x1 -> x0, waiting for transfers between devices: 81.5 us -> none  [body(): piece = lax.all_gather(keyvals[0], 'expert', axis=0, tiled=True)]
    ppermute x0 -> x8, waiting for transfers between devices: none -> 72.8 us  [swap(): return lax.ppermute(block, axis, [(0, 1), (1, 0)])]
    all_to_all x1, blocking collectives: 58.2 us -> 10.6 us  [body(): rows_y = lax.all_to_all(dispatch, 'y', 0, 0, tiled=True)]
    ppermute x0 -> x8, starting transfers between devices: none -> 23.2 us  [swap(): return lax.ppermute(block, axis, [(0, 1), (1, 0)])]
    all_to_all x1 -> x3, waiting for transfers between devices: 50.3 us -> 35 us  [the longest x1 15.5 us: body(): part_y = lax.all_to_all(part_c.astype(jnp.bfloat16), 'y', 0, 0, tiled=True)]
    sub x0 -> x2, other arithmetic: none -> 11.9 us  [the longest x1 11.9 us: body(): weight = jnp.where(visible[None], jnp.exp(score - top), 0.0)]
    all_to_all x1 -> x3, starting transfers between devices: 4.76 us -> 13.1 us  [the longest x1 4.59 us: body(): kv_y = lax.all_to_all(send_kv, 'y', 0, 0, tiled=True)]
  transfers between devices with their start and end apart: 4 -> 12, of which waited for: 4 -> 11; matrix products, arithmetic and copies ran while one was open for 0% -> 2% of each run, Pallas kernels for 0% -> 0%
where the time goes in v1:
time: 240 us; the launch traced here: 237 us
  waiting for transfers between devices  110 us (46%)
  starting transfers between devices  41.4 us (17%)
  other arithmetic  33.8 us (14%)
  matrix products  20.8 us (9%)
  local copies, waits for them, and re-layouts  19.9 us (8%)
  blocking collectives  10.6 us (4%)
    ppermute x8, waiting for transfers between devices, swap(): return lax.ppermute(block, axis, [(0, 1), (1, 0)])  72.8 us
    ppermute x8, starting transfers between devices, swap(): return lax.ppermute(block, axis, [(0, 1), (1, 0)])  23.2 us
    all_to_all x1, waiting for transfers between devices, body(): part_y = lax.all_to_all(part_c.astype(jnp.bfloat16), 'y', 0, 0, tiled=True)  15.5 us
    sub x1, other arithmetic, body(): weight = jnp.where(visible[None], jnp.exp(score - top), 0.0)  11.9 us
    all_to_all x1, blocking collectives, body(): rows_y = lax.all_to_all(dispatch, 'y', 0, 0, tiled=True)  10.6 us
    all_to_all x1, waiting for transfers between devices, body(): picked = lax.all_to_all(back_z.astype(jnp.bfloat16), 'y', 0, 0, tiled=True)  9.9 us
    all_to_all x1, waiting for transfers between devices, body(): kv_y = lax.all_to_all(send_kv, 'y', 0, 0, tiled=True)  9.58 us
    dot_general x1, matrix products, body(): jnp.dot(activated, down_w, preferred_element_type=jnp.float32)  5.45 us
  transfers between devices with their start and end apart: 12, of which 11 were waited for; matrix products, arithmetic and copies ran while one was open for 2% of the time, Pallas kernels for 0%

profile of v1, /device:TPU:32, one launch (start us, length us, event | category | flops | bytes accessed | tf_op | source)
XLA Modules:
  0.0 237.0 jit_solution(12845686551066527088)
XLA Ops:
  0.0 1.2 reshape_squeeze.6
  1.2 0.4 fusion.75
  1.6 0.9 pad_maximum_fusion.4
  2.5 4.6 %all-to-all-start = ((bf16[4,256,256]{2,1,0:T(8,128)(2,1)}), bf16[4,256,256]{2,1,0:T(8,128)(2,1)}, u32[]{:S(2)}, u32[]{:S(2)}) async-start(bf16[4,256,256]{2,1,0:T(8,128)(2,1)} %pad_maximum_fusion.4), calls=%async_computation | async-start | bytes 1048576 | tf_op jit(solution)/shard_map/all_to_all | solution.py:55
  7.0 9.6 %all-to-all-done = bf16[4,256,256]{2,1,0:T(8,128)(2,1)} async-done(((bf16[4,256,256]{2,1,0:T(8,128)(2,1)}), bf16[4,256,256]{2,1,0:T(8,128)(2,1)}, u32[]{:S(2)}, u32[]{:S(2)}) %all-to-all-start) | async-done | bytes 524320 | tf_op jit(solution)/shard_map/all_to_all | solution.py:55
  16.6 6.3 %collective-permute-start = (bf16[4,256,256]{2,1,0:T(8,128)(2,1)}, bf16[4,256,256]{2,1,0:T(8,128)(2,1)S(1)}, u32[]{:S(2)}, u32[]{:S(2)}) collective-permute-start(bf16[4,256,256]{2,1,0:T(8,128)(2,1)} %all-to-all-done), channel_id=1, source_target_pairs={{0,2},{2,0},{1,3},{3,1},{4,6},{6,4},{5,7},{7,5},{8,10},{10,8},{9,1... | collective-permute-start | bytes 1572872 | tf_op jit(solution)/shard_map/ppermute | solution.py:26
  22.9 0.1 add_multiply_fusion.1
  23.0 0.1 add_multiply_fusion
  23.1 21.9 %collective-permute-done = bf16[4,256,256]{2,1,0:T(8,128)(2,1)S(1)} collective-permute-done((bf16[4,256,256]{2,1,0:T(8,128)(2,1)}, bf16[4,256,256]{2,1,0:T(8,128)(2,1)S(1)}, u32[]{:S(2)}, u32[]{:S(2)}) %collective-permute-start) | collective-permute-done | bytes 524320 | tf_op jit(solution)/shard_map/ppermute | solution.py:26
  45.0 2.5 %fusion.73 = (bf16[1,2,4,256,256]{4,3,2,1,0:T(8,128)(2,1)}, bf16[2,4,256,256]{3,2,1,0:T(8,128)(2,1)}) fusion(bf16[1,4,256,256]{3,2,1,0:T(8,128)(2,1)S(1)} %bitcast.124, bf16[1,4,256,256]{3,2,1,0:T(8,128)(2,1)} %bitcast.3), kind=kLoop, calls=%fused_computation.104 | loop fusion | flops 524288 | bytes 3145728 | tf_op jit(solution)/shard_map/stack | solution.py:57
  47.6 1.9 broadcast_compare_fusion
  49.5 1.0 collective-permute-done.1
  50.5 1.7 pad_maximum_fusion
  52.2 4.5 %fusion.35 = f32[4096,2,256]{2,0,1:T(8,128)} fusion(bf16[4096,256]{1,0:T(8,128)(2,1)S(1)} %bitcast.120, bf16[256,2,128]{2,1,0:T(2,128)(2,1)S(1)} %reshape_squeeze.7), kind=kOutput, calls=%fused_computation.39 | convolution fusion | flops 536870912 | bytes 9568256 | tf_op jit(solution)/shard_map/hqd,kd->hqk/dot_general | solution.py:70
  56.7 11.9 %fusion.76 = (f32[2,256]{1,0:T(2,128)S(1)}, bf16[2,256,4096]{1,2,0:T(8,128)(2,1)}) fusion(f32[4096,2,256]{2,0,1:T(8,128)} %fusion.35, pred[256,4096]{0,1:T(8,128)(4,1)S(1)} %broadcast_compare_fusion), kind=kOutput, calls=%fused_computation.107 | output fusion | flops 14684159 | bytes 13633536 | tf_op jit(solution)/shard_map/sub | solution.py:72
  68.6 3.2 %fusion.32 = bf16[256,2,128]{0,2,1:T(8,128)(2,1)S(1)} fusion(bf16[2,256,4096]{1,2,0:T(8,128)(2,1)} %get-tuple-element.20, bf16[4096,256]{1,0:T(8,128)(2,1)S(1)} %bitcast.121, f32[256,2]{0,1:T(2,128)S(1)} %bitcast.131), kind=kOutput, calls=%fused_computation.36 | convolution fusion | flops 537001984 | bytes 5376000 | tf_op jit(solution)/shard_map/hqk,kd->hqd/dot_general | solution.py:74
  71.7 0.7 convolution_convert_fusion
  72.5 1.3 copy-done.1
  73.8 1.1 dynamic-slice_bitcast_fusion
  74.9 0.1 collective-permute-start.2
  75.0 2.9 %collective-permute-done.2 = bf16[4,2,16,4096]{3,2,1,0:T(8,128)(2,1)} collective-permute-done((bf16[4,2,16,4096]{3,2,1,0:T(8,128)(2,1)}, bf16[4,2,16,4096]{3,2,1,0:T(8,128)(2,1)}, u32[]{:S(2)}, u32[]{:S(2)}) %collective-permute-start.2) | collective-permute-done | bytes 1048608 | tf_op jit(solution)/shard_map/ppermute | solution.py:26
  77.9 2.8 %fusion.18 = bf16[4,2,16,4096]{3,2,1,0:T(8,128)(2,1)} fusion(bf16[4,2,16,4096]{3,2,1,0:T(8,128)(2,1)} %collective-permute-done.2, bf16[4,2,2,16,4096]{4,3,2,1,0:T(8,128)(2,1)} %bitcast.119, s32[]{:T(128)S(6)} %select_n.48), kind=kLoop, calls=%fused_computation.27 | loop fusion | flops 2097152 | bytes 3145732 | tf_op jit(solution)/shard_map/convert_element_type | solution.py:85
  80.7 4.4 %all-to-all-start.1 = ((bf16[4,2,16,4096]{3,2,1,0:T(8,128)(2,1)}), bf16[4,2,16,4096]{3,2,1,0:T(8,128)(2,1)}, u32[]{:S(2)}, u32[]{:S(2)}) async-start(bf16[4,2,16,4096]{3,2,1,0:T(8,128)(2,1)} %fusion.18), calls=%async_computation.1 | async-start | bytes 2097152 | tf_op jit(solution)/shard_map/all_to_all | solution.py:85
  85.1 0.1 fusion.64
  85.2 0.1 copy.53
  85.3 15.5 %all-to-all-done.1 = bf16[4,2,16,4096]{3,2,1,0:T(8,128)(2,1)} async-done(((bf16[4,2,16,4096]{3,2,1,0:T(8,128)(2,1)}), bf16[4,2,16,4096]{3,2,1,0:T(8,128)(2,1)}, u32[]{:S(2)}, u32[]{:S(2)}) %all-to-all-start.1) | async-done | bytes 1048608 | tf_op jit(solution)/shard_map/all_to_all | solution.py:85
  100.8 1.4 convert_reduce_fusion
  102.2 0.8 copy-done.4
  103.0 5.8 %collective-permute-start.3 = (bf16[16,4096]{1,0:T(8,128)(2,1)S(1)}, bf16[16,4096]{1,0:T(8,128)(2,1)}, u32[]{:S(2)}, u32[]{:S(2)}) collective-permute-start(bf16[16,4096]{1,0:T(8,128)(2,1)S(1)} %fusion.45), channel_id=1, source_target_pairs={{0,2},{2,0},{1,3},{3,1},{4,6},{6,4},{5,7},{7,5},{8,10},{10,8},{9,1... | collective-permute-start | bytes 393224 | tf_op jit(solution)/shard_map/ppermute | solution.py:26
  108.8 0.1 copy.55
  108.9 3.4 %collective-permute-done.3 = bf16[16,4096]{1,0:T(8,128)(2,1)} collective-permute-done((bf16[16,4096]{1,0:T(8,128)(2,1)S(1)}, bf16[16,4096]{1,0:T(8,128)(2,1)}, u32[]{:S(2)}, u32[]{:S(2)}) %collective-permute-start.3) | collective-permute-done | bytes 131104 | tf_op jit(solution)/shard_map/ppermute | solution.py:26
  112.3 1.2 multiply_reduce_fusion
  113.5 1.1 convolution_convert_fusion.2
  114.6 10.6 %all_to_all.20 = bf16[4,12,4096]{2,1,0:T(8,128)(2,1)S(1)} all-to-all(bf16[4,12,4096]{2,1,0:T(8,128)(2,1)S(1)} %convolution_convert_fusion.2), channel_id=1, replica_groups=mesh['section'=16,'y'=4,'zh'=2,'core'=2] {'y'}, dimensions={0} | all-to-all | bytes 786432 | tf_op jit(solution)/shard_map/all_to_all | solution.py:112
  125.1 5.4 %collective-permute-start.4 = (bf16[4,12,4096]{2,1,0:T(8,128)(2,1)S(1)}, bf16[4,12,4096]{2,1,0:T(8,128)(2,1)S(1)}, u32[]{:S(2)}, u32[]{:S(2)}) collective-permute-start(bf16[4,12,4096]{2,1,0:T(8,128)(2,1)S(1)} %all_to_all.20), channel_id=1, source_target_pairs={{0,2},{2,0},{1,3},{3,1},{4,6},{6,4},{5,7},{7,5},{8,10},{10,8},{9,1... | collective-permute-start | bytes 1179656 | tf_op jit(solution)/shard_map/ppermute | solution.py:26
  130.6 17.4 %collective-permute-done.4 = bf16[4,12,4096]{2,1,0:T(8,128)(2,1)S(1)} collective-permute-done((bf16[4,12,4096]{2,1,0:T(8,128)(2,1)S(1)}, bf16[4,12,4096]{2,1,0:T(8,128)(2,1)S(1)}, u32[]{:S(2)}, u32[]{:S(2)}) %collective-permute-start.4) | collective-permute-done | bytes 393248 | tf_op jit(solution)/shard_map/ppermute | solution.py:26
  148.0 0.2 fusion.72
  148.1 0.6 copy.56
  148.7 0.1 collective-permute-start.5
  148.8 2.3 collective-permute-done.5
  151.1 0.4 copy.74
  151.6 1.6 pad_maximum_fusion.1
  153.2 3.6 %reshape.170 = bf16[192,4096]{1,0:T(8,128)(2,1)} reshape(bf16[2,2,4,12,4096]{4,3,2,1,0:T(8,128)(2,1)} %pad_maximum_fusion.1) | data formatting | bytes 3145728 | tf_op jit(solution)/shard_map/reshape | solution.py:115
  156.8 4.1 %fusion.16 = f32[192,384]{1,0:T(8,128)} fusion(bf16[192,4096]{1,0:T(8,128)(2,1)} %reshape.170, bf16[1,4096,384]{2,1,0:T(8,128)(2,1)} %param.15), kind=kOutput, calls=%fused_computation.22 | convolution fusion | flops 603979776 | bytes 5013504 | tf_op jit(solution)/shard_map/dot_general | solution.py:116
  160.9 5.5 %convolution_convert_fusion.1 = bf16[192,4096]{1,0:T(8,128)(2,1)} fusion(bf16[1,384,4096]{2,1,0:T(8,128)(2,1)S(1)} %copy-done, bf16[192,4096]{1,0:T(8,128)(2,1)} %reshape.170, bf16[1,4096,384]{2,1,0:T(8,128)(2,1)} %param.16, f32[192,384]{1,0:T(8,128)} %fusion.16), kind=kOutput, calls=%fused_computation.8 | convolution fusion | flops 1209188352 | bytes 9732096 | tf_op jit(solution)/shard_map/dot_general | solution.py:120
  166.3 3.0 %fusion.74 = (bf16[96,4096]{1,0:T(8,128)(2,1)}, f32[96,4096]{1,0:T(8,128)}) fusion(bf16[192,4096]{1,0:T(8,128)(2,1)} %convolution_convert_fusion.1), kind=kLoop, calls=%fused_computation.105 | loop fusion | flops 393216 | bytes 3932160 | tf_op jit(solution)/shard_map/slice | solution.py:125
  169.3 2.2 squeeze.39
  171.5 2.7 %copy.58 = bf16[2,4,12,4096]{3,1,2,0:T(4,128)(2,1)} copy(bf16[2,4,12,4096]{3,2,1,0:T(8,128)(2,1)} %squeeze.39) | data formatting | bytes 1572864 | tf_op jit(solution)/shard_map/squeeze | solution.py:125
  174.2 0.1 collective-permute-start.6
  174.3 2.7 %reshape.173 = f32[2,4,12,4096]{3,2,1,0:T(8,128)} reshape(f32[96,4096]{1,0:T(8,128)} %get-tuple-element.8) | data formatting | bytes 3145728 | tf_op jit(solution)/shard_map/convert_element_type | solution.py:125
  177.0 2.3 add_convert_fusion
  179.4 1.0 copy-done.2
  180.3 0.8 slice_bitcast_fusion.4
  181.2 5.4 %collective-permute-start.7 = (bf16[4,12,4096]{2,1,0:T(8,128)(2,1)}, bf16[4,12,4096]{2,1,0:T(8,128)(2,1)}, u32[]{:S(2)}, u32[]{:S(2)}) collective-permute-start(bf16[4,12,4096]{2,1,0:T(8,128)(2,1)} %slice_bitcast_fusion.4), channel_id=1, source_target_pairs={{0,2},{2,0},{1,3},{3,1},{4,6},{6,4},{5,7},{7,5},{8,10},{10,8},{9,1... | collective-permute-start | bytes 1179656 | tf_op jit(solution)/shard_map/ppermute | solution.py:26
  186.5 0.1 fusion.65
  186.6 0.1 copy.54
  186.7 24.0 %collective-permute-done.7 = bf16[4,12,4096]{2,1,0:T(8,128)(2,1)} collective-permute-done((bf16[4,12,4096]{2,1,0:T(8,128)(2,1)}, bf16[4,12,4096]{2,1,0:T(8,128)(2,1)}, u32[]{:S(2)}, u32[]{:S(2)}) %collective-permute-start.7) | collective-permute-done | bytes 393248 | tf_op jit(solution)/shard_map/ppermute | solution.py:26
  210.7 2.1 fusion.36
  212.9 4.1 %all-to-all-start.3 = ((bf16[4,12,4096]{2,1,0:T(8,128)(2,1)}), bf16[4,12,4096]{2,1,0:T(8,128)(2,1)}, u32[]{:S(2)}, u32[]{:S(2)}) async-start(bf16[4,12,4096]{2,1,0:T(8,128)(2,1)} %fusion.36), calls=%async_computation.3 | async-start | bytes 1048576 | tf_op jit(solution)/shard_map/all_to_all | solution.py:128
  217.0 9.9 %all-to-all-done.3 = bf16[4,12,4096]{2,1,0:T(8,128)(2,1)} async-done(((bf16[4,12,4096]{2,1,0:T(8,128)(2,1)}), bf16[4,12,4096]{2,1,0:T(8,128)(2,1)}, u32[]{:S(2)}, u32[]{:S(2)}) %all-to-all-start.3) | async-done | bytes 393248 | tf_op jit(solution)/shard_map/all_to_all | solution.py:128
  226.9 1.8 fusion.7
  228.7 5.1 %collective-permute-start.8 = (bf16[1,16,4096]{2,1,0:T(8,128)(2,1)S(1)}, bf16[1,16,4096]{2,1,0:T(8,128)(2,1)S(1)}, u32[]{:S(2)}, u32[]{:S(2)}) collective-permute-start(bf16[1,16,4096]{2,1,0:T(8,128)(2,1)S(1)} %fusion.7), channel_id=1, source_target_pairs={{240,0},{0,16},{16,32},{32,48},{48,64},{64,80},{80,96},{96,112},{1... | collective-permute-start | bytes 393224 | tf_op jit(solution)/shard_map/ppermute | solution.py:22
  233.8 2.5 %collective-permute-done.8 = bf16[1,16,4096]{2,1,0:T(8,128)(2,1)S(1)} collective-permute-done((bf16[1,16,4096]{2,1,0:T(8,128)(2,1)S(1)}, bf16[1,16,4096]{2,1,0:T(8,128)(2,1)S(1)}, u32[]{:S(2)}, u32[]{:S(2)}) %collective-permute-start.8) | collective-permute-done | bytes 131104 | tf_op jit(solution)/shard_map/ppermute | solution.py:22
  236.3 0.7 copy.76
  (36 shorter events, 0.3 us)
Async XLA Ops:
  0.0 160.9 %copy-start = (bf16[1,384,4096]{2,1,0:T(8,128)(2,1)S(1)}, bf16[1,384,4096]{2,1,0:T(8,128)(2,1)}, u32[]{:S(2)}) copy-start(bf16[1,384,4096]{2,1,0:T(8,128)(2,1)} %param.17) | copy-start | bytes 9437188
  2.4 45.1 %copy-start.5 = (bf16[1,256,256]{2,1,0:T(8,128)(2,1)S(1)}, bf16[1,256,256]{2,1,0:T(8,128)(2,1)}, u32[]{:S(2)}) copy-start(bf16[1,256,256]{2,1,0:T(8,128)(2,1)} %param.11) | copy-start | bytes 393220
  2.5 14.2 %all-to-all-start = ((bf16[4,256,256]{2,1,0:T(8,128)(2,1)}), bf16[4,256,256]{2,1,0:T(8,128)(2,1)}, u32[]{:S(2)}, u32[]{:S(2)}) async-start(bf16[4,256,256]{2,1,0:T(8,128)(2,1)} %pad_maximum_fusion.4), calls=%async_computation | async-start | bytes 1048576 | tf_op jit(solution)/shard_map/all_to_all | solution.py:55
  16.6 28.4 %collective-permute-start = (bf16[4,256,256]{2,1,0:T(8,128)(2,1)}, bf16[4,256,256]{2,1,0:T(8,128)(2,1)S(1)}, u32[]{:S(2)}, u32[]{:S(2)}) collective-permute-start(bf16[4,256,256]{2,1,0:T(8,128)(2,1)} %all-to-all-done), channel_id=1, source_target_pairs={{0,2},{2,0},{1,3},{3,1},{4,6},{6,4},{5,7},{7,5},{8,10},{10,8},{9,1... | collective-permute-start | bytes 1572872 | tf_op jit(solution)/shard_map/ppermute | solution.py:26
  47.5 3.0 %collective-permute-start.1 = (bf16[2,4,256,256]{3,2,1,0:T(8,128)(2,1)}, bf16[2,4,256,256]{3,2,1,0:T(8,128)(2,1)}, u32[]{:S(2)}, u32[]{:S(2)}) collective-permute-start(bf16[2,4,256,256]{3,2,1,0:T(8,128)(2,1)} %get-tuple-element.12), channel_id=1, source_target_pairs={{0,1},{1,0},{2,3},{3,2},{4,5},{5,4},{6,7},{7,6},{8,9},{9,8},{10,11... | collective-permute-start | bytes 3145736 | tf_op jit(solution)/shard_map/ppermute | solution.py:26
  68.6 3.2 %copy-start.3 = (bf16[1,256,4096]{2,1,0:T(8,128)(2,1)S(1)}, bf16[1,256,4096]{2,1,0:T(8,128)(2,1)}, u32[]{:S(2)}) copy-start(bf16[1,256,4096]{2,1,0:T(8,128)(2,1)} %param.13) | copy-start | bytes 6291460
  72.5 1.3 copy-start.1
  74.9 3.0 %collective-permute-start.2 = (bf16[4,2,16,4096]{3,2,1,0:T(8,128)(2,1)}, bf16[4,2,16,4096]{3,2,1,0:T(8,128)(2,1)}, u32[]{:S(2)}, u32[]{:S(2)}) collective-permute-start(bf16[4,2,16,4096]{3,2,1,0:T(8,128)(2,1)} %dynamic-slice_bitcast_fusion), channel_id=1, source_target_pairs={{0,1},{1,0},{2,3},{3,2},{4,5},{5,4},{6,7},{7,6},{8,9},{9,8},{10,11... | collective-permute-start | bytes 3145736 | tf_op jit(solution)/shard_map/ppermute | solution.py:26
  75.0 10.1 %copy-start.10 = (s32[1,256,2]{1,2,0:T(2,128)S(1)}, s32[1,256,2]{1,2,0:T(2,128)}, u32[]{:S(2)}) copy-start(s32[1,256,2]{1,2,0:T(2,128)} %param.18) | copy-start | bytes 6148
  80.7 31.6 %copy-start.6 = (bf16[1,16,4096]{2,1,0:T(8,128)(2,1)S(1)}, bf16[1,16,4096]{2,1,0:T(8,128)(2,1)}, u32[]{:S(2)}) copy-start(bf16[1,16,4096]{2,1,0:T(8,128)(2,1)} %param.10) | copy-start | bytes 393220
  80.7 20.1 %all-to-all-start.1 = ((bf16[4,2,16,4096]{3,2,1,0:T(8,128)(2,1)}), bf16[4,2,16,4096]{3,2,1,0:T(8,128)(2,1)}, u32[]{:S(2)}, u32[]{:S(2)}) async-start(bf16[4,2,16,4096]{3,2,1,0:T(8,128)(2,1)} %fusion.18), calls=%async_computation.1 | async-start | bytes 2097152 | tf_op jit(solution)/shard_map/all_to_all | solution.py:85
  85.1 17.9 %copy-start.7 = (s32[16,2]{0,1:T(2,128)}, s32[16,2]{0,1:T(2,128)S(1)}, u32[]{:S(2)}) copy-start(s32[16,2]{0,1:T(2,128)S(1)} %fusion.64) | copy-start | bytes 388
  102.2 0.8 copy-start.4
  103.0 9.2 %collective-permute-start.3 = (bf16[16,4096]{1,0:T(8,128)(2,1)S(1)}, bf16[16,4096]{1,0:T(8,128)(2,1)}, u32[]{:S(2)}, u32[]{:S(2)}) collective-permute-start(bf16[16,4096]{1,0:T(8,128)(2,1)S(1)} %fusion.45), channel_id=1, source_target_pairs={{0,2},{2,0},{1,3},{3,1},{4,6},{6,4},{5,7},{7,5},{8,10},{10,8},{9,1... | collective-permute-start | bytes 393224 | tf_op jit(solution)/shard_map/ppermute | solution.py:26
  125.1 22.9 %collective-permute-start.4 = (bf16[4,12,4096]{2,1,0:T(8,128)(2,1)S(1)}, bf16[4,12,4096]{2,1,0:T(8,128)(2,1)S(1)}, u32[]{:S(2)}, u32[]{:S(2)}) collective-permute-start(bf16[4,12,4096]{2,1,0:T(8,128)(2,1)S(1)} %all_to_all.20), channel_id=1, source_target_pairs={{0,2},{2,0},{1,3},{3,1},{4,6},{6,4},{5,7},{7,5},{8,10},{10,8},{9,1... | collective-permute-start | bytes 1179656 | tf_op jit(solution)/shard_map/ppermute | solution.py:26
  148.7 2.4 %collective-permute-start.5 = (bf16[2,4,12,4096]{3,1,2,0:T(4,128)(2,1)S(1)}, bf16[2,4,12,4096]{3,1,2,0:T(4,128)(2,1)S(1)}, u32[]{:S(2)}, u32[]{:S(2)}) collective-permute-start(bf16[2,4,12,4096]{3,1,2,0:T(4,128)(2,1)S(1)} %copy.56), channel_id=1, source_target_pairs={{0,1},{1,0},{2,3},{3,2},{4,5},{5,4},{6,7},{7,6},{8,9},{9,8},{10,11... | collective-permute-start | bytes 2359304 | tf_op jit(solution)/shard_map/ppermute | solution.py:26
  174.2 2.9 %collective-permute-start.6 = (bf16[2,4,12,4096]{3,1,2,0:T(4,128)(2,1)}, bf16[2,4,12,4096]{3,1,2,0:T(4,128)(2,1)}, u32[]{:S(2)}, u32[]{:S(2)}) collective-permute-start(bf16[2,4,12,4096]{3,1,2,0:T(4,128)(2,1)} %copy.58), channel_id=1, source_target_pairs={{0,1},{1,0},{2,3},{3,2},{4,5},{5,4},{6,7},{7,6},{8,9},{9,8},{10,11... | collective-permute-start | bytes 2359304 | tf_op jit(solution)/shard_map/ppermute | solution.py:26
  177.0 9.5 %copy-start.9 = (f32[1,256,2]{1,2,0:T(2,128)S(1)}, f32[1,256,2]{1,2,0:T(2,128)}, u32[]{:S(2)}) copy-start(f32[1,256,2]{1,2,0:T(2,128)} %param.19) | copy-start | bytes 6148
  179.4 1.0 copy-start.2
  180.3 36.7 %copy-start.8 = (s32[16,2]{0,1:T(2,128)S(1)}, s32[16,2]{0,1:T(2,128)}, u32[]{:S(2)}) copy-start(s32[16,2]{0,1:T(2,128)} %copy-done.7) | copy-start | bytes 388
  181.2 29.6 %collective-permute-start.7 = (bf16[4,12,4096]{2,1,0:T(8,128)(2,1)}, bf16[4,12,4096]{2,1,0:T(8,128)(2,1)}, u32[]{:S(2)}, u32[]{:S(2)}) collective-permute-start(bf16[4,12,4096]{2,1,0:T(8,128)(2,1)} %slice_bitcast_fusion.4), channel_id=1, source_target_pairs={{0,2},{2,0},{1,3},{3,1},{4,6},{6,4},{5,7},{7,5},{8,10},{10,8},{9,1... | collective-permute-start | bytes 1179656 | tf_op jit(solution)/shard_map/ppermute | solution.py:26
  212.9 14.1 %all-to-all-start.3 = ((bf16[4,12,4096]{2,1,0:T(8,128)(2,1)}), bf16[4,12,4096]{2,1,0:T(8,128)(2,1)}, u32[]{:S(2)}, u32[]{:S(2)}) async-start(bf16[4,12,4096]{2,1,0:T(8,128)(2,1)} %fusion.36), calls=%async_computation.3 | async-start | bytes 1048576 | tf_op jit(solution)/shard_map/all_to_all | solution.py:128
  228.7 7.6 %collective-permute-start.8 = (bf16[1,16,4096]{2,1,0:T(8,128)(2,1)S(1)}, bf16[1,16,4096]{2,1,0:T(8,128)(2,1)S(1)}, u32[]{:S(2)}, u32[]{:S(2)}) collective-permute-start(bf16[1,16,4096]{2,1,0:T(8,128)(2,1)S(1)} %fusion.7), channel_id=1, source_target_pairs={{240,0},{0,16},{16,32},{32,48},{48,64},{64,80},{80,96},{96,112},{1... | collective-permute-start | bytes 393224 | tf_op jit(solution)/shard_map/ppermute | solution.py:22

commit v2 on v1

--- a/solution.py
+++ b/solution.py
@@ -53,20 +53,18 @@
     head_of_y = [y * rows_per_y // group for y in range(ny)]
     send_kv = jnp.stack([kv[:, h] for h in head_of_y])
     kv_y = lax.all_to_all(send_kv, "y", 0, 0, tiled=True)
-    kv_z = jnp.stack([kv_y, swap(kv_y, "zh")])
-    kv_c = jnp.stack([kv_z, swap(kv_z, "core")])
-    piece = kv_c.reshape(-1, 2 * HD)
-    src_c = jnp.where(jnp.arange(2) == 0, ci, 1 - ci)[:, None, None]
-    src_z = jnp.where(jnp.arange(2) == 0, zi, 1 - zi)[None, :, None]
-    src_y = jnp.arange(ny)[None, None, :]
-    src_block = (src_y * nz + src_z) * nc + src_c
-    key_pos = (src_block[..., None] * block + jnp.arange(block)[None, None, None, :]).reshape(-1)
+    piece = jnp.stack([kv_y, swap(kv_y, "core")]).reshape(-1, 2 * HD)
+    src_c = jnp.where(jnp.arange(2) == 0, ci, 1 - ci)[:, None]
+    src_y = jnp.arange(ny)[None, :]
+    src_block = (src_y * nz + zi) * nc + src_c
+    key_pos = (src_block[..., None] * block + jnp.arange(block)[None, None, :]).reshape(-1)
     query_pos = CTX - MB + jnp.arange(MB, dtype=jnp.int32)
     visible = key_pos[None, :] <= query_pos[:, None]
 
+    mine = query_all.reshape(MB, heads_here, HD).transpose(1, 0, 2)
+    query = jnp.concatenate([mine, swap(mine, "zh")])
     keys = piece[:, :HD]
     values = piece[:, HD:]
-    query = query_all.reshape(MB, heads_here, HD).transpose(1, 0, 2)
     score = jnp.einsum("hqd,kd->hqk", query, keys, preferred_element_type=jnp.float32) * scale
     top = jnp.max(jnp.where(visible[None], score, -1e30), axis=2, keepdims=True)
     weight = jnp.where(visible[None], jnp.exp(score - top), 0.0)
@@ -74,7 +72,18 @@
     summed = jnp.einsum(
         "hqk,kd->hqd", weight.astype(jnp.bfloat16), values, preferred_element_type=jnp.float32
     )
-    heads = (summed / total).astype(jnp.bfloat16)
+    stats = jnp.concatenate([top, total], axis=2)
+    far_sum, far_stats = swap(
+        (summed[heads_here:].astype(jnp.bfloat16), stats[heads_here:]), "zh"
+    )
+    near_top = top[:heads_here]
+    far_top = far_stats[:, :, 0:1]
+    both_top = jnp.maximum(near_top, far_top)
+    near_factor = jnp.exp(near_top - both_top)
+    far_factor = jnp.exp(far_top - both_top)
+    both_total = total[:heads_here] * near_factor + far_stats[:, :, 1:2] * far_factor
+    both_sum = summed[:heads_here] * near_factor + far_sum.astype(jnp.float32) * far_factor
+    heads = (both_sum / both_total).astype(jnp.bfloat16)
     heads = heads.transpose(1, 0, 2).reshape(MB, heads_here * HD)
     head_terms = jnp.dot(heads, proj_out, preferred_element_type=jnp.float32).astype(jnp.bfloat16)
 
@@ -110,22 +119,25 @@
     ).astype(jnp.bfloat16)
 
     rows_y = lax.all_to_all(dispatch, "y", 0, 0, tiled=True)
-    rows_z = jnp.stack([rows_y, swap(rows_y, "zh")])
-    rows_c = jnp.stack([rows_z, swap(rows_z, "core")])
-    flat = rows_c.reshape(-1, rows_c.shape[-1])
-    gate = jnp.dot(flat, gate_w, preferred_element_type=jnp.float32)
-    upper = jnp.dot(flat, up_w, preferred_element_type=jnp.float32)
-    activated = (jax.nn.silu(gate) * upper).astype(jnp.bfloat16)
-    computed = (
-        jnp.dot(activated, down_w, preferred_element_type=jnp.float32)
-        .astype(jnp.bfloat16)
-        .reshape(rows_c.shape)
-    )
+    rows_far = swap(rows_y, "zh")
+    near = jnp.stack([rows_y, swap(rows_y, "core")])
+    far = jnp.stack([rows_far, swap(rows_far, "core")])
 
-    back_c = computed[0].astype(jnp.float32) + swap(computed[1], "core").astype(jnp.float32)
-    back_c = back_c.astype(jnp.bfloat16)
-    back_z = back_c[0].astype(jnp.float32) + swap(back_c[1], "zh").astype(jnp.float32)
-    picked = lax.all_to_all(back_z.astype(jnp.bfloat16), "y", 0, 0, tiled=True)
+    def expert(rows):
+        flat = rows.reshape(-1, rows.shape[-1])
+        gate = jnp.dot(flat, gate_w, preferred_element_type=jnp.float32)
+        upper = jnp.dot(flat, up_w, preferred_element_type=jnp.float32)
+        activated = (jax.nn.silu(gate) * upper).astype(jnp.bfloat16)
+        out = jnp.dot(activated, down_w, preferred_element_type=jnp.float32)
+        return out.astype(jnp.bfloat16).reshape(rows.shape)
+
+    near_out = expert(near)
+    far_out = expert(far)
+
+    far_sum = far_out[0].astype(jnp.float32) + swap(far_out[1], "core").astype(jnp.float32)
+    near_sum = near_out[0].astype(jnp.float32) + swap(near_out[1], "core").astype(jnp.float32)
+    back = near_sum + swap(far_sum.astype(jnp.bfloat16), "zh").astype(jnp.float32)
+    picked = lax.all_to_all(back.astype(jnp.bfloat16), "y", 0, 0, tiled=True)
     combine = select.transpose(2, 0, 1).astype(jnp.float32) * share[:, :, None]
     mixed = jnp.einsum(
         "txj,xjd->td", combine, picked.astype(jnp.float32), precision=lax.Precision.HIGHEST

time: 240 us -> 216 us (0.900)
  starting transfers between devices: 41.4 us -> 32.3 us
  other arithmetic: 33.8 us -> 24.7 us
  waiting for transfers between devices: 110 us -> 101 us
    sub x1 -> x0, other arithmetic: 11.9 us -> none  [body(): weight = jnp.where(visible[None], jnp.exp(score - top), 0.0)]
    ppermute x8 -> x12, starting transfers between devices: 23.2 us -> 14.8 us  [swap(): return lax.ppermute(block, axis, [(0, 1), (1, 0)])]
    all_to_all x1, waiting for transfers between devices: 9.58 us -> 2.8 us  [body(): kv_y = lax.all_to_all(send_kv, 'y', 0, 0, tiled=True)]
    dot_general x2 -> x4, matrix products: 9.54 us -> 14.6 us  [the longest x2 9.01 us: expert(): out = jnp.dot(activated, down_w, preferred_element_type=jnp.float32)]
    dot_general x1, matrix products: 4.47 us -> 1.86 us  [body(): jnp.einsum('hqd,kd->hqk', query, keys, preferred_element_type=jnp.float32)]
    ppermute x8 -> x12, waiting for transfers between devices: 72.8 us -> 70.6 us  [swap(): return lax.ppermute(block, axis, [(0, 1), (1, 0)])]
    squeeze x3 -> x2, local copies, waits for them, and re-layouts: 5.73 us -> 3.76 us  [the longest x1 1.89 us: body(): near_out[1]]
    another operation x4 -> x3, other arithmetic: 5.96 us -> 5.61 us  [the longest x1 2.31 us: body(): far = jnp.stack([rows_far, swap(rows_far, 'core')])]
  transfers between devices with their start and end apart: 12 -> 16, of which waited for: 11 -> 11; matrix products, arithmetic and copies ran while one was open for 2% -> 13% of each run, Pallas kernels for 0% -> 0%
where the time goes in v2:
time: 216 us; the launch traced here: 212 us
  waiting for transfers between devices  101 us (47%)
  starting transfers between devices  32.3 us (15%)
  other arithmetic  24.7 us (11%)
  matrix products  21.9 us (10%)
  local copies, waits for them, and re-layouts  19.1 us (9%)
  blocking collectives  12.9 us (6%)
    ppermute x12, waiting for transfers between devices, swap(): return lax.ppermute(block, axis, [(0, 1), (1, 0)])  70.6 us
    all_to_all x1, waiting for transfers between devices, body(): part_y = lax.all_to_all(part_c.astype(jnp.bfloat16), 'y', 0, 0, tiled=True)  15.5 us
    ppermute x12, starting transfers between devices, swap(): return lax.ppermute(block, axis, [(0, 1), (1, 0)])  14.8 us
    all_to_all x1, blocking collectives, body(): rows_y = lax.all_to_all(dispatch, 'y', 0, 0, tiled=True)  12.9 us
    all_to_all x1, waiting for transfers between devices, body(): picked = lax.all_to_all(back.astype(jnp.bfloat16), 'y', 0, 0, tiled=True)  9.93 us
    dot_general x2, matrix products, expert(): out = jnp.dot(activated, down_w, preferred_element_type=jnp.float32)  9.01 us
    dot_general x2, matrix products, expert(): gate = jnp.dot(flat, gate_w, preferred_element_type=jnp.float32)  5.55 us
    all_to_all x1, starting transfers between devices, body(): kv_y = lax.all_to_all(send_kv, 'y', 0, 0, tiled=True)  4.46 us
  transfers between devices with their start and end apart: 16, of which 11 were waited for; matrix products, arithmetic and copies ran while one was open for 13% of the time, Pallas kernels for 0%

profile of v2, /device:TPU:32, one launch (start us, length us, event | category | flops | bytes accessed | tf_op | source)
XLA Modules:
  0.0 212.3 jit_solution(13547324867841444506)
XLA Ops:
  0.0 1.2 reshape_squeeze.7
  1.2 0.4 fusion.91
  1.6 0.9 pad_maximum_fusion.3
  2.5 4.5 %all-to-all-start = ((bf16[4,256,256]{2,1,0:T(8,128)(2,1)}), bf16[4,256,256]{2,1,0:T(8,128)(2,1)}, u32[]{:S(2)}, u32[]{:S(2)}) async-start(bf16[4,256,256]{2,1,0:T(8,128)(2,1)} %pad_maximum_fusion.3), calls=%async_computation | async-start | bytes 1048576 | tf_op jit(solution)/shard_map/all_to_all | solution.py:55
  6.9 0.1 copy.31
  7.0 0.1 copy.32
  7.2 6.4 %collective-permute-start = (bf16[2,256,128]{2,1,0:T(8,128)(2,1)S(1)}, bf16[2,256,128]{2,1,0:T(8,128)(2,1)S(1)}, u32[]{:S(2)}, u32[]{:S(2)}) collective-permute-start(bf16[2,256,128]{2,1,0:T(8,128)(2,1)S(1)} %bitcast.137), channel_id=1, source_target_pairs={{0,2},{2,0},{1,3},{3,1},{4,6},{6,4},{5,7},{7,5},{8,10},{10,8},{9,1... | collective-permute-start | bytes 393224 | tf_op jit(solution)/shard_map/ppermute | solution.py:26
  13.7 2.8 %all-to-all-done = bf16[4,256,256]{2,1,0:T(8,128)(2,1)} async-done(((bf16[4,256,256]{2,1,0:T(8,128)(2,1)}), bf16[4,256,256]{2,1,0:T(8,128)(2,1)}, u32[]{:S(2)}, u32[]{:S(2)}) %all-to-all-start) | async-done | bytes 524320 | tf_op jit(solution)/shard_map/all_to_all | solution.py:55
  16.5 0.4 broadcast_compare_fusion
  16.9 1.7 collective-permute-done.1
  18.6 1.1 pad_maximum_fusion
  19.8 1.9 select_reduce_fusion
  21.6 2.3 %fusion = f32[4,256]{1,0:T(4,128)S(1)} fusion(f32[4,256,2048]{2,1,0:T(8,128)S(1)} %get-tuple-element.21, f32[4,256]{1,0:T(4,128)S(1)} %get-tuple-element.20, pred[256,2048]{1,0:T(8,128)(4,1)S(1)} %broadcast_compare_fusion), kind=kLoop, calls=%fused_computation.2 | loop fusion | flops 8387584 | bytes 8921088 | tf_op jit(solution)/shard_map/reduce_sum | solution.py:71
  24.0 6.4 %collective-permute-start.2 = (f32[2,256,2]{1,0,2:T(2,128)S(1)}, f32[2,256,2]{1,0,2:T(2,128)S(1)}, u32[]{:S(2)}, u32[]{:S(2)}) collective-permute-start(f32[2,256,2]{1,0,2:T(2,128)S(1)} %pad_maximum_fusion.4), channel_id=1, source_target_pairs={{0,2},{2,0},{1,3},{3,1},{4,6},{6,4},{5,7},{7,5},{8,10},{10,8},{9,1... | collective-permute-start | bytes 12296 | tf_op jit(solution)/shard_map/ppermute | solution.py:26
  30.4 1.9 fusion.5
  32.3 0.1 collective-permute-start.3
  32.4 11.9 %collective-permute-done.3 = bf16[2,256,128]{1,2,0:T(8,128)(2,1)S(1)} collective-permute-done((bf16[2,256,128]{1,2,0:T(8,128)(2,1)S(1)}, bf16[2,256,128]{1,2,0:T(8,128)(2,1)S(1)}, u32[]{:S(2)}, u32[]{:S(2)}) %collective-permute-start.3) | collective-permute-done | bytes 131104 | tf_op jit(solution)/shard_map/ppermute | solution.py:26
  44.4 0.7 convolution_convert_fusion
  45.2 1.3 copy-done.1
  46.5 1.0 dynamic-slice_bitcast_fusion
  47.5 3.0 %collective-permute-done.4 = bf16[4,2,16,4096]{3,2,1,0:T(8,128)(2,1)} collective-permute-done((bf16[4,2,16,4096]{3,2,1,0:T(8,128)(2,1)}, bf16[4,2,16,4096]{3,2,1,0:T(8,128)(2,1)}, u32[]{:S(2)}, u32[]{:S(2)}) %collective-permute-start.4) | collective-permute-done | bytes 1048608 | tf_op jit(solution)/shard_map/ppermute | solution.py:26
  50.5 2.8 %fusion.18 = bf16[4,2,16,4096]{3,2,1,0:T(8,128)(2,1)} fusion(bf16[4,2,16,4096]{3,2,1,0:T(8,128)(2,1)} %collective-permute-done.4, bf16[4,2,2,16,4096]{4,3,2,1,0:T(8,128)(2,1)} %bitcast.130, s32[]{:T(128)S(6)} %select_n.40), kind=kLoop, calls=%fused_computation.25 | loop fusion | flops 2097152 | bytes 3145732 | tf_op jit(solution)/shard_map/convert_element_type | solution.py:94
  53.3 4.4 %all-to-all-start.1 = ((bf16[4,2,16,4096]{3,2,1,0:T(8,128)(2,1)}), bf16[4,2,16,4096]{3,2,1,0:T(8,128)(2,1)}, u32[]{:S(2)}, u32[]{:S(2)}) async-start(bf16[4,2,16,4096]{3,2,1,0:T(8,128)(2,1)} %fusion.18), calls=%async_computation.1 | async-start | bytes 2097152 | tf_op jit(solution)/shard_map/all_to_all | solution.py:94
  57.8 0.1 copy.36
  58.0 15.5 %all-to-all-done.1 = bf16[4,2,16,4096]{3,2,1,0:T(8,128)(2,1)} async-done(((bf16[4,2,16,4096]{3,2,1,0:T(8,128)(2,1)}), bf16[4,2,16,4096]{3,2,1,0:T(8,128)(2,1)}, u32[]{:S(2)}, u32[]{:S(2)}) %all-to-all-start.1) | async-done | bytes 1048608 | tf_op jit(solution)/shard_map/all_to_all | solution.py:94
  73.4 1.4 convert_reduce_fusion
  74.9 0.8 copy-done.3
  75.7 0.4 collective-permute-start.5
  76.1 0.6 broadcast_add_fusion
  76.7 0.6 copy.38
  77.4 9.1 %collective-permute-done.5 = bf16[16,4096]{1,0:T(8,128)(2,1)} collective-permute-done((bf16[16,4096]{1,0:T(8,128)(2,1)S(1)}, bf16[16,4096]{1,0:T(8,128)(2,1)}, u32[]{:S(2)}, u32[]{:S(2)}) %collective-permute-start.5) | collective-permute-done | bytes 131104 | tf_op jit(solution)/shard_map/ppermute | solution.py:26
  86.5 1.2 multiply_reduce_fusion
  87.7 1.0 convolution_convert_fusion.3
  88.7 12.9 %all_to_all.20 = bf16[4,12,4096]{2,1,0:T(8,128)(2,1)} all-to-all(bf16[4,12,4096]{2,1,0:T(8,128)(2,1)S(1)} %convolution_convert_fusion.3), channel_id=1, replica_groups=mesh['section'=16,'y'=4,'zh'=2,'core'=2] {'y'}, dimensions={0} | all-to-all | bytes 786432 | tf_op jit(solution)/shard_map/all_to_all | solution.py:121
  101.6 0.4 collective-permute-start.8
  102.0 1.7 collective-permute-done.6
  103.7 2.2 %pad_maximum_fusion.1 = bf16[2,4,12,4096]{3,2,1,0:T(8,128)(2,1)} fusion(bf16[1,4,12,4096]{3,2,1,0:T(8,128)(2,1)S(1)} %bitcast.136, bf16[1,4,12,4096]{3,2,1,0:T(8,128)(2,1)} %bitcast.31), kind=kLoop, calls=%fused_computation.33 | loop fusion | flops 393216 | bytes 1572864 | tf_op jit(solution)/shard_map/stack | solution.py:123
  105.8 2.2 %reshape.170 = bf16[96,4096]{1,0:T(8,128)(2,1)} reshape(bf16[2,4,12,4096]{3,2,1,0:T(8,128)(2,1)} %pad_maximum_fusion.1) | data formatting | bytes 1572864 | tf_op jit(solution)/shard_map/reshape | solution.py:127
  108.0 2.8 %fusion.16 = f32[96,384]{1,0:T(8,128)S(1)} fusion(bf16[96,4096]{1,0:T(8,128)(2,1)} %reshape.170, bf16[1,4096,384]{2,1,0:T(8,128)(2,1)} %param.15), kind=kOutput, calls=%fused_computation.22 | convolution fusion | flops 301989888 | bytes 4079616 | tf_op jit(solution)/shard_map/dot_general | solution.py:128
  110.8 16.4 %collective-permute-done.8 = bf16[4,12,4096]{2,1,0:T(8,128)(2,1)} collective-permute-done((bf16[4,12,4096]{2,1,0:T(8,128)(2,1)}, bf16[4,12,4096]{2,1,0:T(8,128)(2,1)}, u32[]{:S(2)}, u32[]{:S(2)}) %collective-permute-start.8) | collective-permute-done | bytes 393248 | tf_op jit(solution)/shard_map/ppermute | solution.py:26
  127.3 4.5 %convolution_convert_fusion.2 = bf16[96,4096]{1,0:T(8,128)(2,1)} fusion(bf16[1,384,4096]{2,1,0:T(8,128)(2,1)S(1)} %copy-done, bf16[96,4096]{1,0:T(8,128)(2,1)} %reshape.170, bf16[1,4096,384]{2,1,0:T(8,128)(2,1)} %param.16, f32[96,384]{1,0:T(8,128)S(1)} %fusion.16), kind=kOutput, calls=%fused_computation.6 | convolution fusion | flops 604594176 | bytes 8011776 | tf_op jit(solution)/shard_map/dot_general | solution.py:131
  131.8 2.3 %pad_maximum_fusion.2 = bf16[2,4,12,4096]{3,2,1,0:T(8,128)(2,1)} fusion(bf16[1,4,12,4096]{3,2,1,0:T(8,128)(2,1)} %bitcast.37, bf16[1,4,12,4096]{3,2,1,0:T(8,128)(2,1)} %bitcast.36), kind=kLoop, calls=%fused_computation.34 | loop fusion | flops 393216 | bytes 1572864 | tf_op jit(solution)/shard_map/stack | solution.py:124
  134.1 2.2 %reshape.171 = bf16[96,4096]{1,0:T(8,128)(2,1)} reshape(bf16[2,4,12,4096]{3,2,1,0:T(8,128)(2,1)} %pad_maximum_fusion.2) | data formatting | bytes 1572864 | tf_op jit(solution)/shard_map/reshape | solution.py:127
  136.3 2.8 %fusion.14 = f32[96,384]{1,0:T(8,128)S(1)} fusion(bf16[96,4096]{1,0:T(8,128)(2,1)} %reshape.171, bf16[1,4096,384]{2,1,0:T(8,128)(2,1)} %param.15), kind=kOutput, calls=%fused_computation.20 | convolution fusion | flops 301989888 | bytes 4079616 | tf_op jit(solution)/shard_map/dot_general | solution.py:128
  139.0 4.5 %convolution_convert_fusion.1 = bf16[96,4096]{1,0:T(8,128)(2,1)} fusion(bf16[1,384,4096]{2,1,0:T(8,128)(2,1)S(1)} %copy-done, bf16[96,4096]{1,0:T(8,128)(2,1)} %reshape.171, bf16[1,4096,384]{2,1,0:T(8,128)(2,1)} %param.16, f32[96,384]{1,0:T(8,128)S(1)} %fusion.14), kind=kOutput, calls=%fused_computation.5 | convolution fusion | flops 604594176 | bytes 8011776 | tf_op jit(solution)/shard_map/dot_general | solution.py:131
  143.5 2.2 %fusion.90 = (bf16[48,4096]{1,0:T(8,128)(2,1)}, f32[48,4096]{1,0:T(8,128)}) fusion(bf16[96,4096]{1,0:T(8,128)(2,1)} %convolution_convert_fusion.1), kind=kLoop, calls=%fused_computation.124 | loop fusion | flops 196608 | bytes 1966080 | tf_op jit(solution)/shard_map/slice | solution.py:137
  145.7 1.9 squeeze.40
  147.6 0.5 collective-permute-start.10
  148.1 2.2 %fusion.89 = (bf16[48,4096]{1,0:T(8,128)(2,1)}, f32[48,4096]{1,0:T(8,128)}) fusion(bf16[96,4096]{1,0:T(8,128)(2,1)} %convolution_convert_fusion.2), kind=kLoop, calls=%fused_computation.123 | loop fusion | flops 196608 | bytes 1966080 | tf_op jit(solution)/shard_map/slice | solution.py:138
  150.3 1.9 squeeze.39
  152.3 2.2 %reshape.175 = f32[4,12,4096]{2,1,0:T(8,128)} reshape(f32[48,4096]{1,0:T(8,128)} %get-tuple-element.10) | data formatting | bytes 1572864 | tf_op jit(solution)/shard_map/convert_element_type | solution.py:137
  154.5 2.2 %add_convert_fusion.1 = bf16[4,12,4096]{2,1,0:T(8,128)(2,1)} fusion(f32[4,12,4096]{2,1,0:T(8,128)} %reshape.175, bf16[4,12,4096]{2,1,0:T(8,128)(2,1)} %collective-permute-done.10), kind=kLoop, calls=%fused_computation.36 | loop fusion | flops 589824 | bytes 1572864 | tf_op jit(solution)/shard_map/convert_element_type | solution.py:139
  156.7 0.5 collective-permute-start.11
  157.2 0.1 fusion.78
  157.3 0.1 copy.37
  157.4 2.2 %reshape.174 = f32[4,12,4096]{2,1,0:T(8,128)} reshape(f32[48,4096]{1,0:T(8,128)} %get-tuple-element.8) | data formatting | bytes 1572864 | tf_op jit(solution)/shard_map/convert_element_type | solution.py:138
  159.6 26.7 %collective-permute-done.11 = bf16[4,12,4096]{2,1,0:T(8,128)(2,1)} collective-permute-done((bf16[4,12,4096]{2,1,0:T(8,128)(2,1)}, bf16[4,12,4096]{2,1,0:T(8,128)(2,1)}, u32[]{:S(2)}, u32[]{:S(2)}) %collective-permute-start.11) | collective-permute-done | bytes 393248 | tf_op jit(solution)/shard_map/ppermute | solution.py:26
  186.3 2.5 %add_convert_fusion = bf16[4,12,4096]{2,1,0:T(8,128)(2,1)} fusion(bf16[4,12,4096]{2,1,0:T(8,128)(2,1)} %collective-permute-done.11, f32[4,12,4096]{2,1,0:T(8,128)} %reshape.174, bf16[4,12,4096]{2,1,0:T(8,128)(2,1)} %collective-permute-done.7), kind=kLoop, calls=%fused_computation.35 | loop fusion | flops 983040 | bytes 1966080 | tf_op jit(solution)/shard_map/convert_element_type | solution.py:140
  188.8 4.2 %all-to-all-start.3 = ((bf16[4,12,4096]{2,1,0:T(8,128)(2,1)}), bf16[4,12,4096]{2,1,0:T(8,128)(2,1)}, u32[]{:S(2)}, u32[]{:S(2)}) async-start(bf16[4,12,4096]{2,1,0:T(8,128)(2,1)} %add_convert_fusion), calls=%async_computation.3 | async-start | bytes 1048576 | tf_op jit(solution)/shard_map/all_to_all | solution.py:140
  193.0 9.9 %all-to-all-done.3 = bf16[4,12,4096]{2,1,0:T(8,128)(2,1)} async-done(((bf16[4,12,4096]{2,1,0:T(8,128)(2,1)}), bf16[4,12,4096]{2,1,0:T(8,128)(2,1)}, u32[]{:S(2)}, u32[]{:S(2)}) %all-to-all-start.3) | async-done | bytes 393248 | tf_op jit(solution)/shard_map/all_to_all | solution.py:140
  202.9 1.8 fusion.4
  204.7 4.4 %collective-permute-start.12 = (bf16[1,16,4096]{2,1,0:T(8,128)(2,1)S(1)}, bf16[1,16,4096]{2,1,0:T(8,128)(2,1)S(1)}, u32[]{:S(2)}, u32[]{:S(2)}) collective-permute-start(bf16[1,16,4096]{2,1,0:T(8,128)(2,1)S(1)} %fusion.4), channel_id=1, source_target_pairs={{240,0},{0,16},{16,32},{32,48},{48,64},{64,80},{80,96},{96,112},{1... | collective-permute-start | bytes 393224 | tf_op jit(solution)/shard_map/ppermute | solution.py:22
  209.1 2.5 %collective-permute-done.12 = bf16[1,16,4096]{2,1,0:T(8,128)(2,1)S(1)} collective-permute-done((bf16[1,16,4096]{2,1,0:T(8,128)(2,1)S(1)}, bf16[1,16,4096]{2,1,0:T(8,128)(2,1)S(1)}, u32[]{:S(2)}, u32[]{:S(2)}) %collective-permute-start.12) | collective-permute-done | bytes 131104 | tf_op jit(solution)/shard_map/ppermute | solution.py:22
  211.7 0.7 copy.47
  (55 shorter events, 0.7 us)
Async XLA Ops:
  0.0 127.3 %copy-start = (bf16[1,384,4096]{2,1,0:T(8,128)(2,1)S(1)}, bf16[1,384,4096]{2,1,0:T(8,128)(2,1)}, u32[]{:S(2)}) copy-start(bf16[1,384,4096]{2,1,0:T(8,128)(2,1)} %param.17) | copy-start | bytes 9437188
  0.0 6.9 %copy-start.4 = (bf16[1,256,256]{2,1,0:T(8,128)(2,1)S(1)}, bf16[1,256,256]{2,1,0:T(8,128)(2,1)}, u32[]{:S(2)}) copy-start(bf16[1,256,256]{2,1,0:T(8,128)(2,1)} %param.11) | copy-start | bytes 393220
  2.5 14.0 %all-to-all-start = ((bf16[4,256,256]{2,1,0:T(8,128)(2,1)}), bf16[4,256,256]{2,1,0:T(8,128)(2,1)}, u32[]{:S(2)}, u32[]{:S(2)}) async-start(bf16[4,256,256]{2,1,0:T(8,128)(2,1)} %pad_maximum_fusion.3), calls=%async_computation | async-start | bytes 1048576 | tf_op jit(solution)/shard_map/all_to_all | solution.py:55
  7.2 12.6 %collective-permute-start = (bf16[2,256,128]{2,1,0:T(8,128)(2,1)S(1)}, bf16[2,256,128]{2,1,0:T(8,128)(2,1)S(1)}, u32[]{:S(2)}, u32[]{:S(2)}) collective-permute-start(bf16[2,256,128]{2,1,0:T(8,128)(2,1)S(1)} %bitcast.137), channel_id=1, source_target_pairs={{0,2},{2,0},{1,3},{3,1},{4,6},{6,4},{5,7},{7,5},{8,10},{10,8},{9,1... | collective-permute-start | bytes 393224 | tf_op jit(solution)/shard_map/ppermute | solution.py:26
  16.5 2.1 collective-permute-start.1
  24.0 20.5 %copy-start.2 = (bf16[1,256,4096]{2,1,0:T(8,128)(2,1)S(1)}, bf16[1,256,4096]{2,1,0:T(8,128)(2,1)}, u32[]{:S(2)}) copy-start(bf16[1,256,4096]{2,1,0:T(8,128)(2,1)} %param.13) | copy-start | bytes 6291460
  24.0 8.5 %collective-permute-start.2 = (f32[2,256,2]{1,0,2:T(2,128)S(1)}, f32[2,256,2]{1,0,2:T(2,128)S(1)}, u32[]{:S(2)}, u32[]{:S(2)}) collective-permute-start(f32[2,256,2]{1,0,2:T(2,128)S(1)} %pad_maximum_fusion.4), channel_id=1, source_target_pairs={{0,2},{2,0},{1,3},{3,1},{4,6},{6,4},{5,7},{7,5},{8,10},{10,8},{9,1... | collective-permute-start | bytes 12296 | tf_op jit(solution)/shard_map/ppermute | solution.py:26
  32.3 12.0 %collective-permute-start.3 = (bf16[2,256,128]{1,2,0:T(8,128)(2,1)S(1)}, bf16[2,256,128]{1,2,0:T(8,128)(2,1)S(1)}, u32[]{:S(2)}, u32[]{:S(2)}) collective-permute-start(bf16[2,256,128]{1,2,0:T(8,128)(2,1)S(1)} %slice.136), channel_id=1, source_target_pairs={{0,2},{2,0},{1,3},{3,1},{4,6},{6,4},{5,7},{7,5},{8,10},{10,8},{9,1... | collective-permute-start | bytes 393224 | tf_op jit(solution)/shard_map/ppermute | solution.py:26
  45.2 1.3 copy-start.1
  47.5 10.2 %copy-start.13 = (s32[1,256,2]{1,2,0:T(2,128)S(1)}, s32[1,256,2]{1,2,0:T(2,128)}, u32[]{:S(2)}) copy-start(s32[1,256,2]{1,2,0:T(2,128)} %param.18) | copy-start | bytes 6148
  47.5 3.0 %collective-permute-start.4 = (bf16[4,2,16,4096]{3,2,1,0:T(8,128)(2,1)}, bf16[4,2,16,4096]{3,2,1,0:T(8,128)(2,1)}, u32[]{:S(2)}, u32[]{:S(2)}) collective-permute-start(bf16[4,2,16,4096]{3,2,1,0:T(8,128)(2,1)} %dynamic-slice_bitcast_fusion), channel_id=1, source_target_pairs={{0,1},{1,0},{2,3},{3,2},{4,5},{5,4},{6,7},{7,6},{8,9},{9,8},{10,11... | collective-permute-start | bytes 3145736 | tf_op jit(solution)/shard_map/ppermute | solution.py:26
  47.5 38.9 %copy-start.5 = (bf16[1,16,4096]{2,1,0:T(8,128)(2,1)S(1)}, bf16[1,16,4096]{2,1,0:T(8,128)(2,1)}, u32[]{:S(2)}) copy-start(bf16[1,16,4096]{2,1,0:T(8,128)(2,1)} %param.10) | copy-start | bytes 393220
  53.3 34.4 %copy-start.7 = (f32[1,4096]{1,0:T(1,128)S(1)}, f32[1,4096]{1,0:T(1,128)}, u32[]{:S(2)}) copy-start(f32[1,4096]{1,0:T(1,128)} %param.14) | copy-start | bytes 49156
  53.3 20.1 %all-to-all-start.1 = ((bf16[4,2,16,4096]{3,2,1,0:T(8,128)(2,1)}), bf16[4,2,16,4096]{3,2,1,0:T(8,128)(2,1)}, u32[]{:S(2)}, u32[]{:S(2)}) async-start(bf16[4,2,16,4096]{3,2,1,0:T(8,128)(2,1)} %fusion.18), calls=%async_computation.1 | async-start | bytes 2097152 | tf_op jit(solution)/shard_map/all_to_all | solution.py:94
  57.8 19.6 %copy-start.10 = (s32[16,2]{0,1:T(2,128)}, s32[16,2]{0,1:T(2,128)S(1)}, u32[]{:S(2)}) copy-start(s32[16,2]{0,1:T(2,128)S(1)} %fusion.77) | copy-start | bytes 388
  57.8 19.5 %copy-start.8 = (pred[16,4]{0,1:T(4,128)(4,1)}, pred[16,4]{0,1:T(4,128)(4,1)S(1)}, u32[]{:S(2)}) copy-start(pred[16,4]{0,1:T(4,128)(4,1)S(1)} %fusion.71) | copy-start | bytes 196
  74.9 0.8 copy-start.3
  75.7 10.8 %collective-permute-start.5 = (bf16[16,4096]{1,0:T(8,128)(2,1)S(1)}, bf16[16,4096]{1,0:T(8,128)(2,1)}, u32[]{:S(2)}, u32[]{:S(2)}) collective-permute-start(bf16[16,4096]{1,0:T(8,128)(2,1)S(1)} %fusion.53), channel_id=1, source_target_pairs={{0,2},{2,0},{1,3},{3,1},{4,6},{6,4},{5,7},{7,5},{8,10},{10,8},{9,1... | collective-permute-start | bytes 393224 | tf_op jit(solution)/shard_map/ppermute | solution.py:26
  101.6 2.1 collective-permute-start.6
  101.6 25.6 %collective-permute-start.8 = (bf16[4,12,4096]{2,1,0:T(8,128)(2,1)}, bf16[4,12,4096]{2,1,0:T(8,128)(2,1)}, u32[]{:S(2)}, u32[]{:S(2)}) collective-permute-start(bf16[4,12,4096]{2,1,0:T(8,128)(2,1)} %all_to_all.20), channel_id=1, source_target_pairs={{0,2},{2,0},{1,3},{3,1},{4,6},{6,4},{5,7},{7,5},{8,10},{10,8},{9,1... | collective-permute-start | bytes 1179656 | tf_op jit(solution)/shard_map/ppermute | solution.py:26
  127.2 4.6 %collective-permute-start.9 = (bf16[4,12,4096]{2,1,0:T(8,128)(2,1)}, bf16[4,12,4096]{2,1,0:T(8,128)(2,1)}, u32[]{:S(2)}, u32[]{:S(2)}) collective-permute-start(bf16[4,12,4096]{2,1,0:T(8,128)(2,1)} %collective-permute-done.8), channel_id=1, source_target_pairs={{0,1},{1,0},{2,3},{3,2},{4,5},{5,4},{6,7},{7,6},{8,9},{9,8},{10,11... | collective-permute-start | bytes 1179656 | tf_op jit(solution)/shard_map/ppermute | solution.py:26
  147.6 9.6 %copy-start.12 = (f32[1,256,2]{1,2,0:T(2,128)S(1)}, f32[1,256,2]{1,2,0:T(2,128)}, u32[]{:S(2)}) copy-start(f32[1,256,2]{1,2,0:T(2,128)} %param.19) | copy-start | bytes 6148
  147.6 9.7 %copy-start.6 = (s32[16,4]{1,0:T(8,128)S(1)}, s32[16,4]{1,0:T(8,128)}, u32[]{:S(2)}) copy-start(s32[16,4]{1,0:T(8,128)} %get-tuple-element.13) | copy-start | bytes 772
  147.6 6.8 %collective-permute-start.10 = (bf16[4,12,4096]{2,1,0:T(8,128)(2,1)}, bf16[4,12,4096]{2,1,0:T(8,128)(2,1)}, u32[]{:S(2)}, u32[]{:S(2)}) collective-permute-start(bf16[4,12,4096]{2,1,0:T(8,128)(2,1)} %squeeze.40), channel_id=1, source_target_pairs={{0,1},{1,0},{2,3},{3,2},{4,5},{5,4},{6,7},{7,6},{8,9},{9,8},{10,11... | collective-permute-start | bytes 1179656 | tf_op jit(solution)/shard_map/ppermute | solution.py:26
  152.2 7.4 %collective-permute-start.7 = (bf16[4,12,4096]{2,1,0:T(8,128)(2,1)}, bf16[4,12,4096]{2,1,0:T(8,128)(2,1)}, u32[]{:S(2)}, u32[]{:S(2)}) collective-permute-start(bf16[4,12,4096]{2,1,0:T(8,128)(2,1)} %squeeze.39), channel_id=1, source_target_pairs={{0,1},{1,0},{2,3},{3,2},{4,5},{5,4},{6,7},{7,6},{8,9},{9,8},{10,11... | collective-permute-start | bytes 1179656 | tf_op jit(solution)/shard_map/ppermute | solution.py:26
  156.7 36.2 %copy-start.11 = (s32[16,2]{0,1:T(2,128)S(1)}, s32[16,2]{0,1:T(2,128)}, u32[]{:S(2)}) copy-start(s32[16,2]{0,1:T(2,128)} %copy-done.10) | copy-start | bytes 388
  156.7 46.2 %copy-start.9 = (pred[16,4]{0,1:T(4,128)(4,1)S(1)}, pred[16,4]{0,1:T(4,128)(4,1)}, u32[]{:S(2)}) copy-start(pred[16,4]{0,1:T(4,128)(4,1)} %copy-done.8) | copy-start | bytes 196
  156.7 29.6 %collective-permute-start.11 = (bf16[4,12,4096]{2,1,0:T(8,128)(2,1)}, bf16[4,12,4096]{2,1,0:T(8,128)(2,1)}, u32[]{:S(2)}, u32[]{:S(2)}) collective-permute-start(bf16[4,12,4096]{2,1,0:T(8,128)(2,1)} %add_convert_fusion.1), channel_id=1, source_target_pairs={{0,2},{2,0},{1,3},{3,1},{4,6},{6,4},{5,7},{7,5},{8,10},{10,8},{9,1... | collective-permute-start | bytes 1179656 | tf_op jit(solution)/shard_map/ppermute | solution.py:26
  188.8 14.1 %all-to-all-start.3 = ((bf16[4,12,4096]{2,1,0:T(8,128)(2,1)}), bf16[4,12,4096]{2,1,0:T(8,128)(2,1)}, u32[]{:S(2)}, u32[]{:S(2)}) async-start(bf16[4,12,4096]{2,1,0:T(8,128)(2,1)} %add_convert_fusion), calls=%async_computation.3 | async-start | bytes 1048576 | tf_op jit(solution)/shard_map/all_to_all | solution.py:140
  204.7 7.0 %collective-permute-start.12 = (bf16[1,16,4096]{2,1,0:T(8,128)(2,1)S(1)}, bf16[1,16,4096]{2,1,0:T(8,128)(2,1)S(1)}, u32[]{:S(2)}, u32[]{:S(2)}) collective-permute-start(bf16[1,16,4096]{2,1,0:T(8,128)(2,1)S(1)} %fusion.4), channel_id=1, source_target_pairs={{240,0},{0,16},{16,32},{32,48},{48,64},{64,80},{80,96},{96,112},{1... | collective-permute-start | bytes 393224 | tf_op jit(solution)/shard_map/ppermute | solution.py:22

commit v3 on v2

--- a/solution.py
+++ b/solution.py
@@ -113,35 +113,35 @@
     routed = jnp.any(onehot, axis=1)
     slot = jnp.cumsum(routed.astype(jnp.int32), axis=0) - 1
     select = routed[None] & (slot[None] == jnp.arange(CAP)[:, None, None])
-    select = select.transpose(2, 0, 1)
-    dispatch = jnp.einsum(
-        "xjt,td->xjd", select.astype(jnp.bfloat16), normed, preferred_element_type=jnp.float32
+    select = select.transpose(2, 0, 1).reshape(experts_count * CAP, tok_rows)
+    dispatch = jnp.dot(
+        select.astype(jnp.bfloat16), normed, preferred_element_type=jnp.float32
     ).astype(jnp.bfloat16)
 
     rows_y = lax.all_to_all(dispatch, "y", 0, 0, tiled=True)
     rows_far = swap(rows_y, "zh")
-    near = jnp.stack([rows_y, swap(rows_y, "core")])
-    far = jnp.stack([rows_far, swap(rows_far, "core")])
+    near = jnp.concatenate([rows_y, swap(rows_y, "core")])
+    far = jnp.concatenate([rows_far, swap(rows_far, "core")])
+    count = rows_y.shape[0]
 
     def expert(rows):
-        flat = rows.reshape(-1, rows.shape[-1])
-        gate = jnp.dot(flat, gate_w, preferred_element_type=jnp.float32)
-        upper = jnp.dot(flat, up_w, preferred_element_type=jnp.float32)
+        gate = jnp.dot(rows, gate_w, preferred_element_type=jnp.float32)
+        upper = jnp.dot(rows, up_w, preferred_element_type=jnp.float32)
         activated = (jax.nn.silu(gate) * upper).astype(jnp.bfloat16)
         out = jnp.dot(activated, down_w, preferred_element_type=jnp.float32)
-        return out.astype(jnp.bfloat16).reshape(rows.shape)
+        return out.astype(jnp.bfloat16)
 
     near_out = expert(near)
     far_out = expert(far)
 
-    far_sum = far_out[0].astype(jnp.float32) + swap(far_out[1], "core").astype(jnp.float32)
-    near_sum = near_out[0].astype(jnp.float32) + swap(near_out[1], "core").astype(jnp.float32)
+    far_sum = far_out[:count].astype(jnp.float32) + swap(far_out[count:], "core").astype(jnp.float32)
+    near_sum = near_out[:count].astype(jnp.float32) + swap(near_out[count:], "core").astype(
+        jnp.float32
+    )
     back = near_sum + swap(far_sum.astype(jnp.bfloat16), "zh").astype(jnp.float32)
     picked = lax.all_to_all(back.astype(jnp.bfloat16), "y", 0, 0, tiled=True)
-    combine = select.transpose(2, 0, 1).astype(jnp.float32) * share[:, :, None]
-    mixed = jnp.einsum(
-        "txj,xjd->td", combine, picked.astype(jnp.float32), precision=lax.Precision.HIGHEST
-    )
+    combine = select.T.astype(jnp.float32) * jnp.repeat(share, CAP, axis=1)
+    mixed = jnp.dot(combine, picked.astype(jnp.float32), precision=lax.Precision.HIGHEST)
     layer_out = (middle + mixed).astype(jnp.bfloat16)
     return shifted(layer_out[None], "section", 1)
 

time: 216 us -> 193 us (0.89)
  the two profiles are of different devices: /device:TPU:32 before, /device:TPU:8 now
where the time goes in v3:
time: 193 us; the launch traced here: 192 us
  waiting for transfers between devices  94.6 us (49%)
  starting transfers between devices  32.8 us (17%)
  matrix products  20 us (10%)
  local copies, waits for them, and re-layouts  18.7 us (10%)
  other arithmetic  13.2 us (7%)
  blocking collectives  12.3 us (6%)
    ppermute x12, waiting for transfers between devices, swap(): return lax.ppermute(block, axis, [(0, 1), (1, 0)])  67.4 us
    ppermute x12, starting transfers between devices, swap(): return lax.ppermute(block, axis, [(0, 1), (1, 0)])  13.4 us
    all_to_all x1, waiting for transfers between devices, body(): part_y = lax.all_to_all(part_c.astype(jnp.bfloat16), 'y', 0, 0, tiled=True)  13.1 us
    all_to_all x1, blocking collectives, body(): rows_y = lax.all_to_all(dispatch, 'y', 0, 0, tiled=True)  12.3 us
    dot_general x2, matrix products, expert(): out = jnp.dot(activated, down_w, preferred_element_type=jnp.float32)  8.98 us
    ppermute x1, waiting for transfers between devices, shifted(): return lax.ppermute(block, axis, route)  7.18 us
    all_to_all x1, waiting for transfers between devices, body(): picked = lax.all_to_all(back.astype(jnp.bfloat16), 'y', 0, 0, tiled=True)  6.46 us
    all_to_all x1, starting transfers between devices, body(): kv_y = lax.all_to_all(send_kv, 'y', 0, 0, tiled=True)  6.26 us
  transfers between devices with their start and end apart: 16, of which 13 were waited for; matrix products, arithmetic and copies ran while one was open for 9% of the time, Pallas kernels for 0%

profile of v3, /device:TPU:8, one launch (start us, length us, event | category | flops | bytes accessed | tf_op | source)
XLA Modules:
  0.0 191.8 jit_solution(8060067699215067168)
XLA Ops:
  0.0 1.2 reshape_squeeze.7
  1.2 0.4 fusion.59
  1.6 0.8 pad_maximum_fusion.1
  2.5 6.3 %all-to-all-start = ((bf16[4,256,256]{2,1,0:T(8,128)(2,1)}), bf16[4,256,256]{2,1,0:T(8,128)(2,1)}, u32[]{:S(2)}, u32[]{:S(2)}) async-start(bf16[4,256,256]{2,1,0:T(8,128)(2,1)} %pad_maximum_fusion.1), calls=%async_computation | async-start | bytes 1048576 | tf_op jit(solution)/shard_map/all_to_all | solution.py:55
  8.7 0.1 copy.25
  8.8 0.1 copy.26
  8.9 5.9 %collective-permute-start = (bf16[2,256,128]{2,1,0:T(8,128)(2,1)S(1)}, bf16[2,256,128]{2,1,0:T(8,128)(2,1)S(1)}, u32[]{:S(2)}, u32[]{:S(2)}) collective-permute-start(bf16[2,256,128]{2,1,0:T(8,128)(2,1)S(1)} %bitcast.127), channel_id=1, source_target_pairs={{0,2},{2,0},{1,3},{3,1},{4,6},{6,4},{5,7},{7,5},{8,10},{10,8},{9,1... | collective-permute-start | bytes 393224 | tf_op jit(solution)/shard_map/ppermute | solution.py:26
  15.0 0.4 all-to-all-done
  15.5 0.4 broadcast_compare_fusion
  15.9 1.7 collective-permute-done.1
  17.6 1.1 pad_maximum_fusion
  18.8 0.7 collective-permute-done
  19.5 1.9 select_reduce_fusion
  21.3 2.3 %fusion = f32[4,256]{1,0:T(4,128)S(1)} fusion(f32[4,256,2048]{2,1,0:T(8,128)S(1)} %get-tuple-element.15, f32[4,256]{1,0:T(4,128)S(1)} %get-tuple-element.14, pred[256,2048]{1,0:T(8,128)(4,1)S(1)} %broadcast_compare_fusion), kind=kLoop, calls=%fused_computation.2 | loop fusion | flops 8387584 | bytes 8921088 | tf_op jit(solution)/shard_map/reduce_sum | solution.py:71
  23.6 6.6 %collective-permute-start.2 = (f32[2,256,2]{1,0,2:T(2,128)S(1)}, f32[2,256,2]{1,0,2:T(2,128)S(1)}, u32[]{:S(2)}, u32[]{:S(2)}) collective-permute-start(f32[2,256,2]{1,0,2:T(2,128)S(1)} %pad_maximum_fusion.2), channel_id=1, source_target_pairs={{0,2},{2,0},{1,3},{3,1},{4,6},{6,4},{5,7},{7,5},{8,10},{10,8},{9,1... | collective-permute-start | bytes 12296 | tf_op jit(solution)/shard_map/ppermute | solution.py:26
  30.2 1.9 %fusion.4 = f32[4,256,128]{1,2,0:T(8,128)S(1)} fusion(f32[4,256,2048]{2,1,0:T(8,128)S(1)} %get-tuple-element.15, f32[4,256]{1,0:T(4,128)S(1)} %get-tuple-element.14, pred[256,2048]{1,0:T(8,128)(4,1)S(1)} %broadcast_compare_fusion, bf16[2048,256]{1,0:T(8,128)(2,1)S(1)} %bitcast.123), kind=kOutput, calls=%fused_computation.11 | convolution fusion | flops 545259520 | bytes 9965568 | tf_op jit(solution)/shard_map/hqk,kd->hqd/dot_general | solution.py:72
  32.2 0.1 collective-permute-start.3
  32.3 11.2 %collective-permute-done.3 = bf16[2,256,128]{1,2,0:T(8,128)(2,1)S(1)} collective-permute-done((bf16[2,256,128]{1,2,0:T(8,128)(2,1)S(1)}, bf16[2,256,128]{1,2,0:T(8,128)(2,1)S(1)}, u32[]{:S(2)}, u32[]{:S(2)}) %collective-permute-start.3) | collective-permute-done | bytes 131104 | tf_op jit(solution)/shard_map/ppermute | solution.py:26
  43.6 0.7 convolution_convert_fusion
  44.4 1.3 copy-done.2
  45.7 1.0 dynamic-slice_bitcast_fusion
  46.7 3.0 %collective-permute-done.4 = bf16[4,2,16,4096]{3,2,1,0:T(8,128)(2,1)} collective-permute-done((bf16[4,2,16,4096]{3,2,1,0:T(8,128)(2,1)}, bf16[4,2,16,4096]{3,2,1,0:T(8,128)(2,1)}, u32[]{:S(2)}, u32[]{:S(2)}) %collective-permute-start.4) | collective-permute-done | bytes 1048608 | tf_op jit(solution)/shard_map/ppermute | solution.py:26
  49.7 2.8 %fusion.17 = bf16[4,2,16,4096]{3,2,1,0:T(8,128)(2,1)} fusion(bf16[4,2,16,4096]{3,2,1,0:T(8,128)(2,1)} %collective-permute-done.4, bf16[4,2,2,16,4096]{4,3,2,1,0:T(8,128)(2,1)} %bitcast.121, s32[]{:T(128)S(6)} %select_n.40), kind=kLoop, calls=%fused_computation.24 | loop fusion | flops 2097152 | bytes 3145732 | tf_op jit(solution)/shard_map/convert_element_type | solution.py:94
  52.5 5.8 %all-to-all-start.1 = ((bf16[4,2,16,4096]{3,2,1,0:T(8,128)(2,1)}), bf16[4,2,16,4096]{3,2,1,0:T(8,128)(2,1)}, u32[]{:S(2)}, u32[]{:S(2)}) async-start(bf16[4,2,16,4096]{3,2,1,0:T(8,128)(2,1)} %fusion.17), calls=%async_computation.1 | async-start | bytes 2097152 | tf_op jit(solution)/shard_map/all_to_all | solution.py:94
  58.4 0.5 copy-done.11
  58.9 0.1 copy.30
  59.1 0.1 and.19
  59.4 0.1 eq.49
  59.6 13.1 %all-to-all-done.1 = bf16[4,2,16,4096]{3,2,1,0:T(8,128)(2,1)} async-done(((bf16[4,2,16,4096]{3,2,1,0:T(8,128)(2,1)}), bf16[4,2,16,4096]{3,2,1,0:T(8,128)(2,1)}, u32[]{:S(2)}, u32[]{:S(2)}) %all-to-all-start.1) | async-done | bytes 1048608 | tf_op jit(solution)/shard_map/all_to_all | solution.py:94
  72.6 1.4 convert_reduce_fusion
  74.1 0.1 collective-permute-start.5
  74.2 11.5 %collective-permute-done.5 = bf16[16,4096]{1,0:T(8,128)(2,1)S(1)} collective-permute-done((bf16[16,4096]{1,0:T(8,128)(2,1)S(1)}, bf16[16,4096]{1,0:T(8,128)(2,1)S(1)}, u32[]{:S(2)}, u32[]{:S(2)}) %collective-permute-start.5) | collective-permute-done | bytes 131104 | tf_op jit(solution)/shard_map/ppermute | solution.py:26
  85.8 0.2 multiply_reduce_fusion
  86.0 1.1 convolution_convert_fusion.3
  87.0 1.9 all_to_all.24
  88.9 12.3 %all_to_all.34 = bf16[4,12,4096]{2,1,0:T(8,128)(2,1)} all-to-all(bf16[4,12,4096]{2,1,0:T(8,128)(2,1)} %all_to_all.24), channel_id=1, replica_groups=mesh['section'=16,'y'=4,'zh'=2,'core'=2] {'y'}, dimensions={0} | all-to-all | bytes 786432 | tf_op jit(solution)/shard_map/all_to_all | solution.py:121
  101.2 1.9 all_to_all.26
  103.1 1.1 constant_dynamic-update-slice_fusion.1
  104.1 0.9 collective-permute-done.6
  105.0 2.8 %fusion.11 = f32[96,384]{1,0:T(8,128)S(1)} fusion(bf16[96,4096]{1,0:T(8,128)(2,1)S(1)} %constant_dynamic-update-slice_fusion, bf16[1,4096,384]{2,1,0:T(8,128)(2,1)} %param.16), kind=kOutput, calls=%fused_computation.17 | convolution fusion | flops 301989888 | bytes 4079616 | tf_op jit(solution)/shard_map/dot_general | solution.py:129
  107.9 15.2 %collective-permute-done.8 = bf16[48,4096]{1,0:T(8,128)(2,1)S(1)} collective-permute-done((bf16[48,4096]{1,0:T(8,128)(2,1)}, bf16[48,4096]{1,0:T(8,128)(2,1)S(1)}, u32[]{:S(2)}, u32[]{:S(2)}) %collective-permute-start.8) | collective-permute-done | bytes 393248 | tf_op jit(solution)/shard_map/ppermute | solution.py:26
  123.1 1.7 collective-permute-done.9
  124.8 0.9 copy-done.3
  125.7 1.3 fusion.9
  127.0 4.5 %convolution_convert_fusion.1 = bf16[96,4096]{1,0:T(8,128)(2,1)} fusion(bf16[1,384,4096]{2,1,0:T(8,128)(2,1)S(1)} %copy-done, f32[96,384]{1,0:T(8,128)} %fusion.9, bf16[96,4096]{1,0:T(8,128)(2,1)} %copy-done.3, bf16[1,4096,384]{2,1,0:T(8,128)(2,1)} %param.15), kind=kOutput, calls=%fused_computation.5 | convolution fusion | flops 604594176 | bytes 8011776 | tf_op jit(solution)/shard_map/dot_general | solution.py:131
  131.5 1.8 slice.84
  133.3 0.1 collective-permute-start.10
  133.4 4.5 %convolution_convert_fusion.2 = bf16[96,4096]{1,0:T(8,128)(2,1)} fusion(bf16[1,384,4096]{2,1,0:T(8,128)(2,1)S(1)} %copy-done, f32[96,384]{1,0:T(8,128)S(1)} %fusion.11, bf16[96,4096]{1,0:T(8,128)(2,1)} %copy-done.4, bf16[1,4096,384]{2,1,0:T(8,128)(2,1)} %param.15), kind=kOutput, calls=%fused_computation.6 | convolution fusion | flops 604594176 | bytes 8011776 | tf_op jit(solution)/shard_map/dot_general | solution.py:131
  137.9 1.0 slice.82
  139.0 0.4 collective-permute-start.7
  139.4 1.2 add_convert_fusion.1
  140.6 0.1 collective-permute-start.11
  140.7 0.8 fusion.49
  141.5 21.4 %collective-permute-done.11 = bf16[48,4096]{1,0:T(8,128)(2,1)S(1)} collective-permute-done((bf16[48,4096]{1,0:T(8,128)(2,1)S(1)}, bf16[48,4096]{1,0:T(8,128)(2,1)S(1)}, u32[]{:S(2)}, u32[]{:S(2)}) %collective-permute-start.11) | collective-permute-done | bytes 393248 | tf_op jit(solution)/shard_map/ppermute | solution.py:26
  162.9 1.9 add_convert_fusion
  164.8 1.9 all_to_all.27
  166.7 5.6 %all-to-all-start.3 = ((bf16[4,12,4096]{2,1,0:T(8,128)(2,1)}), bf16[4,12,4096]{2,1,0:T(8,128)(2,1)}, u32[]{:S(2)}, u32[]{:S(2)}) async-start(bf16[4,12,4096]{2,1,0:T(8,128)(2,1)} %all_to_all.27), calls=%async_computation.3 | async-start | bytes 1048576 | tf_op jit(solution)/shard_map/all_to_all | solution.py:142
  172.5 0.1 reshape.144
  172.6 6.5 %all-to-all-done.3 = bf16[4,12,4096]{2,1,0:T(8,128)(2,1)} async-done(((bf16[4,12,4096]{2,1,0:T(8,128)(2,1)}), bf16[4,12,4096]{2,1,0:T(8,128)(2,1)}, u32[]{:S(2)}, u32[]{:S(2)}) %all-to-all-start.3) | async-done | bytes 393248 | tf_op jit(solution)/shard_map/all_to_all | solution.py:142
  179.1 1.9 all_to_all.29
  180.9 1.3 fusion.3
  182.2 1.8 collective-permute-start.12
  184.0 7.2 %collective-permute-done.12 = bf16[1,16,4096]{2,1,0:T(8,128)(2,1)S(1)} collective-permute-done((bf16[1,16,4096]{2,1,0:T(8,128)(2,1)S(1)}, bf16[1,16,4096]{2,1,0:T(8,128)(2,1)S(1)}, u32[]{:S(2)}, u32[]{:S(2)}) %collective-permute-start.12) | collective-permute-done | bytes 131104 | tf_op jit(solution)/shard_map/ppermute | solution.py:22
  191.2 0.7 copy.43
  (64 shorter events, 1.1 us)
Async XLA Ops:
  0.0 127.0 %copy-start = (bf16[1,384,4096]{2,1,0:T(8,128)(2,1)S(1)}, bf16[1,384,4096]{2,1,0:T(8,128)(2,1)}, u32[]{:S(2)}) copy-start(bf16[1,384,4096]{2,1,0:T(8,128)(2,1)} %param.17) | copy-start | bytes 9437188
  0.0 8.7 %copy-start.6 = (bf16[1,256,256]{2,1,0:T(8,128)(2,1)S(1)}, bf16[1,256,256]{2,1,0:T(8,128)(2,1)}, u32[]{:S(2)}) copy-start(bf16[1,256,256]{2,1,0:T(8,128)(2,1)} %param.11) | copy-start | bytes 393220
  2.5 13.0 %all-to-all-start = ((bf16[4,256,256]{2,1,0:T(8,128)(2,1)}), bf16[4,256,256]{2,1,0:T(8,128)(2,1)}, u32[]{:S(2)}, u32[]{:S(2)}) async-start(bf16[4,256,256]{2,1,0:T(8,128)(2,1)} %pad_maximum_fusion.1), calls=%async_computation | async-start | bytes 1048576 | tf_op jit(solution)/shard_map/all_to_all | solution.py:55
  8.9 10.5 %collective-permute-start = (bf16[2,256,128]{2,1,0:T(8,128)(2,1)S(1)}, bf16[2,256,128]{2,1,0:T(8,128)(2,1)S(1)}, u32[]{:S(2)}, u32[]{:S(2)}) collective-permute-start(bf16[2,256,128]{2,1,0:T(8,128)(2,1)S(1)} %bitcast.127), channel_id=1, source_target_pairs={{0,2},{2,0},{1,3},{3,1},{4,6},{6,4},{5,7},{7,5},{8,10},{10,8},{9,1... | collective-permute-start | bytes 393224 | tf_op jit(solution)/shard_map/ppermute | solution.py:26
  15.5 2.1 %collective-permute-start.1 = (bf16[4,256,256]{2,1,0:T(8,128)(2,1)}, bf16[4,256,256]{2,1,0:T(8,128)(2,1)S(1)}, u32[]{:S(2)}, u32[]{:S(2)}) collective-permute-start(bf16[4,256,256]{2,1,0:T(8,128)(2,1)} %all-to-all-done), channel_id=1, source_target_pairs={{0,1},{1,0},{2,3},{3,2},{4,5},{5,4},{6,7},{7,6},{8,9},{9,8},{10,11... | collective-permute-start | bytes 1572872 | tf_op jit(solution)/shard_map/ppermute | solution.py:26
  23.6 20.0 %copy-start.5 = (bf16[1,256,4096]{2,1,0:T(8,128)(2,1)S(1)}, bf16[1,256,4096]{2,1,0:T(8,128)(2,1)}, u32[]{:S(2)}) copy-start(bf16[1,256,4096]{2,1,0:T(8,128)(2,1)} %param.13) | copy-start | bytes 6291460
  23.6 8.6 %collective-permute-start.2 = (f32[2,256,2]{1,0,2:T(2,128)S(1)}, f32[2,256,2]{1,0,2:T(2,128)S(1)}, u32[]{:S(2)}, u32[]{:S(2)}) collective-permute-start(f32[2,256,2]{1,0,2:T(2,128)S(1)} %pad_maximum_fusion.2), channel_id=1, source_target_pairs={{0,2},{2,0},{1,3},{3,1},{4,6},{6,4},{5,7},{7,5},{8,10},{10,8},{9,1... | collective-permute-start | bytes 12296 | tf_op jit(solution)/shard_map/ppermute | solution.py:26
  32.2 11.4 %collective-permute-start.3 = (bf16[2,256,128]{1,2,0:T(8,128)(2,1)S(1)}, bf16[2,256,128]{1,2,0:T(8,128)(2,1)S(1)}, u32[]{:S(2)}, u32[]{:S(2)}) collective-permute-start(bf16[2,256,128]{1,2,0:T(8,128)(2,1)S(1)} %slice.132), channel_id=1, source_target_pairs={{0,2},{2,0},{1,3},{3,1},{4,6},{6,4},{5,7},{7,5},{8,10},{10,8},{9,1... | collective-permute-start | bytes 393224 | tf_op jit(solution)/shard_map/ppermute | solution.py:26
  44.3 1.3 copy-start.2
  46.7 11.6 %copy-start.13 = (s32[1,256,2]{1,2,0:T(2,128)S(1)}, s32[1,256,2]{1,2,0:T(2,128)}, u32[]{:S(2)}) copy-start(s32[1,256,2]{1,2,0:T(2,128)} %param.18) | copy-start | bytes 6148
  46.7 3.0 %collective-permute-start.4 = (bf16[4,2,16,4096]{3,2,1,0:T(8,128)(2,1)}, bf16[4,2,16,4096]{3,2,1,0:T(8,128)(2,1)}, u32[]{:S(2)}, u32[]{:S(2)}) collective-permute-start(bf16[4,2,16,4096]{3,2,1,0:T(8,128)(2,1)} %dynamic-slice_bitcast_fusion), channel_id=1, source_target_pairs={{0,1},{1,0},{2,3},{3,2},{4,5},{5,4},{6,7},{7,6},{8,9},{9,8},{10,11... | collective-permute-start | bytes 3145736 | tf_op jit(solution)/shard_map/ppermute | solution.py:26
  46.7 39.0 %copy-start.7 = (bf16[1,16,4096]{2,1,0:T(8,128)(2,1)S(1)}, bf16[1,16,4096]{2,1,0:T(8,128)(2,1)}, u32[]{:S(2)}) copy-start(bf16[1,16,4096]{2,1,0:T(8,128)(2,1)} %param.10) | copy-start | bytes 393220
  52.5 33.5 %copy-start.10 = (f32[1,4096]{1,0:T(1,128)S(1)}, f32[1,4096]{1,0:T(1,128)}, u32[]{:S(2)}) copy-start(f32[1,4096]{1,0:T(1,128)} %param.14) | copy-start | bytes 49156
  52.5 20.1 %all-to-all-start.1 = ((bf16[4,2,16,4096]{3,2,1,0:T(8,128)(2,1)}), bf16[4,2,16,4096]{3,2,1,0:T(8,128)(2,1)}, u32[]{:S(2)}, u32[]{:S(2)}) async-start(bf16[4,2,16,4096]{3,2,1,0:T(8,128)(2,1)} %fusion.17), calls=%async_computation.1 | async-start | bytes 2097152 | tf_op jit(solution)/shard_map/all_to_all | solution.py:94
  58.4 0.5 copy-start.11
  74.1 11.7 %collective-permute-start.5 = (bf16[16,4096]{1,0:T(8,128)(2,1)S(1)}, bf16[16,4096]{1,0:T(8,128)(2,1)S(1)}, u32[]{:S(2)}, u32[]{:S(2)}) collective-permute-start(bf16[16,4096]{1,0:T(8,128)(2,1)S(1)} %fusion.26), channel_id=1, source_target_pairs={{0,2},{2,0},{1,3},{3,1},{4,6},{6,4},{5,7},{7,5},{8,10},{10,8},{9,1... | collective-permute-start | bytes 393224 | tf_op jit(solution)/shard_map/ppermute | solution.py:26
  74.2 11.7 %copy-start.8 = (pred[48,16]{0,1:T(8,128)(4,1)}, pred[48,16]{0,1:T(8,128)(4,1)S(1)}, u32[]{:S(2)}) copy-start(pred[48,16]{0,1:T(8,128)(4,1)S(1)} %compare_and_fusion) | copy-start | bytes 2308
  103.1 20.0 %collective-permute-start.8 = (bf16[48,4096]{1,0:T(8,128)(2,1)}, bf16[48,4096]{1,0:T(8,128)(2,1)S(1)}, u32[]{:S(2)}, u32[]{:S(2)}) collective-permute-start(bf16[48,4096]{1,0:T(8,128)(2,1)} %all_to_all.26), channel_id=1, source_target_pairs={{0,2},{2,0},{1,3},{3,1},{4,6},{6,4},{5,7},{7,5},{8,10},{10,8},{9,1... | collective-permute-start | bytes 1179656 | tf_op jit(solution)/shard_map/ppermute | solution.py:26
  103.1 1.9 %collective-permute-start.6 = (bf16[48,4096]{1,0:T(8,128)(2,1)}, bf16[48,4096]{1,0:T(8,128)(2,1)S(1)}, u32[]{:S(2)}, u32[]{:S(2)}) collective-permute-start(bf16[48,4096]{1,0:T(8,128)(2,1)} %all_to_all.26), channel_id=1, source_target_pairs={{0,1},{1,0},{2,3},{3,2},{4,5},{5,4},{6,7},{7,6},{8,9},{9,8},{10,11... | collective-permute-start | bytes 1179656 | tf_op jit(solution)/shard_map/ppermute | solution.py:26
  104.1 21.6 %copy-start.1 = (bf16[1,4096,384]{2,1,0:T(8,128)(2,1)S(1)}, bf16[1,4096,384]{2,1,0:T(8,128)(2,1)}, u32[]{:S(2)}) copy-start(bf16[1,4096,384]{2,1,0:T(8,128)(2,1)} %param.16) | copy-start | bytes 9437188
  105.0 18.0 %copy-start.4 = (bf16[96,4096]{1,0:T(8,128)(2,1)}, bf16[96,4096]{1,0:T(8,128)(2,1)S(1)}, u32[]{:S(2)}) copy-start(bf16[96,4096]{1,0:T(8,128)(2,1)S(1)} %constant_dynamic-update-slice_fusion) | copy-start | bytes 2359300
  123.1 1.7 collective-permute-start.9
  124.8 0.9 copy-start.3
  133.3 6.1 %collective-permute-start.10 = (bf16[48,4096]{1,0:T(8,128)(2,1)}, bf16[48,4096]{1,0:T(8,128)(2,1)}, u32[]{:S(2)}, u32[]{:S(2)}) collective-permute-start(bf16[48,4096]{1,0:T(8,128)(2,1)} %slice.84), channel_id=1, source_target_pairs={{0,1},{1,0},{2,3},{3,2},{4,5},{5,4},{6,7},{7,6},{8,9},{9,8},{10,11... | collective-permute-start | bytes 1179656 | tf_op jit(solution)/shard_map/ppermute | solution.py:26
  137.9 34.4 %copy-start.12 = (s32[16,2]{0,1:T(2,128)S(1)}, s32[16,2]{0,1:T(2,128)}, u32[]{:S(2)}) copy-start(s32[16,2]{0,1:T(2,128)} %copy-done.11) | copy-start | bytes 388
  137.9 43.0 %copy-start.9 = (pred[48,16]{0,1:T(8,128)(4,1)S(1)}, pred[48,16]{0,1:T(8,128)(4,1)}, u32[]{:S(2)}) copy-start(pred[48,16]{0,1:T(8,128)(4,1)} %copy-done.8) | copy-start | bytes 2308
  139.0 2.5 %collective-permute-start.7 = (bf16[48,4096]{1,0:T(8,128)(2,1)S(1)}, bf16[48,4096]{1,0:T(8,128)(2,1)S(1)}, u32[]{:S(2)}, u32[]{:S(2)}) collective-permute-start(bf16[48,4096]{1,0:T(8,128)(2,1)S(1)} %slice.82), channel_id=1, source_target_pairs={{0,1},{1,0},{2,3},{3,2},{4,5},{5,4},{6,7},{7,6},{8,9},{9,8},{10,11... | collective-permute-start | bytes 1179656 | tf_op jit(solution)/shard_map/ppermute | solution.py:26
  140.6 22.3 %collective-permute-start.11 = (bf16[48,4096]{1,0:T(8,128)(2,1)S(1)}, bf16[48,4096]{1,0:T(8,128)(2,1)S(1)}, u32[]{:S(2)}, u32[]{:S(2)}) collective-permute-start(bf16[48,4096]{1,0:T(8,128)(2,1)S(1)} %add_convert_fusion.1), channel_id=1, source_target_pairs={{0,2},{2,0},{1,3},{3,1},{4,6},{6,4},{5,7},{7,5},{8,10},{10,8},{9,1... | collective-permute-start | bytes 1179656 | tf_op jit(solution)/shard_map/ppermute | solution.py:26
  166.7 12.3 %all-to-all-start.3 = ((bf16[4,12,4096]{2,1,0:T(8,128)(2,1)}), bf16[4,12,4096]{2,1,0:T(8,128)(2,1)}, u32[]{:S(2)}, u32[]{:S(2)}) async-start(bf16[4,12,4096]{2,1,0:T(8,128)(2,1)} %all_to_all.27), calls=%async_computation.3 | async-start | bytes 1048576 | tf_op jit(solution)/shard_map/all_to_all | solution.py:142
  182.2 9.0 %collective-permute-start.12 = (bf16[1,16,4096]{2,1,0:T(8,128)(2,1)S(1)}, bf16[1,16,4096]{2,1,0:T(8,128)(2,1)S(1)}, u32[]{:S(2)}, u32[]{:S(2)}) collective-permute-start(bf16[1,16,4096]{2,1,0:T(8,128)(2,1)S(1)} %fusion.3), channel_id=1, source_target_pairs={{240,0},{0,16},{16,32},{32,48},{48,64},{64,80},{80,96},{96,112},{1... | collective-permute-start | bytes 393224 | tf_op jit(solution)/shard_map/ppermute | solution.py:22

commit v4 on v3

--- a/solution.py
+++ b/solution.py
@@ -104,25 +104,32 @@
 
     split = FF // gate_w.shape[1]
     experts_count = devices // split
-    chosen = lax.dynamic_slice_in_dim(routes[0], my_index * tok_rows, tok_rows, 0)
-    scores_in = lax.dynamic_slice_in_dim(gate_scores[0], my_index * tok_rows, tok_rows, 0)
-    onehot = chosen[:, :, None] == jnp.arange(experts_count, dtype=jnp.int32)[None, None, :]
-    share = jnp.sum(jnp.where(onehot, scores_in[:, :, None], 0.0), axis=1) / jnp.sum(
-        scores_in, axis=1, keepdims=True
-    )
-    routed = jnp.any(onehot, axis=1)
-    slot = jnp.cumsum(routed.astype(jnp.int32), axis=0) - 1
-    select = routed[None] & (slot[None] == jnp.arange(CAP)[:, None, None])
-    select = select.transpose(2, 0, 1).reshape(experts_count * CAP, tok_rows)
-    dispatch = jnp.dot(
-        select.astype(jnp.bfloat16), normed, preferred_element_type=jnp.float32
-    ).astype(jnp.bfloat16)
+    partner = (yi * nz + (1 - zi)) * nc + ci
 
-    rows_y = lax.all_to_all(dispatch, "y", 0, 0, tiled=True)
-    rows_far = swap(rows_y, "zh")
-    near = jnp.concatenate([rows_y, swap(rows_y, "core")])
+    def plan(owner):
+        chosen = lax.dynamic_slice_in_dim(routes[0], owner * tok_rows, tok_rows, 0)
+        scores_in = lax.dynamic_slice_in_dim(gate_scores[0], owner * tok_rows, tok_rows, 0)
+        onehot = chosen[:, :, None] == jnp.arange(experts_count, dtype=jnp.int32)[None, None, :]
+        share = jnp.sum(jnp.where(onehot, scores_in[:, :, None], 0.0), axis=1) / jnp.sum(
+            scores_in, axis=1, keepdims=True
+        )
+        routed = jnp.any(onehot, axis=1)
+        slot = jnp.cumsum(routed.astype(jnp.int32), axis=0) - 1
+        select = routed[None] & (slot[None] == jnp.arange(CAP)[:, None, None])
+        select = select.transpose(2, 0, 1).reshape(experts_count * CAP, tok_rows)
+        combine = select.T.astype(jnp.float32) * jnp.repeat(share, CAP, axis=1)
+        return select.astype(jnp.bfloat16), combine
+
+    normed_far = swap(normed, "zh")
+    select_own, combine_own = plan(my_index)
+    select_far, combine_far = plan(partner)
+    dispatch_own = jnp.dot(select_own, normed, preferred_element_type=jnp.float32)
+    dispatch_far = jnp.dot(select_far, normed_far, preferred_element_type=jnp.float32)
+    rows_own = lax.all_to_all(dispatch_own.astype(jnp.bfloat16), "y", 0, 0, tiled=True)
+    rows_far = lax.all_to_all(dispatch_far.astype(jnp.bfloat16), "y", 0, 0, tiled=True)
+    near = jnp.concatenate([rows_own, swap(rows_own, "core")])
     far = jnp.concatenate([rows_far, swap(rows_far, "core")])
-    count = rows_y.shape[0]
+    count = rows_own.shape[0]
 
     def expert(rows):
         gate = jnp.dot(rows, gate_w, preferred_element_type=jnp.float32)
@@ -138,10 +145,12 @@
     near_sum = near_out[:count].astype(jnp.float32) + swap(near_out[count:], "core").astype(
         jnp.float32
     )
-    back = near_sum + swap(far_sum.astype(jnp.bfloat16), "zh").astype(jnp.float32)
-    picked = lax.all_to_all(back.astype(jnp.bfloat16), "y", 0, 0, tiled=True)
-    combine = select.T.astype(jnp.float32) * jnp.repeat(share, CAP, axis=1)
-    mixed = jnp.dot(combine, picked.astype(jnp.float32), precision=lax.Precision.HIGHEST)
+    back_far = lax.all_to_all(far_sum.astype(jnp.bfloat16), "y", 0, 0, tiled=True)
+    back_own = lax.all_to_all(near_sum.astype(jnp.bfloat16), "y", 0, 0, tiled=True)
+    hi = lax.Precision.HIGHEST
+    mixed_far = jnp.dot(combine_far, back_far.astype(jnp.float32), precision=hi)
+    mixed_own = jnp.dot(combine_own, back_own.astype(jnp.float32), precision=hi)
+    mixed = mixed_own + swap(mixed_far.astype(jnp.bfloat16), "zh").astype(jnp.float32)
     layer_out = (middle + mixed).astype(jnp.bfloat16)
     return shifted(layer_out[None], "section", 1)
 

time: 193 us -> 191 us (0.990)
  waiting for transfers between devices: 94.6 us -> 59.4 us
  starting transfers between devices: 32.8 us -> 54 us
  local copies, waits for them, and re-layouts: 18.7 us -> 35.1 us
  blocking collectives: 12.3 us -> 0 us
  other arithmetic: 13.2 us -> 17.1 us
  matrix products: 20 us -> 23.8 us
    ppermute x12, waiting for transfers between devices: 67.4 us -> 29.2 us  [swap(): return lax.ppermute(block, axis, [(0, 1), (1, 0)])]
    all_to_all x1 -> x4, starting transfers between devices: 5.61 us -> 22.4 us  [the longest x1 5.69 us: body(): lax.all_to_all(far_sum.astype(jnp.bfloat16), 'y', 0, 0, tiled=True)]
    all_to_all x1 -> x0, blocking collectives: 12.3 us -> none  [body(): rows_y = lax.all_to_all(dispatch, 'y', 0, 0, tiled=True)]
    all_to_all x4 -> x8, local copies, waits for them, and re-layouts: 7.53 us -> 15.1 us  [the longest x2 3.8 us: body(): lax.all_to_all(dispatch_far.astype(jnp.bfloat16), 'y', 0, 0, tiled=True)]
    ppermute x12, starting transfers between devices: 13.4 us -> 19.4 us  [swap(): return lax.ppermute(block, axis, [(0, 1), (1, 0)])]
    dot_general x2 -> x4, matrix products: 2.34 us -> 6.24 us  [the longest x1 1.96 us: body(): jnp.dot(select_far, normed_far, preferred_element_type=jnp.float32)]
    unnamed x33 -> x41, local copies, waits for them, and re-layouts: 4.58 us -> 6.77 us
    reshape x1 -> x2, local copies, waits for them, and re-layouts: 0.09 us -> 2.27 us  [plan(): combine = select.T.astype(jnp.float32) * jnp.repeat(share, CAP, axis=1)]
  transfers between devices with their start and end apart: 16 -> 19, of which waited for: 13 -> 11; matrix products, arithmetic and copies ran while one was open for 9% -> 18% of each run, Pallas kernels for 0% -> 0%
where the time goes in v4:
time: 191 us; the launch traced here: 190 us
  waiting for transfers between devices  59.4 us (31%)
  starting transfers between devices  54 us (28%)
  local copies, waits for them, and re-layouts  35.1 us (18%)
  matrix products  23.8 us (12%)
  other arithmetic  17.1 us (9%)
    ppermute x12, waiting for transfers between devices, swap(): return lax.ppermute(block, axis, [(0, 1), (1, 0)])  29.2 us
    ppermute x12, starting transfers between devices, swap(): return lax.ppermute(block, axis, [(0, 1), (1, 0)])  19.4 us
    all_to_all x1, waiting for transfers between devices, body(): part_y = lax.all_to_all(part_c.astype(jnp.bfloat16), 'y', 0, 0, tiled=True)  13 us
    dot_general x2, matrix products, expert(): out = jnp.dot(activated, down_w, preferred_element_type=jnp.float32)  8.96 us
    ppermute x1, waiting for transfers between devices, shifted(): return lax.ppermute(block, axis, route)  8.64 us
    unnamed x41, local copies, waits for them, and re-layouts  6.77 us
    all_to_all x1, starting transfers between devices, body(): kv_y = lax.all_to_all(send_kv, 'y', 0, 0, tiled=True)  6.25 us
    all_to_all x1, starting transfers between devices, body(): lax.all_to_all(far_sum.astype(jnp.bfloat16), 'y', 0, 0, tiled=True)  5.69 us
  transfers between devices with their start and end apart: 19, of which 11 were waited for; matrix products, arithmetic and copies ran while one was open for 18% of the time, Pallas kernels for 0%

profile of v4, /device:TPU:8, one launch (start us, length us, event | category | flops | bytes accessed | tf_op | source)
XLA Modules:
  0.0 189.7 jit_solution(12960411038093621754)
XLA Ops:
  0.0 1.2 reshape_squeeze.7
  1.6 0.9 pad_maximum_fusion.1
  2.5 6.3 %all-to-all-start = ((bf16[4,256,256]{2,1,0:T(8,128)(2,1)}), bf16[4,256,256]{2,1,0:T(8,128)(2,1)}, u32[]{:S(2)}, u32[]{:S(2)}) async-start(bf16[4,256,256]{2,1,0:T(8,128)(2,1)} %pad_maximum_fusion.1), calls=%async_computation | async-start | bytes 1048576 | tf_op jit(solution)/shard_map/all_to_all | solution.py:55
  8.9 5.9 %collective-permute-start = (bf16[2,256,128]{2,1,0:T(8,128)(2,1)S(1)}, bf16[2,256,128]{2,1,0:T(8,128)(2,1)S(1)}, u32[]{:S(2)}, u32[]{:S(2)}) collective-permute-start(bf16[2,256,128]{2,1,0:T(8,128)(2,1)S(1)} %bitcast.147), channel_id=1, source_target_pairs={{0,2},{2,0},{1,3},{3,1},{4,6},{6,4},{5,7},{7,5},{8,10},{10,8},{9,1... | collective-permute-start | bytes 393224 | tf_op jit(solution)/shard_map/ppermute | solution.py:26
  15.9 1.7 collective-permute-done.1
  17.6 1.1 pad_maximum_fusion
  18.8 0.7 collective-permute-done
  19.5 1.9 select_reduce_fusion
  21.3 2.3 %fusion = f32[4,256]{1,0:T(4,128)S(1)} fusion(f32[4,256,2048]{2,1,0:T(8,128)S(1)} %get-tuple-element.21, f32[4,256]{1,0:T(4,128)S(1)} %get-tuple-element.20, pred[256,2048]{1,0:T(8,128)(4,1)S(1)} %broadcast_compare_fusion), kind=kLoop, calls=%fused_computation.2 | loop fusion | flops 8387584 | bytes 8921088 | tf_op jit(solution)/shard_map/reduce_sum | solution.py:71
  23.6 6.6 %collective-permute-start.2 = (f32[2,256,2]{1,0,2:T(2,128)S(1)}, f32[2,256,2]{1,0,2:T(2,128)S(1)}, u32[]{:S(2)}, u32[]{:S(2)}) collective-permute-start(f32[2,256,2]{1,0,2:T(2,128)S(1)} %pad_maximum_fusion.2), channel_id=1, source_target_pairs={{0,2},{2,0},{1,3},{3,1},{4,6},{6,4},{5,7},{7,5},{8,10},{10,8},{9,1... | collective-permute-start | bytes 12296 | tf_op jit(solution)/shard_map/ppermute | solution.py:26
  30.2 1.9 %fusion.2 = f32[4,256,128]{1,2,0:T(8,128)S(1)} fusion(f32[4,256,2048]{2,1,0:T(8,128)S(1)} %get-tuple-element.21, f32[4,256]{1,0:T(4,128)S(1)} %get-tuple-element.20, pred[256,2048]{1,0:T(8,128)(4,1)S(1)} %broadcast_compare_fusion, bf16[2048,256]{1,0:T(8,128)(2,1)S(1)} %bitcast.143), kind=kOutput, calls=%fused_computation.10 | convolution fusion | flops 545259520 | bytes 9965568 | tf_op jit(solution)/shard_map/hqk,kd->hqd/dot_general | solution.py:72
  32.3 11.2 %collective-permute-done.3 = bf16[2,256,128]{1,2,0:T(8,128)(2,1)S(1)} collective-permute-done((bf16[2,256,128]{1,2,0:T(8,128)(2,1)S(1)}, bf16[2,256,128]{1,2,0:T(8,128)(2,1)S(1)}, u32[]{:S(2)}, u32[]{:S(2)}) %collective-permute-start.3) | collective-permute-done | bytes 131104 | tf_op jit(solution)/shard_map/ppermute | solution.py:26
  43.6 0.7 convolution_convert_fusion
  44.4 1.3 copy-done.2
  45.7 1.1 dynamic-slice_bitcast_fusion
  46.8 3.0 %collective-permute-done.4 = bf16[4,2,16,4096]{3,2,1,0:T(8,128)(2,1)} collective-permute-done((bf16[4,2,16,4096]{3,2,1,0:T(8,128)(2,1)}, bf16[4,2,16,4096]{3,2,1,0:T(8,128)(2,1)}, u32[]{:S(2)}, u32[]{:S(2)}) %collective-permute-start.4) | collective-permute-done | bytes 1048608 | tf_op jit(solution)/shard_map/ppermute | solution.py:26
  49.8 2.8 %fusion.15 = bf16[4,2,16,4096]{3,2,1,0:T(8,128)(2,1)} fusion(bf16[4,2,16,4096]{3,2,1,0:T(8,128)(2,1)} %collective-permute-done.4, bf16[4,2,2,16,4096]{4,3,2,1,0:T(8,128)(2,1)} %bitcast.141, s32[]{:T(128)S(6)} %select_n.47), kind=kLoop, calls=%fused_computation.23 | loop fusion | flops 2097152 | bytes 3145732 | tf_op jit(solution)/shard_map/convert_element_type | solution.py:94
  52.6 5.7 %all-to-all-start.1 = ((bf16[4,2,16,4096]{3,2,1,0:T(8,128)(2,1)}), bf16[4,2,16,4096]{3,2,1,0:T(8,128)(2,1)}, u32[]{:S(2)}, u32[]{:S(2)}) async-start(bf16[4,2,16,4096]{3,2,1,0:T(8,128)(2,1)} %fusion.15), calls=%async_computation.1 | async-start | bytes 2097152 | tf_op jit(solution)/shard_map/all_to_all | solution.py:94
  59.6 13.0 %all-to-all-done.1 = bf16[4,2,16,4096]{3,2,1,0:T(8,128)(2,1)} async-done(((bf16[4,2,16,4096]{3,2,1,0:T(8,128)(2,1)}), bf16[4,2,16,4096]{3,2,1,0:T(8,128)(2,1)}, u32[]{:S(2)}, u32[]{:S(2)}) %all-to-all-start.1) | async-done | bytes 1048608 | tf_op jit(solution)/shard_map/all_to_all | solution.py:94
  72.6 1.4 convert_reduce_fusion
  74.0 0.8 copy-done.5
  75.0 0.7 fusion.54
  76.3 10.3 %collective-permute-done.5 = bf16[16,4096]{1,0:T(8,128)(2,1)} collective-permute-done((bf16[16,4096]{1,0:T(8,128)(2,1)S(1)}, bf16[16,4096]{1,0:T(8,128)(2,1)}, u32[]{:S(2)}, u32[]{:S(2)}) %collective-permute-start.5) | collective-permute-done | bytes 131104 | tf_op jit(solution)/shard_map/ppermute | solution.py:26
  86.6 1.2 multiply_reduce_fusion
  87.8 0.8 multiply_convert_fusion
  88.9 1.1 convolution_convert_fusion.4
  90.0 1.9 all_to_all.40
  91.9 5.6 %all-to-all-start.2 = ((bf16[4,12,4096]{2,1,0:T(8,128)(2,1)}), bf16[4,12,4096]{2,1,0:T(8,128)(2,1)}, u32[]{:S(2)}, u32[]{:S(2)}) async-start(bf16[4,12,4096]{2,1,0:T(8,128)(2,1)} %all_to_all.40), calls=%async_computation.2 | async-start | bytes 1048576 | tf_op jit(solution)/shard_map/all_to_all | solution.py:128
  97.4 0.6 broadcast_divide_fusion
  98.1 0.7 broadcast_in_dim.98
  98.8 1.4 reshape.173
  100.3 2.0 %convolution_convert_fusion.3 = bf16[48,4096]{1,0:T(8,128)(2,1)} fusion(pred[48,16]{0,1:T(8,128)(4,1)S(1)} %get-tuple-element.19, bf16[16,4096]{1,0:T(8,128)(2,1)} %collective-permute-done.8), kind=kOutput, calls=%fused_computation.7 | convolution fusion | flops 6488064 | bytes 525056 | tf_op jit(solution)/shard_map/dot_general | solution.py:127
  102.2 1.9 %all_to_all.46 = bf16[4,12,4096]{2,1,0:T(8,128)(2,1)} reshape(bf16[48,4096]{1,0:T(8,128)(2,1)} %convolution_convert_fusion.3) | data formatting | bytes 786432 | tf_op jit(solution)/shard_map/all_to_all | solution.py:129
  104.1 5.6 %all-to-all-start.4 = ((bf16[4,12,4096]{2,1,0:T(8,128)(2,1)}), bf16[4,12,4096]{2,1,0:T(8,128)(2,1)}, u32[]{:S(2)}, u32[]{:S(2)}) async-start(bf16[4,12,4096]{2,1,0:T(8,128)(2,1)} %all_to_all.46), calls=%async_computation.4 | async-start | bytes 1048576 | tf_op jit(solution)/shard_map/all_to_all | solution.py:129
  109.7 1.9 all_to_all.42
  111.6 1.8 constant_dynamic-update-slice_fusion.1
  113.4 3.1 %all-to-all-done.4 = bf16[4,12,4096]{2,1,0:T(8,128)(2,1)} async-done(((bf16[4,12,4096]{2,1,0:T(8,128)(2,1)}), bf16[4,12,4096]{2,1,0:T(8,128)(2,1)}, u32[]{:S(2)}, u32[]{:S(2)}) %all-to-all-start.4) | async-done | bytes 393248 | tf_op jit(solution)/shard_map/all_to_all | solution.py:129
  116.4 1.9 all_to_all.48
  118.3 1.2 constant_dynamic-update-slice_fusion.3
  119.5 1.8 constant_dynamic-update-slice_fusion
  121.3 2.8 %fusion.9 = f32[96,384]{1,0:T(8,128)S(1)} fusion(bf16[96,4096]{1,0:T(8,128)(2,1)} %constant_dynamic-update-slice_fusion, bf16[1,4096,384]{2,1,0:T(8,128)(2,1)} %param.16), kind=kOutput, calls=%fused_computation.16 | convolution fusion | flops 301989888 | bytes 4079616 | tf_op jit(solution)/shard_map/dot_general | solution.py:136
  124.1 0.9 copy-done.3
  125.0 1.3 fusion.7
  126.3 4.5 %convolution_convert_fusion.1 = bf16[96,4096]{1,0:T(8,128)(2,1)} fusion(bf16[1,384,4096]{2,1,0:T(8,128)(2,1)S(1)} %copy-done, f32[96,384]{1,0:T(8,128)} %fusion.7, bf16[96,4096]{1,0:T(8,128)(2,1)} %copy-done.3, bf16[1,4096,384]{2,1,0:T(8,128)(2,1)} %param.15), kind=kOutput, calls=%fused_computation.5 | convolution fusion | flops 604594176 | bytes 8011776 | tf_op jit(solution)/shard_map/dot_general | solution.py:138
  130.8 1.8 slice.84
  132.9 4.5 %convolution_convert_fusion.2 = bf16[96,4096]{1,0:T(8,128)(2,1)} fusion(bf16[1,384,4096]{2,1,0:T(8,128)(2,1)S(1)} %copy-done, f32[96,384]{1,0:T(8,128)S(1)} %fusion.9, bf16[96,4096]{1,0:T(8,128)(2,1)} %constant_dynamic-update-slice_fusion, bf16[1,4096,384]{2,1,0:T(8,128)(2,1)} %param.15), kind=kOutput, calls=%fused_computation.6 | convolution fusion | flops 604594176 | bytes 8011776 | tf_op jit(solution)/shard_map/dot_general | solution.py:138
  137.4 1.8 slice.82
  139.4 1.9 %add_convert_fusion = bf16[48,4096]{1,0:T(8,128)(2,1)} fusion(bf16[48,4096]{1,0:T(8,128)(2,1)} %collective-permute-done.10, bf16[96,4096]{1,0:T(8,128)(2,1)} %convolution_convert_fusion.1), kind=kLoop, calls=%fused_computation.29 | loop fusion | flops 786432 | bytes 1179648 | tf_op jit(solution)/shard_map/convert_element_type | solution.py:148
  141.3 1.9 %all_to_all.49 = bf16[4,12,4096]{2,1,0:T(8,128)(2,1)} reshape(bf16[48,4096]{1,0:T(8,128)(2,1)} %add_convert_fusion) | data formatting | bytes 786432 | tf_op jit(solution)/shard_map/all_to_all | solution.py:148
  143.2 5.7 %all-to-all-start.5 = ((bf16[4,12,4096]{2,1,0:T(8,128)(2,1)}), bf16[4,12,4096]{2,1,0:T(8,128)(2,1)}, u32[]{:S(2)}, u32[]{:S(2)}) async-start(bf16[4,12,4096]{2,1,0:T(8,128)(2,1)} %all_to_all.49), calls=%async_computation.5 | async-start | bytes 1048576 | tf_op jit(solution)/shard_map/all_to_all | solution.py:148
  148.9 2.0 %add_convert_fusion.1 = bf16[48,4096]{1,0:T(8,128)(2,1)} fusion(bf16[48,4096]{1,0:T(8,128)(2,1)} %collective-permute-done.7, bf16[96,4096]{1,0:T(8,128)(2,1)} %convolution_convert_fusion.2), kind=kLoop, calls=%fused_computation.30 | loop fusion | flops 786432 | bytes 1179648 | tf_op jit(solution)/shard_map/convert_element_type | solution.py:149
  150.9 1.9 all_to_all.43
  152.8 5.1 %all-to-all-done.5 = bf16[4,12,4096]{2,1,0:T(8,128)(2,1)} async-done(((bf16[4,12,4096]{2,1,0:T(8,128)(2,1)}), bf16[4,12,4096]{2,1,0:T(8,128)(2,1)}, u32[]{:S(2)}, u32[]{:S(2)}) %all-to-all-start.5) | async-done | bytes 393248 | tf_op jit(solution)/shard_map/all_to_all | solution.py:148
  157.9 5.6 %all-to-all-start.3 = ((bf16[4,12,4096]{2,1,0:T(8,128)(2,1)}), bf16[4,12,4096]{2,1,0:T(8,128)(2,1)}, u32[]{:S(2)}, u32[]{:S(2)}) async-start(bf16[4,12,4096]{2,1,0:T(8,128)(2,1)} %all_to_all.43), calls=%async_computation.3 | async-start | bytes 1048576 | tf_op jit(solution)/shard_map/all_to_all | solution.py:149
  163.4 1.9 all_to_all.51
  165.3 1.9 %convolution_convert_fusion.5 = bf16[16,4096]{1,0:T(8,128)(2,1)} fusion(bf16[48,4096]{1,0:T(8,128)(2,1)} %all_to_all.51, f32[16,48]{1,0:T(8,128)S(1)} %copy-done.8, pred[48,16]{0,1:T(8,128)(4,1)S(1)} %copy-done.12), kind=kOutput, calls=%fused_computation.9 | convolution fusion | flops 37815040 | bytes 528128 | tf_op jit(solution)/shard_map/dot_general | solution.py:151
  167.2 5.9 %collective-permute-start.11 = (bf16[16,4096]{1,0:T(8,128)(2,1)}, bf16[16,4096]{1,0:T(8,128)(2,1)S(1)}, u32[]{:S(2)}, u32[]{:S(2)}) collective-permute-start(bf16[16,4096]{1,0:T(8,128)(2,1)} %convolution_convert_fusion.5), channel_id=1, source_target_pairs={{0,2},{2,0},{1,3},{3,1},{4,6},{6,4},{5,7},{7,5},{8,10},{10,8},{9,1... | collective-permute-start | bytes 393224 | tf_op jit(solution)/shard_map/ppermute | solution.py:26
  173.2 0.7 broadcast_in_dim.95
  173.9 0.8 reshape.172
  174.8 1.9 all_to_all.45
  176.7 2.1 %collective-permute-done.11 = bf16[16,4096]{1,0:T(8,128)(2,1)S(1)} collective-permute-done((bf16[16,4096]{1,0:T(8,128)(2,1)}, bf16[16,4096]{1,0:T(8,128)(2,1)S(1)}, u32[]{:S(2)}, u32[]{:S(2)}) %collective-permute-start.11) | collective-permute-done | bytes 131104 | tf_op jit(solution)/shard_map/ppermute | solution.py:26
  178.8 1.3 fusion.25
  180.4 8.6 %collective-permute-done.12 = bf16[1,16,4096]{2,1,0:T(8,128)(2,1)S(1)} collective-permute-done((bf16[1,16,4096]{2,1,0:T(8,128)(2,1)S(1)}, bf16[1,16,4096]{2,1,0:T(8,128)(2,1)S(1)}, u32[]{:S(2)}, u32[]{:S(2)}) %collective-permute-start.12) | collective-permute-done | bytes 131104 | tf_op jit(solution)/shard_map/ppermute | solution.py:22
  189.0 0.7 copy.52
  (97 shorter events, 5.3 us)
Async XLA Ops:
  0.0 126.3 %copy-start = (bf16[1,384,4096]{2,1,0:T(8,128)(2,1)S(1)}, bf16[1,384,4096]{2,1,0:T(8,128)(2,1)}, u32[]{:S(2)}) copy-start(bf16[1,384,4096]{2,1,0:T(8,128)(2,1)} %param.17) | copy-start | bytes 9437188
  0.0 8.7 %copy-start.6 = (bf16[1,256,256]{2,1,0:T(8,128)(2,1)S(1)}, bf16[1,256,256]{2,1,0:T(8,128)(2,1)}, u32[]{:S(2)}) copy-start(bf16[1,256,256]{2,1,0:T(8,128)(2,1)} %param.11) | copy-start | bytes 393220
  2.5 13.0 %all-to-all-start = ((bf16[4,256,256]{2,1,0:T(8,128)(2,1)}), bf16[4,256,256]{2,1,0:T(8,128)(2,1)}, u32[]{:S(2)}, u32[]{:S(2)}) async-start(bf16[4,256,256]{2,1,0:T(8,128)(2,1)} %pad_maximum_fusion.1), calls=%async_computation | async-start | bytes 1048576 | tf_op jit(solution)/shard_map/all_to_all | solution.py:55
  8.9 10.5 %collective-permute-start = (bf16[2,256,128]{2,1,0:T(8,128)(2,1)S(1)}, bf16[2,256,128]{2,1,0:T(8,128)(2,1)S(1)}, u32[]{:S(2)}, u32[]{:S(2)}) collective-permute-start(bf16[2,256,128]{2,1,0:T(8,128)(2,1)S(1)} %bitcast.147), channel_id=1, source_target_pairs={{0,2},{2,0},{1,3},{3,1},{4,6},{6,4},{5,7},{7,5},{8,10},{10,8},{9,1... | collective-permute-start | bytes 393224 | tf_op jit(solution)/shard_map/ppermute | solution.py:26
  15.5 2.1 %collective-permute-start.1 = (bf16[4,256,256]{2,1,0:T(8,128)(2,1)}, bf16[4,256,256]{2,1,0:T(8,128)(2,1)S(1)}, u32[]{:S(2)}, u32[]{:S(2)}) collective-permute-start(bf16[4,256,256]{2,1,0:T(8,128)(2,1)} %all-to-all-done), channel_id=1, source_target_pairs={{0,1},{1,0},{2,3},{3,2},{4,5},{5,4},{6,7},{7,6},{8,9},{9,8},{10,11... | collective-permute-start | bytes 1572872 | tf_op jit(solution)/shard_map/ppermute | solution.py:26
  23.6 20.0 %copy-start.4 = (bf16[1,256,4096]{2,1,0:T(8,128)(2,1)S(1)}, bf16[1,256,4096]{2,1,0:T(8,128)(2,1)}, u32[]{:S(2)}) copy-start(bf16[1,256,4096]{2,1,0:T(8,128)(2,1)} %param.13) | copy-start | bytes 6291460
  23.6 8.6 %collective-permute-start.2 = (f32[2,256,2]{1,0,2:T(2,128)S(1)}, f32[2,256,2]{1,0,2:T(2,128)S(1)}, u32[]{:S(2)}, u32[]{:S(2)}) collective-permute-start(f32[2,256,2]{1,0,2:T(2,128)S(1)} %pad_maximum_fusion.2), channel_id=1, source_target_pairs={{0,2},{2,0},{1,3},{3,1},{4,6},{6,4},{5,7},{7,5},{8,10},{10,8},{9,1... | collective-permute-start | bytes 12296 | tf_op jit(solution)/shard_map/ppermute | solution.py:26
  32.2 11.4 %collective-permute-start.3 = (bf16[2,256,128]{1,2,0:T(8,128)(2,1)S(1)}, bf16[2,256,128]{1,2,0:T(8,128)(2,1)S(1)}, u32[]{:S(2)}, u32[]{:S(2)}) collective-permute-start(bf16[2,256,128]{1,2,0:T(8,128)(2,1)S(1)} %slice.132), channel_id=1, source_target_pairs={{0,2},{2,0},{1,3},{3,1},{4,6},{6,4},{5,7},{7,5},{8,10},{10,8},{9,1... | collective-permute-start | bytes 393224 | tf_op jit(solution)/shard_map/ppermute | solution.py:26
  44.4 1.3 copy-start.2
  46.8 11.5 %copy-start.17 = (s32[1,256,2]{1,2,0:T(2,128)S(1)}, s32[1,256,2]{1,2,0:T(2,128)}, u32[]{:S(2)}) copy-start(s32[1,256,2]{1,2,0:T(2,128)} %param.18) | copy-start | bytes 6148
  46.8 3.0 %collective-permute-start.4 = (bf16[4,2,16,4096]{3,2,1,0:T(8,128)(2,1)}, bf16[4,2,16,4096]{3,2,1,0:T(8,128)(2,1)}, u32[]{:S(2)}, u32[]{:S(2)}) collective-permute-start(bf16[4,2,16,4096]{3,2,1,0:T(8,128)(2,1)} %dynamic-slice_bitcast_fusion), channel_id=1, source_target_pairs={{0,1},{1,0},{2,3},{3,2},{4,5},{5,4},{6,7},{7,6},{8,9},{9,8},{10,11... | collective-permute-start | bytes 3145736 | tf_op jit(solution)/shard_map/ppermute | solution.py:26
  46.8 28.2 %copy-start.15 = (f32[1,256,2]{1,2,0:T(2,128)S(1)}, f32[1,256,2]{1,2,0:T(2,128)}, u32[]{:S(2)}) copy-start(f32[1,256,2]{1,2,0:T(2,128)} %param.19) | copy-start | bytes 6148
  46.8 39.8 %copy-start.7 = (bf16[1,16,4096]{2,1,0:T(8,128)(2,1)S(1)}, bf16[1,16,4096]{2,1,0:T(8,128)(2,1)}, u32[]{:S(2)}) copy-start(bf16[1,16,4096]{2,1,0:T(8,128)(2,1)} %param.10) | copy-start | bytes 393220
  52.6 20.0 %all-to-all-start.1 = ((bf16[4,2,16,4096]{3,2,1,0:T(8,128)(2,1)}), bf16[4,2,16,4096]{3,2,1,0:T(8,128)(2,1)}, u32[]{:S(2)}, u32[]{:S(2)}) async-start(bf16[4,2,16,4096]{3,2,1,0:T(8,128)(2,1)} %fusion.15), calls=%async_computation.1 | async-start | bytes 2097152 | tf_op jit(solution)/shard_map/all_to_all | solution.py:94
  74.0 0.8 copy-start.5
  74.8 11.8 %collective-permute-start.5 = (bf16[16,4096]{1,0:T(8,128)(2,1)S(1)}, bf16[16,4096]{1,0:T(8,128)(2,1)}, u32[]{:S(2)}, u32[]{:S(2)}) collective-permute-start(bf16[16,4096]{1,0:T(8,128)(2,1)S(1)} %fusion.24), channel_id=1, source_target_pairs={{0,2},{2,0},{1,3},{3,1},{4,6},{6,4},{5,7},{7,5},{8,10},{10,8},{9,1... | collective-permute-start | bytes 393224 | tf_op jit(solution)/shard_map/ppermute | solution.py:26
  74.9 22.5 %copy-start.9 = (pred[48,16]{0,1:T(8,128)(4,1)}, pred[48,16]{0,1:T(8,128)(4,1)S(1)}, u32[]{:S(2)}) copy-start(pred[48,16]{0,1:T(8,128)(4,1)S(1)} %get-tuple-element.18) | copy-start | bytes 2308
  75.0 29.2 %copy-start.11 = (pred[48,16]{0,1:T(8,128)(4,1)}, pred[48,16]{0,1:T(8,128)(4,1)S(1)}, u32[]{:S(2)}) copy-start(pred[48,16]{0,1:T(8,128)(4,1)S(1)} %get-tuple-element.19) | copy-start | bytes 2308
  76.3 21.2 %copy-start.14 = (f32[16,4]{0,1:T(4,128)S(1)}, f32[16,4]{0,1:T(4,128)}, u32[]{:S(2)}) copy-start(f32[16,4]{0,1:T(4,128)} %get-tuple-element.24) | copy-start | bytes 772
  88.6 11.6 %collective-permute-start.8 = (bf16[16,4096]{1,0:T(8,128)(2,1)S(1)}, bf16[16,4096]{1,0:T(8,128)(2,1)}, u32[]{:S(2)}, u32[]{:S(2)}) collective-permute-start(bf16[16,4096]{1,0:T(8,128)(2,1)S(1)} %multiply_convert_fusion), channel_id=1, source_target_pairs={{0,2},{2,0},{1,3},{3,1},{4,6},{6,4},{5,7},{7,5},{8,10},{10,8},{9,1... | collective-permute-start | bytes 393224 | tf_op jit(solution)/shard_map/ppermute | solution.py:26
  91.9 12.3 %all-to-all-start.2 = ((bf16[4,12,4096]{2,1,0:T(8,128)(2,1)}), bf16[4,12,4096]{2,1,0:T(8,128)(2,1)}, u32[]{:S(2)}, u32[]{:S(2)}) async-start(bf16[4,12,4096]{2,1,0:T(8,128)(2,1)} %all_to_all.40), calls=%async_computation.2 | async-start | bytes 1048576 | tf_op jit(solution)/shard_map/all_to_all | solution.py:128
  104.1 12.3 %all-to-all-start.4 = ((bf16[4,12,4096]{2,1,0:T(8,128)(2,1)}), bf16[4,12,4096]{2,1,0:T(8,128)(2,1)}, u32[]{:S(2)}, u32[]{:S(2)}) async-start(bf16[4,12,4096]{2,1,0:T(8,128)(2,1)} %all_to_all.46), calls=%async_computation.4 | async-start | bytes 1048576 | tf_op jit(solution)/shard_map/all_to_all | solution.py:129
  111.6 7.9 %collective-permute-start.6 = (bf16[48,4096]{1,0:T(8,128)(2,1)}, bf16[48,4096]{1,0:T(8,128)(2,1)}, u32[]{:S(2)}, u32[]{:S(2)}) collective-permute-start(bf16[48,4096]{1,0:T(8,128)(2,1)} %all_to_all.42), channel_id=1, source_target_pairs={{0,1},{1,0},{2,3},{3,2},{4,5},{5,4},{6,7},{7,6},{8,9},{9,8},{10,11... | collective-permute-start | bytes 1179656 | tf_op jit(solution)/shard_map/ppermute | solution.py:26
  118.3 6.7 %copy-start.1 = (bf16[1,4096,384]{2,1,0:T(8,128)(2,1)S(1)}, bf16[1,4096,384]{2,1,0:T(8,128)(2,1)}, u32[]{:S(2)}) copy-start(bf16[1,4096,384]{2,1,0:T(8,128)(2,1)} %param.16) | copy-start | bytes 9437188
  118.3 5.7 %collective-permute-start.9 = (bf16[48,4096]{1,0:T(8,128)(2,1)}, bf16[48,4096]{1,0:T(8,128)(2,1)S(1)}, u32[]{:S(2)}, u32[]{:S(2)}) collective-permute-start(bf16[48,4096]{1,0:T(8,128)(2,1)} %all_to_all.48), channel_id=1, source_target_pairs={{0,1},{1,0},{2,3},{3,2},{4,5},{5,4},{6,7},{7,6},{8,9},{9,8},{10,11... | collective-permute-start | bytes 1179656 | tf_op jit(solution)/shard_map/ppermute | solution.py:26
  124.1 0.9 copy-start.3
  132.5 6.8 %collective-permute-start.10 = (bf16[48,4096]{1,0:T(8,128)(2,1)}, bf16[48,4096]{1,0:T(8,128)(2,1)}, u32[]{:S(2)}, u32[]{:S(2)}) collective-permute-start(bf16[48,4096]{1,0:T(8,128)(2,1)} %slice.84), channel_id=1, source_target_pairs={{0,1},{1,0},{2,3},{3,2},{4,5},{5,4},{6,7},{7,6},{8,9},{9,8},{10,11... | collective-permute-start | bytes 1179656 | tf_op jit(solution)/shard_map/ppermute | solution.py:26
  139.2 9.7 %collective-permute-start.7 = (bf16[48,4096]{1,0:T(8,128)(2,1)}, bf16[48,4096]{1,0:T(8,128)(2,1)}, u32[]{:S(2)}, u32[]{:S(2)}) collective-permute-start(bf16[48,4096]{1,0:T(8,128)(2,1)} %slice.82), channel_id=1, source_target_pairs={{0,1},{1,0},{2,3},{3,2},{4,5},{5,4},{6,7},{7,6},{8,9},{9,8},{10,11... | collective-permute-start | bytes 1179656 | tf_op jit(solution)/shard_map/ppermute | solution.py:26
  141.3 24.0 %copy-start.8 = (f32[16,48]{1,0:T(8,128)S(1)}, f32[16,48]{1,0:T(8,128)}, u32[]{:S(2)}) copy-start(f32[16,48]{1,0:T(8,128)} %reshape.173) | copy-start | bytes 9220
  141.3 24.0 %copy-start.12 = (pred[48,16]{0,1:T(8,128)(4,1)S(1)}, pred[48,16]{0,1:T(8,128)(4,1)}, u32[]{:S(2)}) copy-start(pred[48,16]{0,1:T(8,128)(4,1)} %copy-done.11) | copy-start | bytes 2308
  141.3 31.8 %copy-start.13 = (f32[16,4]{0,1:T(4,128)S(1)}, f32[16,4]{0,1:T(4,128)}, u32[]{:S(2)}) copy-start(f32[16,4]{0,1:T(4,128)} %get-tuple-element.25) | copy-start | bytes 772
  141.3 31.8 %copy-start.16 = (f32[16]{0:T(128)S(1)}, f32[16]{0:T(128)}, u32[]{:S(2)}) copy-start(f32[16]{0:T(128)} %get-tuple-element.5) | copy-start | bytes 196
  143.2 35.6 %copy-start.10 = (pred[48,16]{0,1:T(8,128)(4,1)S(1)}, pred[48,16]{0,1:T(8,128)(4,1)}, u32[]{:S(2)}) copy-start(pred[48,16]{0,1:T(8,128)(4,1)} %copy-done.9) | copy-start | bytes 2308
  143.2 14.6 %all-to-all-start.5 = ((bf16[4,12,4096]{2,1,0:T(8,128)(2,1)}), bf16[4,12,4096]{2,1,0:T(8,128)(2,1)}, u32[]{:S(2)}, u32[]{:S(2)}) async-start(bf16[4,12,4096]{2,1,0:T(8,128)(2,1)} %all_to_all.49), calls=%async_computation.5 | async-start | bytes 1048576 | tf_op jit(solution)/shard_map/all_to_all | solution.py:148
  157.9 16.9 %all-to-all-start.3 = ((bf16[4,12,4096]{2,1,0:T(8,128)(2,1)}), bf16[4,12,4096]{2,1,0:T(8,128)(2,1)}, u32[]{:S(2)}, u32[]{:S(2)}) async-start(bf16[4,12,4096]{2,1,0:T(8,128)(2,1)} %all_to_all.43), calls=%async_computation.3 | async-start | bytes 1048576 | tf_op jit(solution)/shard_map/all_to_all | solution.py:149
  167.2 11.5 %collective-permute-start.11 = (bf16[16,4096]{1,0:T(8,128)(2,1)}, bf16[16,4096]{1,0:T(8,128)(2,1)S(1)}, u32[]{:S(2)}, u32[]{:S(2)}) collective-permute-start(bf16[16,4096]{1,0:T(8,128)(2,1)} %convolution_convert_fusion.5), channel_id=1, source_target_pairs={{0,2},{2,0},{1,3},{3,1},{4,6},{6,4},{5,7},{7,5},{8,10},{10,8},{9,1... | collective-permute-start | bytes 393224 | tf_op jit(solution)/shard_map/ppermute | solution.py:26
  180.1 9.0 %collective-permute-start.12 = (bf16[1,16,4096]{2,1,0:T(8,128)(2,1)S(1)}, bf16[1,16,4096]{2,1,0:T(8,128)(2,1)S(1)}, u32[]{:S(2)}, u32[]{:S(2)}) collective-permute-start(bf16[1,16,4096]{2,1,0:T(8,128)(2,1)S(1)} %fusion.25), channel_id=1, source_target_pairs={{240,0},{0,16},{16,32},{32,48},{48,64},{64,80},{80,96},{96,112},{1... | collective-permute-start | bytes 393224 | tf_op jit(solution)/shard_map/ppermute | solution.py:22

commit v5 on v4

--- a/solution.py
+++ b/solution.py
@@ -125,31 +125,30 @@
     select_far, combine_far = plan(partner)
     dispatch_own = jnp.dot(select_own, normed, preferred_element_type=jnp.float32)
     dispatch_far = jnp.dot(select_far, normed_far, preferred_element_type=jnp.float32)
-    rows_own = lax.all_to_all(dispatch_own.astype(jnp.bfloat16), "y", 0, 0, tiled=True)
-    rows_far = lax.all_to_all(dispatch_far.astype(jnp.bfloat16), "y", 0, 0, tiled=True)
-    near = jnp.concatenate([rows_own, swap(rows_own, "core")])
-    far = jnp.concatenate([rows_far, swap(rows_far, "core")])
-    count = rows_own.shape[0]
+    width = normed.shape[1]
+    dispatch = jnp.stack(
+        [dispatch_own.reshape(experts_count, CAP, width), dispatch_far.reshape(experts_count, CAP, width)],
+        axis=1,
+    ).astype(jnp.bfloat16)
+    rows_y = lax.all_to_all(dispatch, "y", 0, 0, tiled=True)
+    rows = jnp.stack([rows_y, swap(rows_y, "core")])
+    flat = rows.reshape(-1, width)
+    gate = jnp.dot(flat, gate_w, preferred_element_type=jnp.float32)
+    upper = jnp.dot(flat, up_w, preferred_element_type=jnp.float32)
+    activated = (jax.nn.silu(gate) * upper).astype(jnp.bfloat16)
+    computed = (
+        jnp.dot(activated, down_w, preferred_element_type=jnp.float32)
+        .astype(jnp.bfloat16)
+        .reshape(rows.shape)
+    )
 
-    def expert(rows):
-        gate = jnp.dot(rows, gate_w, preferred_element_type=jnp.float32)
-        upper = jnp.dot(rows, up_w, preferred_element_type=jnp.float32)
-        activated = (jax.nn.silu(gate) * upper).astype(jnp.bfloat16)
-        out = jnp.dot(activated, down_w, preferred_element_type=jnp.float32)
-        return out.astype(jnp.bfloat16)
-
-    near_out = expert(near)
-    far_out = expert(far)
-
-    far_sum = far_out[:count].astype(jnp.float32) + swap(far_out[count:], "core").astype(jnp.float32)
-    near_sum = near_out[:count].astype(jnp.float32) + swap(near_out[count:], "core").astype(
-        jnp.float32
-    )
-    back_far = lax.all_to_all(far_sum.astype(jnp.bfloat16), "y", 0, 0, tiled=True)
-    back_own = lax.all_to_all(near_sum.astype(jnp.bfloat16), "y", 0, 0, tiled=True)
+    chip_sum = computed[0].astype(jnp.float32) + swap(computed[1], "core").astype(jnp.float32)
+    back = lax.all_to_all(chip_sum.astype(jnp.bfloat16), "y", 0, 0, tiled=True).astype(jnp.float32)
     hi = lax.Precision.HIGHEST
-    mixed_far = jnp.dot(combine_far, back_far.astype(jnp.float32), precision=hi)
-    mixed_own = jnp.dot(combine_own, back_own.astype(jnp.float32), precision=hi)
+    combine_own = combine_own.reshape(tok_rows, experts_count, CAP)
+    combine_far = combine_far.reshape(tok_rows, experts_count, CAP)
+    mixed_own = jnp.einsum("txj,xjd->td", combine_own, back[:, 0], precision=hi)
+    mixed_far = jnp.einsum("txj,xjd->td", combine_far, back[:, 1], precision=hi)
     mixed = mixed_own + swap(mixed_far.astype(jnp.bfloat16), "zh").astype(jnp.float32)
     layer_out = (middle + mixed).astype(jnp.bfloat16)
     return shifted(layer_out[None], "section", 1)

time: 191 us -> 195 us (1.021)
  waiting for transfers between devices: 59.4 us -> 82.9 us
  starting transfers between devices: 54 us -> 30.8 us
  blocking collectives: 0 us -> 11.9 us
  matrix products: 23.8 us -> 18.3 us
  local copies, waits for them, and re-layouts: 35.1 us -> 30.1 us
  other arithmetic: 17.1 us -> 19.4 us
    ppermute x12 -> x10, waiting for transfers between devices: 29.2 us -> 51.3 us  [swap(): return lax.ppermute(block, axis, [(0, 1), (1, 0)])]
    all_to_all x4 -> x1, starting transfers between devices: 22.4 us -> 5.6 us  [body(): lax.all_to_all(chip_sum.astype(jnp.bfloat16), 'y', 0, 0, tiled=True)]
    all_to_all x8 -> x1, local copies, waits for them, and re-layouts: 15.1 us -> 0.62 us  [body(): rows_y = lax.all_to_all(dispatch, 'y', 0, 0, tiled=True)]
    all_to_all x0 -> x1, blocking collectives: none -> 11.9 us  [body(): rows_y = lax.all_to_all(dispatch, 'y', 0, 0, tiled=True)]
    ppermute x12 -> x10, starting transfers between devices: 19.4 us -> 13.2 us  [swap(): return lax.ppermute(block, axis, [(0, 1), (1, 0)])]
    squeeze x0 -> x2, local copies, waits for them, and re-layouts: none -> 4.89 us  [body(): computed[1]]
    convert_element_type x0 -> x2, local copies, waits for them, and re-layouts: none -> 4.48 us  [the longest x1 2.76 us: body(): computed[0].astype(jnp.float32)]
    reshape x0 -> x3, local copies, waits for them, and re-layouts: none -> 4.35 us  [the longest x1 3.58 us: body(): flat = rows.reshape(-1, width)]
  transfers between devices with their start and end apart: 19 -> 14, of which waited for: 11 -> 12; matrix products, arithmetic and copies ran while one was open for 18% -> 6% of each run, Pallas kernels for 0% -> 0%
where the time goes in v5:
time: 195 us; the launch traced here: 194 us
  waiting for transfers between devices  82.9 us (43%)
  starting transfers between devices  30.8 us (16%)
  local copies, waits for them, and re-layouts  30.1 us (15%)
  other arithmetic  19.4 us (10%)
  matrix products  18.3 us (9%)
  blocking collectives  11.9 us (6%)
    ppermute x10, waiting for transfers between devices, swap(): return lax.ppermute(block, axis, [(0, 1), (1, 0)])  51.3 us
    ppermute x10, starting transfers between devices, swap(): return lax.ppermute(block, axis, [(0, 1), (1, 0)])  13.2 us
    all_to_all x1, waiting for transfers between devices, body(): part_y = lax.all_to_all(part_c.astype(jnp.bfloat16), 'y', 0, 0, tiled=True)  11.9 us
    all_to_all x1, blocking collectives, body(): rows_y = lax.all_to_all(dispatch, 'y', 0, 0, tiled=True)  11.9 us
    all_to_all x1, waiting for transfers between devices, body(): lax.all_to_all(chip_sum.astype(jnp.bfloat16), 'y', 0, 0, tiled=True)  10.3 us
    ppermute x1, waiting for transfers between devices, shifted(): return lax.ppermute(block, axis, route)  8.86 us
    all_to_all x1, starting transfers between devices, body(): kv_y = lax.all_to_all(send_kv, 'y', 0, 0, tiled=True)  6.25 us
    all_to_all x1, starting transfers between devices, body(): part_y = lax.all_to_all(part_c.astype(jnp.bfloat16), 'y', 0, 0, tiled=True)  5.67 us
  transfers between devices with their start and end apart: 14, of which 12 were waited for; matrix products, arithmetic and copies ran while one was open for 6% of the time, Pallas kernels for 0%

profile of v5, /device:TPU:8, one launch (start us, length us, event | category | flops | bytes accessed | tf_op | source)
XLA Modules:
  0.0 193.8 jit_solution(1444079158746194325)
XLA Ops:
  0.0 1.2 reshape_squeeze.7
  1.2 0.4 fusion.70
  1.6 0.8 pad_maximum_fusion.3
  2.5 6.3 %all-to-all-start = ((bf16[4,256,256]{2,1,0:T(8,128)(2,1)}), bf16[4,256,256]{2,1,0:T(8,128)(2,1)}, u32[]{:S(2)}, u32[]{:S(2)}) async-start(bf16[4,256,256]{2,1,0:T(8,128)(2,1)} %pad_maximum_fusion.3), calls=%async_computation | async-start | bytes 1048576 | tf_op jit(solution)/shard_map/all_to_all | solution.py:55
  8.8 0.1 copy.63
  8.9 5.9 %collective-permute-start = (bf16[2,256,128]{2,1,0:T(8,128)(2,1)S(1)}, bf16[2,256,128]{2,1,0:T(8,128)(2,1)S(1)}, u32[]{:S(2)}, u32[]{:S(2)}) collective-permute-start(bf16[2,256,128]{2,1,0:T(8,128)(2,1)S(1)} %bitcast.169), channel_id=1, source_target_pairs={{0,2},{2,0},{1,3},{3,1},{4,6},{6,4},{5,7},{7,5},{8,10},{10,8},{9,1... | collective-permute-start | bytes 393224 | tf_op jit(solution)/shard_map/ppermute | solution.py:26
  15.0 0.4 all-to-all-done
  15.5 0.4 broadcast_compare_fusion
  15.9 1.7 collective-permute-done.1
  17.6 1.1 pad_maximum_fusion.1
  18.8 0.7 collective-permute-done
  19.5 1.8 select_reduce_fusion
  21.3 2.3 %fusion = f32[4,256]{1,0:T(4,128)S(1)} fusion(f32[4,256,2048]{2,1,0:T(8,128)S(1)} %get-tuple-element.25, f32[4,256]{1,0:T(4,128)S(1)} %get-tuple-element.24, pred[256,2048]{1,0:T(8,128)(4,1)S(1)} %broadcast_compare_fusion), kind=kLoop, calls=%fused_computation.2 | loop fusion | flops 8387584 | bytes 8921088 | tf_op jit(solution)/shard_map/reduce_sum | solution.py:71
  23.6 6.6 %collective-permute-start.2 = (f32[2,256,2]{1,0,2:T(2,128)S(1)}, f32[2,256,2]{1,0,2:T(2,128)S(1)}, u32[]{:S(2)}, u32[]{:S(2)}) collective-permute-start(f32[2,256,2]{1,0,2:T(2,128)S(1)} %pad_maximum_fusion.4), channel_id=1, source_target_pairs={{0,2},{2,0},{1,3},{3,1},{4,6},{6,4},{5,7},{7,5},{8,10},{10,8},{9,1... | collective-permute-start | bytes 12296 | tf_op jit(solution)/shard_map/ppermute | solution.py:26
  30.2 1.9 fusion.5
  32.2 0.1 collective-permute-start.3
  32.3 11.2 %collective-permute-done.3 = bf16[2,256,128]{1,2,0:T(8,128)(2,1)S(1)} collective-permute-done((bf16[2,256,128]{1,2,0:T(8,128)(2,1)S(1)}, bf16[2,256,128]{1,2,0:T(8,128)(2,1)S(1)}, u32[]{:S(2)}, u32[]{:S(2)}) %collective-permute-start.3) | collective-permute-done | bytes 131104 | tf_op jit(solution)/shard_map/ppermute | solution.py:26
  43.6 0.7 convolution_convert_fusion
  44.4 1.3 copy-done.1
  45.7 1.1 dynamic-slice_bitcast_fusion
  46.8 3.0 %collective-permute-done.4 = bf16[4,2,16,4096]{3,2,1,0:T(8,128)(2,1)} collective-permute-done((bf16[4,2,16,4096]{3,2,1,0:T(8,128)(2,1)}, bf16[4,2,16,4096]{3,2,1,0:T(8,128)(2,1)}, u32[]{:S(2)}, u32[]{:S(2)}) %collective-permute-start.4) | collective-permute-done | bytes 1048608 | tf_op jit(solution)/shard_map/ppermute | solution.py:26
  49.8 2.8 %fusion.13 = bf16[4,2,16,4096]{3,2,1,0:T(8,128)(2,1)} fusion(bf16[4,2,16,4096]{3,2,1,0:T(8,128)(2,1)} %collective-permute-done.4, bf16[4,2,2,16,4096]{4,3,2,1,0:T(8,128)(2,1)} %bitcast.161, s32[]{:T(128)S(6)} %select_n.47), kind=kLoop, calls=%fused_computation.21 | loop fusion | flops 2097152 | bytes 3145732 | tf_op jit(solution)/shard_map/convert_element_type | solution.py:94
  52.5 5.7 %all-to-all-start.1 = ((bf16[4,2,16,4096]{3,2,1,0:T(8,128)(2,1)}), bf16[4,2,16,4096]{3,2,1,0:T(8,128)(2,1)}, u32[]{:S(2)}, u32[]{:S(2)}) async-start(bf16[4,2,16,4096]{3,2,1,0:T(8,128)(2,1)} %fusion.13), calls=%async_computation.1 | async-start | bytes 2097152 | tf_op jit(solution)/shard_map/all_to_all | solution.py:94
  58.3 0.6 copy-done.9
  59.2 0.7 copy.67
  59.9 0.7 fusion.46
  60.6 11.9 %all-to-all-done.1 = bf16[4,2,16,4096]{3,2,1,0:T(8,128)(2,1)} async-done(((bf16[4,2,16,4096]{3,2,1,0:T(8,128)(2,1)}), bf16[4,2,16,4096]{3,2,1,0:T(8,128)(2,1)}, u32[]{:S(2)}, u32[]{:S(2)}) %all-to-all-start.1) | async-done | bytes 1048608 | tf_op jit(solution)/shard_map/all_to_all | solution.py:94
  72.5 1.4 convert_reduce_fusion
  74.1 11.6 %collective-permute-done.5 = bf16[16,4096]{1,0:T(8,128)(2,1)S(1)} collective-permute-done((bf16[16,4096]{1,0:T(8,128)(2,1)S(1)}, bf16[16,4096]{1,0:T(8,128)(2,1)S(1)}, u32[]{:S(2)}, u32[]{:S(2)}) %collective-permute-start.5) | collective-permute-done | bytes 131104 | tf_op jit(solution)/shard_map/ppermute | solution.py:26
  85.7 0.2 multiply_reduce_fusion
  85.8 0.8 multiply_convert_fusion
  86.7 0.3 collective-permute-start.6
  86.9 0.8 fusion.45
  87.7 0.3 fusion.2
  88.1 9.6 %collective-permute-done.6 = bf16[16,4096]{1,0:T(8,128)(2,1)S(1)} collective-permute-done((bf16[16,4096]{1,0:T(8,128)(2,1)S(1)}, bf16[16,4096]{1,0:T(8,128)(2,1)S(1)}, u32[]{:S(2)}, u32[]{:S(2)}) %collective-permute-start.6) | collective-permute-done | bytes 131104 | tf_op jit(solution)/shard_map/ppermute | solution.py:26
  97.7 0.3 fusion.3
  98.0 0.1 pad_maximum_fusion.2
  98.2 0.8 copy.74
  99.0 11.9 %all_to_all.20 = bf16[4,2,12,4096]{3,1,2,0:T(2,128)(2,1)S(1)} all-to-all(bf16[4,2,12,4096]{3,1,2,0:T(2,128)(2,1)S(1)} %copy.74), channel_id=1, replica_groups=mesh['section'=16,'y'=4,'zh'=2,'core'=2] {'y'}, dimensions={0} | all-to-all | bytes 1572864 | tf_op jit(solution)/shard_map/all_to_all | solution.py:133
  110.9 0.6 copy.75
  111.6 2.3 %collective-permute-done.7 = bf16[4,2,12,4096]{3,0,2,1:T(4,128)(2,1)S(1)} collective-permute-done((bf16[4,2,12,4096]{3,0,2,1:T(4,128)(2,1)S(1)}, bf16[4,2,12,4096]{3,0,2,1:T(4,128)(2,1)S(1)}, u32[]{:S(2)}, u32[]{:S(2)}) %collective-permute-start.7) | collective-permute-done | bytes 786464 | tf_op jit(solution)/shard_map/ppermute | solution.py:26
  113.9 0.8 copy.117
  114.7 2.2 %pad_maximum_fusion = bf16[2,4,2,12,4096]{4,2,3,1,0:T(2,128)(2,1)S(1)} fusion(bf16[1,4,2,12,4096]{4,2,3,1,0:T(2,128)(2,1)S(1)} %bitcast.163, bf16[1,4,2,12,4096]{4,2,3,1,0:T(2,128)(2,1)S(1)} %bitcast.162), kind=kLoop, calls=%fused_computation.25 | loop fusion | flops 786432 | bytes 3145728 | tf_op jit(solution)/shard_map/stack | solution.py:134
  116.9 2.5 %copy.77 = bf16[2,4,2,12,4096]{4,3,2,1,0:T(8,128)(2,1)} copy(bf16[2,4,2,12,4096]{4,2,3,1,0:T(2,128)(2,1)S(1)} %pad_maximum_fusion) | data formatting | bytes 3145728 | tf_op jit(solution)/shard_map/stack | solution.py:134
  119.4 3.6 %reshape.220 = bf16[192,4096]{1,0:T(8,128)(2,1)} reshape(bf16[2,4,2,12,4096]{4,3,2,1,0:T(8,128)(2,1)} %copy.77) | data formatting | bytes 3145728 | tf_op jit(solution)/shard_map/reshape | solution.py:135
  123.0 4.1 %fusion.11 = f32[192,384]{1,0:T(8,128)} fusion(bf16[192,4096]{1,0:T(8,128)(2,1)} %reshape.220, bf16[1,4096,384]{2,1,0:T(8,128)(2,1)} %param.15), kind=kOutput, calls=%fused_computation.18 | convolution fusion | flops 603979776 | bytes 5013504 | tf_op jit(solution)/shard_map/dot_general | solution.py:136
  127.0 5.4 %convolution_convert_fusion.1 = bf16[192,4096]{1,0:T(8,128)(2,1)} fusion(bf16[1,384,4096]{2,1,0:T(8,128)(2,1)S(1)} %copy-done, bf16[192,4096]{1,0:T(8,128)(2,1)} %reshape.220, bf16[1,4096,384]{2,1,0:T(8,128)(2,1)} %param.16, f32[192,384]{1,0:T(8,128)} %fusion.11), kind=kOutput, calls=%fused_computation.5 | convolution fusion | flops 1209188352 | bytes 9732096 | tf_op jit(solution)/shard_map/dot_general | solution.py:140
  132.5 3.0 %fusion.68 = (bf16[96,4096]{1,0:T(8,128)(2,1)}, f32[96,4096]{1,0:T(8,128)}) fusion(bf16[192,4096]{1,0:T(8,128)(2,1)} %convolution_convert_fusion.1), kind=kLoop, calls=%fused_computation.121 | loop fusion | flops 393216 | bytes 3932160 | tf_op jit(solution)/shard_map/slice | solution.py:145
  135.5 2.2 %squeeze.43 = bf16[4,2,12,4096]{3,2,1,0:T(8,128)(2,1)} reshape(bf16[96,4096]{1,0:T(8,128)(2,1)} %get-tuple-element.9) | data formatting | bytes 1572864 | tf_op jit(solution)/shard_map/squeeze | solution.py:145
  137.6 2.7 %copy.78 = bf16[4,2,12,4096]{3,0,2,1:T(4,128)(2,1)} copy(bf16[4,2,12,4096]{3,2,1,0:T(8,128)(2,1)} %squeeze.43) | data formatting | bytes 1572864 | tf_op jit(solution)/shard_map/squeeze | solution.py:145
  140.3 0.1 collective-permute-start.8
  140.6 2.8 %reshape.225 = f32[4,2,12,4096]{3,2,1,0:T(8,128)} reshape(f32[96,4096]{1,0:T(8,128)} %get-tuple-element.10) | data formatting | bytes 3145728 | tf_op jit(solution)/shard_map/convert_element_type | solution.py:145
  143.4 2.3 %add_convert_fusion = bf16[4,2,12,4096]{3,2,1,0:T(8,128)(2,1)S(1)} fusion(f32[4,2,12,4096]{3,2,1,0:T(8,128)} %reshape.225, bf16[4,2,12,4096]{3,0,2,1:T(4,128)(2,1)} %collective-permute-done.8), kind=kLoop, calls=%fused_computation.23 | loop fusion | flops 1179648 | bytes 3145728 | tf_op jit(solution)/shard_map/convert_element_type | solution.py:146
  145.7 1.7 copy.80
  147.4 5.6 %all-to-all-start.3 = ((bf16[4,2,12,4096]{3,1,2,0:T(2,128)(2,1)}), bf16[4,2,12,4096]{3,1,2,0:T(2,128)(2,1)}, u32[]{:S(2)}, u32[]{:S(2)}) async-start(bf16[4,2,12,4096]{3,1,2,0:T(2,128)(2,1)} %copy.80), calls=%async_computation.3 | async-start | bytes 1572864 | tf_op jit(solution)/shard_map/all_to_all | solution.py:146
  153.9 0.1 reshape.221
  154.4 10.3 %all-to-all-done.3 = bf16[4,2,12,4096]{3,1,2,0:T(2,128)(2,1)} async-done(((bf16[4,2,12,4096]{3,1,2,0:T(2,128)(2,1)}), bf16[4,2,12,4096]{3,1,2,0:T(2,128)(2,1)}, u32[]{:S(2)}, u32[]{:S(2)}) %all-to-all-start.3) | async-done | bytes 786464 | tf_op jit(solution)/shard_map/all_to_all | solution.py:146
  164.8 3.9 %fusion.69 = (bf16[4,1,12,4096]{3,1,2,0:T(2,128)(2,1)S(1)}, bf16[4,1,12,4096]{3,1,2,0:T(2,128)(2,1)}) fusion(bf16[4,2,12,4096]{3,1,2,0:T(2,128)(2,1)} %all-to-all-done.3), kind=kLoop, calls=%fused_computation.122 | loop fusion | bytes 1572864 | tf_op jit(solution)/shard_map/slice | solution.py:151
  168.7 1.6 fusion.4
  170.2 0.7 reshape.219
  170.9 11.2 %collective-permute-done.9 = bf16[16,4096]{1,0:T(8,128)(2,1)S(1)} collective-permute-done((bf16[16,4096]{1,0:T(8,128)(2,1)}, bf16[16,4096]{1,0:T(8,128)(2,1)S(1)}, u32[]{:S(2)}, u32[]{:S(2)}) %collective-permute-start.9) | collective-permute-done | bytes 131104 | tf_op jit(solution)/shard_map/ppermute | solution.py:26
  182.1 2.0 %fusion.27 = bf16[1,16,4096]{2,1,0:T(8,128)(2,1)S(1)} fusion(f32[16,4096]{1,0:T(8,128)S(1)} %get-tuple-element.8, bf16[4,1,12,4096]{3,1,2,0:T(2,128)(2,1)} %get-tuple-element.12, bf16[16,4096]{1,0:T(8,128)(2,1)S(1)} %collective-permute-done.9, f32[16,4,12]{2,1,0:T(4,128)} %reshape.219), kind=kOutput, calls=%fused_computation.43 | convolution fusion | flops 38010880 | bytes 920576 | tf_op jit(solution)/shard_map/txj,xjd->td/dot_general | solution.py:150
  184.2 8.9 %collective-permute-done.10 = bf16[1,16,4096]{2,1,0:T(8,128)(2,1)S(1)} collective-permute-done((bf16[1,16,4096]{2,1,0:T(8,128)(2,1)S(1)}, bf16[1,16,4096]{2,1,0:T(8,128)(2,1)S(1)}, u32[]{:S(2)}, u32[]{:S(2)}) %collective-permute-start.10) | collective-permute-done | bytes 131104 | tf_op jit(solution)/shard_map/ppermute | solution.py:22
  193.1 0.7 copy.119
  (82 shorter events, 2.6 us)
Async XLA Ops:
  0.0 127.0 %copy-start = (bf16[1,384,4096]{2,1,0:T(8,128)(2,1)S(1)}, bf16[1,384,4096]{2,1,0:T(8,128)(2,1)}, u32[]{:S(2)}) copy-start(bf16[1,384,4096]{2,1,0:T(8,128)(2,1)} %param.17) | copy-start | bytes 9437188
  0.0 8.7 %copy-start.3 = (bf16[1,256,256]{2,1,0:T(8,128)(2,1)S(1)}, bf16[1,256,256]{2,1,0:T(8,128)(2,1)}, u32[]{:S(2)}) copy-start(bf16[1,256,256]{2,1,0:T(8,128)(2,1)} %param.11) | copy-start | bytes 393220
  2.5 13.0 %all-to-all-start = ((bf16[4,256,256]{2,1,0:T(8,128)(2,1)}), bf16[4,256,256]{2,1,0:T(8,128)(2,1)}, u32[]{:S(2)}, u32[]{:S(2)}) async-start(bf16[4,256,256]{2,1,0:T(8,128)(2,1)} %pad_maximum_fusion.3), calls=%async_computation | async-start | bytes 1048576 | tf_op jit(solution)/shard_map/all_to_all | solution.py:55
  8.9 10.5 %collective-permute-start = (bf16[2,256,128]{2,1,0:T(8,128)(2,1)S(1)}, bf16[2,256,128]{2,1,0:T(8,128)(2,1)S(1)}, u32[]{:S(2)}, u32[]{:S(2)}) collective-permute-start(bf16[2,256,128]{2,1,0:T(8,128)(2,1)S(1)} %bitcast.169), channel_id=1, source_target_pairs={{0,2},{2,0},{1,3},{3,1},{4,6},{6,4},{5,7},{7,5},{8,10},{10,8},{9,1... | collective-permute-start | bytes 393224 | tf_op jit(solution)/shard_map/ppermute | solution.py:26
  15.5 2.1 %collective-permute-start.1 = (bf16[4,256,256]{2,1,0:T(8,128)(2,1)}, bf16[4,256,256]{2,1,0:T(8,128)(2,1)S(1)}, u32[]{:S(2)}, u32[]{:S(2)}) collective-permute-start(bf16[4,256,256]{2,1,0:T(8,128)(2,1)} %all-to-all-done), channel_id=1, source_target_pairs={{0,1},{1,0},{2,3},{3,2},{4,5},{5,4},{6,7},{7,6},{8,9},{9,8},{10,11... | collective-permute-start | bytes 1572872 | tf_op jit(solution)/shard_map/ppermute | solution.py:26
  23.6 20.0 %copy-start.2 = (bf16[1,256,4096]{2,1,0:T(8,128)(2,1)S(1)}, bf16[1,256,4096]{2,1,0:T(8,128)(2,1)}, u32[]{:S(2)}) copy-start(bf16[1,256,4096]{2,1,0:T(8,128)(2,1)} %param.13) | copy-start | bytes 6291460
  23.6 8.6 %collective-permute-start.2 = (f32[2,256,2]{1,0,2:T(2,128)S(1)}, f32[2,256,2]{1,0,2:T(2,128)S(1)}, u32[]{:S(2)}, u32[]{:S(2)}) collective-permute-start(f32[2,256,2]{1,0,2:T(2,128)S(1)} %pad_maximum_fusion.4), channel_id=1, source_target_pairs={{0,2},{2,0},{1,3},{3,1},{4,6},{6,4},{5,7},{7,5},{8,10},{10,8},{9,1... | collective-permute-start | bytes 12296 | tf_op jit(solution)/shard_map/ppermute | solution.py:26
  32.2 11.4 %collective-permute-start.3 = (bf16[2,256,128]{1,2,0:T(8,128)(2,1)S(1)}, bf16[2,256,128]{1,2,0:T(8,128)(2,1)S(1)}, u32[]{:S(2)}, u32[]{:S(2)}) collective-permute-start(bf16[2,256,128]{1,2,0:T(8,128)(2,1)S(1)} %slice.133), channel_id=1, source_target_pairs={{0,2},{2,0},{1,3},{3,1},{4,6},{6,4},{5,7},{7,5},{8,10},{10,8},{9,1... | collective-permute-start | bytes 393224 | tf_op jit(solution)/shard_map/ppermute | solution.py:26
  44.3 1.3 copy-start.1
  46.7 11.5 %copy-start.14 = (s32[1,256,2]{1,2,0:T(2,128)S(1)}, s32[1,256,2]{1,2,0:T(2,128)}, u32[]{:S(2)}) copy-start(s32[1,256,2]{1,2,0:T(2,128)} %param.18) | copy-start | bytes 6148
  46.7 3.0 %collective-permute-start.4 = (bf16[4,2,16,4096]{3,2,1,0:T(8,128)(2,1)}, bf16[4,2,16,4096]{3,2,1,0:T(8,128)(2,1)}, u32[]{:S(2)}, u32[]{:S(2)}) collective-permute-start(bf16[4,2,16,4096]{3,2,1,0:T(8,128)(2,1)} %dynamic-slice_bitcast_fusion), channel_id=1, source_target_pairs={{0,1},{1,0},{2,3},{3,2},{4,5},{5,4},{6,7},{7,6},{8,9},{9,8},{10,11... | collective-permute-start | bytes 3145736 | tf_op jit(solution)/shard_map/ppermute | solution.py:26
  46.8 38.9 %copy-start.4 = (bf16[1,16,4096]{2,1,0:T(8,128)(2,1)S(1)}, bf16[1,16,4096]{2,1,0:T(8,128)(2,1)}, u32[]{:S(2)}) copy-start(bf16[1,16,4096]{2,1,0:T(8,128)(2,1)} %param.10) | copy-start | bytes 393220
  52.5 20.0 %all-to-all-start.1 = ((bf16[4,2,16,4096]{3,2,1,0:T(8,128)(2,1)}), bf16[4,2,16,4096]{3,2,1,0:T(8,128)(2,1)}, u32[]{:S(2)}, u32[]{:S(2)}) async-start(bf16[4,2,16,4096]{3,2,1,0:T(8,128)(2,1)} %fusion.13), calls=%async_computation.1 | async-start | bytes 2097152 | tf_op jit(solution)/shard_map/all_to_all | solution.py:94
  58.3 0.6 copy-start.9
  58.3 0.6 copy-start.11
  59.1 15.0 %copy-start.6 = (pred[4,16]{0,1:T(8,128)(4,1)}, pred[4,16]{0,1:T(8,128)(4,1)S(1)}, u32[]{:S(2)}) copy-start(pred[4,16]{0,1:T(8,128)(4,1)S(1)} %copy.71) | copy-start | bytes 196
  72.5 25.2 %copy-start.5 = (pred[4,12,16]{1,0,2:T(4,128)(4,1)S(1)}, pred[4,12,16]{1,0,2:T(4,128)(4,1)}, u32[]{:S(2)}) copy-start(pred[4,12,16]{1,0,2:T(4,128)(4,1)} %fusion.46) | copy-start | bytes 2308
  74.0 11.7 %collective-permute-start.5 = (bf16[16,4096]{1,0:T(8,128)(2,1)S(1)}, bf16[16,4096]{1,0:T(8,128)(2,1)S(1)}, u32[]{:S(2)}, u32[]{:S(2)}) collective-permute-start(bf16[16,4096]{1,0:T(8,128)(2,1)S(1)} %fusion.40), channel_id=1, source_target_pairs={{0,2},{2,0},{1,3},{3,1},{4,6},{6,4},{5,7},{7,5},{8,10},{10,8},{9,1... | collective-permute-start | bytes 393224 | tf_op jit(solution)/shard_map/ppermute | solution.py:26
  86.7 11.0 %collective-permute-start.6 = (bf16[16,4096]{1,0:T(8,128)(2,1)S(1)}, bf16[16,4096]{1,0:T(8,128)(2,1)S(1)}, u32[]{:S(2)}, u32[]{:S(2)}) collective-permute-start(bf16[16,4096]{1,0:T(8,128)(2,1)S(1)} %multiply_convert_fusion), channel_id=1, source_target_pairs={{0,2},{2,0},{1,3},{3,1},{4,6},{6,4},{5,7},{7,5},{8,10},{10,8},{9,1... | collective-permute-start | bytes 393224 | tf_op jit(solution)/shard_map/ppermute | solution.py:26
  111.5 2.4 %collective-permute-start.7 = (bf16[4,2,12,4096]{3,0,2,1:T(4,128)(2,1)S(1)}, bf16[4,2,12,4096]{3,0,2,1:T(4,128)(2,1)S(1)}, u32[]{:S(2)}, u32[]{:S(2)}) collective-permute-start(bf16[4,2,12,4096]{3,0,2,1:T(4,128)(2,1)S(1)} %copy.75), channel_id=1, source_target_pairs={{0,1},{1,0},{2,3},{3,2},{4,5},{5,4},{6,7},{7,6},{8,9},{9,8},{10,11... | collective-permute-start | bytes 2359304 | tf_op jit(solution)/shard_map/ppermute | solution.py:26
  132.5 8.0 %copy-start.13 = (f32[1,256,2]{1,2,0:T(2,128)S(1)}, f32[1,256,2]{1,2,0:T(2,128)}, u32[]{:S(2)}) copy-start(f32[1,256,2]{1,2,0:T(2,128)} %param.19) | copy-start | bytes 6148
  132.5 8.1 %copy-start.10 = (s32[16,2]{0,1:T(2,128)S(1)}, s32[16,2]{0,1:T(2,128)}, u32[]{:S(2)}) copy-start(s32[16,2]{0,1:T(2,128)} %copy-done.9) | copy-start | bytes 388
  132.5 8.1 %copy-start.12 = (s32[16,2]{0,1:T(2,128)S(1)}, s32[16,2]{0,1:T(2,128)}, u32[]{:S(2)}) copy-start(s32[16,2]{0,1:T(2,128)} %copy-done.11) | copy-start | bytes 388
  140.3 3.0 %collective-permute-start.8 = (bf16[4,2,12,4096]{3,0,2,1:T(4,128)(2,1)}, bf16[4,2,12,4096]{3,0,2,1:T(4,128)(2,1)}, u32[]{:S(2)}, u32[]{:S(2)}) collective-permute-start(bf16[4,2,12,4096]{3,0,2,1:T(4,128)(2,1)} %copy.78), channel_id=1, source_target_pairs={{0,1},{1,0},{2,3},{3,2},{4,5},{5,4},{6,7},{7,6},{8,9},{9,8},{10,11... | collective-permute-start | bytes 2359304 | tf_op jit(solution)/shard_map/ppermute | solution.py:26
  143.4 9.9 %copy-start.8 = (pred[4,16]{0,1:T(8,128)(4,1)S(1)}, pred[4,16]{0,1:T(8,128)(4,1)}, u32[]{:S(2)}) copy-start(pred[4,16]{0,1:T(8,128)(4,1)} %copy.67) | copy-start | bytes 196
  143.4 10.6 %copy-start.7 = (pred[4,16]{0,1:T(8,128)(4,1)S(1)}, pred[4,16]{0,1:T(8,128)(4,1)}, u32[]{:S(2)}) copy-start(pred[4,16]{0,1:T(8,128)(4,1)} %copy-done.6) | copy-start | bytes 196
  147.4 17.4 %all-to-all-start.3 = ((bf16[4,2,12,4096]{3,1,2,0:T(2,128)(2,1)}), bf16[4,2,12,4096]{3,1,2,0:T(2,128)(2,1)}, u32[]{:S(2)}, u32[]{:S(2)}) async-start(bf16[4,2,12,4096]{3,1,2,0:T(2,128)(2,1)} %copy.80), calls=%async_computation.3 | async-start | bytes 1572864 | tf_op jit(solution)/shard_map/all_to_all | solution.py:146
  170.2 11.9 %collective-permute-start.9 = (bf16[16,4096]{1,0:T(8,128)(2,1)}, bf16[16,4096]{1,0:T(8,128)(2,1)S(1)}, u32[]{:S(2)}, u32[]{:S(2)}) collective-permute-start(bf16[16,4096]{1,0:T(8,128)(2,1)} %fusion.4), channel_id=1, source_target_pairs={{0,2},{2,0},{1,3},{3,1},{4,6},{6,4},{5,7},{7,5},{8,10},{10,8},{9,1... | collective-permute-start | bytes 393224 | tf_op jit(solution)/shard_map/ppermute | solution.py:26
  184.2 9.0 %collective-permute-start.10 = (bf16[1,16,4096]{2,1,0:T(8,128)(2,1)S(1)}, bf16[1,16,4096]{2,1,0:T(8,128)(2,1)S(1)}, u32[]{:S(2)}, u32[]{:S(2)}) collective-permute-start(bf16[1,16,4096]{2,1,0:T(8,128)(2,1)S(1)} %fusion.27), channel_id=1, source_target_pairs={{240,0},{0,16},{16,32},{32,48},{48,64},{64,80},{80,96},{96,112},{1... | collective-permute-start | bytes 393224 | tf_op jit(solution)/shard_map/ppermute | solution.py:22

commit v6 on v5

--- a/solution.py
+++ b/solution.py
@@ -12,7 +12,7 @@
 KVHEADS = 2
 CTX = 4096
 MB = 256
-CAP = 12
+CAP = 16
 EXPERT_AXES = ("y", "zh", "core")
 
 

time: 195 us -> 175 us (0.90)
  the two profiles are of different devices: /device:TPU:8 before, /device:TPU:32 now
where the time goes in v6:
time: 175 us; the launch traced here: 172 us
  waiting for transfers between devices  80.6 us (46%)
  starting transfers between devices  30.7 us (18%)
  matrix products  19.1 us (11%)
  blocking collectives  17.1 us (10%)
  other arithmetic  13.2 us (8%)
  local copies, waits for them, and re-layouts  11.3 us (6%)
    ppermute x10, waiting for transfers between devices, swap(): return lax.ppermute(block, axis, [(0, 1), (1, 0)])  46.3 us
    all_to_all x1, blocking collectives, body(): rows_y = lax.all_to_all(dispatch, 'y', 0, 0, tiled=True)  17.1 us
    ppermute x10, starting transfers between devices, swap(): return lax.ppermute(block, axis, [(0, 1), (1, 0)])  14.9 us
    all_to_all x1, waiting for transfers between devices, body(): lax.all_to_all(chip_sum.astype(jnp.bfloat16), 'y', 0, 0, tiled=True)  14.6 us
    all_to_all x1, waiting for transfers between devices, body(): part_y = lax.all_to_all(part_c.astype(jnp.bfloat16), 'y', 0, 0, tiled=True)  14.2 us
    dot_general x1, matrix products, body(): jnp.dot(activated, down_w, preferred_element_type=jnp.float32)  6.36 us
    all_to_all x1, starting transfers between devices, body(): kv_y = lax.all_to_all(send_kv, 'y', 0, 0, tiled=True)  4.46 us
    all_to_all x1, starting transfers between devices, body(): part_y = lax.all_to_all(part_c.astype(jnp.bfloat16), 'y', 0, 0, tiled=True)  4.24 us
  transfers between devices with their start and end apart: 14, of which 12 were waited for; matrix products, arithmetic and copies ran while one was open for 5% of the time, Pallas kernels for 0%

profile of v6, /device:TPU:32, one launch (start us, length us, event | category | flops | bytes accessed | tf_op | source)
XLA Modules:
  0.0 172.4 jit_solution(8328707962246723119)
XLA Ops:
  0.0 1.2 reshape_squeeze.7
  1.2 0.4 fusion.65
  1.6 0.8 pad_maximum_fusion.3
  2.4 4.5 %all-to-all-start = ((bf16[4,256,256]{2,1,0:T(8,128)(2,1)}), bf16[4,256,256]{2,1,0:T(8,128)(2,1)}, u32[]{:S(2)}, u32[]{:S(2)}) async-start(bf16[4,256,256]{2,1,0:T(8,128)(2,1)} %pad_maximum_fusion.3), calls=%async_computation | async-start | bytes 1048576 | tf_op jit(solution)/shard_map/all_to_all | solution.py:55
  6.9 0.1 copy.68
  7.0 0.1 copy.69
  7.1 6.4 %collective-permute-start = (bf16[2,256,128]{2,1,0:T(8,128)(2,1)S(1)}, bf16[2,256,128]{2,1,0:T(8,128)(2,1)S(1)}, u32[]{:S(2)}, u32[]{:S(2)}) collective-permute-start(bf16[2,256,128]{2,1,0:T(8,128)(2,1)S(1)} %bitcast.175), channel_id=1, source_target_pairs={{0,2},{2,0},{1,3},{3,1},{4,6},{6,4},{5,7},{7,5},{8,10},{10,8},{9,1... | collective-permute-start | bytes 393224 | tf_op jit(solution)/shard_map/ppermute | solution.py:26
  13.7 2.8 %all-to-all-done = bf16[4,256,256]{2,1,0:T(8,128)(2,1)} async-done(((bf16[4,256,256]{2,1,0:T(8,128)(2,1)}), bf16[4,256,256]{2,1,0:T(8,128)(2,1)}, u32[]{:S(2)}, u32[]{:S(2)}) %all-to-all-start) | async-done | bytes 524320 | tf_op jit(solution)/shard_map/all_to_all | solution.py:55
  16.5 0.4 broadcast_compare_fusion
  16.9 1.7 %collective-permute-done.1 = bf16[4,256,256]{2,1,0:T(8,128)(2,1)S(1)} collective-permute-done((bf16[4,256,256]{2,1,0:T(8,128)(2,1)}, bf16[4,256,256]{2,1,0:T(8,128)(2,1)S(1)}, u32[]{:S(2)}, u32[]{:S(2)}) %collective-permute-start.1) | collective-permute-done | bytes 524320 | tf_op jit(solution)/shard_map/ppermute | solution.py:26
  18.6 1.1 pad_maximum_fusion.1
  19.8 1.9 %select_reduce_fusion = (f32[4,256]{1,0:T(4,128)S(1)}, f32[4,256,2048]{2,1,0:T(8,128)S(1)}) fusion(pred[256,2048]{1,0:T(8,128)(4,1)S(1)} %broadcast_compare_fusion, bf16[2048,256]{1,0:T(8,128)(2,1)S(1)} %bitcast.166, bf16[2,256,128]{2,1,0:T(8,128)(2,1)S(1)} %collective-permute-done, bf16[2,256,128]{2,1,0:T(8,128)(2,1)S(1)} %bitcast.176), kind=kOutput, calls=%fused_computation.1 | convolution fusion | flops 543292416 | bytes 9703424 | tf_op jit(solution)/shard_map/hqd,kd->hqk/dot_general | solution.py:68
  21.6 2.3 %fusion = f32[4,256]{1,0:T(4,128)S(1)} fusion(f32[4,256,2048]{2,1,0:T(8,128)S(1)} %get-tuple-element.23, f32[4,256]{1,0:T(4,128)S(1)} %get-tuple-element.22, pred[256,2048]{1,0:T(8,128)(4,1)S(1)} %broadcast_compare_fusion), kind=kLoop, calls=%fused_computation.2 | loop fusion | flops 8387584 | bytes 8921088 | tf_op jit(solution)/shard_map/reduce_sum | solution.py:71
  23.9 6.4 %collective-permute-start.2 = (f32[2,256,2]{1,0,2:T(2,128)S(1)}, f32[2,256,2]{1,0,2:T(2,128)S(1)}, u32[]{:S(2)}, u32[]{:S(2)}) collective-permute-start(f32[2,256,2]{1,0,2:T(2,128)S(1)} %pad_maximum_fusion.4), channel_id=1, source_target_pairs={{0,2},{2,0},{1,3},{3,1},{4,6},{6,4},{5,7},{7,5},{8,10},{10,8},{9,1... | collective-permute-start | bytes 12296 | tf_op jit(solution)/shard_map/ppermute | solution.py:26
  30.3 1.9 %fusion.5 = f32[4,256,128]{1,2,0:T(8,128)S(1)} fusion(f32[4,256,2048]{2,1,0:T(8,128)S(1)} %get-tuple-element.23, f32[4,256]{1,0:T(4,128)S(1)} %get-tuple-element.22, pred[256,2048]{1,0:T(8,128)(4,1)S(1)} %broadcast_compare_fusion, bf16[2048,256]{1,0:T(8,128)(2,1)S(1)} %bitcast.167), kind=kOutput, calls=%fused_computation.13 | convolution fusion | flops 545259520 | bytes 9965568 | tf_op jit(solution)/shard_map/hqk,kd->hqd/dot_general | solution.py:72
  32.3 0.1 collective-permute-start.3
  32.4 11.9 %collective-permute-done.3 = bf16[2,256,128]{1,2,0:T(8,128)(2,1)S(1)} collective-permute-done((bf16[2,256,128]{1,2,0:T(8,128)(2,1)S(1)}, bf16[2,256,128]{1,2,0:T(8,128)(2,1)S(1)}, u32[]{:S(2)}, u32[]{:S(2)}) %collective-permute-start.3) | collective-permute-done | bytes 131104 | tf_op jit(solution)/shard_map/ppermute | solution.py:26
  44.4 0.7 convolution_convert_fusion.1
  45.2 1.3 copy-done.1
  46.5 1.1 dynamic-slice_bitcast_fusion
  47.6 3.0 %collective-permute-done.4 = bf16[4,2,16,4096]{3,2,1,0:T(8,128)(2,1)} collective-permute-done((bf16[4,2,16,4096]{3,2,1,0:T(8,128)(2,1)}, bf16[4,2,16,4096]{3,2,1,0:T(8,128)(2,1)}, u32[]{:S(2)}, u32[]{:S(2)}) %collective-permute-start.4) | collective-permute-done | bytes 1048608 | tf_op jit(solution)/shard_map/ppermute | solution.py:26
  50.6 2.8 %fusion.14 = bf16[4,2,16,4096]{3,2,1,0:T(8,128)(2,1)} fusion(bf16[4,2,16,4096]{3,2,1,0:T(8,128)(2,1)} %collective-permute-done.4, bf16[4,2,2,16,4096]{4,3,2,1,0:T(8,128)(2,1)} %bitcast.161, s32[]{:T(128)S(6)} %select_n.47), kind=kLoop, calls=%fused_computation.24 | loop fusion | flops 2097152 | bytes 3145732 | tf_op jit(solution)/shard_map/convert_element_type | solution.py:94
  53.3 4.2 %all-to-all-start.1 = ((bf16[4,2,16,4096]{3,2,1,0:T(8,128)(2,1)}), bf16[4,2,16,4096]{3,2,1,0:T(8,128)(2,1)}, u32[]{:S(2)}, u32[]{:S(2)}) async-start(bf16[4,2,16,4096]{3,2,1,0:T(8,128)(2,1)} %fusion.14), calls=%async_computation.1 | async-start | bytes 2097152 | tf_op jit(solution)/shard_map/all_to_all | solution.py:94
  57.7 0.5 copy-done.7
  58.5 0.6 reduce_window_sum.17
  59.1 14.2 %all-to-all-done.1 = bf16[4,2,16,4096]{3,2,1,0:T(8,128)(2,1)} async-done(((bf16[4,2,16,4096]{3,2,1,0:T(8,128)(2,1)}), bf16[4,2,16,4096]{3,2,1,0:T(8,128)(2,1)}, u32[]{:S(2)}, u32[]{:S(2)}) %all-to-all-start.1) | async-done | bytes 1048608 | tf_op jit(solution)/shard_map/all_to_all | solution.py:94
  73.3 1.4 convert_reduce_fusion
  74.8 0.4 collective-permute-start.5
  75.2 10.3 %collective-permute-done.5 = bf16[16,4096]{1,0:T(8,128)(2,1)S(1)} collective-permute-done((bf16[16,4096]{1,0:T(8,128)(2,1)S(1)}, bf16[16,4096]{1,0:T(8,128)(2,1)S(1)}, u32[]{:S(2)}, u32[]{:S(2)}) %collective-permute-start.5) | collective-permute-done | bytes 131104 | tf_op jit(solution)/shard_map/ppermute | solution.py:26
  85.6 0.2 multiply_reduce_fusion
  85.7 0.8 multiply_convert_fusion.1
  86.6 0.7 collective-permute-start.6
  87.3 0.7 add_bitcast_fusion.1
  88.0 0.7 copy.79
  88.7 0.9 fusion.2
  89.6 6.4 %collective-permute-done.6 = bf16[16,4096]{1,0:T(8,128)(2,1)} collective-permute-done((bf16[16,4096]{1,0:T(8,128)(2,1)S(1)}, bf16[16,4096]{1,0:T(8,128)(2,1)}, u32[]{:S(2)}, u32[]{:S(2)}) %collective-permute-start.6) | collective-permute-done | bytes 131104 | tf_op jit(solution)/shard_map/ppermute | solution.py:26
  96.0 1.2 fusion.3
  97.2 0.1 pad_maximum_fusion.2
  97.3 0.1 copy.80
  97.4 17.1 %all_to_all.20 = bf16[4,2,16,4096]{3,2,1,0:T(8,128)(2,1)S(1)} all-to-all(bf16[4,2,16,4096]{3,2,1,0:T(8,128)(2,1)S(1)} %copy.80), channel_id=1, replica_groups=mesh['section'=16,'y'=4,'zh'=2,'core'=2] {'y'}, dimensions={0} | all-to-all | bytes 2097152 | tf_op jit(solution)/shard_map/all_to_all | solution.py:133
  114.5 2.7 %collective-permute-done.7 = bf16[4,2,16,4096]{3,2,1,0:T(8,128)(2,1)S(1)} collective-permute-done((bf16[4,2,16,4096]{3,2,1,0:T(8,128)(2,1)S(1)}, bf16[4,2,16,4096]{3,2,1,0:T(8,128)(2,1)S(1)}, u32[]{:S(2)}, u32[]{:S(2)}) %collective-permute-start.7) | collective-permute-done | bytes 1048608 | tf_op jit(solution)/shard_map/ppermute | solution.py:26
  117.2 0.2 pad_maximum_fusion
  117.4 1.3 copy-done.3
  118.7 2.0 %fusion.9 = f32[256,384]{1,0:T(8,128)} fusion(bf16[256,4096]{1,0:T(8,128)(2,1)S(1)} %bitcast.164, bf16[1,4096,384]{2,1,0:T(8,128)(2,1)S(1)} %copy-done.17), kind=kOutput, calls=%fused_computation.16 | convolution fusion | flops 805306368 | bytes 5636096 | tf_op jit(solution)/shard_map/dot_general | solution.py:137
  120.8 6.4 %convolution_convert_fusion = bf16[256,4096]{1,0:T(8,128)(2,1)} fusion(bf16[1,384,4096]{2,1,0:T(8,128)(2,1)S(1)} %copy-done, f32[256,384]{1,0:T(8,128)} %fusion.9, bf16[256,4096]{1,0:T(8,128)(2,1)} %bitcast.165, bf16[1,4096,384]{2,1,0:T(8,128)(2,1)} %param.15), kind=kOutput, calls=%fused_computation.4 | convolution fusion | flops 1612251136 | bytes 10878976 | tf_op jit(solution)/shard_map/dot_general | solution.py:140
  127.1 1.7 fusion.64
  128.9 0.2 collective-permute-start.8
  129.1 0.1 fusion.54
  129.2 2.4 %collective-permute-done.8 = bf16[4,2,16,4096]{3,2,1,0:T(8,128)(2,1)S(1)} collective-permute-done((bf16[4,2,16,4096]{3,2,1,0:T(8,128)(2,1)S(1)}, bf16[4,2,16,4096]{3,2,1,0:T(8,128)(2,1)S(1)}, u32[]{:S(2)}, u32[]{:S(2)}) %collective-permute-start.8) | collective-permute-done | bytes 1048608 | tf_op jit(solution)/shard_map/ppermute | solution.py:26
  131.6 1.3 fusion.13
  132.9 4.2 %all-to-all-start.3 = ((bf16[4,2,16,4096]{3,2,1,0:T(8,128)(2,1)}), bf16[4,2,16,4096]{3,2,1,0:T(8,128)(2,1)}, u32[]{:S(2)}, u32[]{:S(2)}) async-start(bf16[4,2,16,4096]{3,2,1,0:T(8,128)(2,1)} %fusion.13), calls=%async_computation.3 | async-start | bytes 2097152 | tf_op jit(solution)/shard_map/all_to_all | solution.py:146
  137.4 0.1 reshape.218
  137.6 0.1 eq.103
  137.7 0.1 copy.85
  137.9 0.1 reshape.221
  138.3 14.6 %all-to-all-done.3 = bf16[4,2,16,4096]{3,2,1,0:T(8,128)(2,1)} async-done(((bf16[4,2,16,4096]{3,2,1,0:T(8,128)(2,1)}), bf16[4,2,16,4096]{3,2,1,0:T(8,128)(2,1)}, u32[]{:S(2)}, u32[]{:S(2)}) %all-to-all-start.3) | async-done | bytes 1048608 | tf_op jit(solution)/shard_map/all_to_all | solution.py:146
  152.9 2.4 %fusion.4 = bf16[16,4096]{1,0:T(8,128)(2,1)} fusion(bf16[4,2,16,4096]{3,2,1,0:T(8,128)(2,1)} %all-to-all-done.3, f32[16,4,16]{2,1,0:T(4,128)S(1)} %reshape.222), kind=kOutput, calls=%fused_computation.12 | convolution fusion | flops 50397184 | bytes 659456 | tf_op jit(solution)/shard_map/txj,xjd->td/dot_general | solution.py:151
  155.3 0.7 collective-permute-start.9
  155.9 0.7 reshape.219
  156.6 7.7 %collective-permute-done.9 = bf16[16,4096]{1,0:T(8,128)(2,1)S(1)} collective-permute-done((bf16[16,4096]{1,0:T(8,128)(2,1)}, bf16[16,4096]{1,0:T(8,128)(2,1)S(1)}, u32[]{:S(2)}, u32[]{:S(2)}) %collective-permute-start.9) | collective-permute-done | bytes 131104 | tf_op jit(solution)/shard_map/ppermute | solution.py:26
  164.4 1.8 %fusion.19 = bf16[1,16,4096]{2,1,0:T(8,128)(2,1)S(1)} fusion(f32[16,4096]{1,0:T(8,128)S(1)} %get-tuple-element.8, bf16[4,2,16,4096]{3,2,1,0:T(8,128)(2,1)} %all-to-all-done.3, bf16[16,4096]{1,0:T(8,128)(2,1)S(1)} %collective-permute-done.9, f32[16,4,16]{2,1,0:T(4,128)} %reshape.219), kind=kOutput, calls=%fused_computation.36 | convolution fusion | flops 50593792 | bytes 1081344 | tf_op jit(solution)/shard_map/txj,xjd->td/dot_general | solution.py:150
  166.1 2.8 %collective-permute-start.10 = (bf16[1,16,4096]{2,1,0:T(8,128)(2,1)S(1)}, bf16[1,16,4096]{2,1,0:T(8,128)(2,1)S(1)}, u32[]{:S(2)}, u32[]{:S(2)}) collective-permute-start(bf16[1,16,4096]{2,1,0:T(8,128)(2,1)S(1)} %fusion.19), channel_id=1, source_target_pairs={{240,0},{0,16},{16,32},{32,48},{48,64},{64,80},{80,96},{96,112},{1... | collective-permute-start | bytes 393224 | tf_op jit(solution)/shard_map/ppermute | solution.py:22
  168.9 2.8 %collective-permute-done.10 = bf16[1,16,4096]{2,1,0:T(8,128)(2,1)S(1)} collective-permute-done((bf16[1,16,4096]{2,1,0:T(8,128)(2,1)S(1)}, bf16[1,16,4096]{2,1,0:T(8,128)(2,1)S(1)}, u32[]{:S(2)}, u32[]{:S(2)}) %collective-permute-start.10) | collective-permute-done | bytes 131104 | tf_op jit(solution)/shard_map/ppermute | solution.py:22
  171.7 0.7 copy.106
  (78 shorter events, 1.5 us)
Async XLA Ops:
  0.0 120.8 %copy-start = (bf16[1,384,4096]{2,1,0:T(8,128)(2,1)S(1)}, bf16[1,384,4096]{2,1,0:T(8,128)(2,1)}, u32[]{:S(2)}) copy-start(bf16[1,384,4096]{2,1,0:T(8,128)(2,1)} %param.17) | copy-start | bytes 9437188
  0.0 6.9 %copy-start.4 = (bf16[1,256,256]{2,1,0:T(8,128)(2,1)S(1)}, bf16[1,256,256]{2,1,0:T(8,128)(2,1)}, u32[]{:S(2)}) copy-start(bf16[1,256,256]{2,1,0:T(8,128)(2,1)} %param.11) | copy-start | bytes 393220
  2.4 14.0 %all-to-all-start = ((bf16[4,256,256]{2,1,0:T(8,128)(2,1)}), bf16[4,256,256]{2,1,0:T(8,128)(2,1)}, u32[]{:S(2)}, u32[]{:S(2)}) async-start(bf16[4,256,256]{2,1,0:T(8,128)(2,1)} %pad_maximum_fusion.3), calls=%async_computation | async-start | bytes 1048576 | tf_op jit(solution)/shard_map/all_to_all | solution.py:55
  7.1 12.6 %collective-permute-start = (bf16[2,256,128]{2,1,0:T(8,128)(2,1)S(1)}, bf16[2,256,128]{2,1,0:T(8,128)(2,1)S(1)}, u32[]{:S(2)}, u32[]{:S(2)}) collective-permute-start(bf16[2,256,128]{2,1,0:T(8,128)(2,1)S(1)} %bitcast.175), channel_id=1, source_target_pairs={{0,2},{2,0},{1,3},{3,1},{4,6},{6,4},{5,7},{7,5},{8,10},{10,8},{9,1... | collective-permute-start | bytes 393224 | tf_op jit(solution)/shard_map/ppermute | solution.py:26
  16.5 2.1 %collective-permute-start.1 = (bf16[4,256,256]{2,1,0:T(8,128)(2,1)}, bf16[4,256,256]{2,1,0:T(8,128)(2,1)S(1)}, u32[]{:S(2)}, u32[]{:S(2)}) collective-permute-start(bf16[4,256,256]{2,1,0:T(8,128)(2,1)} %all-to-all-done), channel_id=1, source_target_pairs={{0,1},{1,0},{2,3},{3,2},{4,5},{5,4},{6,7},{7,6},{8,9},{9,8},{10,11... | collective-permute-start | bytes 1572872 | tf_op jit(solution)/shard_map/ppermute | solution.py:26
  23.9 20.5 %copy-start.2 = (bf16[1,256,4096]{2,1,0:T(8,128)(2,1)S(1)}, bf16[1,256,4096]{2,1,0:T(8,128)(2,1)}, u32[]{:S(2)}) copy-start(bf16[1,256,4096]{2,1,0:T(8,128)(2,1)} %param.13) | copy-start | bytes 6291460
  23.9 8.5 %collective-permute-start.2 = (f32[2,256,2]{1,0,2:T(2,128)S(1)}, f32[2,256,2]{1,0,2:T(2,128)S(1)}, u32[]{:S(2)}, u32[]{:S(2)}) collective-permute-start(f32[2,256,2]{1,0,2:T(2,128)S(1)} %pad_maximum_fusion.4), channel_id=1, source_target_pairs={{0,2},{2,0},{1,3},{3,1},{4,6},{6,4},{5,7},{7,5},{8,10},{10,8},{9,1... | collective-permute-start | bytes 12296 | tf_op jit(solution)/shard_map/ppermute | solution.py:26
  32.3 12.1 %collective-permute-start.3 = (bf16[2,256,128]{1,2,0:T(8,128)(2,1)S(1)}, bf16[2,256,128]{1,2,0:T(8,128)(2,1)S(1)}, u32[]{:S(2)}, u32[]{:S(2)}) collective-permute-start(bf16[2,256,128]{1,2,0:T(8,128)(2,1)S(1)} %slice.144), channel_id=1, source_target_pairs={{0,2},{2,0},{1,3},{3,1},{4,6},{6,4},{5,7},{7,5},{8,10},{10,8},{9,1... | collective-permute-start | bytes 393224 | tf_op jit(solution)/shard_map/ppermute | solution.py:26
  45.2 1.3 copy-start.1
  47.5 10.0 %copy-start.16 = (s32[1,256,2]{1,2,0:T(2,128)S(1)}, s32[1,256,2]{1,2,0:T(2,128)}, u32[]{:S(2)}) copy-start(s32[1,256,2]{1,2,0:T(2,128)} %param.18) | copy-start | bytes 6148
  47.6 3.0 %collective-permute-start.4 = (bf16[4,2,16,4096]{3,2,1,0:T(8,128)(2,1)}, bf16[4,2,16,4096]{3,2,1,0:T(8,128)(2,1)}, u32[]{:S(2)}, u32[]{:S(2)}) collective-permute-start(bf16[4,2,16,4096]{3,2,1,0:T(8,128)(2,1)} %dynamic-slice_bitcast_fusion), channel_id=1, source_target_pairs={{0,1},{1,0},{2,3},{3,2},{4,5},{5,4},{6,7},{7,6},{8,9},{9,8},{10,11... | collective-permute-start | bytes 3145736 | tf_op jit(solution)/shard_map/ppermute | solution.py:26
  47.6 38.0 %copy-start.5 = (bf16[1,16,4096]{2,1,0:T(8,128)(2,1)S(1)}, bf16[1,16,4096]{2,1,0:T(8,128)(2,1)}, u32[]{:S(2)}) copy-start(bf16[1,16,4096]{2,1,0:T(8,128)(2,1)} %param.10) | copy-start | bytes 393220
  53.3 20.0 %all-to-all-start.1 = ((bf16[4,2,16,4096]{3,2,1,0:T(8,128)(2,1)}), bf16[4,2,16,4096]{3,2,1,0:T(8,128)(2,1)}, u32[]{:S(2)}, u32[]{:S(2)}) async-start(bf16[4,2,16,4096]{3,2,1,0:T(8,128)(2,1)} %fusion.14), calls=%async_computation.1 | async-start | bytes 2097152 | tf_op jit(solution)/shard_map/all_to_all | solution.py:94
  57.7 0.7 copy-start.13
  57.7 0.7 copy-start.11
  57.7 0.6 copy-start.7
  58.4 16.8 %copy-start.9 = (pred[16,4]{0,1:T(4,128)(4,1)}, pred[16,4]{0,1:T(4,128)(4,1)S(1)}, u32[]{:S(2)}) copy-start(pred[16,4]{0,1:T(4,128)(4,1)S(1)} %fusion.46) | copy-start | bytes 196
  74.8 10.8 %collective-permute-start.5 = (bf16[16,4096]{1,0:T(8,128)(2,1)S(1)}, bf16[16,4096]{1,0:T(8,128)(2,1)S(1)}, u32[]{:S(2)}, u32[]{:S(2)}) collective-permute-start(bf16[16,4096]{1,0:T(8,128)(2,1)S(1)} %fusion.32), channel_id=1, source_target_pairs={{0,2},{2,0},{1,3},{3,1},{4,6},{6,4},{5,7},{7,5},{8,10},{10,8},{9,1... | collective-permute-start | bytes 393224 | tf_op jit(solution)/shard_map/ppermute | solution.py:26
  86.6 9.4 %collective-permute-start.6 = (bf16[16,4096]{1,0:T(8,128)(2,1)S(1)}, bf16[16,4096]{1,0:T(8,128)(2,1)}, u32[]{:S(2)}, u32[]{:S(2)}) collective-permute-start(bf16[16,4096]{1,0:T(8,128)(2,1)S(1)} %multiply_convert_fusion.1), channel_id=1, source_target_pairs={{0,2},{2,0},{1,3},{3,1},{4,6},{6,4},{5,7},{7,5},{8,10},{10,8},{9,1... | collective-permute-start | bytes 393224 | tf_op jit(solution)/shard_map/ppermute | solution.py:26
  97.4 21.3 %copy-start.17 = (bf16[1,4096,384]{2,1,0:T(8,128)(2,1)S(1)}, bf16[1,4096,384]{2,1,0:T(8,128)(2,1)}, u32[]{:S(2)}) copy-start(bf16[1,4096,384]{2,1,0:T(8,128)(2,1)} %param.16) | copy-start | bytes 9437188
  114.5 2.7 %collective-permute-start.7 = (bf16[4,2,16,4096]{3,2,1,0:T(8,128)(2,1)S(1)}, bf16[4,2,16,4096]{3,2,1,0:T(8,128)(2,1)S(1)}, u32[]{:S(2)}, u32[]{:S(2)}) collective-permute-start(bf16[4,2,16,4096]{3,2,1,0:T(8,128)(2,1)S(1)} %all_to_all.20), channel_id=1, source_target_pairs={{0,1},{1,0},{2,3},{3,2},{4,5},{5,4},{6,7},{7,6},{8,9},{9,8},{10,11... | collective-permute-start | bytes 3145736 | tf_op jit(solution)/shard_map/ppermute | solution.py:26
  117.4 1.3 copy-start.3
  127.1 2.0 %copy-start.15 = (f32[1,256,2]{1,2,0:T(2,128)S(1)}, f32[1,256,2]{1,2,0:T(2,128)}, u32[]{:S(2)}) copy-start(f32[1,256,2]{1,2,0:T(2,128)} %param.19) | copy-start | bytes 6148
  128.8 8.3 %copy-start.12 = (s32[16,2]{0,1:T(2,128)S(1)}, s32[16,2]{0,1:T(2,128)}, u32[]{:S(2)}) copy-start(s32[16,2]{0,1:T(2,128)} %copy-done.11) | copy-start | bytes 388
  128.8 8.3 %copy-start.14 = (s32[16,2]{0,1:T(2,128)S(1)}, s32[16,2]{0,1:T(2,128)}, u32[]{:S(2)}) copy-start(s32[16,2]{0,1:T(2,128)} %copy-done.13) | copy-start | bytes 388
  128.9 8.6 %copy-start.10 = (pred[16,4]{0,1:T(4,128)(4,1)S(1)}, pred[16,4]{0,1:T(4,128)(4,1)}, u32[]{:S(2)}) copy-start(pred[16,4]{0,1:T(4,128)(4,1)} %copy-done.9) | copy-start | bytes 196
  128.9 9.1 %copy-start.8 = (pred[16,4]{0,1:T(4,128)(4,1)S(1)}, pred[16,4]{0,1:T(4,128)(4,1)}, u32[]{:S(2)}) copy-start(pred[16,4]{0,1:T(4,128)(4,1)} %copy-done.7) | copy-start | bytes 196
  128.9 9.2 %copy-start.6 = (s32[4,16]{1,0:T(4,128)S(1)}, s32[4,16]{1,0:T(4,128)}, u32[]{:S(2)}) copy-start(s32[4,16]{1,0:T(4,128)} %copy.79) | copy-start | bytes 772
  128.9 2.7 %collective-permute-start.8 = (bf16[4,2,16,4096]{3,2,1,0:T(8,128)(2,1)S(1)}, bf16[4,2,16,4096]{3,2,1,0:T(8,128)(2,1)S(1)}, u32[]{:S(2)}, u32[]{:S(2)}) collective-permute-start(bf16[4,2,16,4096]{3,2,1,0:T(8,128)(2,1)S(1)} %bitcast.168), channel_id=1, source_target_pairs={{0,1},{1,0},{2,3},{3,2},{4,5},{5,4},{6,7},{7,6},{8,9},{9,8},{10,11... | collective-permute-start | bytes 3145736 | tf_op jit(solution)/shard_map/ppermute | solution.py:26
  132.9 20.0 %all-to-all-start.3 = ((bf16[4,2,16,4096]{3,2,1,0:T(8,128)(2,1)}), bf16[4,2,16,4096]{3,2,1,0:T(8,128)(2,1)}, u32[]{:S(2)}, u32[]{:S(2)}) async-start(bf16[4,2,16,4096]{3,2,1,0:T(8,128)(2,1)} %fusion.13), calls=%async_computation.3 | async-start | bytes 2097152 | tf_op jit(solution)/shard_map/all_to_all | solution.py:146
  155.3 9.1 %collective-permute-start.9 = (bf16[16,4096]{1,0:T(8,128)(2,1)}, bf16[16,4096]{1,0:T(8,128)(2,1)S(1)}, u32[]{:S(2)}, u32[]{:S(2)}) collective-permute-start(bf16[16,4096]{1,0:T(8,128)(2,1)} %fusion.4), channel_id=1, source_target_pairs={{0,2},{2,0},{1,3},{3,1},{4,6},{6,4},{5,7},{7,5},{8,10},{10,8},{9,1... | collective-permute-start | bytes 393224 | tf_op jit(solution)/shard_map/ppermute | solution.py:26
  166.1 5.6 %collective-permute-start.10 = (bf16[1,16,4096]{2,1,0:T(8,128)(2,1)S(1)}, bf16[1,16,4096]{2,1,0:T(8,128)(2,1)S(1)}, u32[]{:S(2)}, u32[]{:S(2)}) collective-permute-start(bf16[1,16,4096]{2,1,0:T(8,128)(2,1)S(1)} %fusion.19), channel_id=1, source_target_pairs={{240,0},{0,16},{16,32},{32,48},{48,64},{64,80},{80,96},{96,112},{1... | collective-permute-start | bytes 393224 | tf_op jit(solution)/shard_map/ppermute | solution.py:22

commit v7 on v6

--- a/solution.py
+++ b/solution.py
@@ -62,27 +62,30 @@
     visible = key_pos[None, :] <= query_pos[:, None]
 
     mine = query_all.reshape(MB, heads_here, HD).transpose(1, 0, 2)
-    query = jnp.concatenate([mine, swap(mine, "zh")])
     keys = piece[:, :HD]
     values = piece[:, HD:]
-    score = jnp.einsum("hqd,kd->hqk", query, keys, preferred_element_type=jnp.float32) * scale
-    top = jnp.max(jnp.where(visible[None], score, -1e30), axis=2, keepdims=True)
-    weight = jnp.where(visible[None], jnp.exp(score - top), 0.0)
-    total = jnp.sum(weight, axis=2, keepdims=True)
-    summed = jnp.einsum(
-        "hqk,kd->hqd", weight.astype(jnp.bfloat16), values, preferred_element_type=jnp.float32
+
+    def partial(query):
+        score = jnp.einsum("hqd,kd->hqk", query, keys, preferred_element_type=jnp.float32) * scale
+        top = jnp.max(jnp.where(visible[None], score, -1e30), axis=2, keepdims=True)
+        weight = jnp.where(visible[None], jnp.exp(score - top), 0.0)
+        total = jnp.sum(weight, axis=2, keepdims=True)
+        summed = jnp.einsum(
+            "hqk,kd->hqd", weight.astype(jnp.bfloat16), values, preferred_element_type=jnp.float32
+        )
+        return summed, top, total
+
+    other_sum, other_top, other_total = partial(swap(mine, "zh"))
+    far_sum, far_stats = swap(
+        (other_sum.astype(jnp.bfloat16), jnp.concatenate([other_top, other_total], axis=2)), "zh"
     )
-    stats = jnp.concatenate([top, total], axis=2)
-    far_sum, far_stats = swap(
-        (summed[heads_here:].astype(jnp.bfloat16), stats[heads_here:]), "zh"
-    )
-    near_top = top[:heads_here]
+    near_sum, near_top, near_total = partial(mine)
     far_top = far_stats[:, :, 0:1]
     both_top = jnp.maximum(near_top, far_top)
     near_factor = jnp.exp(near_top - both_top)
     far_factor = jnp.exp(far_top - both_top)
-    both_total = total[:heads_here] * near_factor + far_stats[:, :, 1:2] * far_factor
-    both_sum = summed[:heads_here] * near_factor + far_sum.astype(jnp.float32) * far_factor
+    both_total = near_total * near_factor + far_stats[:, :, 1:2] * far_factor
+    both_sum = near_sum * near_factor + far_sum.astype(jnp.float32) * far_factor
     heads = (both_sum / both_total).astype(jnp.bfloat16)
     heads = heads.transpose(1, 0, 2).reshape(MB, heads_here * HD)
     head_terms = jnp.dot(heads, proj_out, preferred_element_type=jnp.float32).astype(jnp.bfloat16)
@@ -149,9 +152,14 @@
     combine_far = combine_far.reshape(tok_rows, experts_count, CAP)
     mixed_own = jnp.einsum("txj,xjd->td", combine_own, back[:, 0], precision=hi)
     mixed_far = jnp.einsum("txj,xjd->td", combine_far, back[:, 1], precision=hi)
-    mixed = mixed_own + swap(mixed_far.astype(jnp.bfloat16), "zh").astype(jnp.float32)
-    layer_out = (middle + mixed).astype(jnp.bfloat16)
-    return shifted(layer_out[None], "section", 1)
+    own_part = shifted((middle + mixed_own).astype(jnp.bfloat16), "section", 1)
+    sections = lax.axis_size("section")
+    route = [
+        (s * nz + z, ((s + 1) % sections) * nz + (nz - 1 - z)) for s in range(sections) for z in range(nz)
+    ]
+    far_part = lax.ppermute(mixed_far.astype(jnp.bfloat16), ("section", "zh"), route)
+    layer_out = own_part.astype(jnp.float32) + far_part.astype(jnp.float32)
+    return layer_out.astype(jnp.bfloat16)[None]
 
 
 def solution(mesh):

time: 175 us -> 171 us (0.977); the launches traced: 172 us -> 170 us
    ppermute x0 -> x1, waiting for transfers between devices: none -> 10.1 us  [body(): lax.ppermute(mixed_far.astype(jnp.bfloat16), ('section', 'zh'), route)]
    ppermute x10 -> x9, waiting for transfers between devices: 46.3 us -> 38.5 us  [swap(): return lax.ppermute(block, axis, [(0, 1), (1, 0)])]
    ppermute x0 -> x1, starting transfers between devices: none -> 2.4 us  [body(): lax.ppermute(mixed_far.astype(jnp.bfloat16), ('section', 'zh'), route)]
    ppermute x1, waiting for transfers between devices: 2.75 us -> 0.37 us  [shifted(): return lax.ppermute(block, axis, route)]
    ppermute x1, starting transfers between devices: 2.82 us -> 0.54 us  [shifted(): return lax.ppermute(block, axis, route)]
    dot_general x2 -> x4, matrix products: 3.78 us -> 4.44 us  [the longest x2 2.46 us: partial(): jnp.einsum('hqd,kd->hqk', query, keys, preferred_element_type=jnp.float32)]
    ppermute x10 -> x9, starting transfers between devices: 14.9 us -> 14.3 us  [swap(): return lax.ppermute(block, axis, [(0, 1), (1, 0)])]
    unnamed x39 -> x38, local copies, waits for them, and re-layouts: 4.04 us -> 3.89 us
  transfers between devices with their start and end apart: 14 -> 14, of which waited for: 12 -> 13; matrix products, arithmetic and copies ran while one was open for 5% -> 6% of each run, Pallas kernels for 0% -> 0%
where the time goes in v7:
time: 171 us; the launch traced here: 170 us
  waiting for transfers between devices  80.5 us (47%)
  starting transfers between devices  30.1 us (18%)
  matrix products  19 us (11%)
  blocking collectives  17.1 us (10%)
  other arithmetic  12.6 us (7%)
  local copies, waits for them, and re-layouts  10.5 us (6%)
    ppermute x9, waiting for transfers between devices, swap(): return lax.ppermute(block, axis, [(0, 1), (1, 0)])  38.5 us
    all_to_all x1, blocking collectives, body(): rows_y = lax.all_to_all(dispatch, 'y', 0, 0, tiled=True)  17.1 us
    all_to_all x1, waiting for transfers between devices, body(): lax.all_to_all(chip_sum.astype(jnp.bfloat16), 'y', 0, 0, tiled=True)  14.5 us
    ppermute x9, starting transfers between devices, swap(): return lax.ppermute(block, axis, [(0, 1), (1, 0)])  14.3 us
    all_to_all x1, waiting for transfers between devices, body(): part_y = lax.all_to_all(part_c.astype(jnp.bfloat16), 'y', 0, 0, tiled=True)  14.2 us
    ppermute x1, waiting for transfers between devices, body(): lax.ppermute(mixed_far.astype(jnp.bfloat16), ('section', 'zh'), route)  10.1 us
    dot_general x1, matrix products, body(): jnp.dot(activated, down_w, preferred_element_type=jnp.float32)  6.36 us
    all_to_all x1, starting transfers between devices, body(): kv_y = lax.all_to_all(send_kv, 'y', 0, 0, tiled=True)  4.46 us
  transfers between devices with their start and end apart: 14, of which 13 were waited for; matrix products, arithmetic and copies ran while one was open for 6% of the time, Pallas kernels for 0%

profile of v7, /device:TPU:32, one launch (start us, length us, event | category | flops | bytes accessed | tf_op | source)
XLA Modules:
  0.0 170.2 jit_solution(195207787720384124)
XLA Ops:
  0.0 1.2 reshape_squeeze.6
  1.2 0.4 fusion.86
  1.6 0.8 pad_maximum_fusion.3
  2.5 4.5 %all-to-all-start = ((bf16[4,256,256]{2,1,0:T(8,128)(2,1)}), bf16[4,256,256]{2,1,0:T(8,128)(2,1)}, u32[]{:S(2)}, u32[]{:S(2)}) async-start(bf16[4,256,256]{2,1,0:T(8,128)(2,1)} %pad_maximum_fusion.3), calls=%async_computation | async-start | bytes 1048576 | tf_op jit(solution)/shard_map/all_to_all | solution.py:55
  6.9 0.1 copy.79
  7.0 0.1 copy.80
  7.1 6.4 %collective-permute-start.1 = (bf16[2,256,128]{2,1,0:T(8,128)(2,1)S(1)}, bf16[2,256,128]{2,1,0:T(8,128)(2,1)S(1)}, u32[]{:S(2)}, u32[]{:S(2)}) collective-permute-start(bf16[2,256,128]{2,1,0:T(8,128)(2,1)S(1)} %bitcast.214), channel_id=1, source_target_pairs={{0,2},{2,0},{1,3},{3,1},{4,6},{6,4},{5,7},{7,5},{8,10},{10,8},{9,1... | collective-permute-start | bytes 393224 | tf_op jit(solution)/shard_map/ppermute | solution.py:26
  13.7 2.8 %all-to-all-done = bf16[4,256,256]{2,1,0:T(8,128)(2,1)} async-done(((bf16[4,256,256]{2,1,0:T(8,128)(2,1)}), bf16[4,256,256]{2,1,0:T(8,128)(2,1)}, u32[]{:S(2)}, u32[]{:S(2)}) %all-to-all-start) | async-done | bytes 524320 | tf_op jit(solution)/shard_map/all_to_all | solution.py:55
  16.5 0.4 broadcast_compare_fusion
  17.0 1.7 collective-permute-done
  18.6 1.1 pad_maximum_fusion.1
  19.8 0.7 fusion.8
  20.5 1.7 %fusion.11 = (f32[2,256]{1,0:T(2,128)S(1)}, f32[2,256]{1,0:T(2,128)S(1)}, f32[2048,2,256]{2,0,1:T(8,128)S(1)}) fusion(f32[2048,2,256]{2,0,1:T(8,128)S(1)} %get-tuple-element.25, f32[2,256]{1,0:T(2,128)S(1)} %get-tuple-element.24, pred[256,2048]{0,1:T(8,128)(4,1)S(1)} %broadcast_compare_fusion, bf16[2,256,128]{2,1,0:T(8,128)(2,1)S(1)} %collective-permute-done.1, ...), kind=kOutput, calls=%fused_computation.21 | convolution fusion | flops 275774464 | bytes 9574400 | tf_op jit(solution)/shard_map/hqd,kd->hqk/dot_general | solution.py:69
  22.2 1.0 fusion.14
  23.2 6.4 %collective-permute-start.2 = (f32[2,256,2]{1,0,2:T(2,128)S(1)}, f32[2,256,2]{1,0,2:T(2,128)S(1)}, u32[]{:S(2)}, u32[]{:S(2)}) collective-permute-start(f32[2,256,2]{1,0,2:T(2,128)S(1)} %pad_maximum_fusion.4), channel_id=1, source_target_pairs={{0,2},{2,0},{1,3},{3,1},{4,6},{6,4},{5,7},{7,5},{8,10},{10,8},{9,1... | collective-permute-start | bytes 12296 | tf_op jit(solution)/shard_map/ppermute | solution.py:26
  29.6 1.0 fusion.32
  30.6 0.1 collective-permute-start.3
  30.7 0.5 collective-permute-done.2
  31.2 11.5 %collective-permute-done.3 = bf16[2,256,128]{1,2,0:T(8,128)(2,1)S(1)} collective-permute-done((bf16[2,256,128]{1,2,0:T(8,128)(2,1)S(1)}, bf16[2,256,128]{1,2,0:T(8,128)(2,1)S(1)}, u32[]{:S(2)}, u32[]{:S(2)}) %collective-permute-start.3) | collective-permute-done | bytes 131104 | tf_op jit(solution)/shard_map/ppermute | solution.py:26
  42.7 1.0 fusion.43
  43.7 0.6 copy-done.2
  44.2 0.7 convolution_convert_fusion.1
  45.0 1.3 copy-done.1
  46.3 1.1 dynamic-slice_bitcast_fusion
  47.4 3.0 %collective-permute-done.4 = bf16[4,2,16,4096]{3,2,1,0:T(8,128)(2,1)} collective-permute-done((bf16[4,2,16,4096]{3,2,1,0:T(8,128)(2,1)}, bf16[4,2,16,4096]{3,2,1,0:T(8,128)(2,1)}, u32[]{:S(2)}, u32[]{:S(2)}) %collective-permute-start.4) | collective-permute-done | bytes 1048608 | tf_op jit(solution)/shard_map/ppermute | solution.py:26
  50.4 2.8 %fusion.21 = bf16[4,2,16,4096]{3,2,1,0:T(8,128)(2,1)} fusion(bf16[4,2,16,4096]{3,2,1,0:T(8,128)(2,1)} %collective-permute-done.4, bf16[4,2,2,16,4096]{4,3,2,1,0:T(8,128)(2,1)} %bitcast.198, s32[]{:T(128)S(6)} %select_n.55), kind=kLoop, calls=%fused_computation.34 | loop fusion | flops 2097152 | bytes 3145732 | tf_op jit(solution)/shard_map/convert_element_type | solution.py:97
  53.2 4.2 %all-to-all-start.1 = ((bf16[4,2,16,4096]{3,2,1,0:T(8,128)(2,1)}), bf16[4,2,16,4096]{3,2,1,0:T(8,128)(2,1)}, u32[]{:S(2)}, u32[]{:S(2)}) async-start(bf16[4,2,16,4096]{3,2,1,0:T(8,128)(2,1)} %fusion.21), calls=%async_computation.1 | async-start | bytes 2097152 | tf_op jit(solution)/shard_map/all_to_all | solution.py:97
  57.5 0.5 copy-done.7
  58.3 0.6 reduce_window_sum.17
  58.9 14.2 %all-to-all-done.1 = bf16[4,2,16,4096]{3,2,1,0:T(8,128)(2,1)} async-done(((bf16[4,2,16,4096]{3,2,1,0:T(8,128)(2,1)}), bf16[4,2,16,4096]{3,2,1,0:T(8,128)(2,1)}, u32[]{:S(2)}, u32[]{:S(2)}) %all-to-all-start.1) | async-done | bytes 1048608 | tf_op jit(solution)/shard_map/all_to_all | solution.py:97
  73.1 1.4 convert_reduce_fusion
  74.6 0.5 collective-permute-start.5
  75.1 10.3 %collective-permute-done.5 = bf16[16,4096]{1,0:T(8,128)(2,1)S(1)} collective-permute-done((bf16[16,4096]{1,0:T(8,128)(2,1)S(1)}, bf16[16,4096]{1,0:T(8,128)(2,1)S(1)}, u32[]{:S(2)}, u32[]{:S(2)}) %collective-permute-start.5) | collective-permute-done | bytes 131104 | tf_op jit(solution)/shard_map/ppermute | solution.py:26
  85.4 0.2 multiply_reduce_fusion
  85.6 0.8 multiply_convert_fusion.1
  86.4 0.7 collective-permute-start.6
  87.1 0.7 add_bitcast_fusion.1
  87.8 0.7 copy.91
  88.5 0.8 fusion
  89.4 6.5 %collective-permute-done.6 = bf16[16,4096]{1,0:T(8,128)(2,1)} collective-permute-done((bf16[16,4096]{1,0:T(8,128)(2,1)S(1)}, bf16[16,4096]{1,0:T(8,128)(2,1)}, u32[]{:S(2)}, u32[]{:S(2)}) %collective-permute-start.6) | collective-permute-done | bytes 131104 | tf_op jit(solution)/shard_map/ppermute | solution.py:26
  95.8 1.2 fusion.1
  97.0 0.1 pad_maximum_fusion.2
  97.1 0.1 copy.92
  97.2 17.1 %all_to_all.20 = bf16[4,2,16,4096]{3,2,1,0:T(8,128)(2,1)S(1)} all-to-all(bf16[4,2,16,4096]{3,2,1,0:T(8,128)(2,1)S(1)} %copy.92), channel_id=1, replica_groups=mesh['section'=16,'y'=4,'zh'=2,'core'=2] {'y'}, dimensions={0} | all-to-all | bytes 2097152 | tf_op jit(solution)/shard_map/all_to_all | solution.py:136
  114.4 2.7 %collective-permute-done.7 = bf16[4,2,16,4096]{3,2,1,0:T(8,128)(2,1)S(1)} collective-permute-done((bf16[4,2,16,4096]{3,2,1,0:T(8,128)(2,1)S(1)}, bf16[4,2,16,4096]{3,2,1,0:T(8,128)(2,1)S(1)}, u32[]{:S(2)}, u32[]{:S(2)}) %collective-permute-start.7) | collective-permute-done | bytes 1048608 | tf_op jit(solution)/shard_map/ppermute | solution.py:26
  117.0 0.2 pad_maximum_fusion
  117.2 1.3 copy-done.3
  118.6 2.0 %fusion.16 = f32[256,384]{1,0:T(8,128)} fusion(bf16[256,4096]{1,0:T(8,128)(2,1)S(1)} %bitcast.201, bf16[1,4096,384]{2,1,0:T(8,128)(2,1)S(1)} %copy-done.17), kind=kOutput, calls=%fused_computation.26 | convolution fusion | flops 805306368 | bytes 5636096 | tf_op jit(solution)/shard_map/dot_general | solution.py:140
  120.6 6.4 %convolution_convert_fusion = bf16[256,4096]{1,0:T(8,128)(2,1)} fusion(bf16[1,384,4096]{2,1,0:T(8,128)(2,1)S(1)} %copy-done, f32[256,384]{1,0:T(8,128)} %fusion.16, bf16[256,4096]{1,0:T(8,128)(2,1)} %bitcast.202, bf16[1,4096,384]{2,1,0:T(8,128)(2,1)} %param.15), kind=kOutput, calls=%fused_computation | convolution fusion | flops 1612251136 | bytes 10878976 | tf_op jit(solution)/shard_map/dot_general | solution.py:143
  127.0 1.7 fusion.85
  128.7 0.2 collective-permute-start.8
  128.9 0.1 fusion.73
  129.0 2.4 %collective-permute-done.8 = bf16[4,2,16,4096]{3,2,1,0:T(8,128)(2,1)S(1)} collective-permute-done((bf16[4,2,16,4096]{3,2,1,0:T(8,128)(2,1)S(1)}, bf16[4,2,16,4096]{3,2,1,0:T(8,128)(2,1)S(1)}, u32[]{:S(2)}, u32[]{:S(2)}) %collective-permute-start.8) | collective-permute-done | bytes 1048608 | tf_op jit(solution)/shard_map/ppermute | solution.py:26
  131.5 1.3 fusion.20
  132.7 4.2 %all-to-all-start.3 = ((bf16[4,2,16,4096]{3,2,1,0:T(8,128)(2,1)}), bf16[4,2,16,4096]{3,2,1,0:T(8,128)(2,1)}, u32[]{:S(2)}, u32[]{:S(2)}) async-start(bf16[4,2,16,4096]{3,2,1,0:T(8,128)(2,1)} %fusion.20), calls=%async_computation.3 | async-start | bytes 2097152 | tf_op jit(solution)/shard_map/all_to_all | solution.py:149
  137.4 0.1 reshape.220
  138.2 14.5 %all-to-all-done.3 = bf16[4,2,16,4096]{3,2,1,0:T(8,128)(2,1)} async-done(((bf16[4,2,16,4096]{3,2,1,0:T(8,128)(2,1)}), bf16[4,2,16,4096]{3,2,1,0:T(8,128)(2,1)}, u32[]{:S(2)}, u32[]{:S(2)}) %all-to-all-start.3) | async-done | bytes 1048608 | tf_op jit(solution)/shard_map/all_to_all | solution.py:149
  152.7 1.7 %fusion.3 = bf16[16,4096]{1,0:T(8,128)(2,1)S(1)} fusion(f32[16,4096]{1,0:T(8,128)S(1)} %get-tuple-element.10, bf16[4,2,16,4096]{3,2,1,0:T(8,128)(2,1)} %all-to-all-done.3, f32[16,4,16]{2,1,0:T(4,128)S(1)} %reshape.218), kind=kOutput, calls=%fused_computation.9 | convolution fusion | flops 50462720 | bytes 921600 | tf_op jit(solution)/shard_map/txj,xjd->td/dot_general | solution.py:153
  154.4 0.5 collective-permute-start.9
  155.0 1.7 %fusion.4 = bf16[16,4096]{1,0:T(8,128)(2,1)S(1)} fusion(bf16[4,2,16,4096]{3,2,1,0:T(8,128)(2,1)} %all-to-all-done.3, f32[16,4,16]{2,1,0:T(4,128)S(1)} %reshape.221), kind=kOutput, calls=%fused_computation.10 | convolution fusion | flops 50397184 | bytes 659456 | tf_op jit(solution)/shard_map/txj,xjd->td/dot_general | solution.py:154
  156.7 2.4 %collective-permute-start.10 = (bf16[16,4096]{1,0:T(8,128)(2,1)S(1)}, bf16[16,4096]{1,0:T(8,128)(2,1)S(1)}, u32[]{:S(2)}, u32[]{:S(2)}) collective-permute-start(bf16[16,4096]{1,0:T(8,128)(2,1)S(1)} %fusion.4), channel_id=1, source_target_pairs={{0,18},{2,16},{16,34},{18,32},{32,50},{34,48},{48,66},{50,64},{64,... | collective-permute-start | bytes 393224 | tf_op jit(solution)/shard_map/ppermute | solution.py:160
  159.1 0.4 collective-permute-done.9
  159.5 10.1 %collective-permute-done.10 = bf16[16,4096]{1,0:T(8,128)(2,1)S(1)} collective-permute-done((bf16[16,4096]{1,0:T(8,128)(2,1)S(1)}, bf16[16,4096]{1,0:T(8,128)(2,1)S(1)}, u32[]{:S(2)}, u32[]{:S(2)}) %collective-permute-start.10) | collective-permute-done | bytes 131104 | tf_op jit(solution)/shard_map/ppermute | solution.py:160
  169.5 0.7 fusion.52
  (78 shorter events, 1.8 us)
Async XLA Ops:
  0.0 120.6 %copy-start = (bf16[1,384,4096]{2,1,0:T(8,128)(2,1)S(1)}, bf16[1,384,4096]{2,1,0:T(8,128)(2,1)}, u32[]{:S(2)}) copy-start(bf16[1,384,4096]{2,1,0:T(8,128)(2,1)} %param.17) | copy-start | bytes 9437188
  0.0 6.9 %copy-start.4 = (bf16[1,256,256]{2,1,0:T(8,128)(2,1)S(1)}, bf16[1,256,256]{2,1,0:T(8,128)(2,1)}, u32[]{:S(2)}) copy-start(bf16[1,256,256]{2,1,0:T(8,128)(2,1)} %param.11) | copy-start | bytes 393220
  2.5 14.0 %all-to-all-start = ((bf16[4,256,256]{2,1,0:T(8,128)(2,1)}), bf16[4,256,256]{2,1,0:T(8,128)(2,1)}, u32[]{:S(2)}, u32[]{:S(2)}) async-start(bf16[4,256,256]{2,1,0:T(8,128)(2,1)} %pad_maximum_fusion.3), calls=%async_computation | async-start | bytes 1048576 | tf_op jit(solution)/shard_map/all_to_all | solution.py:55
  7.1 13.4 %collective-permute-start.1 = (bf16[2,256,128]{2,1,0:T(8,128)(2,1)S(1)}, bf16[2,256,128]{2,1,0:T(8,128)(2,1)S(1)}, u32[]{:S(2)}, u32[]{:S(2)}) collective-permute-start(bf16[2,256,128]{2,1,0:T(8,128)(2,1)S(1)} %bitcast.214), channel_id=1, source_target_pairs={{0,2},{2,0},{1,3},{3,1},{4,6},{6,4},{5,7},{7,5},{8,10},{10,8},{9,1... | collective-permute-start | bytes 393224 | tf_op jit(solution)/shard_map/ppermute | solution.py:26
  16.5 2.1 %collective-permute-start = (bf16[4,256,256]{2,1,0:T(8,128)(2,1)}, bf16[4,256,256]{2,1,0:T(8,128)(2,1)S(1)}, u32[]{:S(2)}, u32[]{:S(2)}) collective-permute-start(bf16[4,256,256]{2,1,0:T(8,128)(2,1)} %all-to-all-done), channel_id=1, source_target_pairs={{0,1},{1,0},{2,3},{3,2},{4,5},{5,4},{6,7},{7,6},{8,9},{9,8},{10,11... | collective-permute-start | bytes 1572872 | tf_op jit(solution)/shard_map/ppermute | solution.py:26
  23.2 8.0 %collective-permute-start.2 = (f32[2,256,2]{1,0,2:T(2,128)S(1)}, f32[2,256,2]{1,0,2:T(2,128)S(1)}, u32[]{:S(2)}, u32[]{:S(2)}) collective-permute-start(f32[2,256,2]{1,0,2:T(2,128)S(1)} %pad_maximum_fusion.4), channel_id=1, source_target_pairs={{0,2},{2,0},{1,3},{3,1},{4,6},{6,4},{5,7},{7,5},{8,10},{10,8},{9,1... | collective-permute-start | bytes 12296 | tf_op jit(solution)/shard_map/ppermute | solution.py:26
  30.6 12.1 %collective-permute-start.3 = (bf16[2,256,128]{1,2,0:T(8,128)(2,1)S(1)}, bf16[2,256,128]{1,2,0:T(8,128)(2,1)S(1)}, u32[]{:S(2)}, u32[]{:S(2)}) collective-permute-start(bf16[2,256,128]{1,2,0:T(8,128)(2,1)S(1)} %fusion.32), channel_id=1, source_target_pairs={{0,2},{2,0},{1,3},{3,1},{4,6},{6,4},{5,7},{7,5},{8,10},{10,8},{9,1... | collective-permute-start | bytes 393224 | tf_op jit(solution)/shard_map/ppermute | solution.py:26
  42.7 1.6 copy-start.2
  45.0 1.3 copy-start.1
  47.4 10.0 %copy-start.16 = (s32[1,256,2]{1,2,0:T(2,128)S(1)}, s32[1,256,2]{1,2,0:T(2,128)}, u32[]{:S(2)}) copy-start(s32[1,256,2]{1,2,0:T(2,128)} %param.18) | copy-start | bytes 6148
  47.4 3.0 %collective-permute-start.4 = (bf16[4,2,16,4096]{3,2,1,0:T(8,128)(2,1)}, bf16[4,2,16,4096]{3,2,1,0:T(8,128)(2,1)}, u32[]{:S(2)}, u32[]{:S(2)}) collective-permute-start(bf16[4,2,16,4096]{3,2,1,0:T(8,128)(2,1)} %dynamic-slice_bitcast_fusion), channel_id=1, source_target_pairs={{0,1},{1,0},{2,3},{3,2},{4,5},{5,4},{6,7},{7,6},{8,9},{9,8},{10,11... | collective-permute-start | bytes 3145736 | tf_op jit(solution)/shard_map/ppermute | solution.py:26
  47.4 38.0 %copy-start.5 = (bf16[1,16,4096]{2,1,0:T(8,128)(2,1)S(1)}, bf16[1,16,4096]{2,1,0:T(8,128)(2,1)}, u32[]{:S(2)}) copy-start(bf16[1,16,4096]{2,1,0:T(8,128)(2,1)} %param.10) | copy-start | bytes 393220
  53.2 20.0 %all-to-all-start.1 = ((bf16[4,2,16,4096]{3,2,1,0:T(8,128)(2,1)}), bf16[4,2,16,4096]{3,2,1,0:T(8,128)(2,1)}, u32[]{:S(2)}, u32[]{:S(2)}) async-start(bf16[4,2,16,4096]{3,2,1,0:T(8,128)(2,1)} %fusion.21), calls=%async_computation.1 | async-start | bytes 2097152 | tf_op jit(solution)/shard_map/all_to_all | solution.py:97
  57.5 0.6 copy-start.13
  57.5 0.6 copy-start.11
  57.5 0.5 copy-start.7
  58.2 16.9 %copy-start.9 = (pred[16,4]{0,1:T(4,128)(4,1)}, pred[16,4]{0,1:T(4,128)(4,1)S(1)}, u32[]{:S(2)}) copy-start(pred[16,4]{0,1:T(4,128)(4,1)S(1)} %fusion.66) | copy-start | bytes 196
  74.6 10.8 %collective-permute-start.5 = (bf16[16,4096]{1,0:T(8,128)(2,1)S(1)}, bf16[16,4096]{1,0:T(8,128)(2,1)S(1)}, u32[]{:S(2)}, u32[]{:S(2)}) collective-permute-start(bf16[16,4096]{1,0:T(8,128)(2,1)S(1)} %fusion.51), channel_id=1, source_target_pairs={{0,2},{2,0},{1,3},{3,1},{4,6},{6,4},{5,7},{7,5},{8,10},{10,8},{9,1... | collective-permute-start | bytes 393224 | tf_op jit(solution)/shard_map/ppermute | solution.py:26
  86.4 9.4 %collective-permute-start.6 = (bf16[16,4096]{1,0:T(8,128)(2,1)S(1)}, bf16[16,4096]{1,0:T(8,128)(2,1)}, u32[]{:S(2)}, u32[]{:S(2)}) collective-permute-start(bf16[16,4096]{1,0:T(8,128)(2,1)S(1)} %multiply_convert_fusion.1), channel_id=1, source_target_pairs={{0,2},{2,0},{1,3},{3,1},{4,6},{6,4},{5,7},{7,5},{8,10},{10,8},{9,1... | collective-permute-start | bytes 393224 | tf_op jit(solution)/shard_map/ppermute | solution.py:26
  97.2 21.3 %copy-start.17 = (bf16[1,4096,384]{2,1,0:T(8,128)(2,1)S(1)}, bf16[1,4096,384]{2,1,0:T(8,128)(2,1)}, u32[]{:S(2)}) copy-start(bf16[1,4096,384]{2,1,0:T(8,128)(2,1)} %param.16) | copy-start | bytes 9437188
  114.4 2.7 %collective-permute-start.7 = (bf16[4,2,16,4096]{3,2,1,0:T(8,128)(2,1)S(1)}, bf16[4,2,16,4096]{3,2,1,0:T(8,128)(2,1)S(1)}, u32[]{:S(2)}, u32[]{:S(2)}) collective-permute-start(bf16[4,2,16,4096]{3,2,1,0:T(8,128)(2,1)S(1)} %all_to_all.20), channel_id=1, source_target_pairs={{0,1},{1,0},{2,3},{3,2},{4,5},{5,4},{6,7},{7,6},{8,9},{9,8},{10,11... | collective-permute-start | bytes 3145736 | tf_op jit(solution)/shard_map/ppermute | solution.py:26
  117.2 1.3 copy-start.3
  127.0 2.0 %copy-start.15 = (f32[1,256,2]{1,2,0:T(2,128)S(1)}, f32[1,256,2]{1,2,0:T(2,128)}, u32[]{:S(2)}) copy-start(f32[1,256,2]{1,2,0:T(2,128)} %param.19) | copy-start | bytes 6148
  128.7 8.3 %copy-start.12 = (s32[16,2]{0,1:T(2,128)S(1)}, s32[16,2]{0,1:T(2,128)}, u32[]{:S(2)}) copy-start(s32[16,2]{0,1:T(2,128)} %copy-done.11) | copy-start | bytes 388
  128.7 8.3 %copy-start.14 = (s32[16,2]{0,1:T(2,128)S(1)}, s32[16,2]{0,1:T(2,128)}, u32[]{:S(2)}) copy-start(s32[16,2]{0,1:T(2,128)} %copy-done.13) | copy-start | bytes 388
  128.7 8.9 %copy-start.6 = (s32[4,16]{1,0:T(4,128)S(1)}, s32[4,16]{1,0:T(4,128)}, u32[]{:S(2)}) copy-start(s32[4,16]{1,0:T(4,128)} %copy.91) | copy-start | bytes 772
  128.7 9.0 %copy-start.10 = (pred[16,4]{0,1:T(4,128)(4,1)S(1)}, pred[16,4]{0,1:T(4,128)(4,1)}, u32[]{:S(2)}) copy-start(pred[16,4]{0,1:T(4,128)(4,1)} %copy-done.9) | copy-start | bytes 196
  128.7 9.1 %copy-start.8 = (pred[16,4]{0,1:T(4,128)(4,1)S(1)}, pred[16,4]{0,1:T(4,128)(4,1)}, u32[]{:S(2)}) copy-start(pred[16,4]{0,1:T(4,128)(4,1)} %copy-done.7) | copy-start | bytes 196
  128.7 2.7 %collective-permute-start.8 = (bf16[4,2,16,4096]{3,2,1,0:T(8,128)(2,1)S(1)}, bf16[4,2,16,4096]{3,2,1,0:T(8,128)(2,1)S(1)}, u32[]{:S(2)}, u32[]{:S(2)}) collective-permute-start(bf16[4,2,16,4096]{3,2,1,0:T(8,128)(2,1)S(1)} %bitcast.207), channel_id=1, source_target_pairs={{0,1},{1,0},{2,3},{3,2},{4,5},{5,4},{6,7},{7,6},{8,9},{9,8},{10,11... | collective-permute-start | bytes 3145736 | tf_op jit(solution)/shard_map/ppermute | solution.py:26
  132.7 20.0 %all-to-all-start.3 = ((bf16[4,2,16,4096]{3,2,1,0:T(8,128)(2,1)}), bf16[4,2,16,4096]{3,2,1,0:T(8,128)(2,1)}, u32[]{:S(2)}, u32[]{:S(2)}) async-start(bf16[4,2,16,4096]{3,2,1,0:T(8,128)(2,1)} %fusion.20), calls=%async_computation.3 | async-start | bytes 2097152 | tf_op jit(solution)/shard_map/all_to_all | solution.py:149
  154.4 5.0 %collective-permute-start.9 = (bf16[16,4096]{1,0:T(8,128)(2,1)S(1)}, bf16[16,4096]{1,0:T(8,128)(2,1)S(1)}, u32[]{:S(2)}, u32[]{:S(2)}) collective-permute-start(bf16[16,4096]{1,0:T(8,128)(2,1)S(1)} %fusion.3), channel_id=1, source_target_pairs={{240,0},{0,16},{16,32},{32,48},{48,64},{64,80},{80,96},{96,112},{1... | collective-permute-start | bytes 393224 | tf_op jit(solution)/shard_map/ppermute | solution.py:22
  156.7 12.8 %collective-permute-start.10 = (bf16[16,4096]{1,0:T(8,128)(2,1)S(1)}, bf16[16,4096]{1,0:T(8,128)(2,1)S(1)}, u32[]{:S(2)}, u32[]{:S(2)}) collective-permute-start(bf16[16,4096]{1,0:T(8,128)(2,1)S(1)} %fusion.4), channel_id=1, source_target_pairs={{0,18},{2,16},{16,34},{18,32},{32,50},{34,48},{48,66},{50,64},{64,... | collective-permute-start | bytes 393224 | tf_op jit(solution)/shard_map/ppermute | solution.py:160

commit v8 on v7

--- a/solution.py
+++ b/solution.py
@@ -37,6 +37,7 @@
     devices = ny * nz * nc
     tok_rows = stream.shape[1]
     residual = stream[0]
+    residual_far = swap(residual, "zh")
     query_all = queries[0]
     proj_out = w_out[0]
     gain = norm_gain[0]
@@ -98,12 +99,18 @@
     part_y = jnp.sum(part_y.astype(jnp.float32), axis=0)
     keep_z = lax.dynamic_index_in_dim(part_y, zi, 0, keepdims=False)
     give_z = lax.dynamic_index_in_dim(part_y, 1 - zi, 0, keepdims=False)
-    attended = keep_z + swap(give_z.astype(jnp.bfloat16), "zh").astype(jnp.float32)
+    got = swap(jnp.stack([give_z, keep_z]).astype(jnp.bfloat16), "zh").astype(jnp.float32)
+    attended = keep_z.astype(jnp.bfloat16).astype(jnp.float32) + got[0]
+    attended_far = give_z.astype(jnp.bfloat16).astype(jnp.float32) + got[1]
+
+    def norm(middle):
+        return (
+            middle * lax.rsqrt(jnp.mean(middle * middle, axis=1, keepdims=True) + 1e-06) * gain
+        ).astype(jnp.bfloat16)
 
     middle = residual.astype(jnp.float32) + attended
-    normed = (
-        middle * lax.rsqrt(jnp.mean(middle * middle, axis=1, keepdims=True) + 1e-06) * gain
-    ).astype(jnp.bfloat16)
+    normed = norm(middle)
+    normed_far = norm(residual_far.astype(jnp.float32) + attended_far)
 
     split = FF // gate_w.shape[1]
     experts_count = devices // split
@@ -123,7 +130,6 @@
         combine = select.T.astype(jnp.float32) * jnp.repeat(share, CAP, axis=1)
         return select.astype(jnp.bfloat16), combine
 
-    normed_far = swap(normed, "zh")
     select_own, combine_own = plan(my_index)
     select_far, combine_far = plan(partner)
     dispatch_own = jnp.dot(select_own, normed, preferred_element_type=jnp.float32)

time: 171 us -> 171 us (level)
  waiting for transfers between devices: 80.5 us -> 69.5 us
  other arithmetic: 12.6 us -> 19.5 us
  local copies, waits for them, and re-layouts: 10.5 us -> 15 us
  starting transfers between devices: 30.1 us -> 28.2 us
    ppermute x9, waiting for transfers between devices: 38.5 us -> 28.7 us  [swap(): return lax.ppermute(block, axis, [(0, 1), (1, 0)])]
    ppermute x1, starting transfers between devices: 2.4 us -> 0.1 us  [body(): lax.ppermute(mixed_far.astype(jnp.bfloat16), ('section', 'zh'), route)]
    sub x2, local copies, waits for them, and re-layouts: 0.73 us -> 2.68 us  [plan(): slot = jnp.cumsum(routed.astype(jnp.int32), axis=0) - 1]
    sub x2, other arithmetic: 0.7 us -> 2.59 us  [plan(): slot = jnp.cumsum(routed.astype(jnp.int32), axis=0) - 1]
    ppermute x1, waiting for transfers between devices: 0.37 us -> 2.14 us  [shifted(): return lax.ppermute(block, axis, route)]
    unnamed x38 -> x42, local copies, waits for them, and re-layouts: 3.89 us -> 3.92 us
  transfers between devices with their start and end apart: 14 -> 14, of which waited for: 13 -> 12; matrix products, arithmetic and copies ran while one was open for 6% -> 13% of each run, Pallas kernels for 0% -> 0%
where the time goes in v8:
time: 171 us; the launch traced here: 170 us
  waiting for transfers between devices  69.5 us (41%)
  starting transfers between devices  28.2 us (16%)
  other arithmetic  19.5 us (11%)
  matrix products  19.4 us (11%)
  blocking collectives  18.2 us (11%)
  local copies, waits for them, and re-layouts  15 us (9%)
    ppermute x9, waiting for transfers between devices, swap(): return lax.ppermute(block, axis, [(0, 1), (1, 0)])  28.7 us
    all_to_all x1, blocking collectives, body(): rows_y = lax.all_to_all(dispatch, 'y', 0, 0, tiled=True)  18.2 us
    ppermute x9, starting transfers between devices, swap(): return lax.ppermute(block, axis, [(0, 1), (1, 0)])  13.9 us
    all_to_all x1, waiting for transfers between devices, body(): part_y = lax.all_to_all(part_c.astype(jnp.bfloat16), 'y', 0, 0, tiled=True)  13.3 us
    all_to_all x1, waiting for transfers between devices, body(): lax.all_to_all(chip_sum.astype(jnp.bfloat16), 'y', 0, 0, tiled=True)  13.3 us
    ppermute x1, waiting for transfers between devices, body(): lax.ppermute(mixed_far.astype(jnp.bfloat16), ('section', 'zh'), route)  9.2 us
    dot_general x1, matrix products, body(): jnp.dot(activated, down_w, preferred_element_type=jnp.float32)  6.35 us
    all_to_all x1, starting transfers between devices, body(): kv_y = lax.all_to_all(send_kv, 'y', 0, 0, tiled=True)  4.46 us
  transfers between devices with their start and end apart: 14, of which 12 were waited for; matrix products, arithmetic and copies ran while one was open for 13% of the time, Pallas kernels for 0%

profile of v8, /device:TPU:32, one launch (start us, length us, event | category | flops | bytes accessed | tf_op | source)
XLA Modules:
  0.0 170.1 jit_solution(611531603992235513)
XLA Ops:
  0.0 1.2 reshape_squeeze.6
  1.2 0.4 fusion.94
  1.6 0.8 pad_maximum_fusion.3
  2.4 4.5 %all-to-all-start = ((bf16[4,256,256]{2,1,0:T(8,128)(2,1)}), bf16[4,256,256]{2,1,0:T(8,128)(2,1)}, u32[]{:S(2)}, u32[]{:S(2)}) async-start(bf16[4,256,256]{2,1,0:T(8,128)(2,1)} %pad_maximum_fusion.3), calls=%async_computation | async-start | bytes 1048576 | tf_op jit(solution)/shard_map/all_to_all | solution.py:56
  7.1 6.4 %collective-permute-start.1 = (bf16[2,256,128]{2,1,0:T(8,128)(2,1)S(1)}, bf16[2,256,128]{2,1,0:T(8,128)(2,1)S(1)}, u32[]{:S(2)}, u32[]{:S(2)}) collective-permute-start(bf16[2,256,128]{2,1,0:T(8,128)(2,1)S(1)} %bitcast.223), channel_id=1, source_target_pairs={{0,2},{2,0},{1,3},{3,1},{4,6},{6,4},{5,7},{7,5},{8,10},{10,8},{9,1... | collective-permute-start | bytes 393224 | tf_op jit(solution)/shard_map/ppermute | solution.py:26
  13.7 2.8 %all-to-all-done = bf16[4,256,256]{2,1,0:T(8,128)(2,1)} async-done(((bf16[4,256,256]{2,1,0:T(8,128)(2,1)}), bf16[4,256,256]{2,1,0:T(8,128)(2,1)}, u32[]{:S(2)}, u32[]{:S(2)}) %all-to-all-start) | async-done | bytes 524320 | tf_op jit(solution)/shard_map/all_to_all | solution.py:56
  16.5 0.4 broadcast_compare_fusion
  17.0 1.7 collective-permute-done
  18.6 1.1 pad_maximum_fusion.1
  19.8 0.7 fusion.8
  20.5 1.7 %fusion.11 = (f32[2,256]{1,0:T(2,128)S(1)}, f32[2,256]{1,0:T(2,128)S(1)}, f32[2048,2,256]{2,0,1:T(8,128)S(1)}) fusion(f32[2048,2,256]{2,0,1:T(8,128)S(1)} %get-tuple-element.27, f32[2,256]{1,0:T(2,128)S(1)} %get-tuple-element.26, pred[256,2048]{0,1:T(8,128)(4,1)S(1)} %broadcast_compare_fusion, bf16[2,256,128]{2,1,0:T(8,128)(2,1)S(1)} %collective-permute-done.1, ...), kind=kOutput, calls=%fused_computation.21 | convolution fusion | flops 275774464 | bytes 9574400 | tf_op jit(solution)/shard_map/hqd,kd->hqk/dot_general | solution.py:70
  22.2 1.0 fusion.14
  23.2 6.4 %collective-permute-start.2 = (f32[2,256,2]{1,0,2:T(2,128)S(1)}, f32[2,256,2]{1,0,2:T(2,128)S(1)}, u32[]{:S(2)}, u32[]{:S(2)}) collective-permute-start(f32[2,256,2]{1,0,2:T(2,128)S(1)} %pad_maximum_fusion.5), channel_id=1, source_target_pairs={{0,2},{2,0},{1,3},{3,1},{4,6},{6,4},{5,7},{7,5},{8,10},{10,8},{9,1... | collective-permute-start | bytes 12296 | tf_op jit(solution)/shard_map/ppermute | solution.py:26
  29.6 1.0 fusion.32
  30.7 0.5 collective-permute-done.2
  31.2 11.5 %collective-permute-done.3 = bf16[2,256,128]{1,2,0:T(8,128)(2,1)S(1)} collective-permute-done((bf16[2,256,128]{1,2,0:T(8,128)(2,1)S(1)}, bf16[2,256,128]{1,2,0:T(8,128)(2,1)S(1)}, u32[]{:S(2)}, u32[]{:S(2)}) %collective-permute-start.3) | collective-permute-done | bytes 131104 | tf_op jit(solution)/shard_map/ppermute | solution.py:26
  42.7 1.0 fusion.43
  43.7 0.6 copy-done.3
  44.2 0.7 convolution_convert_fusion.1
  45.0 1.3 copy-done.1
  46.3 1.1 dynamic-slice_bitcast_fusion
  47.4 3.0 %collective-permute-done.4 = bf16[4,2,16,4096]{3,2,1,0:T(8,128)(2,1)} collective-permute-done((bf16[4,2,16,4096]{3,2,1,0:T(8,128)(2,1)}, bf16[4,2,16,4096]{3,2,1,0:T(8,128)(2,1)}, u32[]{:S(2)}, u32[]{:S(2)}) %collective-permute-start.4) | collective-permute-done | bytes 1048608 | tf_op jit(solution)/shard_map/ppermute | solution.py:26
  50.4 2.8 %fusion.21 = bf16[4,2,16,4096]{3,2,1,0:T(8,128)(2,1)} fusion(bf16[4,2,16,4096]{3,2,1,0:T(8,128)(2,1)} %collective-permute-done.4, bf16[4,2,2,16,4096]{4,3,2,1,0:T(8,128)(2,1)} %bitcast.206, s32[]{:T(128)S(6)} %select_n.55), kind=kLoop, calls=%fused_computation.34 | loop fusion | flops 2097152 | bytes 3145732 | tf_op jit(solution)/shard_map/convert_element_type | solution.py:98
  53.2 4.4 %all-to-all-start.1 = ((bf16[4,2,16,4096]{3,2,1,0:T(8,128)(2,1)}), bf16[4,2,16,4096]{3,2,1,0:T(8,128)(2,1)}, u32[]{:S(2)}, u32[]{:S(2)}) async-start(bf16[4,2,16,4096]{3,2,1,0:T(8,128)(2,1)} %fusion.21), calls=%async_computation.1 | async-start | bytes 2097152 | tf_op jit(solution)/shard_map/all_to_all | solution.py:98
  57.6 0.5 collective-permute-start.6
  58.1 0.6 fusion.73
  58.7 0.5 copy-done.15
  59.3 0.6 reduce_window_sum.17
  59.9 13.3 %all-to-all-done.1 = bf16[4,2,16,4096]{3,2,1,0:T(8,128)(2,1)} async-done(((bf16[4,2,16,4096]{3,2,1,0:T(8,128)(2,1)}), bf16[4,2,16,4096]{3,2,1,0:T(8,128)(2,1)}, u32[]{:S(2)}, u32[]{:S(2)}) %all-to-all-start.1) | async-done | bytes 1048608 | tf_op jit(solution)/shard_map/all_to_all | solution.py:98
  73.3 1.4 convert_reduce_fusion
  74.7 0.7 pad_maximum_fusion.4
  75.4 0.4 collective-permute-start.5
  75.8 1.3 add_bitcast_fusion.1
  77.1 1.3 copy.87
  78.4 1.3 convert_element_type.143
  79.7 1.3 copy.90
  81.0 1.3 reduce_window_sum.18
  82.3 1.3 add_bitcast_fusion
  83.6 1.3 copy.91
  85.0 7.0 %collective-permute-done.5 = bf16[2,16,4096]{2,1,0:T(8,128)(2,1)} collective-permute-done((bf16[2,16,4096]{2,1,0:T(8,128)(2,1)}, bf16[2,16,4096]{2,1,0:T(8,128)(2,1)}, u32[]{:S(2)}, u32[]{:S(2)}) %collective-permute-start.5) | collective-permute-done | bytes 262176 | tf_op jit(solution)/shard_map/ppermute | solution.py:26
  91.9 1.0 convert_element_type.138
  92.9 1.3 multiply_reduce_fusion.1
  94.3 1.0 fusion
  95.3 1.3 fusion.1
  96.8 18.2 %all_to_all.20 = bf16[4,2,16,4096]{3,2,1,0:T(8,128)(2,1)S(1)} all-to-all(bf16[4,2,16,4096]{3,2,1,0:T(8,128)(2,1)S(1)} %copy.92), channel_id=1, replica_groups=mesh['section'=16,'y'=4,'zh'=2,'core'=2] {'y'}, dimensions={0} | all-to-all | bytes 2097152 | tf_op jit(solution)/shard_map/all_to_all | solution.py:142
  115.0 2.7 %collective-permute-done.7 = bf16[4,2,16,4096]{3,2,1,0:T(8,128)(2,1)S(1)} collective-permute-done((bf16[4,2,16,4096]{3,2,1,0:T(8,128)(2,1)S(1)}, bf16[4,2,16,4096]{3,2,1,0:T(8,128)(2,1)S(1)}, u32[]{:S(2)}, u32[]{:S(2)}) %collective-permute-start.7) | collective-permute-done | bytes 1048608 | tf_op jit(solution)/shard_map/ppermute | solution.py:26
  117.7 0.2 pad_maximum_fusion
  117.9 1.3 copy-done.4
  119.2 2.1 %fusion.16 = f32[256,384]{1,0:T(8,128)} fusion(bf16[256,4096]{1,0:T(8,128)(2,1)S(1)} %bitcast.209, bf16[1,4096,384]{2,1,0:T(8,128)(2,1)S(1)} %copy-done.19), kind=kOutput, calls=%fused_computation.26 | convolution fusion | flops 805306368 | bytes 5636096 | tf_op jit(solution)/shard_map/dot_general | solution.py:146
  121.3 6.3 %convolution_convert_fusion = bf16[256,4096]{1,0:T(8,128)(2,1)} fusion(bf16[1,384,4096]{2,1,0:T(8,128)(2,1)S(1)} %copy-done, f32[256,384]{1,0:T(8,128)} %fusion.16, bf16[256,4096]{1,0:T(8,128)(2,1)} %bitcast.210, bf16[1,4096,384]{2,1,0:T(8,128)(2,1)} %param.15), kind=kOutput, calls=%fused_computation | convolution fusion | flops 1612251136 | bytes 10878976 | tf_op jit(solution)/shard_map/dot_general | solution.py:149
  127.6 1.7 fusion.93
  129.4 0.2 collective-permute-start.8
  129.7 2.4 %collective-permute-done.8 = bf16[4,2,16,4096]{3,2,1,0:T(8,128)(2,1)S(1)} collective-permute-done((bf16[4,2,16,4096]{3,2,1,0:T(8,128)(2,1)S(1)}, bf16[4,2,16,4096]{3,2,1,0:T(8,128)(2,1)S(1)}, u32[]{:S(2)}, u32[]{:S(2)}) %collective-permute-start.8) | collective-permute-done | bytes 1048608 | tf_op jit(solution)/shard_map/ppermute | solution.py:26
  132.1 1.3 fusion.20
  133.4 4.2 %all-to-all-start.3 = ((bf16[4,2,16,4096]{3,2,1,0:T(8,128)(2,1)}), bf16[4,2,16,4096]{3,2,1,0:T(8,128)(2,1)}, u32[]{:S(2)}, u32[]{:S(2)}) async-start(bf16[4,2,16,4096]{3,2,1,0:T(8,128)(2,1)} %fusion.20), calls=%async_computation.3 | async-start | bytes 2097152 | tf_op jit(solution)/shard_map/all_to_all | solution.py:155
  138.7 0.7 reshape.241
  139.4 0.7 reshape.244
  140.1 13.3 %all-to-all-done.3 = bf16[4,2,16,4096]{3,2,1,0:T(8,128)(2,1)} async-done(((bf16[4,2,16,4096]{3,2,1,0:T(8,128)(2,1)}), bf16[4,2,16,4096]{3,2,1,0:T(8,128)(2,1)}, u32[]{:S(2)}, u32[]{:S(2)}) %all-to-all-start.3) | async-done | bytes 1048608 | tf_op jit(solution)/shard_map/all_to_all | solution.py:155
  153.4 1.8 %fusion.3 = bf16[16,4096]{1,0:T(8,128)(2,1)S(1)} fusion(bf16[4,2,16,4096]{3,2,1,0:T(8,128)(2,1)} %all-to-all-done.3, f32[2,16,4096]{2,1,0:T(8,128)} %copy-done.2, bf16[1,16,4096]{2,1,0:T(8,128)(2,1)S(1)} %get-tuple-element.14, f32[16,4,16]{2,1,0:T(4,128)} %reshape.241, bf16[1,16,4096]{2,1,0:T(8,128)(2,1)S(1)} %copy-done.5), kind=kOutput, calls=%fused_computation.9 | convolution fusion | flops 50724864 | bytes 1212416 | tf_op jit(solution)/shard_map/txj,xjd->td/dot_general | solution.py:159
  155.2 1.1 collective-permute-start.9
  156.2 1.7 %fusion.4 = bf16[16,4096]{1,0:T(8,128)(2,1)S(1)} fusion(bf16[4,2,16,4096]{3,2,1,0:T(8,128)(2,1)} %all-to-all-done.3, f32[16,4,16]{2,1,0:T(4,128)} %reshape.244), kind=kOutput, calls=%fused_computation.10 | convolution fusion | flops 50397184 | bytes 688128 | tf_op jit(solution)/shard_map/txj,xjd->td/dot_general | solution.py:160
  158.1 2.1 %collective-permute-done.9 = bf16[16,4096]{1,0:T(8,128)(2,1)S(1)} collective-permute-done((bf16[16,4096]{1,0:T(8,128)(2,1)S(1)}, bf16[16,4096]{1,0:T(8,128)(2,1)S(1)}, u32[]{:S(2)}, u32[]{:S(2)}) %collective-permute-start.9) | collective-permute-done | bytes 131104 | tf_op jit(solution)/shard_map/ppermute | solution.py:22
  160.2 9.2 %collective-permute-done.10 = bf16[16,4096]{1,0:T(8,128)(2,1)S(1)} collective-permute-done((bf16[16,4096]{1,0:T(8,128)(2,1)S(1)}, bf16[16,4096]{1,0:T(8,128)(2,1)S(1)}, u32[]{:S(2)}, u32[]{:S(2)}) %collective-permute-start.10) | collective-permute-done | bytes 131104 | tf_op jit(solution)/shard_map/ppermute | solution.py:166
  169.4 0.7 fusion.57
  (83 shorter events, 2.2 us)
Async XLA Ops:
  0.0 121.3 %copy-start = (bf16[1,384,4096]{2,1,0:T(8,128)(2,1)S(1)}, bf16[1,384,4096]{2,1,0:T(8,128)(2,1)}, u32[]{:S(2)}) copy-start(bf16[1,384,4096]{2,1,0:T(8,128)(2,1)} %param.17) | copy-start | bytes 9437188
  0.0 6.9 %copy-start.6 = (bf16[1,256,256]{2,1,0:T(8,128)(2,1)S(1)}, bf16[1,256,256]{2,1,0:T(8,128)(2,1)}, u32[]{:S(2)}) copy-start(bf16[1,256,256]{2,1,0:T(8,128)(2,1)} %param.11) | copy-start | bytes 393220
  2.4 14.0 %all-to-all-start = ((bf16[4,256,256]{2,1,0:T(8,128)(2,1)}), bf16[4,256,256]{2,1,0:T(8,128)(2,1)}, u32[]{:S(2)}, u32[]{:S(2)}) async-start(bf16[4,256,256]{2,1,0:T(8,128)(2,1)} %pad_maximum_fusion.3), calls=%async_computation | async-start | bytes 1048576 | tf_op jit(solution)/shard_map/all_to_all | solution.py:56
  7.1 13.4 %collective-permute-start.1 = (bf16[2,256,128]{2,1,0:T(8,128)(2,1)S(1)}, bf16[2,256,128]{2,1,0:T(8,128)(2,1)S(1)}, u32[]{:S(2)}, u32[]{:S(2)}) collective-permute-start(bf16[2,256,128]{2,1,0:T(8,128)(2,1)S(1)} %bitcast.223), channel_id=1, source_target_pairs={{0,2},{2,0},{1,3},{3,1},{4,6},{6,4},{5,7},{7,5},{8,10},{10,8},{9,1... | collective-permute-start | bytes 393224 | tf_op jit(solution)/shard_map/ppermute | solution.py:26
  16.5 2.1 %collective-permute-start = (bf16[4,256,256]{2,1,0:T(8,128)(2,1)}, bf16[4,256,256]{2,1,0:T(8,128)(2,1)S(1)}, u32[]{:S(2)}, u32[]{:S(2)}) collective-permute-start(bf16[4,256,256]{2,1,0:T(8,128)(2,1)} %all-to-all-done), channel_id=1, source_target_pairs={{0,1},{1,0},{2,3},{3,2},{4,5},{5,4},{6,7},{7,6},{8,9},{9,8},{10,11... | collective-permute-start | bytes 1572872 | tf_op jit(solution)/shard_map/ppermute | solution.py:26
  23.2 8.0 %collective-permute-start.2 = (f32[2,256,2]{1,0,2:T(2,128)S(1)}, f32[2,256,2]{1,0,2:T(2,128)S(1)}, u32[]{:S(2)}, u32[]{:S(2)}) collective-permute-start(f32[2,256,2]{1,0,2:T(2,128)S(1)} %pad_maximum_fusion.5), channel_id=1, source_target_pairs={{0,2},{2,0},{1,3},{3,1},{4,6},{6,4},{5,7},{7,5},{8,10},{10,8},{9,1... | collective-permute-start | bytes 12296 | tf_op jit(solution)/shard_map/ppermute | solution.py:26
  30.6 12.1 %collective-permute-start.3 = (bf16[2,256,128]{1,2,0:T(8,128)(2,1)S(1)}, bf16[2,256,128]{1,2,0:T(8,128)(2,1)S(1)}, u32[]{:S(2)}, u32[]{:S(2)}) collective-permute-start(bf16[2,256,128]{1,2,0:T(8,128)(2,1)S(1)} %fusion.32), channel_id=1, source_target_pairs={{0,2},{2,0},{1,3},{3,1},{4,6},{6,4},{5,7},{7,5},{8,10},{10,8},{9,1... | collective-permute-start | bytes 393224 | tf_op jit(solution)/shard_map/ppermute | solution.py:26
  42.6 1.6 copy-start.3
  45.0 1.3 copy-start.1
  47.4 10.2 %copy-start.5 = (bf16[1,16,4096]{2,1,0:T(8,128)(2,1)S(1)}, bf16[1,16,4096]{2,1,0:T(8,128)(2,1)}, u32[]{:S(2)}) copy-start(bf16[1,16,4096]{2,1,0:T(8,128)(2,1)} %param.10) | copy-start | bytes 393220
  47.4 10.7 %copy-start.18 = (s32[1,256,2]{1,2,0:T(2,128)S(1)}, s32[1,256,2]{1,2,0:T(2,128)}, u32[]{:S(2)}) copy-start(s32[1,256,2]{1,2,0:T(2,128)} %param.18) | copy-start | bytes 6148
  47.4 3.0 %collective-permute-start.4 = (bf16[4,2,16,4096]{3,2,1,0:T(8,128)(2,1)}, bf16[4,2,16,4096]{3,2,1,0:T(8,128)(2,1)}, u32[]{:S(2)}, u32[]{:S(2)}) collective-permute-start(bf16[4,2,16,4096]{3,2,1,0:T(8,128)(2,1)} %dynamic-slice_bitcast_fusion), channel_id=1, source_target_pairs={{0,1},{1,0},{2,3},{3,2},{4,5},{5,4},{6,7},{7,6},{8,9},{9,8},{10,11... | collective-permute-start | bytes 3145736 | tf_op jit(solution)/shard_map/ppermute | solution.py:26
  53.2 41.1 %copy-start.7 = (f32[1,4096]{1,0:T(1,128)S(1)}, f32[1,4096]{1,0:T(1,128)}, u32[]{:S(2)}) copy-start(f32[1,4096]{1,0:T(1,128)} %param.14) | copy-start | bytes 49156
  53.2 20.1 %all-to-all-start.1 = ((bf16[4,2,16,4096]{3,2,1,0:T(8,128)(2,1)}), bf16[4,2,16,4096]{3,2,1,0:T(8,128)(2,1)}, u32[]{:S(2)}, u32[]{:S(2)}) async-start(bf16[4,2,16,4096]{3,2,1,0:T(8,128)(2,1)} %fusion.21), calls=%async_computation.1 | async-start | bytes 2097152 | tf_op jit(solution)/shard_map/all_to_all | solution.py:98
  57.6 35.4 %collective-permute-start.6 = (bf16[16,4096]{1,0:T(8,128)(2,1)S(1)}, bf16[16,4096]{1,0:T(8,128)(2,1)}, u32[]{:S(2)}, u32[]{:S(2)}) collective-permute-start(bf16[16,4096]{1,0:T(8,128)(2,1)S(1)} %bitcast.211), channel_id=1, source_target_pairs={{0,2},{2,0},{1,3},{3,1},{4,6},{6,4},{5,7},{7,5},{8,10},{10,8},{9,1... | collective-permute-start | bytes 393224 | tf_op jit(solution)/shard_map/ppermute | solution.py:26
  58.1 0.6 copy-start.10
  58.1 0.6 copy-start.12
  58.7 0.5 copy-start.15
  75.4 16.5 %collective-permute-start.5 = (bf16[2,16,4096]{2,1,0:T(8,128)(2,1)}, bf16[2,16,4096]{2,1,0:T(8,128)(2,1)}, u32[]{:S(2)}, u32[]{:S(2)}) collective-permute-start(bf16[2,16,4096]{2,1,0:T(8,128)(2,1)} %pad_maximum_fusion.4), channel_id=1, source_target_pairs={{0,2},{2,0},{1,3},{3,1},{4,6},{6,4},{5,7},{7,5},{8,10},{10,8},{9,1... | collective-permute-start | bytes 786440 | tf_op jit(solution)/shard_map/ppermute | solution.py:26
  92.9 2.3 %copy-start.2 = (f32[2,16,4096]{2,1,0:T(8,128)}, f32[2,16,4096]{2,1,0:T(8,128)S(1)}, u32[]{:S(2)}) copy-start(f32[2,16,4096]{2,1,0:T(8,128)S(1)} %convert_element_type.138) | copy-start | bytes 1572868
  96.8 22.4 %copy-start.19 = (bf16[1,4096,384]{2,1,0:T(8,128)(2,1)S(1)}, bf16[1,4096,384]{2,1,0:T(8,128)(2,1)}, u32[]{:S(2)}) copy-start(bf16[1,4096,384]{2,1,0:T(8,128)(2,1)} %param.16) | copy-start | bytes 9437188
  115.0 2.7 %collective-permute-start.7 = (bf16[4,2,16,4096]{3,2,1,0:T(8,128)(2,1)S(1)}, bf16[4,2,16,4096]{3,2,1,0:T(8,128)(2,1)S(1)}, u32[]{:S(2)}, u32[]{:S(2)}) collective-permute-start(bf16[4,2,16,4096]{3,2,1,0:T(8,128)(2,1)S(1)} %all_to_all.20), channel_id=1, source_target_pairs={{0,1},{1,0},{2,3},{3,2},{4,5},{5,4},{6,7},{7,6},{8,9},{9,8},{10,11... | collective-permute-start | bytes 3145736 | tf_op jit(solution)/shard_map/ppermute | solution.py:26
  117.9 1.3 copy-start.4
  127.6 2.0 %copy-start.17 = (f32[1,256,2]{1,2,0:T(2,128)S(1)}, f32[1,256,2]{1,2,0:T(2,128)}, u32[]{:S(2)}) copy-start(f32[1,256,2]{1,2,0:T(2,128)} %param.19) | copy-start | bytes 6148
  129.3 8.3 %copy-start.11 = (s32[16,2]{0,1:T(2,128)S(1)}, s32[16,2]{0,1:T(2,128)}, u32[]{:S(2)}) copy-start(s32[16,2]{0,1:T(2,128)} %copy-done.10) | copy-start | bytes 388
  129.3 8.3 %copy-start.13 = (s32[16,2]{0,1:T(2,128)S(1)}, s32[16,2]{0,1:T(2,128)}, u32[]{:S(2)}) copy-start(s32[16,2]{0,1:T(2,128)} %copy-done.12) | copy-start | bytes 388
  129.3 8.9 %copy-start.8 = (s32[4,16]{1,0:T(4,128)S(1)}, s32[4,16]{1,0:T(4,128)}, u32[]{:S(2)}) copy-start(s32[4,16]{1,0:T(4,128)} %copy.87) | copy-start | bytes 772
  129.3 8.9 %copy-start.9 = (s32[4,16]{1,0:T(4,128)S(1)}, s32[4,16]{1,0:T(4,128)}, u32[]{:S(2)}) copy-start(s32[4,16]{1,0:T(4,128)} %copy.91) | copy-start | bytes 772
  129.3 9.0 %copy-start.16 = (pred[16,4]{0,1:T(4,128)(4,1)S(1)}, pred[16,4]{0,1:T(4,128)(4,1)}, u32[]{:S(2)}) copy-start(pred[16,4]{0,1:T(4,128)(4,1)} %copy-done.15) | copy-start | bytes 196
  129.4 9.1 %copy-start.14 = (pred[16,4]{0,1:T(4,128)(4,1)S(1)}, pred[16,4]{0,1:T(4,128)(4,1)}, u32[]{:S(2)}) copy-start(pred[16,4]{0,1:T(4,128)(4,1)} %get-tuple-element.33) | copy-start | bytes 196
  129.4 2.7 %collective-permute-start.8 = (bf16[4,2,16,4096]{3,2,1,0:T(8,128)(2,1)S(1)}, bf16[4,2,16,4096]{3,2,1,0:T(8,128)(2,1)S(1)}, u32[]{:S(2)}, u32[]{:S(2)}) collective-permute-start(bf16[4,2,16,4096]{3,2,1,0:T(8,128)(2,1)S(1)} %bitcast.216), channel_id=1, source_target_pairs={{0,1},{1,0},{2,3},{3,2},{4,5},{5,4},{6,7},{7,6},{8,9},{9,8},{10,11... | collective-permute-start | bytes 3145736 | tf_op jit(solution)/shard_map/ppermute | solution.py:26
  133.4 20.0 %all-to-all-start.3 = ((bf16[4,2,16,4096]{3,2,1,0:T(8,128)(2,1)}), bf16[4,2,16,4096]{3,2,1,0:T(8,128)(2,1)}, u32[]{:S(2)}, u32[]{:S(2)}) async-start(bf16[4,2,16,4096]{3,2,1,0:T(8,128)(2,1)} %fusion.20), calls=%async_computation.3 | async-start | bytes 2097152 | tf_op jit(solution)/shard_map/all_to_all | solution.py:155
  155.2 5.0 %collective-permute-start.9 = (bf16[16,4096]{1,0:T(8,128)(2,1)S(1)}, bf16[16,4096]{1,0:T(8,128)(2,1)S(1)}, u32[]{:S(2)}, u32[]{:S(2)}) collective-permute-start(bf16[16,4096]{1,0:T(8,128)(2,1)S(1)} %fusion.3), channel_id=1, source_target_pairs={{240,0},{0,16},{16,32},{32,48},{48,64},{64,80},{80,96},{96,112},{1... | collective-permute-start | bytes 393224 | tf_op jit(solution)/shard_map/ppermute | solution.py:22
  158.0 11.4 %collective-permute-start.10 = (bf16[16,4096]{1,0:T(8,128)(2,1)S(1)}, bf16[16,4096]{1,0:T(8,128)(2,1)S(1)}, u32[]{:S(2)}, u32[]{:S(2)}) collective-permute-start(bf16[16,4096]{1,0:T(8,128)(2,1)S(1)} %fusion.4), channel_id=1, source_target_pairs={{0,18},{2,16},{16,34},{18,32},{32,50},{34,48},{48,66},{50,64},{64,... | collective-permute-start | bytes 393224 | tf_op jit(solution)/shard_map/ppermute | solution.py:166

commit v9 on v8

--- a/solution.py
+++ b/solution.py
@@ -152,18 +152,19 @@
     )
 
     chip_sum = computed[0].astype(jnp.float32) + swap(computed[1], "core").astype(jnp.float32)
-    back = lax.all_to_all(chip_sum.astype(jnp.bfloat16), "y", 0, 0, tiled=True).astype(jnp.float32)
     hi = lax.Precision.HIGHEST
     combine_own = combine_own.reshape(tok_rows, experts_count, CAP)
     combine_far = combine_far.reshape(tok_rows, experts_count, CAP)
-    mixed_own = jnp.einsum("txj,xjd->td", combine_own, back[:, 0], precision=hi)
-    mixed_far = jnp.einsum("txj,xjd->td", combine_far, back[:, 1], precision=hi)
-    own_part = shifted((middle + mixed_own).astype(jnp.bfloat16), "section", 1)
+    back_far = lax.all_to_all(chip_sum[:, 1].astype(jnp.bfloat16), "y", 0, 0, tiled=True)
+    mixed_far = jnp.einsum("txj,xjd->td", combine_far, back_far.astype(jnp.float32), precision=hi)
     sections = lax.axis_size("section")
     route = [
         (s * nz + z, ((s + 1) % sections) * nz + (nz - 1 - z)) for s in range(sections) for z in range(nz)
     ]
     far_part = lax.ppermute(mixed_far.astype(jnp.bfloat16), ("section", "zh"), route)
+    back_own = lax.all_to_all(chip_sum[:, 0].astype(jnp.bfloat16), "y", 0, 0, tiled=True)
+    mixed_own = jnp.einsum("txj,xjd->td", combine_own, back_own.astype(jnp.float32), precision=hi)
+    own_part = shifted((middle + mixed_own).astype(jnp.bfloat16), "section", 1)
     layer_out = own_part.astype(jnp.float32) + far_part.astype(jnp.float32)
     return layer_out.astype(jnp.bfloat16)[None]
 

time: 171 us -> 175 us (1.023)
  starting transfers between devices: 28.2 us -> 33.2 us
    all_to_all x1 -> x2, starting transfers between devices: 4.24 us -> 8.29 us  [the longest x1 4.15 us: body(): lax.all_to_all(chip_sum[:, 1].astype(jnp.bfloat16), 'y', 0, 0, tiled=True)]
    ppermute x1, waiting for transfers between devices: 2.14 us -> 0.01 us  [shifted(): return lax.ppermute(block, axis, route)]
    all_to_all x1 -> x2, waiting for transfers between devices: 13.3 us -> 14.1 us  [the longest x1 9.15 us: body(): lax.all_to_all(chip_sum[:, 0].astype(jnp.bfloat16), 'y', 0, 0, tiled=True)]
  transfers between devices with their start and end apart: 14 -> 15, of which waited for: 12 -> 12; matrix products, arithmetic and copies ran while one was open for 13% -> 13% of each run, Pallas kernels for 0% -> 0%
where the time goes in v9:
time: 175 us; the launch traced here: 174 us
  waiting for transfers between devices  68.5 us (39%)
  starting transfers between devices  33.2 us (19%)
  matrix products  19.4 us (11%)
  other arithmetic  18.3 us (10%)
  blocking collectives  18.2 us (10%)
  local copies, waits for them, and re-layouts  16.1 us (9%)
    ppermute x9, waiting for transfers between devices, swap(): return lax.ppermute(block, axis, [(0, 1), (1, 0)])  28.7 us
    all_to_all x1, blocking collectives, body(): rows_y = lax.all_to_all(dispatch, 'y', 0, 0, tiled=True)  18.2 us
    ppermute x9, starting transfers between devices, swap(): return lax.ppermute(block, axis, [(0, 1), (1, 0)])  13.9 us
    all_to_all x1, waiting for transfers between devices, body(): part_y = lax.all_to_all(part_c.astype(jnp.bfloat16), 'y', 0, 0, tiled=True)  13.4 us
    ppermute x1, waiting for transfers between devices, body(): lax.ppermute(mixed_far.astype(jnp.bfloat16), ('section', 'zh'), route)  9.48 us
    all_to_all x1, waiting for transfers between devices, body(): lax.all_to_all(chip_sum[:, 0].astype(jnp.bfloat16), 'y', 0, 0, tiled=True)  9.15 us
    dot_general x1, matrix products, body(): jnp.dot(activated, down_w, preferred_element_type=jnp.float32)  6.35 us
    all_to_all x1, waiting for transfers between devices, body(): lax.all_to_all(chip_sum[:, 1].astype(jnp.bfloat16), 'y', 0, 0, tiled=True)  4.96 us
  transfers between devices with their start and end apart: 15, of which 12 were waited for; matrix products, arithmetic and copies ran while one was open for 13% of the time, Pallas kernels for 0%

profile of v9, /device:TPU:32, one launch (start us, length us, event | category | flops | bytes accessed | tf_op | source)
XLA Modules:
  0.0 174.1 jit_solution(7852838353832582348)
XLA Ops:
  0.0 1.2 reshape_squeeze.6
  1.2 0.4 fusion.94
  1.6 0.8 pad_maximum_fusion.3
  2.5 4.5 %all-to-all-start = ((bf16[4,256,256]{2,1,0:T(8,128)(2,1)}), bf16[4,256,256]{2,1,0:T(8,128)(2,1)}, u32[]{:S(2)}, u32[]{:S(2)}) async-start(bf16[4,256,256]{2,1,0:T(8,128)(2,1)} %pad_maximum_fusion.3), calls=%async_computation | async-start | bytes 1048576 | tf_op jit(solution)/shard_map/all_to_all | solution.py:56
  7.1 6.4 %collective-permute-start.1 = (bf16[2,256,128]{2,1,0:T(8,128)(2,1)S(1)}, bf16[2,256,128]{2,1,0:T(8,128)(2,1)S(1)}, u32[]{:S(2)}, u32[]{:S(2)}) collective-permute-start(bf16[2,256,128]{2,1,0:T(8,128)(2,1)S(1)} %bitcast.219), channel_id=1, source_target_pairs={{0,2},{2,0},{1,3},{3,1},{4,6},{6,4},{5,7},{7,5},{8,10},{10,8},{9,1... | collective-permute-start | bytes 393224 | tf_op jit(solution)/shard_map/ppermute | solution.py:26
  13.7 2.8 %all-to-all-done = bf16[4,256,256]{2,1,0:T(8,128)(2,1)} async-done(((bf16[4,256,256]{2,1,0:T(8,128)(2,1)}), bf16[4,256,256]{2,1,0:T(8,128)(2,1)}, u32[]{:S(2)}, u32[]{:S(2)}) %all-to-all-start) | async-done | bytes 524320 | tf_op jit(solution)/shard_map/all_to_all | solution.py:56
  16.5 0.4 broadcast_compare_fusion
  17.0 1.7 collective-permute-done
  18.6 1.1 pad_maximum_fusion.1
  19.8 0.7 fusion.8
  20.5 1.7 fusion.11
  22.2 1.0 fusion.14
  23.2 6.4 %collective-permute-start.2 = (f32[2,256,2]{1,0,2:T(2,128)S(1)}, f32[2,256,2]{1,0,2:T(2,128)S(1)}, u32[]{:S(2)}, u32[]{:S(2)}) collective-permute-start(f32[2,256,2]{1,0,2:T(2,128)S(1)} %pad_maximum_fusion.5), channel_id=1, source_target_pairs={{0,2},{2,0},{1,3},{3,1},{4,6},{6,4},{5,7},{7,5},{8,10},{10,8},{9,1... | collective-permute-start | bytes 12296 | tf_op jit(solution)/shard_map/ppermute | solution.py:26
  29.6 1.0 fusion.32
  30.7 0.5 collective-permute-done.2
  31.2 11.5 %collective-permute-done.3 = bf16[2,256,128]{1,2,0:T(8,128)(2,1)S(1)} collective-permute-done((bf16[2,256,128]{1,2,0:T(8,128)(2,1)S(1)}, bf16[2,256,128]{1,2,0:T(8,128)(2,1)S(1)}, u32[]{:S(2)}, u32[]{:S(2)}) %collective-permute-start.3) | collective-permute-done | bytes 131104 | tf_op jit(solution)/shard_map/ppermute | solution.py:26
  42.7 1.0 fusion.43
  43.7 0.6 copy-done.3
  44.2 0.7 convolution_convert_fusion.1
  45.0 1.3 copy-done.1
  46.3 1.1 dynamic-slice_bitcast_fusion
  47.4 3.0 %collective-permute-done.4 = bf16[4,2,16,4096]{3,2,1,0:T(8,128)(2,1)} collective-permute-done((bf16[4,2,16,4096]{3,2,1,0:T(8,128)(2,1)}, bf16[4,2,16,4096]{3,2,1,0:T(8,128)(2,1)}, u32[]{:S(2)}, u32[]{:S(2)}) %collective-permute-start.4) | collective-permute-done | bytes 1048608 | tf_op jit(solution)/shard_map/ppermute | solution.py:26
  50.4 2.8 %fusion.20 = bf16[4,2,16,4096]{3,2,1,0:T(8,128)(2,1)} fusion(bf16[4,2,16,4096]{3,2,1,0:T(8,128)(2,1)} %collective-permute-done.4, bf16[4,2,2,16,4096]{4,3,2,1,0:T(8,128)(2,1)} %bitcast.202, s32[]{:T(128)S(6)} %select_n.55), kind=kLoop, calls=%fused_computation.32 | loop fusion | flops 2097152 | bytes 3145732 | tf_op jit(solution)/shard_map/convert_element_type | solution.py:98
  53.2 4.4 %all-to-all-start.1 = ((bf16[4,2,16,4096]{3,2,1,0:T(8,128)(2,1)}), bf16[4,2,16,4096]{3,2,1,0:T(8,128)(2,1)}, u32[]{:S(2)}, u32[]{:S(2)}) async-start(bf16[4,2,16,4096]{3,2,1,0:T(8,128)(2,1)} %fusion.20), calls=%async_computation.1 | async-start | bytes 2097152 | tf_op jit(solution)/shard_map/all_to_all | solution.py:98
  57.6 0.5 collective-permute-start.6
  58.1 0.5 fusion.73
  58.7 0.5 copy-done.15
  59.3 0.6 reduce_window_sum.17
  59.9 13.4 %all-to-all-done.1 = bf16[4,2,16,4096]{3,2,1,0:T(8,128)(2,1)} async-done(((bf16[4,2,16,4096]{3,2,1,0:T(8,128)(2,1)}), bf16[4,2,16,4096]{3,2,1,0:T(8,128)(2,1)}, u32[]{:S(2)}, u32[]{:S(2)}) %all-to-all-start.1) | async-done | bytes 1048608 | tf_op jit(solution)/shard_map/all_to_all | solution.py:98
  73.3 1.4 convert_reduce_fusion
  74.7 0.7 pad_maximum_fusion.4
  75.4 0.4 collective-permute-start.5
  75.8 1.3 add_bitcast_fusion.1
  77.1 1.3 copy.87
  78.4 1.2 convert_element_type.149
  79.6 1.3 copy.90
  81.0 1.3 reduce_window_sum.18
  82.3 1.3 add_bitcast_fusion
  83.6 1.4 copy.91
  84.9 7.0 %collective-permute-done.5 = bf16[2,16,4096]{2,1,0:T(8,128)(2,1)} collective-permute-done((bf16[2,16,4096]{2,1,0:T(8,128)(2,1)}, bf16[2,16,4096]{2,1,0:T(8,128)(2,1)}, u32[]{:S(2)}, u32[]{:S(2)}) %collective-permute-start.5) | collective-permute-done | bytes 262176 | tf_op jit(solution)/shard_map/ppermute | solution.py:26
  91.9 1.0 convert_element_type.144
  92.9 1.3 multiply_reduce_fusion.1
  94.3 1.0 fusion
  95.3 1.3 fusion.1
  96.8 18.2 %all_to_all.25 = bf16[4,2,16,4096]{3,2,1,0:T(8,128)(2,1)S(1)} all-to-all(bf16[4,2,16,4096]{3,2,1,0:T(8,128)(2,1)S(1)} %copy.92), channel_id=1, replica_groups=mesh['section'=16,'y'=4,'zh'=2,'core'=2] {'y'}, dimensions={0} | all-to-all | bytes 2097152 | tf_op jit(solution)/shard_map/all_to_all | solution.py:142
  115.0 2.7 %collective-permute-done.7 = bf16[4,2,16,4096]{3,2,1,0:T(8,128)(2,1)S(1)} collective-permute-done((bf16[4,2,16,4096]{3,2,1,0:T(8,128)(2,1)S(1)}, bf16[4,2,16,4096]{3,2,1,0:T(8,128)(2,1)S(1)}, u32[]{:S(2)}, u32[]{:S(2)}) %collective-permute-start.7) | collective-permute-done | bytes 1048608 | tf_op jit(solution)/shard_map/ppermute | solution.py:26
  117.9 1.3 copy-done.4
  119.2 2.1 %fusion.16 = f32[256,384]{1,0:T(8,128)} fusion(bf16[256,4096]{1,0:T(8,128)(2,1)S(1)} %bitcast.206, bf16[1,4096,384]{2,1,0:T(8,128)(2,1)S(1)} %copy-done.19), kind=kOutput, calls=%fused_computation.26 | convolution fusion | flops 805306368 | bytes 5636096 | tf_op jit(solution)/shard_map/dot_general | solution.py:146
  121.3 6.4 %convolution_convert_fusion = bf16[256,4096]{1,0:T(8,128)(2,1)} fusion(bf16[1,384,4096]{2,1,0:T(8,128)(2,1)S(1)} %copy-done, f32[256,384]{1,0:T(8,128)} %fusion.16, bf16[256,4096]{1,0:T(8,128)(2,1)} %bitcast.207, bf16[1,4096,384]{2,1,0:T(8,128)(2,1)} %param.15), kind=kOutput, calls=%fused_computation | convolution fusion | flops 1612251136 | bytes 10878976 | tf_op jit(solution)/shard_map/dot_general | solution.py:149
  127.7 1.7 fusion.93
  129.8 2.4 %collective-permute-done.8 = bf16[4,2,16,4096]{3,2,0,1:T(8,128)(2,1)S(1)} collective-permute-done((bf16[4,2,16,4096]{3,2,0,1:T(8,128)(2,1)S(1)}, bf16[4,2,16,4096]{3,2,0,1:T(8,128)(2,1)S(1)}, u32[]{:S(2)}, u32[]{:S(2)}) %collective-permute-start.8) | collective-permute-done | bytes 1048608 | tf_op jit(solution)/shard_map/ppermute | solution.py:26
  132.4 1.0 slice_bitcast_fusion.1
  133.5 4.1 %all-to-all-start.3 = ((bf16[4,16,4096]{2,1,0:T(8,128)(2,1)}), bf16[4,16,4096]{2,1,0:T(8,128)(2,1)}, u32[]{:S(2)}, u32[]{:S(2)}) async-start(bf16[4,16,4096]{2,1,0:T(8,128)(2,1)} %get-tuple-element.13), calls=%async_computation.3 | async-start | bytes 1048576 | tf_op jit(solution)/shard_map/all_to_all | solution.py:165
  138.6 9.1 %all-to-all-done.3 = bf16[4,16,4096]{2,1,0:T(8,128)(2,1)} async-done(((bf16[4,16,4096]{2,1,0:T(8,128)(2,1)}), bf16[4,16,4096]{2,1,0:T(8,128)(2,1)}, u32[]{:S(2)}, u32[]{:S(2)}) %all-to-all-start.3) | async-done | bytes 524320 | tf_op jit(solution)/shard_map/all_to_all | solution.py:165
  147.7 4.1 %all-to-all-start.4 = ((bf16[4,16,4096]{2,1,0:T(8,128)(2,1)}), bf16[4,16,4096]{2,1,0:T(8,128)(2,1)}, u32[]{:S(2)}, u32[]{:S(2)}) async-start(bf16[4,16,4096]{2,1,0:T(8,128)(2,1)} %get-tuple-element.14), calls=%async_computation.4 | async-start | bytes 1048576 | tf_op jit(solution)/shard_map/all_to_all | solution.py:158
  151.9 0.7 reshape.243
  152.6 0.7 reshape.246
  153.3 1.8 %fusion.3 = bf16[16,4096]{1,0:T(8,128)(2,1)S(1)} fusion(bf16[4,16,4096]{2,1,0:T(8,128)(2,1)} %all-to-all-done.3, f32[2,16,4096]{2,1,0:T(8,128)} %copy-done.2, bf16[1,16,4096]{2,1,0:T(8,128)(2,1)S(1)} %get-tuple-element.16, f32[16,4,16]{2,1,0:T(4,128)} %reshape.243, bf16[1,16,4096]{2,1,0:T(8,128)(2,1)S(1)} %copy-done.5), kind=kOutput, calls=%fused_computation.9 | convolution fusion | flops 50724864 | bytes 1183744 | tf_op jit(solution)/shard_map/txj,xjd->td/dot_general | solution.py:166
  155.1 1.1 collective-permute-start.9
  156.2 5.0 %all-to-all-done.4 = bf16[4,16,4096]{2,1,0:T(8,128)(2,1)} async-done(((bf16[4,16,4096]{2,1,0:T(8,128)(2,1)}), bf16[4,16,4096]{2,1,0:T(8,128)(2,1)}, u32[]{:S(2)}, u32[]{:S(2)}) %all-to-all-start.4) | async-done | bytes 524320 | tf_op jit(solution)/shard_map/all_to_all | solution.py:158
  161.2 1.7 %fusion.4 = bf16[16,4096]{1,0:T(8,128)(2,1)S(1)} fusion(bf16[4,16,4096]{2,1,0:T(8,128)(2,1)} %all-to-all-done.4, f32[16,4,16]{2,1,0:T(4,128)} %reshape.246), kind=kOutput, calls=%fused_computation.10 | convolution fusion | flops 50397184 | bytes 659456 | tf_op jit(solution)/shard_map/txj,xjd->td/dot_general | solution.py:159
  162.9 1.0 collective-permute-start.10
  164.0 9.5 %collective-permute-done.10 = bf16[16,4096]{1,0:T(8,128)(2,1)S(1)} collective-permute-done((bf16[16,4096]{1,0:T(8,128)(2,1)S(1)}, bf16[16,4096]{1,0:T(8,128)(2,1)S(1)}, u32[]{:S(2)}, u32[]{:S(2)}) %collective-permute-start.10) | collective-permute-done | bytes 131104 | tf_op jit(solution)/shard_map/ppermute | solution.py:164
  173.4 0.7 fusion.57
  (87 shorter events, 2.9 us)
Async XLA Ops:
  0.0 121.3 %copy-start = (bf16[1,384,4096]{2,1,0:T(8,128)(2,1)S(1)}, bf16[1,384,4096]{2,1,0:T(8,128)(2,1)}, u32[]{:S(2)}) copy-start(bf16[1,384,4096]{2,1,0:T(8,128)(2,1)} %param.17) | copy-start | bytes 9437188
  0.0 6.9 %copy-start.6 = (bf16[1,256,256]{2,1,0:T(8,128)(2,1)S(1)}, bf16[1,256,256]{2,1,0:T(8,128)(2,1)}, u32[]{:S(2)}) copy-start(bf16[1,256,256]{2,1,0:T(8,128)(2,1)} %param.11) | copy-start | bytes 393220
  2.5 14.0 %all-to-all-start = ((bf16[4,256,256]{2,1,0:T(8,128)(2,1)}), bf16[4,256,256]{2,1,0:T(8,128)(2,1)}, u32[]{:S(2)}, u32[]{:S(2)}) async-start(bf16[4,256,256]{2,1,0:T(8,128)(2,1)} %pad_maximum_fusion.3), calls=%async_computation | async-start | bytes 1048576 | tf_op jit(solution)/shard_map/all_to_all | solution.py:56
  7.1 13.4 %collective-permute-start.1 = (bf16[2,256,128]{2,1,0:T(8,128)(2,1)S(1)}, bf16[2,256,128]{2,1,0:T(8,128)(2,1)S(1)}, u32[]{:S(2)}, u32[]{:S(2)}) collective-permute-start(bf16[2,256,128]{2,1,0:T(8,128)(2,1)S(1)} %bitcast.219), channel_id=1, source_target_pairs={{0,2},{2,0},{1,3},{3,1},{4,6},{6,4},{5,7},{7,5},{8,10},{10,8},{9,1... | collective-permute-start | bytes 393224 | tf_op jit(solution)/shard_map/ppermute | solution.py:26
  16.5 2.1 %collective-permute-start = (bf16[4,256,256]{2,1,0:T(8,128)(2,1)}, bf16[4,256,256]{2,1,0:T(8,128)(2,1)S(1)}, u32[]{:S(2)}, u32[]{:S(2)}) collective-permute-start(bf16[4,256,256]{2,1,0:T(8,128)(2,1)} %all-to-all-done), channel_id=1, source_target_pairs={{0,1},{1,0},{2,3},{3,2},{4,5},{5,4},{6,7},{7,6},{8,9},{9,8},{10,11... | collective-permute-start | bytes 1572872 | tf_op jit(solution)/shard_map/ppermute | solution.py:26
  23.2 8.0 %collective-permute-start.2 = (f32[2,256,2]{1,0,2:T(2,128)S(1)}, f32[2,256,2]{1,0,2:T(2,128)S(1)}, u32[]{:S(2)}, u32[]{:S(2)}) collective-permute-start(f32[2,256,2]{1,0,2:T(2,128)S(1)} %pad_maximum_fusion.5), channel_id=1, source_target_pairs={{0,2},{2,0},{1,3},{3,1},{4,6},{6,4},{5,7},{7,5},{8,10},{10,8},{9,1... | collective-permute-start | bytes 12296 | tf_op jit(solution)/shard_map/ppermute | solution.py:26
  30.6 12.1 %collective-permute-start.3 = (bf16[2,256,128]{1,2,0:T(8,128)(2,1)S(1)}, bf16[2,256,128]{1,2,0:T(8,128)(2,1)S(1)}, u32[]{:S(2)}, u32[]{:S(2)}) collective-permute-start(bf16[2,256,128]{1,2,0:T(8,128)(2,1)S(1)} %fusion.32), channel_id=1, source_target_pairs={{0,2},{2,0},{1,3},{3,1},{4,6},{6,4},{5,7},{7,5},{8,10},{10,8},{9,1... | collective-permute-start | bytes 393224 | tf_op jit(solution)/shard_map/ppermute | solution.py:26
  42.7 1.6 copy-start.3
  45.0 1.3 copy-start.1
  47.4 10.2 %copy-start.5 = (bf16[1,16,4096]{2,1,0:T(8,128)(2,1)S(1)}, bf16[1,16,4096]{2,1,0:T(8,128)(2,1)}, u32[]{:S(2)}) copy-start(bf16[1,16,4096]{2,1,0:T(8,128)(2,1)} %param.10) | copy-start | bytes 393220
  47.4 10.6 %copy-start.18 = (s32[1,256,2]{1,2,0:T(2,128)S(1)}, s32[1,256,2]{1,2,0:T(2,128)}, u32[]{:S(2)}) copy-start(s32[1,256,2]{1,2,0:T(2,128)} %param.18) | copy-start | bytes 6148
  47.4 3.0 %collective-permute-start.4 = (bf16[4,2,16,4096]{3,2,1,0:T(8,128)(2,1)}, bf16[4,2,16,4096]{3,2,1,0:T(8,128)(2,1)}, u32[]{:S(2)}, u32[]{:S(2)}) collective-permute-start(bf16[4,2,16,4096]{3,2,1,0:T(8,128)(2,1)} %dynamic-slice_bitcast_fusion), channel_id=1, source_target_pairs={{0,1},{1,0},{2,3},{3,2},{4,5},{5,4},{6,7},{7,6},{8,9},{9,8},{10,11... | collective-permute-start | bytes 3145736 | tf_op jit(solution)/shard_map/ppermute | solution.py:26
  53.2 41.1 %copy-start.7 = (f32[1,4096]{1,0:T(1,128)S(1)}, f32[1,4096]{1,0:T(1,128)}, u32[]{:S(2)}) copy-start(f32[1,4096]{1,0:T(1,128)} %param.14) | copy-start | bytes 49156
  53.2 20.1 %all-to-all-start.1 = ((bf16[4,2,16,4096]{3,2,1,0:T(8,128)(2,1)}), bf16[4,2,16,4096]{3,2,1,0:T(8,128)(2,1)}, u32[]{:S(2)}, u32[]{:S(2)}) async-start(bf16[4,2,16,4096]{3,2,1,0:T(8,128)(2,1)} %fusion.20), calls=%async_computation.1 | async-start | bytes 2097152 | tf_op jit(solution)/shard_map/all_to_all | solution.py:98
  57.6 35.4 %collective-permute-start.6 = (bf16[16,4096]{1,0:T(8,128)(2,1)S(1)}, bf16[16,4096]{1,0:T(8,128)(2,1)}, u32[]{:S(2)}, u32[]{:S(2)}) collective-permute-start(bf16[16,4096]{1,0:T(8,128)(2,1)S(1)} %bitcast.208), channel_id=1, source_target_pairs={{0,2},{2,0},{1,3},{3,1},{4,6},{6,4},{5,7},{7,5},{8,10},{10,8},{9,1... | collective-permute-start | bytes 393224 | tf_op jit(solution)/shard_map/ppermute | solution.py:26
  58.1 0.5 copy-start.10
  58.1 0.6 copy-start.12
  58.6 0.5 copy-start.15
  75.4 16.5 %collective-permute-start.5 = (bf16[2,16,4096]{2,1,0:T(8,128)(2,1)}, bf16[2,16,4096]{2,1,0:T(8,128)(2,1)}, u32[]{:S(2)}, u32[]{:S(2)}) collective-permute-start(bf16[2,16,4096]{2,1,0:T(8,128)(2,1)} %pad_maximum_fusion.4), channel_id=1, source_target_pairs={{0,2},{2,0},{1,3},{3,1},{4,6},{6,4},{5,7},{7,5},{8,10},{10,8},{9,1... | collective-permute-start | bytes 786440 | tf_op jit(solution)/shard_map/ppermute | solution.py:26
  92.9 2.4 %copy-start.2 = (f32[2,16,4096]{2,1,0:T(8,128)}, f32[2,16,4096]{2,1,0:T(8,128)S(1)}, u32[]{:S(2)}) copy-start(f32[2,16,4096]{2,1,0:T(8,128)S(1)} %convert_element_type.144) | copy-start | bytes 1572868
  96.8 22.5 %copy-start.19 = (bf16[1,4096,384]{2,1,0:T(8,128)(2,1)S(1)}, bf16[1,4096,384]{2,1,0:T(8,128)(2,1)}, u32[]{:S(2)}) copy-start(bf16[1,4096,384]{2,1,0:T(8,128)(2,1)} %param.16) | copy-start | bytes 9437188
  115.0 2.7 %collective-permute-start.7 = (bf16[4,2,16,4096]{3,2,1,0:T(8,128)(2,1)S(1)}, bf16[4,2,16,4096]{3,2,1,0:T(8,128)(2,1)S(1)}, u32[]{:S(2)}, u32[]{:S(2)}) collective-permute-start(bf16[4,2,16,4096]{3,2,1,0:T(8,128)(2,1)S(1)} %all_to_all.25), channel_id=1, source_target_pairs={{0,1},{1,0},{2,3},{3,2},{4,5},{5,4},{6,7},{7,6},{8,9},{9,8},{10,11... | collective-permute-start | bytes 3145736 | tf_op jit(solution)/shard_map/ppermute | solution.py:26
  117.9 1.3 copy-start.4
  127.6 2.0 %copy-start.17 = (f32[1,256,2]{1,2,0:T(2,128)S(1)}, f32[1,256,2]{1,2,0:T(2,128)}, u32[]{:S(2)}) copy-start(f32[1,256,2]{1,2,0:T(2,128)} %param.19) | copy-start | bytes 6148
  127.6 2.1 %copy-start.11 = (s32[16,2]{0,1:T(2,128)S(1)}, s32[16,2]{0,1:T(2,128)}, u32[]{:S(2)}) copy-start(s32[16,2]{0,1:T(2,128)} %copy-done.10) | copy-start | bytes 388
  127.7 2.1 %copy-start.13 = (s32[16,2]{0,1:T(2,128)S(1)}, s32[16,2]{0,1:T(2,128)}, u32[]{:S(2)}) copy-start(s32[16,2]{0,1:T(2,128)} %copy-done.12) | copy-start | bytes 388
  129.4 2.7 %collective-permute-start.8 = (bf16[4,2,16,4096]{3,2,0,1:T(8,128)(2,1)S(1)}, bf16[4,2,16,4096]{3,2,0,1:T(8,128)(2,1)S(1)}, u32[]{:S(2)}, u32[]{:S(2)}) collective-permute-start(bf16[4,2,16,4096]{3,2,0,1:T(8,128)(2,1)S(1)} %copy.93), channel_id=1, source_target_pairs={{0,1},{1,0},{2,3},{3,2},{4,5},{5,4},{6,7},{7,6},{8,9},{9,8},{10,11... | collective-permute-start | bytes 3145736 | tf_op jit(solution)/shard_map/ppermute | solution.py:26
  132.2 6.0 %copy-start.8 = (s32[4,16]{1,0:T(4,128)S(1)}, s32[4,16]{1,0:T(4,128)}, u32[]{:S(2)}) copy-start(s32[4,16]{1,0:T(4,128)} %copy.87) | copy-start | bytes 772
  132.2 6.1 %copy-start.9 = (s32[4,16]{1,0:T(4,128)S(1)}, s32[4,16]{1,0:T(4,128)}, u32[]{:S(2)}) copy-start(s32[4,16]{1,0:T(4,128)} %copy.91) | copy-start | bytes 772
  132.2 6.1 %copy-start.16 = (pred[16,4]{0,1:T(4,128)(4,1)S(1)}, pred[16,4]{0,1:T(4,128)(4,1)}, u32[]{:S(2)}) copy-start(pred[16,4]{0,1:T(4,128)(4,1)} %copy-done.15) | copy-start | bytes 196
  132.2 6.2 %copy-start.14 = (pred[16,4]{0,1:T(4,128)(4,1)S(1)}, pred[16,4]{0,1:T(4,128)(4,1)}, u32[]{:S(2)}) copy-start(pred[16,4]{0,1:T(4,128)(4,1)} %get-tuple-element.35) | copy-start | bytes 196
  133.5 14.3 %all-to-all-start.3 = ((bf16[4,16,4096]{2,1,0:T(8,128)(2,1)}), bf16[4,16,4096]{2,1,0:T(8,128)(2,1)}, u32[]{:S(2)}, u32[]{:S(2)}) async-start(bf16[4,16,4096]{2,1,0:T(8,128)(2,1)} %get-tuple-element.13), calls=%async_computation.3 | async-start | bytes 1048576 | tf_op jit(solution)/shard_map/all_to_all | solution.py:165
  147.7 13.4 %all-to-all-start.4 = ((bf16[4,16,4096]{2,1,0:T(8,128)(2,1)}), bf16[4,16,4096]{2,1,0:T(8,128)(2,1)}, u32[]{:S(2)}, u32[]{:S(2)}) async-start(bf16[4,16,4096]{2,1,0:T(8,128)(2,1)} %get-tuple-element.14), calls=%async_computation.4 | async-start | bytes 1048576 | tf_op jit(solution)/shard_map/all_to_all | solution.py:158
  155.1 8.8 %collective-permute-start.9 = (bf16[16,4096]{1,0:T(8,128)(2,1)S(1)}, bf16[16,4096]{1,0:T(8,128)(2,1)S(1)}, u32[]{:S(2)}, u32[]{:S(2)}) collective-permute-start(bf16[16,4096]{1,0:T(8,128)(2,1)S(1)} %fusion.3), channel_id=1, source_target_pairs={{240,0},{0,16},{16,32},{32,48},{48,64},{64,80},{80,96},{96,112},{1... | collective-permute-start | bytes 393224 | tf_op jit(solution)/shard_map/ppermute | solution.py:22
  162.9 10.5 %collective-permute-start.10 = (bf16[16,4096]{1,0:T(8,128)(2,1)S(1)}, bf16[16,4096]{1,0:T(8,128)(2,1)S(1)}, u32[]{:S(2)}, u32[]{:S(2)}) collective-permute-start(bf16[16,4096]{1,0:T(8,128)(2,1)S(1)} %fusion.4), channel_id=1, source_target_pairs={{0,18},{2,16},{16,34},{18,32},{32,50},{34,48},{48,66},{50,64},{64,... | collective-permute-start | bytes 393224 | tf_op jit(solution)/shard_map/ppermute | solution.py:164

commit v10 on v8

--- a/solution.py
+++ b/solution.py
@@ -76,7 +76,8 @@
         )
         return summed, top, total
 
-    other_sum, other_top, other_total = partial(swap(mine, "zh"))
+    other = swap(query_all, "zh").reshape(MB, heads_here, HD).transpose(1, 0, 2)
+    other_sum, other_top, other_total = partial(other)
     far_sum, far_stats = swap(
         (other_sum.astype(jnp.bfloat16), jnp.concatenate([other_top, other_total], axis=2)), "zh"
     )

time: 171 us -> 173 us (1.012)
    unnamed x42 -> x44, local copies, waits for them, and re-layouts: 3.92 us -> 3.99 us
  transfers between devices with their start and end apart: 14 -> 14, of which waited for: 12 -> 12; matrix products, arithmetic and copies ran while one was open for 13% -> 12% of each run, Pallas kernels for 0% -> 0%
where the time goes in v10:
time: 173 us; the launch traced here: 172 us
  waiting for transfers between devices  68.8 us (40%)
  starting transfers between devices  27.8 us (16%)
  matrix products  20.6 us (12%)
  other arithmetic  20.2 us (12%)
  blocking collectives  18.2 us (11%)
  local copies, waits for them, and re-layouts  15.8 us (9%)
    ppermute x9, waiting for transfers between devices, swap(): return lax.ppermute(block, axis, [(0, 1), (1, 0)])  27.8 us
    all_to_all x1, blocking collectives, body(): rows_y = lax.all_to_all(dispatch, 'y', 0, 0, tiled=True)  18.2 us
    ppermute x9, starting transfers between devices, swap(): return lax.ppermute(block, axis, [(0, 1), (1, 0)])  13.6 us
    all_to_all x1, waiting for transfers between devices, body(): part_y = lax.all_to_all(part_c.astype(jnp.bfloat16), 'y', 0, 0, tiled=True)  13.4 us
    all_to_all x1, waiting for transfers between devices, body(): lax.all_to_all(chip_sum.astype(jnp.bfloat16), 'y', 0, 0, tiled=True)  13.3 us
    ppermute x1, waiting for transfers between devices, body(): lax.ppermute(mixed_far.astype(jnp.bfloat16), ('section', 'zh'), route)  9.2 us
    dot_general x1, matrix products, body(): jnp.dot(activated, down_w, preferred_element_type=jnp.float32)  6.36 us
    all_to_all x1, starting transfers between devices, body(): kv_y = lax.all_to_all(send_kv, 'y', 0, 0, tiled=True)  4.46 us
  transfers between devices with their start and end apart: 14, of which 12 were waited for; matrix products, arithmetic and copies ran while one was open for 12% of the time, Pallas kernels for 0%

profile of v10, /device:TPU:32, one launch (start us, length us, event | category | flops | bytes accessed | tf_op | source)
XLA Modules:
  0.0 171.8 jit_solution(9859452173493656272)
XLA Ops:
  0.0 1.2 reshape_squeeze.6
  1.2 0.4 fusion.96
  1.6 0.8 pad_maximum_fusion.3
  2.4 4.5 %all-to-all-start = ((bf16[4,256,256]{2,1,0:T(8,128)(2,1)}), bf16[4,256,256]{2,1,0:T(8,128)(2,1)}, u32[]{:S(2)}, u32[]{:S(2)}) async-start(bf16[4,256,256]{2,1,0:T(8,128)(2,1)} %pad_maximum_fusion.3), calls=%async_computation | async-start | bytes 1048576 | tf_op jit(solution)/shard_map/all_to_all | solution.py:56
  7.0 6.4 %collective-permute-start.1 = (bf16[256,256]{0,1:T(8,128)(2,1)S(1)}, bf16[256,256]{0,1:T(8,128)(2,1)S(1)}, u32[]{:S(2)}, u32[]{:S(2)}) collective-permute-start(bf16[256,256]{0,1:T(8,128)(2,1)S(1)} %bitcast.227), channel_id=1, source_target_pairs={{0,2},{2,0},{1,3},{3,1},{4,6},{6,4},{5,7},{7,5},{8,10},{10,8},{9,1... | collective-permute-start | bytes 393224 | tf_op jit(solution)/shard_map/ppermute | solution.py:26
  13.6 2.9 %all-to-all-done = bf16[4,256,256]{2,1,0:T(8,128)(2,1)} async-done(((bf16[4,256,256]{2,1,0:T(8,128)(2,1)}), bf16[4,256,256]{2,1,0:T(8,128)(2,1)}, u32[]{:S(2)}, u32[]{:S(2)}) %all-to-all-start) | async-done | bytes 524320 | tf_op jit(solution)/shard_map/all_to_all | solution.py:56
  16.5 1.1 broadcast_compare_fusion
  17.6 0.7 reshape_squeeze.7
  18.3 1.1 collective-permute-done.1
  19.6 1.3 pad_maximum_fusion.1
  20.9 1.9 %fusion.8 = (f32[2,256]{1,0:T(2,128)S(1)}, f32[2048,2,256]{2,0,1:T(8,128)S(1)}) fusion(pred[256,2048]{0,1:T(8,128)(4,1)} %broadcast_compare_fusion, bf16[256,2,128]{2,1,0:T(2,128)(2,1)} %reshape_squeeze.7, bf16[2048,256]{1,0:T(8,128)(2,1)S(1)} %bitcast.217), kind=kOutput, calls=%fused_computation.18 | convolution fusion | flops 271580672 | bytes 5376000 | tf_op jit(solution)/shard_map/hqd,kd->hqk/dot_general | solution.py:70
  22.8 1.7 %fusion.11 = (f32[2,256]{1,0:T(2,128)S(1)}, f32[2,256]{1,0:T(2,128)S(1)}, f32[2048,2,256]{2,0,1:T(8,128)S(1)}) fusion(f32[2048,2,256]{2,0,1:T(8,128)S(1)} %get-tuple-element.27, f32[2,256]{1,0:T(2,128)S(1)} %get-tuple-element.26, pred[256,2048]{0,1:T(8,128)(4,1)S(1)} %copy-done.5, bf16[256,2,128]{2,0,1:T(8,128)(2,1)S(1)} %copy.86, ...), kind=kOutput, calls=%fused_computation.21 | convolution fusion | flops 275774464 | bytes 9574400 | tf_op jit(solution)/shard_map/hqd,kd->hqk/dot_general | solution.py:70
  24.6 1.0 fusion.14
  25.5 5.7 %collective-permute-start.2 = (f32[2,256,2]{1,0,2:T(2,128)S(1)}, f32[2,256,2]{1,0,2:T(2,128)S(1)}, u32[]{:S(2)}, u32[]{:S(2)}) collective-permute-start(f32[2,256,2]{1,0,2:T(2,128)S(1)} %pad_maximum_fusion.5), channel_id=1, source_target_pairs={{0,2},{2,0},{1,3},{3,1},{4,6},{6,4},{5,7},{7,5},{8,10},{10,8},{9,1... | collective-permute-start | bytes 12296 | tf_op jit(solution)/shard_map/ppermute | solution.py:26
  31.2 1.0 fusion.32
  32.2 0.4 collective-permute-start.3
  32.6 0.5 collective-permute-done.2
  33.1 11.0 %collective-permute-done.3 = bf16[2,256,128]{1,2,0:T(8,128)(2,1)S(1)} collective-permute-done((bf16[2,256,128]{1,2,0:T(8,128)(2,1)S(1)}, bf16[2,256,128]{1,2,0:T(8,128)(2,1)S(1)}, u32[]{:S(2)}, u32[]{:S(2)}) %collective-permute-start.3) | collective-permute-done | bytes 131104 | tf_op jit(solution)/shard_map/ppermute | solution.py:26
  44.2 1.0 fusion.43
  45.2 0.6 copy-done.3
  45.8 0.7 convolution_convert_fusion.1
  46.5 1.3 copy-done.1
  47.9 1.1 dynamic-slice_bitcast_fusion
  49.0 3.0 %collective-permute-done.4 = bf16[4,2,16,4096]{3,2,1,0:T(8,128)(2,1)} collective-permute-done((bf16[4,2,16,4096]{3,2,1,0:T(8,128)(2,1)}, bf16[4,2,16,4096]{3,2,1,0:T(8,128)(2,1)}, u32[]{:S(2)}, u32[]{:S(2)}) %collective-permute-start.4) | collective-permute-done | bytes 1048608 | tf_op jit(solution)/shard_map/ppermute | solution.py:26
  52.0 2.8 %fusion.21 = bf16[4,2,16,4096]{3,2,1,0:T(8,128)(2,1)} fusion(bf16[4,2,16,4096]{3,2,1,0:T(8,128)(2,1)} %collective-permute-done.4, bf16[4,2,2,16,4096]{4,3,2,1,0:T(8,128)(2,1)} %bitcast.211, s32[]{:T(128)S(6)} %select_n.55), kind=kLoop, calls=%fused_computation.34 | loop fusion | flops 2097152 | bytes 3145732 | tf_op jit(solution)/shard_map/convert_element_type | solution.py:99
  54.8 4.4 %all-to-all-start.1 = ((bf16[4,2,16,4096]{3,2,1,0:T(8,128)(2,1)}), bf16[4,2,16,4096]{3,2,1,0:T(8,128)(2,1)}, u32[]{:S(2)}, u32[]{:S(2)}) async-start(bf16[4,2,16,4096]{3,2,1,0:T(8,128)(2,1)} %fusion.21), calls=%async_computation.1 | async-start | bytes 2097152 | tf_op jit(solution)/shard_map/all_to_all | solution.py:99
  59.2 0.5 collective-permute-start.6
  59.7 0.5 fusion.76
  60.3 0.5 copy-done.16
  60.9 0.6 reduce_window_sum.17
  61.5 13.4 %all-to-all-done.1 = bf16[4,2,16,4096]{3,2,1,0:T(8,128)(2,1)} async-done(((bf16[4,2,16,4096]{3,2,1,0:T(8,128)(2,1)}), bf16[4,2,16,4096]{3,2,1,0:T(8,128)(2,1)}, u32[]{:S(2)}, u32[]{:S(2)}) %all-to-all-start.1) | async-done | bytes 1048608 | tf_op jit(solution)/shard_map/all_to_all | solution.py:99
  74.9 1.4 convert_reduce_fusion
  76.3 0.7 pad_maximum_fusion.4
  77.0 0.4 collective-permute-start.5
  77.4 1.3 add_bitcast_fusion.1
  78.7 1.3 copy.91
  80.0 1.2 convert_element_type.143
  81.2 1.3 copy.94
  82.6 1.3 reduce_window_sum.18
  83.9 1.3 add_bitcast_fusion
  85.2 1.3 copy.95
  86.5 7.0 %collective-permute-done.5 = bf16[2,16,4096]{2,1,0:T(8,128)(2,1)} collective-permute-done((bf16[2,16,4096]{2,1,0:T(8,128)(2,1)}, bf16[2,16,4096]{2,1,0:T(8,128)(2,1)}, u32[]{:S(2)}, u32[]{:S(2)}) %collective-permute-start.5) | collective-permute-done | bytes 262176 | tf_op jit(solution)/shard_map/ppermute | solution.py:26
  93.5 1.0 convert_element_type.138
  94.6 1.3 multiply_reduce_fusion.1
  95.9 1.0 fusion
  96.9 1.3 fusion.1
  98.4 18.2 %all_to_all.20 = bf16[4,2,16,4096]{3,2,1,0:T(8,128)(2,1)S(1)} all-to-all(bf16[4,2,16,4096]{3,2,1,0:T(8,128)(2,1)S(1)} %copy.96), channel_id=1, replica_groups=mesh['section'=16,'y'=4,'zh'=2,'core'=2] {'y'}, dimensions={0} | all-to-all | bytes 2097152 | tf_op jit(solution)/shard_map/all_to_all | solution.py:143
  116.6 2.7 %collective-permute-done.7 = bf16[4,2,16,4096]{3,2,1,0:T(8,128)(2,1)S(1)} collective-permute-done((bf16[4,2,16,4096]{3,2,1,0:T(8,128)(2,1)S(1)}, bf16[4,2,16,4096]{3,2,1,0:T(8,128)(2,1)S(1)}, u32[]{:S(2)}, u32[]{:S(2)}) %collective-permute-start.7) | collective-permute-done | bytes 1048608 | tf_op jit(solution)/shard_map/ppermute | solution.py:26
  119.5 1.3 copy-done.4
  120.8 2.1 %fusion.16 = f32[256,384]{1,0:T(8,128)} fusion(bf16[256,4096]{1,0:T(8,128)(2,1)S(1)} %bitcast.214, bf16[1,4096,384]{2,1,0:T(8,128)(2,1)S(1)} %copy-done.20), kind=kOutput, calls=%fused_computation.26 | convolution fusion | flops 805306368 | bytes 5636096 | tf_op jit(solution)/shard_map/dot_general | solution.py:147
  122.9 6.4 %convolution_convert_fusion = bf16[256,4096]{1,0:T(8,128)(2,1)} fusion(bf16[1,384,4096]{2,1,0:T(8,128)(2,1)S(1)} %copy-done, f32[256,384]{1,0:T(8,128)} %fusion.16, bf16[256,4096]{1,0:T(8,128)(2,1)} %bitcast.215, bf16[1,4096,384]{2,1,0:T(8,128)(2,1)} %param.15), kind=kOutput, calls=%fused_computation | convolution fusion | flops 1612251136 | bytes 10878976 | tf_op jit(solution)/shard_map/dot_general | solution.py:150
  129.3 1.7 fusion.95
  131.3 2.4 %collective-permute-done.8 = bf16[4,2,16,4096]{3,2,1,0:T(8,128)(2,1)S(1)} collective-permute-done((bf16[4,2,16,4096]{3,2,1,0:T(8,128)(2,1)S(1)}, bf16[4,2,16,4096]{3,2,1,0:T(8,128)(2,1)S(1)}, u32[]{:S(2)}, u32[]{:S(2)}) %collective-permute-start.8) | collective-permute-done | bytes 1048608 | tf_op jit(solution)/shard_map/ppermute | solution.py:26
  133.8 1.3 fusion.20
  135.1 4.2 %all-to-all-start.3 = ((bf16[4,2,16,4096]{3,2,1,0:T(8,128)(2,1)}), bf16[4,2,16,4096]{3,2,1,0:T(8,128)(2,1)}, u32[]{:S(2)}, u32[]{:S(2)}) async-start(bf16[4,2,16,4096]{3,2,1,0:T(8,128)(2,1)} %fusion.20), calls=%async_computation.3 | async-start | bytes 2097152 | tf_op jit(solution)/shard_map/all_to_all | solution.py:156
  140.4 0.7 reshape.245
  141.1 0.7 reshape.248
  141.8 13.3 %all-to-all-done.3 = bf16[4,2,16,4096]{3,2,1,0:T(8,128)(2,1)} async-done(((bf16[4,2,16,4096]{3,2,1,0:T(8,128)(2,1)}), bf16[4,2,16,4096]{3,2,1,0:T(8,128)(2,1)}, u32[]{:S(2)}, u32[]{:S(2)}) %all-to-all-start.3) | async-done | bytes 1048608 | tf_op jit(solution)/shard_map/all_to_all | solution.py:156
  155.1 1.8 %fusion.3 = bf16[16,4096]{1,0:T(8,128)(2,1)S(1)} fusion(bf16[4,2,16,4096]{3,2,1,0:T(8,128)(2,1)} %all-to-all-done.3, f32[2,16,4096]{2,1,0:T(8,128)} %copy-done.2, bf16[1,16,4096]{2,1,0:T(8,128)(2,1)S(1)} %get-tuple-element.14, f32[16,4,16]{2,1,0:T(4,128)} %reshape.245, bf16[1,16,4096]{2,1,0:T(8,128)(2,1)S(1)} %copy-done.6), kind=kOutput, calls=%fused_computation.9 | convolution fusion | flops 50724864 | bytes 1212416 | tf_op jit(solution)/shard_map/txj,xjd->td/dot_general | solution.py:160
  156.9 1.1 collective-permute-start.9
  157.9 1.7 %fusion.4 = bf16[16,4096]{1,0:T(8,128)(2,1)S(1)} fusion(bf16[4,2,16,4096]{3,2,1,0:T(8,128)(2,1)} %all-to-all-done.3, f32[16,4,16]{2,1,0:T(4,128)} %reshape.248), kind=kOutput, calls=%fused_computation.10 | convolution fusion | flops 50397184 | bytes 688128 | tf_op jit(solution)/shard_map/txj,xjd->td/dot_general | solution.py:161
  159.8 2.1 %collective-permute-done.9 = bf16[16,4096]{1,0:T(8,128)(2,1)S(1)} collective-permute-done((bf16[16,4096]{1,0:T(8,128)(2,1)S(1)}, bf16[16,4096]{1,0:T(8,128)(2,1)S(1)}, u32[]{:S(2)}, u32[]{:S(2)}) %collective-permute-start.9) | collective-permute-done | bytes 131104 | tf_op jit(solution)/shard_map/ppermute | solution.py:22
  161.9 9.2 %collective-permute-done.10 = bf16[16,4096]{1,0:T(8,128)(2,1)S(1)} collective-permute-done((bf16[16,4096]{1,0:T(8,128)(2,1)S(1)}, bf16[16,4096]{1,0:T(8,128)(2,1)S(1)}, u32[]{:S(2)}, u32[]{:S(2)}) %collective-permute-start.10) | collective-permute-done | bytes 131104 | tf_op jit(solution)/shard_map/ppermute | solution.py:167
  171.1 0.7 fusion.57
  (86 shorter events, 2.5 us)
Async XLA Ops:
  0.0 122.9 %copy-start = (bf16[1,384,4096]{2,1,0:T(8,128)(2,1)S(1)}, bf16[1,384,4096]{2,1,0:T(8,128)(2,1)}, u32[]{:S(2)}) copy-start(bf16[1,384,4096]{2,1,0:T(8,128)(2,1)} %param.17) | copy-start | bytes 9437188
  0.0 6.9 %copy-start.7 = (bf16[1,256,256]{2,1,0:T(8,128)(2,1)S(1)}, bf16[1,256,256]{2,1,0:T(8,128)(2,1)}, u32[]{:S(2)}) copy-start(bf16[1,256,256]{2,1,0:T(8,128)(2,1)} %param.11) | copy-start | bytes 393220
  2.4 14.0 %all-to-all-start = ((bf16[4,256,256]{2,1,0:T(8,128)(2,1)}), bf16[4,256,256]{2,1,0:T(8,128)(2,1)}, u32[]{:S(2)}, u32[]{:S(2)}) async-start(bf16[4,256,256]{2,1,0:T(8,128)(2,1)} %pad_maximum_fusion.3), calls=%async_computation | async-start | bytes 1048576 | tf_op jit(solution)/shard_map/all_to_all | solution.py:56
  7.0 12.4 %collective-permute-start.1 = (bf16[256,256]{0,1:T(8,128)(2,1)S(1)}, bf16[256,256]{0,1:T(8,128)(2,1)S(1)}, u32[]{:S(2)}, u32[]{:S(2)}) collective-permute-start(bf16[256,256]{0,1:T(8,128)(2,1)S(1)} %bitcast.227), channel_id=1, source_target_pairs={{0,2},{2,0},{1,3},{3,1},{4,6},{6,4},{5,7},{7,5},{8,10},{10,8},{9,1... | collective-permute-start | bytes 393224 | tf_op jit(solution)/shard_map/ppermute | solution.py:26
  16.5 3.1 %collective-permute-start = (bf16[4,256,256]{2,1,0:T(8,128)(2,1)}, bf16[4,256,256]{2,1,0:T(8,128)(2,1)}, u32[]{:S(2)}, u32[]{:S(2)}) collective-permute-start(bf16[4,256,256]{2,1,0:T(8,128)(2,1)} %all-to-all-done), channel_id=1, source_target_pairs={{0,1},{1,0},{2,3},{3,2},{4,5},{5,4},{6,7},{7,6},{8,9},{9,8},{10,11... | collective-permute-start | bytes 1572872 | tf_op jit(solution)/shard_map/ppermute | solution.py:26
  20.9 1.9 %copy-start.5 = (pred[256,2048]{0,1:T(8,128)(4,1)S(1)}, pred[256,2048]{0,1:T(8,128)(4,1)}, u32[]{:S(2)}) copy-start(pred[256,2048]{0,1:T(8,128)(4,1)} %broadcast_compare_fusion) | copy-start | bytes 1572868
  25.5 7.6 %collective-permute-start.2 = (f32[2,256,2]{1,0,2:T(2,128)S(1)}, f32[2,256,2]{1,0,2:T(2,128)S(1)}, u32[]{:S(2)}, u32[]{:S(2)}) collective-permute-start(f32[2,256,2]{1,0,2:T(2,128)S(1)} %pad_maximum_fusion.5), channel_id=1, source_target_pairs={{0,2},{2,0},{1,3},{3,1},{4,6},{6,4},{5,7},{7,5},{8,10},{10,8},{9,1... | collective-permute-start | bytes 12296 | tf_op jit(solution)/shard_map/ppermute | solution.py:26
  32.2 12.0 %collective-permute-start.3 = (bf16[2,256,128]{1,2,0:T(8,128)(2,1)S(1)}, bf16[2,256,128]{1,2,0:T(8,128)(2,1)S(1)}, u32[]{:S(2)}, u32[]{:S(2)}) collective-permute-start(bf16[2,256,128]{1,2,0:T(8,128)(2,1)S(1)} %fusion.32), channel_id=1, source_target_pairs={{0,2},{2,0},{1,3},{3,1},{4,6},{6,4},{5,7},{7,5},{8,10},{10,8},{9,1... | collective-permute-start | bytes 393224 | tf_op jit(solution)/shard_map/ppermute | solution.py:26
  44.2 1.6 copy-start.3
  46.5 1.4 copy-start.1
  49.0 10.2 %copy-start.6 = (bf16[1,16,4096]{2,1,0:T(8,128)(2,1)S(1)}, bf16[1,16,4096]{2,1,0:T(8,128)(2,1)}, u32[]{:S(2)}) copy-start(bf16[1,16,4096]{2,1,0:T(8,128)(2,1)} %param.10) | copy-start | bytes 393220
  49.0 10.7 %copy-start.19 = (s32[1,256,2]{1,2,0:T(2,128)S(1)}, s32[1,256,2]{1,2,0:T(2,128)}, u32[]{:S(2)}) copy-start(s32[1,256,2]{1,2,0:T(2,128)} %param.18) | copy-start | bytes 6148
  49.0 3.0 %collective-permute-start.4 = (bf16[4,2,16,4096]{3,2,1,0:T(8,128)(2,1)}, bf16[4,2,16,4096]{3,2,1,0:T(8,128)(2,1)}, u32[]{:S(2)}, u32[]{:S(2)}) collective-permute-start(bf16[4,2,16,4096]{3,2,1,0:T(8,128)(2,1)} %dynamic-slice_bitcast_fusion), channel_id=1, source_target_pairs={{0,1},{1,0},{2,3},{3,2},{4,5},{5,4},{6,7},{7,6},{8,9},{9,8},{10,11... | collective-permute-start | bytes 3145736 | tf_op jit(solution)/shard_map/ppermute | solution.py:26
  54.8 41.1 %copy-start.8 = (f32[1,4096]{1,0:T(1,128)S(1)}, f32[1,4096]{1,0:T(1,128)}, u32[]{:S(2)}) copy-start(f32[1,4096]{1,0:T(1,128)} %param.14) | copy-start | bytes 49156
  54.8 20.1 %all-to-all-start.1 = ((bf16[4,2,16,4096]{3,2,1,0:T(8,128)(2,1)}), bf16[4,2,16,4096]{3,2,1,0:T(8,128)(2,1)}, u32[]{:S(2)}, u32[]{:S(2)}) async-start(bf16[4,2,16,4096]{3,2,1,0:T(8,128)(2,1)} %fusion.21), calls=%async_computation.1 | async-start | bytes 2097152 | tf_op jit(solution)/shard_map/all_to_all | solution.py:99
  59.2 35.4 %collective-permute-start.6 = (bf16[16,4096]{1,0:T(8,128)(2,1)S(1)}, bf16[16,4096]{1,0:T(8,128)(2,1)}, u32[]{:S(2)}, u32[]{:S(2)}) collective-permute-start(bf16[16,4096]{1,0:T(8,128)(2,1)S(1)} %bitcast.216), channel_id=1, source_target_pairs={{0,2},{2,0},{1,3},{3,1},{4,6},{6,4},{5,7},{7,5},{8,10},{10,8},{9,1... | collective-permute-start | bytes 393224 | tf_op jit(solution)/shard_map/ppermute | solution.py:26
  59.7 0.6 copy-start.11
  59.7 0.6 copy-start.13
  60.2 0.5 copy-start.16
  77.0 16.5 %collective-permute-start.5 = (bf16[2,16,4096]{2,1,0:T(8,128)(2,1)}, bf16[2,16,4096]{2,1,0:T(8,128)(2,1)}, u32[]{:S(2)}, u32[]{:S(2)}) collective-permute-start(bf16[2,16,4096]{2,1,0:T(8,128)(2,1)} %pad_maximum_fusion.4), channel_id=1, source_target_pairs={{0,2},{2,0},{1,3},{3,1},{4,6},{6,4},{5,7},{7,5},{8,10},{10,8},{9,1... | collective-permute-start | bytes 786440 | tf_op jit(solution)/shard_map/ppermute | solution.py:26
  94.5 2.4 %copy-start.2 = (f32[2,16,4096]{2,1,0:T(8,128)}, f32[2,16,4096]{2,1,0:T(8,128)S(1)}, u32[]{:S(2)}) copy-start(f32[2,16,4096]{2,1,0:T(8,128)S(1)} %convert_element_type.138) | copy-start | bytes 1572868
  98.4 22.5 %copy-start.20 = (bf16[1,4096,384]{2,1,0:T(8,128)(2,1)S(1)}, bf16[1,4096,384]{2,1,0:T(8,128)(2,1)}, u32[]{:S(2)}) copy-start(bf16[1,4096,384]{2,1,0:T(8,128)(2,1)} %param.16) | copy-start | bytes 9437188
  116.6 2.7 %collective-permute-start.7 = (bf16[4,2,16,4096]{3,2,1,0:T(8,128)(2,1)S(1)}, bf16[4,2,16,4096]{3,2,1,0:T(8,128)(2,1)S(1)}, u32[]{:S(2)}, u32[]{:S(2)}) collective-permute-start(bf16[4,2,16,4096]{3,2,1,0:T(8,128)(2,1)S(1)} %all_to_all.20), channel_id=1, source_target_pairs={{0,1},{1,0},{2,3},{3,2},{4,5},{5,4},{6,7},{7,6},{8,9},{9,8},{10,11... | collective-permute-start | bytes 3145736 | tf_op jit(solution)/shard_map/ppermute | solution.py:26
  119.5 1.4 copy-start.4
  129.3 2.0 %copy-start.18 = (f32[1,256,2]{1,2,0:T(2,128)S(1)}, f32[1,256,2]{1,2,0:T(2,128)}, u32[]{:S(2)}) copy-start(f32[1,256,2]{1,2,0:T(2,128)} %param.19) | copy-start | bytes 6148
  131.0 8.4 %copy-start.12 = (s32[16,2]{0,1:T(2,128)S(1)}, s32[16,2]{0,1:T(2,128)}, u32[]{:S(2)}) copy-start(s32[16,2]{0,1:T(2,128)} %copy-done.11) | copy-start | bytes 388
  131.0 8.4 %copy-start.14 = (s32[16,2]{0,1:T(2,128)S(1)}, s32[16,2]{0,1:T(2,128)}, u32[]{:S(2)}) copy-start(s32[16,2]{0,1:T(2,128)} %copy-done.13) | copy-start | bytes 388
  131.0 8.9 %copy-start.9 = (s32[4,16]{1,0:T(4,128)S(1)}, s32[4,16]{1,0:T(4,128)}, u32[]{:S(2)}) copy-start(s32[4,16]{1,0:T(4,128)} %copy.91) | copy-start | bytes 772
  131.0 9.0 %copy-start.10 = (s32[4,16]{1,0:T(4,128)S(1)}, s32[4,16]{1,0:T(4,128)}, u32[]{:S(2)}) copy-start(s32[4,16]{1,0:T(4,128)} %copy.95) | copy-start | bytes 772
  131.0 9.0 %copy-start.17 = (pred[16,4]{0,1:T(4,128)(4,1)S(1)}, pred[16,4]{0,1:T(4,128)(4,1)}, u32[]{:S(2)}) copy-start(pred[16,4]{0,1:T(4,128)(4,1)} %copy-done.16) | copy-start | bytes 196
  131.0 9.1 %copy-start.15 = (pred[16,4]{0,1:T(4,128)(4,1)S(1)}, pred[16,4]{0,1:T(4,128)(4,1)}, u32[]{:S(2)}) copy-start(pred[16,4]{0,1:T(4,128)(4,1)} %get-tuple-element.33) | copy-start | bytes 196
  131.0 2.7 %collective-permute-start.8 = (bf16[4,2,16,4096]{3,2,1,0:T(8,128)(2,1)S(1)}, bf16[4,2,16,4096]{3,2,1,0:T(8,128)(2,1)S(1)}, u32[]{:S(2)}, u32[]{:S(2)}) collective-permute-start(bf16[4,2,16,4096]{3,2,1,0:T(8,128)(2,1)S(1)} %bitcast.221), channel_id=1, source_target_pairs={{0,1},{1,0},{2,3},{3,2},{4,5},{5,4},{6,7},{7,6},{8,9},{9,8},{10,11... | collective-permute-start | bytes 3145736 | tf_op jit(solution)/shard_map/ppermute | solution.py:26
  135.1 20.0 %all-to-all-start.3 = ((bf16[4,2,16,4096]{3,2,1,0:T(8,128)(2,1)}), bf16[4,2,16,4096]{3,2,1,0:T(8,128)(2,1)}, u32[]{:S(2)}, u32[]{:S(2)}) async-start(bf16[4,2,16,4096]{3,2,1,0:T(8,128)(2,1)} %fusion.20), calls=%async_computation.3 | async-start | bytes 2097152 | tf_op jit(solution)/shard_map/all_to_all | solution.py:156
  156.9 5.0 %collective-permute-start.9 = (bf16[16,4096]{1,0:T(8,128)(2,1)S(1)}, bf16[16,4096]{1,0:T(8,128)(2,1)S(1)}, u32[]{:S(2)}, u32[]{:S(2)}) collective-permute-start(bf16[16,4096]{1,0:T(8,128)(2,1)S(1)} %fusion.3), channel_id=1, source_target_pairs={{240,0},{0,16},{16,32},{32,48},{48,64},{64,80},{80,96},{96,112},{1... | collective-permute-start | bytes 393224 | tf_op jit(solution)/shard_map/ppermute | solution.py:22
  159.7 11.4 %collective-permute-start.10 = (bf16[16,4096]{1,0:T(8,128)(2,1)S(1)}, bf16[16,4096]{1,0:T(8,128)(2,1)S(1)}, u32[]{:S(2)}, u32[]{:S(2)}) collective-permute-start(bf16[16,4096]{1,0:T(8,128)(2,1)S(1)} %fusion.4), channel_id=1, source_target_pairs={{0,18},{2,16},{16,34},{18,32},{32,50},{34,48},{48,66},{50,64},{64,... | collective-permute-start | bytes 393224 | tf_op jit(solution)/shard_map/ppermute | solution.py:167

commit v11 on v8

--- a/solution.py
+++ b/solution.py
@@ -144,7 +144,7 @@
     flat = rows.reshape(-1, width)
     gate = jnp.dot(flat, gate_w, preferred_element_type=jnp.float32)
     upper = jnp.dot(flat, up_w, preferred_element_type=jnp.float32)
-    activated = (jax.nn.silu(gate) * upper).astype(jnp.bfloat16)
+    activated = lax.optimization_barrier((jax.nn.silu(gate) * upper).astype(jnp.bfloat16))
     computed = (
         jnp.dot(activated, down_w, preferred_element_type=jnp.float32)
         .astype(jnp.bfloat16)

time: 171 us -> 164 us (0.959)
  matrix products: 19.4 us -> 14.8 us
  local copies, waits for them, and re-layouts: 15 us -> 12.6 us
    dot_general x1, matrix products: 6.35 us -> 1.28 us  [body(): jnp.dot(activated, down_w, preferred_element_type=jnp.float32)]
where the time goes in v11:
time: 164 us; the launch traced here: 163 us
  waiting for transfers between devices  69.5 us (42%)
  starting transfers between devices  28 us (17%)
  other arithmetic  19.3 us (12%)
  blocking collectives  18.2 us (11%)
  matrix products  14.8 us (9%)
  local copies, waits for them, and re-layouts  12.6 us (8%)
    ppermute x9, waiting for transfers between devices, swap(): return lax.ppermute(block, axis, [(0, 1), (1, 0)])  28.7 us
    all_to_all x1, blocking collectives, body(): rows_y = lax.all_to_all(dispatch, 'y', 0, 0, tiled=True)  18.2 us
    ppermute x9, starting transfers between devices, swap(): return lax.ppermute(block, axis, [(0, 1), (1, 0)])  13.9 us
    all_to_all x1, waiting for transfers between devices, body(): part_y = lax.all_to_all(part_c.astype(jnp.bfloat16), 'y', 0, 0, tiled=True)  13.4 us
    all_to_all x1, waiting for transfers between devices, body(): lax.all_to_all(chip_sum.astype(jnp.bfloat16), 'y', 0, 0, tiled=True)  13.3 us
    ppermute x1, waiting for transfers between devices, body(): lax.ppermute(mixed_far.astype(jnp.bfloat16), ('section', 'zh'), route)  9.2 us
    all_to_all x1, starting transfers between devices, body(): kv_y = lax.all_to_all(send_kv, 'y', 0, 0, tiled=True)  4.46 us
    all_to_all x1, starting transfers between devices, body(): part_y = lax.all_to_all(part_c.astype(jnp.bfloat16), 'y', 0, 0, tiled=True)  4.24 us
  transfers between devices with their start and end apart: 14, of which 12 were waited for; matrix products, arithmetic and copies ran while one was open for 13% of the time, Pallas kernels for 0%

profile of v11, /device:TPU:32, one launch (start us, length us, event | category | flops | bytes accessed | tf_op | source)
XLA Modules:
  0.0 163.1 jit_solution(1587484956395376030)
XLA Ops:
  0.0 1.2 reshape_squeeze.6
  1.2 0.4 fusion.88
  1.6 0.8 pad_maximum_fusion.3
  2.4 4.5 %all-to-all-start = ((bf16[4,256,256]{2,1,0:T(8,128)(2,1)}), bf16[4,256,256]{2,1,0:T(8,128)(2,1)}, u32[]{:S(2)}, u32[]{:S(2)}) async-start(bf16[4,256,256]{2,1,0:T(8,128)(2,1)} %pad_maximum_fusion.3), calls=%async_computation | async-start | bytes 1048576 | tf_op jit(solution)/shard_map/all_to_all | solution.py:56
  7.1 6.4 %collective-permute-start.1 = (bf16[2,256,128]{2,1,0:T(8,128)(2,1)S(1)}, bf16[2,256,128]{2,1,0:T(8,128)(2,1)S(1)}, u32[]{:S(2)}, u32[]{:S(2)}) collective-permute-start(bf16[2,256,128]{2,1,0:T(8,128)(2,1)S(1)} %bitcast.222), channel_id=1, source_target_pairs={{0,2},{2,0},{1,3},{3,1},{4,6},{6,4},{5,7},{7,5},{8,10},{10,8},{9,1... | collective-permute-start | bytes 393224 | tf_op jit(solution)/shard_map/ppermute | solution.py:26
  13.7 2.8 %all-to-all-done = bf16[4,256,256]{2,1,0:T(8,128)(2,1)} async-done(((bf16[4,256,256]{2,1,0:T(8,128)(2,1)}), bf16[4,256,256]{2,1,0:T(8,128)(2,1)}, u32[]{:S(2)}, u32[]{:S(2)}) %all-to-all-start) | async-done | bytes 524320 | tf_op jit(solution)/shard_map/all_to_all | solution.py:56
  16.5 0.4 broadcast_compare_fusion
  17.0 1.7 %collective-permute-done = bf16[4,256,256]{2,1,0:T(8,128)(2,1)S(1)} collective-permute-done((bf16[4,256,256]{2,1,0:T(8,128)(2,1)}, bf16[4,256,256]{2,1,0:T(8,128)(2,1)S(1)}, u32[]{:S(2)}, u32[]{:S(2)}) %collective-permute-start) | collective-permute-done | bytes 524320 | tf_op jit(solution)/shard_map/ppermute | solution.py:26
  18.6 1.1 pad_maximum_fusion.1
  19.8 0.7 fusion.8
  20.5 1.7 %fusion.11 = (f32[2,256]{1,0:T(2,128)S(1)}, f32[2,256]{1,0:T(2,128)S(1)}, f32[2048,2,256]{2,0,1:T(8,128)S(1)}) fusion(f32[2048,2,256]{2,0,1:T(8,128)S(1)} %get-tuple-element.27, f32[2,256]{1,0:T(2,128)S(1)} %get-tuple-element.26, pred[256,2048]{0,1:T(8,128)(4,1)S(1)} %broadcast_compare_fusion, bf16[2,256,128]{2,1,0:T(8,128)(2,1)S(1)} %collective-permute-done.1, ...), kind=kOutput, calls=%fused_computation.21 | convolution fusion | flops 275774464 | bytes 9574400 | tf_op jit(solution)/shard_map/hqd,kd->hqk/dot_general | solution.py:70
  22.2 1.0 fusion.14
  23.2 6.4 %collective-permute-start.2 = (f32[2,256,2]{1,0,2:T(2,128)S(1)}, f32[2,256,2]{1,0,2:T(2,128)S(1)}, u32[]{:S(2)}, u32[]{:S(2)}) collective-permute-start(f32[2,256,2]{1,0,2:T(2,128)S(1)} %pad_maximum_fusion.5), channel_id=1, source_target_pairs={{0,2},{2,0},{1,3},{3,1},{4,6},{6,4},{5,7},{7,5},{8,10},{10,8},{9,1... | collective-permute-start | bytes 12296 | tf_op jit(solution)/shard_map/ppermute | solution.py:26
  29.6 1.0 fusion.32
  30.7 0.5 collective-permute-done.2
  31.2 11.5 %collective-permute-done.3 = bf16[2,256,128]{1,2,0:T(8,128)(2,1)S(1)} collective-permute-done((bf16[2,256,128]{1,2,0:T(8,128)(2,1)S(1)}, bf16[2,256,128]{1,2,0:T(8,128)(2,1)S(1)}, u32[]{:S(2)}, u32[]{:S(2)}) %collective-permute-start.3) | collective-permute-done | bytes 131104 | tf_op jit(solution)/shard_map/ppermute | solution.py:26
  42.7 1.0 fusion.43
  43.7 0.6 copy-done.3
  44.2 0.7 convolution_convert_fusion.1
  45.0 1.3 copy-done.1
  46.3 1.1 dynamic-slice_bitcast_fusion
  47.4 3.0 %collective-permute-done.4 = bf16[4,2,16,4096]{3,2,1,0:T(8,128)(2,1)} collective-permute-done((bf16[4,2,16,4096]{3,2,1,0:T(8,128)(2,1)}, bf16[4,2,16,4096]{3,2,1,0:T(8,128)(2,1)}, u32[]{:S(2)}, u32[]{:S(2)}) %collective-permute-start.4) | collective-permute-done | bytes 1048608 | tf_op jit(solution)/shard_map/ppermute | solution.py:26
  50.4 2.8 %fusion.21 = bf16[4,2,16,4096]{3,2,1,0:T(8,128)(2,1)} fusion(bf16[4,2,16,4096]{3,2,1,0:T(8,128)(2,1)} %collective-permute-done.4, bf16[4,2,2,16,4096]{4,3,2,1,0:T(8,128)(2,1)} %bitcast.205, s32[]{:T(128)S(6)} %select_n.55), kind=kLoop, calls=%fused_computation.34 | loop fusion | flops 2097152 | bytes 3145732 | tf_op jit(solution)/shard_map/convert_element_type | solution.py:98
  53.2 4.2 %all-to-all-start.1 = ((bf16[4,2,16,4096]{3,2,1,0:T(8,128)(2,1)}), bf16[4,2,16,4096]{3,2,1,0:T(8,128)(2,1)}, u32[]{:S(2)}, u32[]{:S(2)}) async-start(bf16[4,2,16,4096]{3,2,1,0:T(8,128)(2,1)} %fusion.21), calls=%async_computation.1 | async-start | bytes 2097152 | tf_op jit(solution)/shard_map/all_to_all | solution.py:98
  57.4 0.5 collective-permute-start.6
  58.0 0.5 fusion.68
  58.6 0.5 copy-done.14
  59.1 0.6 reduce_window_sum.17
  59.8 13.4 %all-to-all-done.1 = bf16[4,2,16,4096]{3,2,1,0:T(8,128)(2,1)} async-done(((bf16[4,2,16,4096]{3,2,1,0:T(8,128)(2,1)}), bf16[4,2,16,4096]{3,2,1,0:T(8,128)(2,1)}, u32[]{:S(2)}, u32[]{:S(2)}) %all-to-all-start.1) | async-done | bytes 1048608 | tf_op jit(solution)/shard_map/all_to_all | solution.py:98
  73.1 1.4 convert_reduce_fusion
  74.5 0.7 pad_maximum_fusion.4
  75.3 0.4 collective-permute-start.5
  75.7 1.3 add_bitcast_fusion.1
  77.0 1.4 copy.87
  78.3 1.2 convert_element_type.143
  79.5 1.3 copy.90
  80.8 1.3 reduce_window_sum.18
  82.2 1.3 add_bitcast_fusion
  83.5 1.4 copy.91
  84.8 7.0 %collective-permute-done.5 = bf16[2,16,4096]{2,1,0:T(8,128)(2,1)} collective-permute-done((bf16[2,16,4096]{2,1,0:T(8,128)(2,1)}, bf16[2,16,4096]{2,1,0:T(8,128)(2,1)}, u32[]{:S(2)}, u32[]{:S(2)}) %collective-permute-start.5) | collective-permute-done | bytes 262176 | tf_op jit(solution)/shard_map/ppermute | solution.py:26
  91.8 1.0 convert_element_type.138
  92.8 1.3 multiply_reduce_fusion.1
  94.1 1.0 fusion
  95.2 1.3 fusion.1
  96.7 18.2 %all_to_all.20 = bf16[4,2,16,4096]{3,2,1,0:T(8,128)(2,1)S(1)} all-to-all(bf16[4,2,16,4096]{3,2,1,0:T(8,128)(2,1)S(1)} %copy.92), channel_id=1, replica_groups=mesh['section'=16,'y'=4,'zh'=2,'core'=2] {'y'}, dimensions={0} | all-to-all | bytes 2097152 | tf_op jit(solution)/shard_map/all_to_all | solution.py:142
  114.9 2.7 %collective-permute-done.7 = bf16[4,2,16,4096]{3,2,1,0:T(8,128)(2,1)S(1)} collective-permute-done((bf16[4,2,16,4096]{3,2,1,0:T(8,128)(2,1)S(1)}, bf16[4,2,16,4096]{3,2,1,0:T(8,128)(2,1)S(1)}, u32[]{:S(2)}, u32[]{:S(2)}) %collective-permute-start.7) | collective-permute-done | bytes 1048608 | tf_op jit(solution)/shard_map/ppermute | solution.py:26
  117.8 1.3 fusion.18
  119.0 0.4 copy-done.19
  119.4 1.3 multiply_convert_fusion
  120.7 1.3 convolution_convert_fusion
  122.1 0.2 fusion.87
  122.3 0.2 collective-permute-start.8
  122.6 2.4 %collective-permute-done.8 = bf16[4,2,16,4096]{3,2,1,0:T(8,128)(2,1)S(1)} collective-permute-done((bf16[4,2,16,4096]{3,2,1,0:T(8,128)(2,1)S(1)}, bf16[4,2,16,4096]{3,2,1,0:T(8,128)(2,1)S(1)}, u32[]{:S(2)}, u32[]{:S(2)}) %collective-permute-start.8) | collective-permute-done | bytes 1048608 | tf_op jit(solution)/shard_map/ppermute | solution.py:26
  125.0 1.3 fusion.20
  126.3 4.2 %all-to-all-start.3 = ((bf16[4,2,16,4096]{3,2,1,0:T(8,128)(2,1)}), bf16[4,2,16,4096]{3,2,1,0:T(8,128)(2,1)}, u32[]{:S(2)}, u32[]{:S(2)}) async-start(bf16[4,2,16,4096]{3,2,1,0:T(8,128)(2,1)} %fusion.20), calls=%async_computation.3 | async-start | bytes 2097152 | tf_op jit(solution)/shard_map/all_to_all | solution.py:155
  131.6 0.7 reshape.241
  132.3 0.7 reshape.244
  133.0 13.3 %all-to-all-done.3 = bf16[4,2,16,4096]{3,2,1,0:T(8,128)(2,1)} async-done(((bf16[4,2,16,4096]{3,2,1,0:T(8,128)(2,1)}), bf16[4,2,16,4096]{3,2,1,0:T(8,128)(2,1)}, u32[]{:S(2)}, u32[]{:S(2)}) %all-to-all-start.3) | async-done | bytes 1048608 | tf_op jit(solution)/shard_map/all_to_all | solution.py:155
  146.3 1.8 %fusion.3 = bf16[16,4096]{1,0:T(8,128)(2,1)S(1)} fusion(bf16[4,2,16,4096]{3,2,1,0:T(8,128)(2,1)} %all-to-all-done.3, f32[2,16,4096]{2,1,0:T(8,128)} %copy-done.2, bf16[1,16,4096]{2,1,0:T(8,128)(2,1)S(1)} %get-tuple-element.14, f32[16,4,16]{2,1,0:T(4,128)} %reshape.241, bf16[1,16,4096]{2,1,0:T(8,128)(2,1)S(1)} %copy-done.4), kind=kOutput, calls=%fused_computation.9 | convolution fusion | flops 50724864 | bytes 1212416 | tf_op jit(solution)/shard_map/txj,xjd->td/dot_general | solution.py:159
  148.1 1.1 collective-permute-start.9
  149.2 1.7 %fusion.4 = bf16[16,4096]{1,0:T(8,128)(2,1)S(1)} fusion(bf16[4,2,16,4096]{3,2,1,0:T(8,128)(2,1)} %all-to-all-done.3, f32[16,4,16]{2,1,0:T(4,128)} %reshape.244), kind=kOutput, calls=%fused_computation.10 | convolution fusion | flops 50397184 | bytes 688128 | tf_op jit(solution)/shard_map/txj,xjd->td/dot_general | solution.py:160
  151.0 2.1 %collective-permute-done.9 = bf16[16,4096]{1,0:T(8,128)(2,1)S(1)} collective-permute-done((bf16[16,4096]{1,0:T(8,128)(2,1)S(1)}, bf16[16,4096]{1,0:T(8,128)(2,1)S(1)}, u32[]{:S(2)}, u32[]{:S(2)}) %collective-permute-start.9) | collective-permute-done | bytes 131104 | tf_op jit(solution)/shard_map/ppermute | solution.py:22
  153.2 9.2 %collective-permute-done.10 = bf16[16,4096]{1,0:T(8,128)(2,1)S(1)} collective-permute-done((bf16[16,4096]{1,0:T(8,128)(2,1)S(1)}, bf16[16,4096]{1,0:T(8,128)(2,1)S(1)}, u32[]{:S(2)}, u32[]{:S(2)}) %collective-permute-start.10) | collective-permute-done | bytes 131104 | tf_op jit(solution)/shard_map/ppermute | solution.py:166
  162.4 0.7 fusion.52
  (84 shorter events, 2.4 us)
Async XLA Ops:
  0.0 120.7 %copy-start = (bf16[1,384,4096]{2,1,0:T(8,128)(2,1)S(1)}, bf16[1,384,4096]{2,1,0:T(8,128)(2,1)}, u32[]{:S(2)}) copy-start(bf16[1,384,4096]{2,1,0:T(8,128)(2,1)} %param.17) | copy-start | bytes 9437188
  0.0 6.9 %copy-start.5 = (bf16[1,256,256]{2,1,0:T(8,128)(2,1)S(1)}, bf16[1,256,256]{2,1,0:T(8,128)(2,1)}, u32[]{:S(2)}) copy-start(bf16[1,256,256]{2,1,0:T(8,128)(2,1)} %param.11) | copy-start | bytes 393220
  2.4 14.0 %all-to-all-start = ((bf16[4,256,256]{2,1,0:T(8,128)(2,1)}), bf16[4,256,256]{2,1,0:T(8,128)(2,1)}, u32[]{:S(2)}, u32[]{:S(2)}) async-start(bf16[4,256,256]{2,1,0:T(8,128)(2,1)} %pad_maximum_fusion.3), calls=%async_computation | async-start | bytes 1048576 | tf_op jit(solution)/shard_map/all_to_all | solution.py:56
  7.1 13.4 %collective-permute-start.1 = (bf16[2,256,128]{2,1,0:T(8,128)(2,1)S(1)}, bf16[2,256,128]{2,1,0:T(8,128)(2,1)S(1)}, u32[]{:S(2)}, u32[]{:S(2)}) collective-permute-start(bf16[2,256,128]{2,1,0:T(8,128)(2,1)S(1)} %bitcast.222), channel_id=1, source_target_pairs={{0,2},{2,0},{1,3},{3,1},{4,6},{6,4},{5,7},{7,5},{8,10},{10,8},{9,1... | collective-permute-start | bytes 393224 | tf_op jit(solution)/shard_map/ppermute | solution.py:26
  16.5 2.1 %collective-permute-start = (bf16[4,256,256]{2,1,0:T(8,128)(2,1)}, bf16[4,256,256]{2,1,0:T(8,128)(2,1)S(1)}, u32[]{:S(2)}, u32[]{:S(2)}) collective-permute-start(bf16[4,256,256]{2,1,0:T(8,128)(2,1)} %all-to-all-done), channel_id=1, source_target_pairs={{0,1},{1,0},{2,3},{3,2},{4,5},{5,4},{6,7},{7,6},{8,9},{9,8},{10,11... | collective-permute-start | bytes 1572872 | tf_op jit(solution)/shard_map/ppermute | solution.py:26
  23.2 8.0 %collective-permute-start.2 = (f32[2,256,2]{1,0,2:T(2,128)S(1)}, f32[2,256,2]{1,0,2:T(2,128)S(1)}, u32[]{:S(2)}, u32[]{:S(2)}) collective-permute-start(f32[2,256,2]{1,0,2:T(2,128)S(1)} %pad_maximum_fusion.5), channel_id=1, source_target_pairs={{0,2},{2,0},{1,3},{3,1},{4,6},{6,4},{5,7},{7,5},{8,10},{10,8},{9,1... | collective-permute-start | bytes 12296 | tf_op jit(solution)/shard_map/ppermute | solution.py:26
  30.6 12.1 %collective-permute-start.3 = (bf16[2,256,128]{1,2,0:T(8,128)(2,1)S(1)}, bf16[2,256,128]{1,2,0:T(8,128)(2,1)S(1)}, u32[]{:S(2)}, u32[]{:S(2)}) collective-permute-start(bf16[2,256,128]{1,2,0:T(8,128)(2,1)S(1)} %fusion.32), channel_id=1, source_target_pairs={{0,2},{2,0},{1,3},{3,1},{4,6},{6,4},{5,7},{7,5},{8,10},{10,8},{9,1... | collective-permute-start | bytes 393224 | tf_op jit(solution)/shard_map/ppermute | solution.py:26
  42.6 1.6 copy-start.3
  45.0 1.3 copy-start.1
  45.0 12.4 %copy-start.4 = (bf16[1,16,4096]{2,1,0:T(8,128)(2,1)S(1)}, bf16[1,16,4096]{2,1,0:T(8,128)(2,1)}, u32[]{:S(2)}) copy-start(bf16[1,16,4096]{2,1,0:T(8,128)(2,1)} %param.10) | copy-start | bytes 393220
  45.0 12.9 %copy-start.17 = (s32[1,256,2]{1,2,0:T(2,128)S(1)}, s32[1,256,2]{1,2,0:T(2,128)}, u32[]{:S(2)}) copy-start(s32[1,256,2]{1,2,0:T(2,128)} %param.18) | copy-start | bytes 6148
  47.4 3.0 %collective-permute-start.4 = (bf16[4,2,16,4096]{3,2,1,0:T(8,128)(2,1)}, bf16[4,2,16,4096]{3,2,1,0:T(8,128)(2,1)}, u32[]{:S(2)}, u32[]{:S(2)}) collective-permute-start(bf16[4,2,16,4096]{3,2,1,0:T(8,128)(2,1)} %dynamic-slice_bitcast_fusion), channel_id=1, source_target_pairs={{0,1},{1,0},{2,3},{3,2},{4,5},{5,4},{6,7},{7,6},{8,9},{9,8},{10,11... | collective-permute-start | bytes 3145736 | tf_op jit(solution)/shard_map/ppermute | solution.py:26
  47.4 46.7 %copy-start.6 = (f32[1,4096]{1,0:T(1,128)S(1)}, f32[1,4096]{1,0:T(1,128)}, u32[]{:S(2)}) copy-start(f32[1,4096]{1,0:T(1,128)} %param.14) | copy-start | bytes 49156
  53.2 20.0 %all-to-all-start.1 = ((bf16[4,2,16,4096]{3,2,1,0:T(8,128)(2,1)}), bf16[4,2,16,4096]{3,2,1,0:T(8,128)(2,1)}, u32[]{:S(2)}, u32[]{:S(2)}) async-start(bf16[4,2,16,4096]{3,2,1,0:T(8,128)(2,1)} %fusion.21), calls=%async_computation.1 | async-start | bytes 2097152 | tf_op jit(solution)/shard_map/all_to_all | solution.py:98
  57.4 35.4 %collective-permute-start.6 = (bf16[16,4096]{1,0:T(8,128)(2,1)S(1)}, bf16[16,4096]{1,0:T(8,128)(2,1)}, u32[]{:S(2)}, u32[]{:S(2)}) collective-permute-start(bf16[16,4096]{1,0:T(8,128)(2,1)S(1)} %bitcast.210), channel_id=1, source_target_pairs={{0,2},{2,0},{1,3},{3,1},{4,6},{6,4},{5,7},{7,5},{8,10},{10,8},{9,1... | collective-permute-start | bytes 393224 | tf_op jit(solution)/shard_map/ppermute | solution.py:26
  58.0 0.6 copy-start.9
  58.0 0.6 copy-start.11
  58.5 0.5 copy-start.14
  75.3 16.5 %collective-permute-start.5 = (bf16[2,16,4096]{2,1,0:T(8,128)(2,1)}, bf16[2,16,4096]{2,1,0:T(8,128)(2,1)}, u32[]{:S(2)}, u32[]{:S(2)}) collective-permute-start(bf16[2,16,4096]{2,1,0:T(8,128)(2,1)} %pad_maximum_fusion.4), channel_id=1, source_target_pairs={{0,2},{2,0},{1,3},{3,1},{4,6},{6,4},{5,7},{7,5},{8,10},{10,8},{9,1... | collective-permute-start | bytes 786440 | tf_op jit(solution)/shard_map/ppermute | solution.py:26
  92.8 2.4 %copy-start.2 = (f32[2,16,4096]{2,1,0:T(8,128)}, f32[2,16,4096]{2,1,0:T(8,128)S(1)}, u32[]{:S(2)}) copy-start(f32[2,16,4096]{2,1,0:T(8,128)S(1)} %convert_element_type.138) | copy-start | bytes 1572868
  96.5 21.2 %copy-start.18 = (bf16[1,4096,384]{2,1,0:T(8,128)(2,1)S(1)}, bf16[1,4096,384]{2,1,0:T(8,128)(2,1)}, u32[]{:S(2)}) copy-start(bf16[1,4096,384]{2,1,0:T(8,128)(2,1)} %param.15) | copy-start | bytes 9437188
  114.9 2.7 %collective-permute-start.7 = (bf16[4,2,16,4096]{3,2,1,0:T(8,128)(2,1)S(1)}, bf16[4,2,16,4096]{3,2,1,0:T(8,128)(2,1)S(1)}, u32[]{:S(2)}, u32[]{:S(2)}) collective-permute-start(bf16[4,2,16,4096]{3,2,1,0:T(8,128)(2,1)S(1)} %all_to_all.20), channel_id=1, source_target_pairs={{0,1},{1,0},{2,3},{3,2},{4,5},{5,4},{6,7},{7,6},{8,9},{9,8},{10,11... | collective-permute-start | bytes 3145736 | tf_op jit(solution)/shard_map/ppermute | solution.py:26
  117.6 1.9 %copy-start.19 = (bf16[1,4096,384]{2,1,0:T(8,128)(2,1)S(1)}, bf16[1,4096,384]{2,1,0:T(8,128)(2,1)}, u32[]{:S(2)}) copy-start(bf16[1,4096,384]{2,1,0:T(8,128)(2,1)} %param.16) | copy-start | bytes 9437188
  120.7 1.8 %copy-start.16 = (f32[1,256,2]{1,2,0:T(2,128)S(1)}, f32[1,256,2]{1,2,0:T(2,128)}, u32[]{:S(2)}) copy-start(f32[1,256,2]{1,2,0:T(2,128)} %param.19) | copy-start | bytes 6148
  122.0 8.6 %copy-start.10 = (s32[16,2]{0,1:T(2,128)S(1)}, s32[16,2]{0,1:T(2,128)}, u32[]{:S(2)}) copy-start(s32[16,2]{0,1:T(2,128)} %copy-done.9) | copy-start | bytes 388
  122.0 8.6 %copy-start.12 = (s32[16,2]{0,1:T(2,128)S(1)}, s32[16,2]{0,1:T(2,128)}, u32[]{:S(2)}) copy-start(s32[16,2]{0,1:T(2,128)} %copy-done.11) | copy-start | bytes 388
  122.0 9.1 %copy-start.7 = (s32[4,16]{1,0:T(4,128)S(1)}, s32[4,16]{1,0:T(4,128)}, u32[]{:S(2)}) copy-start(s32[4,16]{1,0:T(4,128)} %copy.87) | copy-start | bytes 772
  122.0 9.2 %copy-start.8 = (s32[4,16]{1,0:T(4,128)S(1)}, s32[4,16]{1,0:T(4,128)}, u32[]{:S(2)}) copy-start(s32[4,16]{1,0:T(4,128)} %copy.91) | copy-start | bytes 772
  122.1 9.2 %copy-start.15 = (pred[16,4]{0,1:T(4,128)(4,1)S(1)}, pred[16,4]{0,1:T(4,128)(4,1)}, u32[]{:S(2)}) copy-start(pred[16,4]{0,1:T(4,128)(4,1)} %copy-done.14) | copy-start | bytes 196
  122.1 9.3 %copy-start.13 = (pred[16,4]{0,1:T(4,128)(4,1)S(1)}, pred[16,4]{0,1:T(4,128)(4,1)}, u32[]{:S(2)}) copy-start(pred[16,4]{0,1:T(4,128)(4,1)} %get-tuple-element.33) | copy-start | bytes 196
  122.3 2.7 %collective-permute-start.8 = (bf16[4,2,16,4096]{3,2,1,0:T(8,128)(2,1)S(1)}, bf16[4,2,16,4096]{3,2,1,0:T(8,128)(2,1)S(1)}, u32[]{:S(2)}, u32[]{:S(2)}) collective-permute-start(bf16[4,2,16,4096]{3,2,1,0:T(8,128)(2,1)S(1)} %bitcast.215), channel_id=1, source_target_pairs={{0,1},{1,0},{2,3},{3,2},{4,5},{5,4},{6,7},{7,6},{8,9},{9,8},{10,11... | collective-permute-start | bytes 3145736 | tf_op jit(solution)/shard_map/ppermute | solution.py:26
  126.3 20.0 %all-to-all-start.3 = ((bf16[4,2,16,4096]{3,2,1,0:T(8,128)(2,1)}), bf16[4,2,16,4096]{3,2,1,0:T(8,128)(2,1)}, u32[]{:S(2)}, u32[]{:S(2)}) async-start(bf16[4,2,16,4096]{3,2,1,0:T(8,128)(2,1)} %fusion.20), calls=%async_computation.3 | async-start | bytes 2097152 | tf_op jit(solution)/shard_map/all_to_all | solution.py:155
  148.1 5.0 %collective-permute-start.9 = (bf16[16,4096]{1,0:T(8,128)(2,1)S(1)}, bf16[16,4096]{1,0:T(8,128)(2,1)S(1)}, u32[]{:S(2)}, u32[]{:S(2)}) collective-permute-start(bf16[16,4096]{1,0:T(8,128)(2,1)S(1)} %fusion.3), channel_id=1, source_target_pairs={{240,0},{0,16},{16,32},{32,48},{48,64},{64,80},{80,96},{96,112},{1... | collective-permute-start | bytes 393224 | tf_op jit(solution)/shard_map/ppermute | solution.py:22
  150.9 11.4 %collective-permute-start.10 = (bf16[16,4096]{1,0:T(8,128)(2,1)S(1)}, bf16[16,4096]{1,0:T(8,128)(2,1)S(1)}, u32[]{:S(2)}, u32[]{:S(2)}) collective-permute-start(bf16[16,4096]{1,0:T(8,128)(2,1)S(1)} %fusion.4), channel_id=1, source_target_pairs={{0,18},{2,16},{16,34},{18,32},{32,50},{34,48},{48,66},{50,64},{64,... | collective-permute-start | bytes 393224 | tf_op jit(solution)/shard_map/ppermute | solution.py:166

commit v12 on v11

--- a/solution.py
+++ b/solution.py
@@ -152,12 +152,19 @@
     )
 
     chip_sum = computed[0].astype(jnp.float32) + swap(computed[1], "core").astype(jnp.float32)
-    back = lax.all_to_all(chip_sum.astype(jnp.bfloat16), "y", 0, 0, tiled=True).astype(jnp.float32)
-    hi = lax.Precision.HIGHEST
-    combine_own = combine_own.reshape(tok_rows, experts_count, CAP)
-    combine_far = combine_far.reshape(tok_rows, experts_count, CAP)
-    mixed_own = jnp.einsum("txj,xjd->td", combine_own, back[:, 0], precision=hi)
-    mixed_far = jnp.einsum("txj,xjd->td", combine_far, back[:, 1], precision=hi)
+    back = lax.all_to_all(chip_sum.astype(jnp.bfloat16), "y", 0, 0, tiled=True)
+
+    def mix(combine, outs):
+        combine = combine.reshape(tok_rows, experts_count, CAP)
+        high = combine.astype(jnp.bfloat16)
+        low = (combine - high.astype(jnp.float32)).astype(jnp.bfloat16)
+        return sum(
+            jnp.einsum("txj,xjd->td", part, outs, preferred_element_type=jnp.float32)
+            for part in (high, low)
+        )
+
+    mixed_own = mix(combine_own, back[:, 0])
+    mixed_far = mix(combine_far, back[:, 1])
     own_part = shifted((middle + mixed_own).astype(jnp.bfloat16), "section", 1)
     sections = lax.axis_size("section")
     route = [

time: 164 us -> 166 us (1.012)
  matrix products: 14.8 us -> 16.8 us
    dot_general x2 -> x4, matrix products: 3.57 us -> 5.55 us  [mix(): jnp.einsum('txj,xjd->td', part, outs, preferred_element_type=jnp.float32)]
  transfers between devices with their start and end apart: 14 -> 14, of which waited for: 12 -> 12; matrix products, arithmetic and copies ran while one was open for 13% -> 14% of each run, Pallas kernels for 0% -> 0%
where the time goes in v12:
time: 166 us; the launch traced here: 165 us
  waiting for transfers between devices  69.6 us (42%)
  starting transfers between devices  28 us (17%)
  other arithmetic  20.5 us (12%)
  blocking collectives  18.2 us (11%)
  matrix products  16.8 us (10%)
  local copies, waits for them, and re-layouts  11.4 us (7%)
    ppermute x9, waiting for transfers between devices, swap(): return lax.ppermute(block, axis, [(0, 1), (1, 0)])  28.7 us
    all_to_all x1, blocking collectives, body(): rows_y = lax.all_to_all(dispatch, 'y', 0, 0, tiled=True)  18.2 us
    ppermute x9, starting transfers between devices, swap(): return lax.ppermute(block, axis, [(0, 1), (1, 0)])  13.9 us
    all_to_all x1, waiting for transfers between devices, body(): part_y = lax.all_to_all(part_c.astype(jnp.bfloat16), 'y', 0, 0, tiled=True)  13.4 us
    all_to_all x1, waiting for transfers between devices, body(): back = lax.all_to_all(chip_sum.astype(jnp.bfloat16), 'y', 0, 0, tiled=True)  13.4 us
    ppermute x1, waiting for transfers between devices, body(): lax.ppermute(mixed_far.astype(jnp.bfloat16), ('section', 'zh'), route)  10.2 us
    dot_general x4, matrix products, mix(): jnp.einsum('txj,xjd->td', part, outs, preferred_element_type=jnp.float32)  5.55 us
    all_to_all x1, starting transfers between devices, body(): kv_y = lax.all_to_all(send_kv, 'y', 0, 0, tiled=True)  4.46 us
  transfers between devices with their start and end apart: 14, of which 12 were waited for; matrix products, arithmetic and copies ran while one was open for 14% of the time, Pallas kernels for 0%

profile of v12, /device:TPU:32, one launch (start us, length us, event | category | flops | bytes accessed | tf_op | source)
XLA Modules:
  0.0 165.0 jit_solution(14020240427351316991)
XLA Ops:
  0.0 1.2 reshape_squeeze.6
  1.2 0.4 fusion.92
  1.6 0.8 pad_maximum_fusion.3
  2.4 4.5 %all-to-all-start = ((bf16[4,256,256]{2,1,0:T(8,128)(2,1)}), bf16[4,256,256]{2,1,0:T(8,128)(2,1)}, u32[]{:S(2)}, u32[]{:S(2)}) async-start(bf16[4,256,256]{2,1,0:T(8,128)(2,1)} %pad_maximum_fusion.3), calls=%async_computation | async-start | bytes 1048576 | tf_op jit(solution)/shard_map/all_to_all | solution.py:56
  7.1 6.4 %collective-permute-start.1 = (bf16[2,256,128]{2,1,0:T(8,128)(2,1)S(1)}, bf16[2,256,128]{2,1,0:T(8,128)(2,1)S(1)}, u32[]{:S(2)}, u32[]{:S(2)}) collective-permute-start(bf16[2,256,128]{2,1,0:T(8,128)(2,1)S(1)} %bitcast.232), channel_id=1, source_target_pairs={{0,2},{2,0},{1,3},{3,1},{4,6},{6,4},{5,7},{7,5},{8,10},{10,8},{9,1... | collective-permute-start | bytes 393224 | tf_op jit(solution)/shard_map/ppermute | solution.py:26
  13.7 2.8 %all-to-all-done = bf16[4,256,256]{2,1,0:T(8,128)(2,1)} async-done(((bf16[4,256,256]{2,1,0:T(8,128)(2,1)}), bf16[4,256,256]{2,1,0:T(8,128)(2,1)}, u32[]{:S(2)}, u32[]{:S(2)}) %all-to-all-start) | async-done | bytes 524320 | tf_op jit(solution)/shard_map/all_to_all | solution.py:56
  16.5 0.4 broadcast_compare_fusion
  17.0 1.7 %collective-permute-done = bf16[4,256,256]{2,1,0:T(8,128)(2,1)S(1)} collective-permute-done((bf16[4,256,256]{2,1,0:T(8,128)(2,1)}, bf16[4,256,256]{2,1,0:T(8,128)(2,1)S(1)}, u32[]{:S(2)}, u32[]{:S(2)}) %collective-permute-start) | collective-permute-done | bytes 524320 | tf_op jit(solution)/shard_map/ppermute | solution.py:26
  18.6 1.1 pad_maximum_fusion.1
  19.8 0.7 fusion.10
  20.5 1.7 %fusion.13 = (f32[2,256]{1,0:T(2,128)S(1)}, f32[2,256]{1,0:T(2,128)S(1)}, f32[2048,2,256]{2,0,1:T(8,128)S(1)}) fusion(f32[2048,2,256]{2,0,1:T(8,128)S(1)} %get-tuple-element.31, f32[2,256]{1,0:T(2,128)S(1)} %get-tuple-element.30, pred[256,2048]{0,1:T(8,128)(4,1)S(1)} %broadcast_compare_fusion, bf16[2,256,128]{2,1,0:T(8,128)(2,1)S(1)} %collective-permute-done.1, ...), kind=kOutput, calls=%fused_computation.25 | convolution fusion | flops 275774464 | bytes 9574400 | tf_op jit(solution)/shard_map/hqd,kd->hqk/dot_general | solution.py:70
  22.2 1.0 fusion.16
  23.2 6.4 %collective-permute-start.2 = (f32[2,256,2]{1,0,2:T(2,128)S(1)}, f32[2,256,2]{1,0,2:T(2,128)S(1)}, u32[]{:S(2)}, u32[]{:S(2)}) collective-permute-start(f32[2,256,2]{1,0,2:T(2,128)S(1)} %pad_maximum_fusion.5), channel_id=1, source_target_pairs={{0,2},{2,0},{1,3},{3,1},{4,6},{6,4},{5,7},{7,5},{8,10},{10,8},{9,1... | collective-permute-start | bytes 12296 | tf_op jit(solution)/shard_map/ppermute | solution.py:26
  29.6 1.0 fusion.34
  30.7 0.5 collective-permute-done.2
  31.2 11.5 %collective-permute-done.3 = bf16[2,256,128]{1,2,0:T(8,128)(2,1)S(1)} collective-permute-done((bf16[2,256,128]{1,2,0:T(8,128)(2,1)S(1)}, bf16[2,256,128]{1,2,0:T(8,128)(2,1)S(1)}, u32[]{:S(2)}, u32[]{:S(2)}) %collective-permute-start.3) | collective-permute-done | bytes 131104 | tf_op jit(solution)/shard_map/ppermute | solution.py:26
  42.7 1.0 fusion.45
  43.7 0.6 copy-done.3
  44.2 0.7 convolution_convert_fusion.1
  45.0 1.3 copy-done.1
  46.3 1.1 dynamic-slice_bitcast_fusion
  47.4 3.0 %collective-permute-done.4 = bf16[4,2,16,4096]{3,2,1,0:T(8,128)(2,1)} collective-permute-done((bf16[4,2,16,4096]{3,2,1,0:T(8,128)(2,1)}, bf16[4,2,16,4096]{3,2,1,0:T(8,128)(2,1)}, u32[]{:S(2)}, u32[]{:S(2)}) %collective-permute-start.4) | collective-permute-done | bytes 1048608 | tf_op jit(solution)/shard_map/ppermute | solution.py:26
  50.4 2.8 %fusion.23 = bf16[4,2,16,4096]{3,2,1,0:T(8,128)(2,1)} fusion(bf16[4,2,16,4096]{3,2,1,0:T(8,128)(2,1)} %collective-permute-done.4, bf16[4,2,2,16,4096]{4,3,2,1,0:T(8,128)(2,1)} %bitcast.215, s32[]{:T(128)S(6)} %select_n.55), kind=kLoop, calls=%fused_computation.38 | loop fusion | flops 2097152 | bytes 3145732 | tf_op jit(solution)/shard_map/convert_element_type | solution.py:98
  53.2 4.2 %all-to-all-start.1 = ((bf16[4,2,16,4096]{3,2,1,0:T(8,128)(2,1)}), bf16[4,2,16,4096]{3,2,1,0:T(8,128)(2,1)}, u32[]{:S(2)}, u32[]{:S(2)}) async-start(bf16[4,2,16,4096]{3,2,1,0:T(8,128)(2,1)} %fusion.23), calls=%async_computation.1 | async-start | bytes 2097152 | tf_op jit(solution)/shard_map/all_to_all | solution.py:98
  57.4 0.5 collective-permute-start.6
  58.0 0.5 fusion.72
  58.5 0.5 copy-done.14
  59.1 0.6 reduce_window_sum.17
  59.8 13.4 %all-to-all-done.1 = bf16[4,2,16,4096]{3,2,1,0:T(8,128)(2,1)} async-done(((bf16[4,2,16,4096]{3,2,1,0:T(8,128)(2,1)}), bf16[4,2,16,4096]{3,2,1,0:T(8,128)(2,1)}, u32[]{:S(2)}, u32[]{:S(2)}) %all-to-all-start.1) | async-done | bytes 1048608 | tf_op jit(solution)/shard_map/all_to_all | solution.py:98
  73.2 1.4 convert_reduce_fusion
  74.6 0.7 pad_maximum_fusion.4
  75.3 0.4 collective-permute-start.5
  75.7 1.3 add_bitcast_fusion.1
  77.0 1.3 copy.91
  78.3 1.1 convert_element_type.161
  79.5 1.3 copy.94
  80.8 1.3 reduce_window_sum.18
  82.1 1.3 add_bitcast_fusion
  83.4 1.4 copy.95
  84.7 7.1 %collective-permute-done.5 = bf16[2,16,4096]{2,1,0:T(8,128)(2,1)} collective-permute-done((bf16[2,16,4096]{2,1,0:T(8,128)(2,1)}, bf16[2,16,4096]{2,1,0:T(8,128)(2,1)}, u32[]{:S(2)}, u32[]{:S(2)}) %collective-permute-start.5) | collective-permute-done | bytes 262176 | tf_op jit(solution)/shard_map/ppermute | solution.py:26
  91.8 1.0 convert_element_type.155
  92.8 1.3 multiply_reduce_fusion.1
  94.1 1.0 fusion
  95.2 1.3 fusion.1
  96.7 18.2 %all_to_all.20 = bf16[4,2,16,4096]{3,2,1,0:T(8,128)(2,1)S(1)} all-to-all(bf16[4,2,16,4096]{3,2,1,0:T(8,128)(2,1)S(1)} %copy.96), channel_id=1, replica_groups=mesh['section'=16,'y'=4,'zh'=2,'core'=2] {'y'}, dimensions={0} | all-to-all | bytes 2097152 | tf_op jit(solution)/shard_map/all_to_all | solution.py:142
  114.9 2.7 %collective-permute-done.7 = bf16[4,2,16,4096]{3,2,1,0:T(8,128)(2,1)S(1)} collective-permute-done((bf16[4,2,16,4096]{3,2,1,0:T(8,128)(2,1)S(1)}, bf16[4,2,16,4096]{3,2,1,0:T(8,128)(2,1)S(1)}, u32[]{:S(2)}, u32[]{:S(2)}) %collective-permute-start.7) | collective-permute-done | bytes 1048608 | tf_op jit(solution)/shard_map/ppermute | solution.py:26
  117.8 1.3 fusion.20
  119.0 0.4 copy-done.19
  119.4 1.3 multiply_convert_fusion
  120.7 1.3 convolution_convert_fusion
  122.7 2.4 %collective-permute-done.8 = bf16[4,2,16,4096]{3,2,1,0:T(8,128)(2,1)S(1)} collective-permute-done((bf16[4,2,16,4096]{3,2,1,0:T(8,128)(2,1)S(1)}, bf16[4,2,16,4096]{3,2,1,0:T(8,128)(2,1)S(1)}, u32[]{:S(2)}, u32[]{:S(2)}) %collective-permute-start.8) | collective-permute-done | bytes 1048608 | tf_op jit(solution)/shard_map/ppermute | solution.py:26
  125.0 1.3 fusion.22
  126.3 4.2 %all-to-all-start.3 = ((bf16[4,2,16,4096]{3,2,1,0:T(8,128)(2,1)}), bf16[4,2,16,4096]{3,2,1,0:T(8,128)(2,1)}, u32[]{:S(2)}, u32[]{:S(2)}) async-start(bf16[4,2,16,4096]{3,2,1,0:T(8,128)(2,1)} %fusion.22), calls=%async_computation.3 | async-start | bytes 2097152 | tf_op jit(solution)/shard_map/all_to_all | solution.py:155
  131.7 0.6 subtract_convert_fusion.1
  132.3 0.6 subtract_convert_fusion
  133.0 13.4 %all-to-all-done.3 = bf16[4,2,16,4096]{3,2,1,0:T(8,128)(2,1)} async-done(((bf16[4,2,16,4096]{3,2,1,0:T(8,128)(2,1)}), bf16[4,2,16,4096]{3,2,1,0:T(8,128)(2,1)}, u32[]{:S(2)}, u32[]{:S(2)}) %all-to-all-start.3) | async-done | bytes 1048608 | tf_op jit(solution)/shard_map/all_to_all | solution.py:155
  146.3 1.4 convolution_bitcast_fusion.2
  147.7 1.5 fusion.6
  149.1 1.0 collective-permute-start.9
  150.2 1.4 convolution_bitcast_fusion
  151.5 1.4 fusion.5
  153.0 1.2 collective-permute-done.9
  154.2 10.2 %collective-permute-done.10 = bf16[16,4096]{1,0:T(8,128)(2,1)S(1)} collective-permute-done((bf16[16,4096]{1,0:T(8,128)(2,1)S(1)}, bf16[16,4096]{1,0:T(8,128)(2,1)S(1)}, u32[]{:S(2)}, u32[]{:S(2)}) %collective-permute-start.10) | collective-permute-done | bytes 131104 | tf_op jit(solution)/shard_map/ppermute | solution.py:173
  164.3 0.7 fusion.54
  (88 shorter events, 3.0 us)
Async XLA Ops:
  0.0 120.7 %copy-start = (bf16[1,384,4096]{2,1,0:T(8,128)(2,1)S(1)}, bf16[1,384,4096]{2,1,0:T(8,128)(2,1)}, u32[]{:S(2)}) copy-start(bf16[1,384,4096]{2,1,0:T(8,128)(2,1)} %param.17) | copy-start | bytes 9437188
  0.0 6.9 %copy-start.5 = (bf16[1,256,256]{2,1,0:T(8,128)(2,1)S(1)}, bf16[1,256,256]{2,1,0:T(8,128)(2,1)}, u32[]{:S(2)}) copy-start(bf16[1,256,256]{2,1,0:T(8,128)(2,1)} %param.11) | copy-start | bytes 393220
  2.4 14.0 %all-to-all-start = ((bf16[4,256,256]{2,1,0:T(8,128)(2,1)}), bf16[4,256,256]{2,1,0:T(8,128)(2,1)}, u32[]{:S(2)}, u32[]{:S(2)}) async-start(bf16[4,256,256]{2,1,0:T(8,128)(2,1)} %pad_maximum_fusion.3), calls=%async_computation | async-start | bytes 1048576 | tf_op jit(solution)/shard_map/all_to_all | solution.py:56
  7.1 13.4 %collective-permute-start.1 = (bf16[2,256,128]{2,1,0:T(8,128)(2,1)S(1)}, bf16[2,256,128]{2,1,0:T(8,128)(2,1)S(1)}, u32[]{:S(2)}, u32[]{:S(2)}) collective-permute-start(bf16[2,256,128]{2,1,0:T(8,128)(2,1)S(1)} %bitcast.232), channel_id=1, source_target_pairs={{0,2},{2,0},{1,3},{3,1},{4,6},{6,4},{5,7},{7,5},{8,10},{10,8},{9,1... | collective-permute-start | bytes 393224 | tf_op jit(solution)/shard_map/ppermute | solution.py:26
  16.5 2.1 %collective-permute-start = (bf16[4,256,256]{2,1,0:T(8,128)(2,1)}, bf16[4,256,256]{2,1,0:T(8,128)(2,1)S(1)}, u32[]{:S(2)}, u32[]{:S(2)}) collective-permute-start(bf16[4,256,256]{2,1,0:T(8,128)(2,1)} %all-to-all-done), channel_id=1, source_target_pairs={{0,1},{1,0},{2,3},{3,2},{4,5},{5,4},{6,7},{7,6},{8,9},{9,8},{10,11... | collective-permute-start | bytes 1572872 | tf_op jit(solution)/shard_map/ppermute | solution.py:26
  23.2 8.0 %collective-permute-start.2 = (f32[2,256,2]{1,0,2:T(2,128)S(1)}, f32[2,256,2]{1,0,2:T(2,128)S(1)}, u32[]{:S(2)}, u32[]{:S(2)}) collective-permute-start(f32[2,256,2]{1,0,2:T(2,128)S(1)} %pad_maximum_fusion.5), channel_id=1, source_target_pairs={{0,2},{2,0},{1,3},{3,1},{4,6},{6,4},{5,7},{7,5},{8,10},{10,8},{9,1... | collective-permute-start | bytes 12296 | tf_op jit(solution)/shard_map/ppermute | solution.py:26
  30.6 12.1 %collective-permute-start.3 = (bf16[2,256,128]{1,2,0:T(8,128)(2,1)S(1)}, bf16[2,256,128]{1,2,0:T(8,128)(2,1)S(1)}, u32[]{:S(2)}, u32[]{:S(2)}) collective-permute-start(bf16[2,256,128]{1,2,0:T(8,128)(2,1)S(1)} %fusion.34), channel_id=1, source_target_pairs={{0,2},{2,0},{1,3},{3,1},{4,6},{6,4},{5,7},{7,5},{8,10},{10,8},{9,1... | collective-permute-start | bytes 393224 | tf_op jit(solution)/shard_map/ppermute | solution.py:26
  42.6 1.6 copy-start.3
  45.0 1.3 copy-start.1
  45.0 12.4 %copy-start.4 = (bf16[1,16,4096]{2,1,0:T(8,128)(2,1)S(1)}, bf16[1,16,4096]{2,1,0:T(8,128)(2,1)}, u32[]{:S(2)}) copy-start(bf16[1,16,4096]{2,1,0:T(8,128)(2,1)} %param.10) | copy-start | bytes 393220
  45.0 12.9 %copy-start.17 = (s32[1,256,2]{1,2,0:T(2,128)S(1)}, s32[1,256,2]{1,2,0:T(2,128)}, u32[]{:S(2)}) copy-start(s32[1,256,2]{1,2,0:T(2,128)} %param.18) | copy-start | bytes 6148
  47.4 3.0 %collective-permute-start.4 = (bf16[4,2,16,4096]{3,2,1,0:T(8,128)(2,1)}, bf16[4,2,16,4096]{3,2,1,0:T(8,128)(2,1)}, u32[]{:S(2)}, u32[]{:S(2)}) collective-permute-start(bf16[4,2,16,4096]{3,2,1,0:T(8,128)(2,1)} %dynamic-slice_bitcast_fusion), channel_id=1, source_target_pairs={{0,1},{1,0},{2,3},{3,2},{4,5},{5,4},{6,7},{7,6},{8,9},{9,8},{10,11... | collective-permute-start | bytes 3145736 | tf_op jit(solution)/shard_map/ppermute | solution.py:26
  47.4 46.7 %copy-start.6 = (f32[1,4096]{1,0:T(1,128)S(1)}, f32[1,4096]{1,0:T(1,128)}, u32[]{:S(2)}) copy-start(f32[1,4096]{1,0:T(1,128)} %param.14) | copy-start | bytes 49156
  53.2 20.0 %all-to-all-start.1 = ((bf16[4,2,16,4096]{3,2,1,0:T(8,128)(2,1)}), bf16[4,2,16,4096]{3,2,1,0:T(8,128)(2,1)}, u32[]{:S(2)}, u32[]{:S(2)}) async-start(bf16[4,2,16,4096]{3,2,1,0:T(8,128)(2,1)} %fusion.23), calls=%async_computation.1 | async-start | bytes 2097152 | tf_op jit(solution)/shard_map/all_to_all | solution.py:98
  57.4 35.4 %collective-permute-start.6 = (bf16[16,4096]{1,0:T(8,128)(2,1)S(1)}, bf16[16,4096]{1,0:T(8,128)(2,1)}, u32[]{:S(2)}, u32[]{:S(2)}) collective-permute-start(bf16[16,4096]{1,0:T(8,128)(2,1)S(1)} %bitcast.220), channel_id=1, source_target_pairs={{0,2},{2,0},{1,3},{3,1},{4,6},{6,4},{5,7},{7,5},{8,10},{10,8},{9,1... | collective-permute-start | bytes 393224 | tf_op jit(solution)/shard_map/ppermute | solution.py:26
  58.0 0.5 copy-start.9
  58.0 0.5 copy-start.11
  58.5 0.5 copy-start.14
  75.3 16.5 %collective-permute-start.5 = (bf16[2,16,4096]{2,1,0:T(8,128)(2,1)}, bf16[2,16,4096]{2,1,0:T(8,128)(2,1)}, u32[]{:S(2)}, u32[]{:S(2)}) collective-permute-start(bf16[2,16,4096]{2,1,0:T(8,128)(2,1)} %pad_maximum_fusion.4), channel_id=1, source_target_pairs={{0,2},{2,0},{1,3},{3,1},{4,6},{6,4},{5,7},{7,5},{8,10},{10,8},{9,1... | collective-permute-start | bytes 786440 | tf_op jit(solution)/shard_map/ppermute | solution.py:26
  92.8 2.4 %copy-start.2 = (f32[2,16,4096]{2,1,0:T(8,128)}, f32[2,16,4096]{2,1,0:T(8,128)S(1)}, u32[]{:S(2)}) copy-start(f32[2,16,4096]{2,1,0:T(8,128)S(1)} %convert_element_type.155) | copy-start | bytes 1572868
  96.5 21.2 %copy-start.18 = (bf16[1,4096,384]{2,1,0:T(8,128)(2,1)S(1)}, bf16[1,4096,384]{2,1,0:T(8,128)(2,1)}, u32[]{:S(2)}) copy-start(bf16[1,4096,384]{2,1,0:T(8,128)(2,1)} %param.15) | copy-start | bytes 9437188
  114.9 2.7 %collective-permute-start.7 = (bf16[4,2,16,4096]{3,2,1,0:T(8,128)(2,1)S(1)}, bf16[4,2,16,4096]{3,2,1,0:T(8,128)(2,1)S(1)}, u32[]{:S(2)}, u32[]{:S(2)}) collective-permute-start(bf16[4,2,16,4096]{3,2,1,0:T(8,128)(2,1)S(1)} %all_to_all.20), channel_id=1, source_target_pairs={{0,1},{1,0},{2,3},{3,2},{4,5},{5,4},{6,7},{7,6},{8,9},{9,8},{10,11... | collective-permute-start | bytes 3145736 | tf_op jit(solution)/shard_map/ppermute | solution.py:26
  117.6 1.9 %copy-start.19 = (bf16[1,4096,384]{2,1,0:T(8,128)(2,1)S(1)}, bf16[1,4096,384]{2,1,0:T(8,128)(2,1)}, u32[]{:S(2)}) copy-start(bf16[1,4096,384]{2,1,0:T(8,128)(2,1)} %param.16) | copy-start | bytes 9437188
  120.7 1.8 %copy-start.16 = (f32[1,256,2]{1,2,0:T(2,128)S(1)}, f32[1,256,2]{1,2,0:T(2,128)}, u32[]{:S(2)}) copy-start(f32[1,256,2]{1,2,0:T(2,128)} %param.19) | copy-start | bytes 6148
  120.7 1.9 %copy-start.10 = (s32[16,2]{0,1:T(2,128)S(1)}, s32[16,2]{0,1:T(2,128)}, u32[]{:S(2)}) copy-start(s32[16,2]{0,1:T(2,128)} %copy-done.9) | copy-start | bytes 388
  120.7 1.9 %copy-start.12 = (s32[16,2]{0,1:T(2,128)S(1)}, s32[16,2]{0,1:T(2,128)}, u32[]{:S(2)}) copy-start(s32[16,2]{0,1:T(2,128)} %copy-done.11) | copy-start | bytes 388
  122.0 9.1 %copy-start.7 = (s32[4,16]{1,0:T(4,128)S(1)}, s32[4,16]{1,0:T(4,128)}, u32[]{:S(2)}) copy-start(s32[4,16]{1,0:T(4,128)} %copy.91) | copy-start | bytes 772
  122.0 9.1 %copy-start.8 = (s32[4,16]{1,0:T(4,128)S(1)}, s32[4,16]{1,0:T(4,128)}, u32[]{:S(2)}) copy-start(s32[4,16]{1,0:T(4,128)} %copy.95) | copy-start | bytes 772
  122.1 9.2 %copy-start.15 = (pred[16,4]{0,1:T(4,128)(4,1)S(1)}, pred[16,4]{0,1:T(4,128)(4,1)}, u32[]{:S(2)}) copy-start(pred[16,4]{0,1:T(4,128)(4,1)} %copy-done.14) | copy-start | bytes 196
  122.1 9.3 %copy-start.13 = (pred[16,4]{0,1:T(4,128)(4,1)S(1)}, pred[16,4]{0,1:T(4,128)(4,1)}, u32[]{:S(2)}) copy-start(pred[16,4]{0,1:T(4,128)(4,1)} %get-tuple-element.37) | copy-start | bytes 196
  122.3 2.7 %collective-permute-start.8 = (bf16[4,2,16,4096]{3,2,1,0:T(8,128)(2,1)S(1)}, bf16[4,2,16,4096]{3,2,1,0:T(8,128)(2,1)S(1)}, u32[]{:S(2)}, u32[]{:S(2)}) collective-permute-start(bf16[4,2,16,4096]{3,2,1,0:T(8,128)(2,1)S(1)} %bitcast.225), channel_id=1, source_target_pairs={{0,1},{1,0},{2,3},{3,2},{4,5},{5,4},{6,7},{7,6},{8,9},{9,8},{10,11... | collective-permute-start | bytes 3145736 | tf_op jit(solution)/shard_map/ppermute | solution.py:26
  126.3 20.0 %all-to-all-start.3 = ((bf16[4,2,16,4096]{3,2,1,0:T(8,128)(2,1)}), bf16[4,2,16,4096]{3,2,1,0:T(8,128)(2,1)}, u32[]{:S(2)}, u32[]{:S(2)}) async-start(bf16[4,2,16,4096]{3,2,1,0:T(8,128)(2,1)} %fusion.22), calls=%async_computation.3 | async-start | bytes 2097152 | tf_op jit(solution)/shard_map/all_to_all | solution.py:155
  149.1 5.0 %collective-permute-start.9 = (bf16[16,4096]{1,0:T(8,128)(2,1)S(1)}, bf16[16,4096]{1,0:T(8,128)(2,1)S(1)}, u32[]{:S(2)}, u32[]{:S(2)}) collective-permute-start(bf16[16,4096]{1,0:T(8,128)(2,1)S(1)} %fusion.6), channel_id=1, source_target_pairs={{240,0},{0,16},{16,32},{32,48},{48,64},{64,80},{80,96},{96,112},{1... | collective-permute-start | bytes 393224 | tf_op jit(solution)/shard_map/ppermute | solution.py:22
  152.9 11.4 %collective-permute-start.10 = (bf16[16,4096]{1,0:T(8,128)(2,1)S(1)}, bf16[16,4096]{1,0:T(8,128)(2,1)S(1)}, u32[]{:S(2)}, u32[]{:S(2)}) collective-permute-start(bf16[16,4096]{1,0:T(8,128)(2,1)S(1)} %fusion.5), channel_id=1, source_target_pairs={{0,18},{2,16},{16,34},{18,32},{32,50},{34,48},{48,66},{50,64},{64,... | collective-permute-start | bytes 393224 | tf_op jit(solution)/shard_map/ppermute | solution.py:173

commit v13 on v11

--- a/solution.py
+++ b/solution.py
@@ -92,8 +92,9 @@
     head_terms = jnp.dot(heads, proj_out, preferred_element_type=jnp.float32).astype(jnp.bfloat16)
 
     terms = head_terms.reshape(ny, nz, nc, tok_rows, -1)
-    keep_c = lax.dynamic_index_in_dim(terms, ci, 2, keepdims=False)
-    give_c = lax.dynamic_index_in_dim(terms, 1 - ci, 2, keepdims=False)
+    first = ci == 0
+    keep_c = jnp.where(first, terms[:, :, 0], terms[:, :, 1])
+    give_c = jnp.where(first, terms[:, :, 1], terms[:, :, 0])
     part_c = keep_c.astype(jnp.float32) + swap(give_c, "core").astype(jnp.float32)
     part_y = lax.all_to_all(part_c.astype(jnp.bfloat16), "y", 0, 0, tiled=True)
     part_y = jnp.sum(part_y.astype(jnp.float32), axis=0)

time: 164 us -> 160 us (0.976)
  local copies, waits for them, and re-layouts: 12.6 us -> 10.3 us
where the time goes in v13:
time: 160 us; the launch traced here: 159 us
  waiting for transfers between devices  69.2 us (43%)
  starting transfers between devices  28.3 us (18%)
  other arithmetic  18.2 us (11%)
  blocking collectives  18.2 us (11%)
  matrix products  14.8 us (9%)
  local copies, waits for them, and re-layouts  10.3 us (6%)
    ppermute x9, waiting for transfers between devices, swap(): return lax.ppermute(block, axis, [(0, 1), (1, 0)])  28.3 us
    all_to_all x1, blocking collectives, body(): rows_y = lax.all_to_all(dispatch, 'y', 0, 0, tiled=True)  18.2 us
    ppermute x9, starting transfers between devices, swap(): return lax.ppermute(block, axis, [(0, 1), (1, 0)])  14 us
    all_to_all x1, waiting for transfers between devices, body(): part_y = lax.all_to_all(part_c.astype(jnp.bfloat16), 'y', 0, 0, tiled=True)  13.4 us
    all_to_all x1, waiting for transfers between devices, body(): lax.all_to_all(chip_sum.astype(jnp.bfloat16), 'y', 0, 0, tiled=True)  13.3 us
    ppermute x1, waiting for transfers between devices, body(): lax.ppermute(mixed_far.astype(jnp.bfloat16), ('section', 'zh'), route)  9.21 us
    all_to_all x1, starting transfers between devices, body(): kv_y = lax.all_to_all(send_kv, 'y', 0, 0, tiled=True)  4.46 us
    all_to_all x1, starting transfers between devices, body(): part_y = lax.all_to_all(part_c.astype(jnp.bfloat16), 'y', 0, 0, tiled=True)  4.37 us
  transfers between devices with their start and end apart: 14, of which 12 were waited for; matrix products, arithmetic and copies ran while one was open for 13% of the time, Pallas kernels for 0%

profile of v13, /device:TPU:32, one launch (start us, length us, event | category | flops | bytes accessed | tf_op | source)
XLA Modules:
  0.0 159.4 jit_solution(2133919775649726189)
XLA Ops:
  0.0 1.2 reshape_squeeze.6
  1.2 0.4 fusion.90
  1.6 0.8 pad_maximum_fusion.3
  2.5 4.5 %all-to-all-start = ((bf16[4,256,256]{2,1,0:T(8,128)(2,1)}), bf16[4,256,256]{2,1,0:T(8,128)(2,1)}, u32[]{:S(2)}, u32[]{:S(2)}) async-start(bf16[4,256,256]{2,1,0:T(8,128)(2,1)} %pad_maximum_fusion.3), calls=%async_computation | async-start | bytes 1048576 | tf_op jit(solution)/shard_map/all_to_all | solution.py:56
  7.0 0.1 copy.92
  7.1 6.4 %collective-permute-start.1 = (bf16[2,256,128]{2,1,0:T(8,128)(2,1)S(1)}, bf16[2,256,128]{2,1,0:T(8,128)(2,1)S(1)}, u32[]{:S(2)}, u32[]{:S(2)}) collective-permute-start(bf16[2,256,128]{2,1,0:T(8,128)(2,1)S(1)} %bitcast.238), channel_id=1, source_target_pairs={{0,2},{2,0},{1,3},{3,1},{4,6},{6,4},{5,7},{7,5},{8,10},{10,8},{9,1... | collective-permute-start | bytes 393224 | tf_op jit(solution)/shard_map/ppermute | solution.py:26
  13.7 2.8 %all-to-all-done = bf16[4,256,256]{2,1,0:T(8,128)(2,1)} async-done(((bf16[4,256,256]{2,1,0:T(8,128)(2,1)}), bf16[4,256,256]{2,1,0:T(8,128)(2,1)}, u32[]{:S(2)}, u32[]{:S(2)}) %all-to-all-start) | async-done | bytes 524320 | tf_op jit(solution)/shard_map/all_to_all | solution.py:56
  16.5 0.4 broadcast_compare_fusion
  17.0 1.7 %collective-permute-done = bf16[4,256,256]{2,1,0:T(8,128)(2,1)S(1)} collective-permute-done((bf16[4,256,256]{2,1,0:T(8,128)(2,1)}, bf16[4,256,256]{2,1,0:T(8,128)(2,1)S(1)}, u32[]{:S(2)}, u32[]{:S(2)}) %collective-permute-start) | collective-permute-done | bytes 524320 | tf_op jit(solution)/shard_map/ppermute | solution.py:26
  18.6 1.1 pad_maximum_fusion.1
  19.8 0.7 fusion.8
  20.5 1.7 %fusion.11 = (f32[2,256]{1,0:T(2,128)S(1)}, f32[2,256]{1,0:T(2,128)S(1)}, f32[2048,2,256]{2,0,1:T(8,128)S(1)}) fusion(f32[2048,2,256]{2,0,1:T(8,128)S(1)} %get-tuple-element.27, f32[2,256]{1,0:T(2,128)S(1)} %get-tuple-element.26, pred[256,2048]{0,1:T(8,128)(4,1)S(1)} %broadcast_compare_fusion, bf16[2,256,128]{2,1,0:T(8,128)(2,1)S(1)} %collective-permute-done.1, ...), kind=kOutput, calls=%fused_computation.21 | convolution fusion | flops 275774464 | bytes 9574400 | tf_op jit(solution)/shard_map/hqd,kd->hqk/dot_general | solution.py:70
  22.2 1.0 fusion.14
  23.2 6.4 %collective-permute-start.2 = (f32[2,256,2]{1,0,2:T(2,128)S(1)}, f32[2,256,2]{1,0,2:T(2,128)S(1)}, u32[]{:S(2)}, u32[]{:S(2)}) collective-permute-start(f32[2,256,2]{1,0,2:T(2,128)S(1)} %pad_maximum_fusion.5), channel_id=1, source_target_pairs={{0,2},{2,0},{1,3},{3,1},{4,6},{6,4},{5,7},{7,5},{8,10},{10,8},{9,1... | collective-permute-start | bytes 12296 | tf_op jit(solution)/shard_map/ppermute | solution.py:26
  29.6 1.0 fusion.32
  30.7 0.5 collective-permute-done.2
  31.2 11.5 %collective-permute-done.3 = bf16[2,256,128]{1,2,0:T(8,128)(2,1)S(1)} collective-permute-done((bf16[2,256,128]{1,2,0:T(8,128)(2,1)S(1)}, bf16[2,256,128]{1,2,0:T(8,128)(2,1)S(1)}, u32[]{:S(2)}, u32[]{:S(2)}) %collective-permute-start.3) | collective-permute-done | bytes 131104 | tf_op jit(solution)/shard_map/ppermute | solution.py:26
  42.7 1.0 fusion.45
  43.7 0.6 copy-done.2
  44.2 0.7 convolution_convert_fusion.1
  45.2 2.6 %collective-permute-done.4 = bf16[4,2,16,4096]{3,2,1,0:T(8,128)(2,1)S(1)} collective-permute-done((bf16[4,2,16,4096]{3,2,1,0:T(8,128)(2,1)S(1)}, bf16[4,2,16,4096]{3,2,1,0:T(8,128)(2,1)S(1)}, u32[]{:S(2)}, u32[]{:S(2)}) %collective-permute-start.4) | collective-permute-done | bytes 1048608 | tf_op jit(solution)/shard_map/ppermute | solution.py:26
  47.9 1.5 fusion.21
  49.4 4.4 %all-to-all-start.1 = ((bf16[4,2,16,4096]{3,2,1,0:T(8,128)(2,1)}), bf16[4,2,16,4096]{3,2,1,0:T(8,128)(2,1)}, u32[]{:S(2)}, u32[]{:S(2)}) async-start(bf16[4,2,16,4096]{3,2,1,0:T(8,128)(2,1)} %fusion.21), calls=%async_computation.1 | async-start | bytes 2097152 | tf_op jit(solution)/shard_map/all_to_all | solution.py:99
  53.8 0.5 collective-permute-start.6
  54.3 0.5 fusion.70
  54.9 0.5 copy-done.13
  55.5 0.6 reduce_window_sum.17
  56.1 13.4 %all-to-all-done.1 = bf16[4,2,16,4096]{3,2,1,0:T(8,128)(2,1)} async-done(((bf16[4,2,16,4096]{3,2,1,0:T(8,128)(2,1)}), bf16[4,2,16,4096]{3,2,1,0:T(8,128)(2,1)}, u32[]{:S(2)}, u32[]{:S(2)}) %all-to-all-start.1) | async-done | bytes 1048608 | tf_op jit(solution)/shard_map/all_to_all | solution.py:99
  69.5 1.4 convert_reduce_fusion
  70.9 0.7 pad_maximum_fusion.4
  71.6 0.4 collective-permute-start.5
  72.0 1.3 add_bitcast_fusion.1
  73.3 1.4 copy.103
  74.7 1.2 convert_element_type.143
  75.8 1.3 copy.106
  77.2 1.3 reduce_window_sum.18
  78.5 1.3 add_bitcast_fusion
  79.8 1.4 copy.107
  81.2 7.0 %collective-permute-done.5 = bf16[2,16,4096]{2,1,0:T(8,128)(2,1)} collective-permute-done((bf16[2,16,4096]{2,1,0:T(8,128)(2,1)}, bf16[2,16,4096]{2,1,0:T(8,128)(2,1)}, u32[]{:S(2)}, u32[]{:S(2)}) %collective-permute-start.5) | collective-permute-done | bytes 262176 | tf_op jit(solution)/shard_map/ppermute | solution.py:26
  88.1 1.0 convert_element_type.138
  89.2 1.3 multiply_reduce_fusion.1
  90.5 1.0 fusion
  91.5 1.3 fusion.1
  93.0 18.2 %all_to_all.20 = bf16[4,2,16,4096]{3,2,1,0:T(8,128)(2,1)S(1)} all-to-all(bf16[4,2,16,4096]{3,2,1,0:T(8,128)(2,1)S(1)} %copy.108), channel_id=1, replica_groups=mesh['section'=16,'y'=4,'zh'=2,'core'=2] {'y'}, dimensions={0} | all-to-all | bytes 2097152 | tf_op jit(solution)/shard_map/all_to_all | solution.py:143
  111.2 2.7 %collective-permute-done.7 = bf16[4,2,16,4096]{3,2,1,0:T(8,128)(2,1)S(1)} collective-permute-done((bf16[4,2,16,4096]{3,2,1,0:T(8,128)(2,1)S(1)}, bf16[4,2,16,4096]{3,2,1,0:T(8,128)(2,1)S(1)}, u32[]{:S(2)}, u32[]{:S(2)}) %collective-permute-start.7) | collective-permute-done | bytes 1048608 | tf_op jit(solution)/shard_map/ppermute | solution.py:26
  113.9 0.2 pad_maximum_fusion
  114.1 1.3 fusion.18
  115.4 0.4 copy-done.18
  115.8 1.3 multiply_convert_fusion
  117.1 1.3 convolution_convert_fusion
  118.4 0.2 fusion.89
  118.6 0.2 collective-permute-start.8
  119.0 2.4 %collective-permute-done.8 = bf16[4,2,16,4096]{3,2,1,0:T(8,128)(2,1)S(1)} collective-permute-done((bf16[4,2,16,4096]{3,2,1,0:T(8,128)(2,1)S(1)}, bf16[4,2,16,4096]{3,2,1,0:T(8,128)(2,1)S(1)}, u32[]{:S(2)}, u32[]{:S(2)}) %collective-permute-start.8) | collective-permute-done | bytes 1048608 | tf_op jit(solution)/shard_map/ppermute | solution.py:26
  121.4 1.3 fusion.20
  122.6 4.2 %all-to-all-start.3 = ((bf16[4,2,16,4096]{3,2,1,0:T(8,128)(2,1)}), bf16[4,2,16,4096]{3,2,1,0:T(8,128)(2,1)}, u32[]{:S(2)}, u32[]{:S(2)}) async-start(bf16[4,2,16,4096]{3,2,1,0:T(8,128)(2,1)} %fusion.20), calls=%async_computation.3 | async-start | bytes 2097152 | tf_op jit(solution)/shard_map/all_to_all | solution.py:156
  127.9 0.7 reshape.245
  128.6 0.7 reshape.248
  129.3 13.3 %all-to-all-done.3 = bf16[4,2,16,4096]{3,2,1,0:T(8,128)(2,1)} async-done(((bf16[4,2,16,4096]{3,2,1,0:T(8,128)(2,1)}), bf16[4,2,16,4096]{3,2,1,0:T(8,128)(2,1)}, u32[]{:S(2)}, u32[]{:S(2)}) %all-to-all-start.3) | async-done | bytes 1048608 | tf_op jit(solution)/shard_map/all_to_all | solution.py:156
  142.6 1.8 %fusion.3 = bf16[16,4096]{1,0:T(8,128)(2,1)S(1)} fusion(bf16[4,2,16,4096]{3,2,1,0:T(8,128)(2,1)} %all-to-all-done.3, f32[2,16,4096]{2,1,0:T(8,128)} %copy-done.1, bf16[1,16,4096]{2,1,0:T(8,128)(2,1)S(1)} %get-tuple-element.14, f32[16,4,16]{2,1,0:T(4,128)} %reshape.245, bf16[1,16,4096]{2,1,0:T(8,128)(2,1)S(1)} %copy-done.3), kind=kOutput, calls=%fused_computation.9 | convolution fusion | flops 50724864 | bytes 1212416 | tf_op jit(solution)/shard_map/txj,xjd->td/dot_general | solution.py:160
  144.4 1.1 collective-permute-start.9
  145.5 1.7 %fusion.4 = bf16[16,4096]{1,0:T(8,128)(2,1)S(1)} fusion(bf16[4,2,16,4096]{3,2,1,0:T(8,128)(2,1)} %all-to-all-done.3, f32[16,4,16]{2,1,0:T(4,128)} %reshape.248), kind=kOutput, calls=%fused_computation.10 | convolution fusion | flops 50397184 | bytes 688128 | tf_op jit(solution)/shard_map/txj,xjd->td/dot_general | solution.py:161
  147.4 2.1 %collective-permute-done.9 = bf16[16,4096]{1,0:T(8,128)(2,1)S(1)} collective-permute-done((bf16[16,4096]{1,0:T(8,128)(2,1)S(1)}, bf16[16,4096]{1,0:T(8,128)(2,1)S(1)}, u32[]{:S(2)}, u32[]{:S(2)}) %collective-permute-start.9) | collective-permute-done | bytes 131104 | tf_op jit(solution)/shard_map/ppermute | solution.py:22
  149.5 9.2 %collective-permute-done.10 = bf16[16,4096]{1,0:T(8,128)(2,1)S(1)} collective-permute-done((bf16[16,4096]{1,0:T(8,128)(2,1)S(1)}, bf16[16,4096]{1,0:T(8,128)(2,1)S(1)}, u32[]{:S(2)}, u32[]{:S(2)}) %collective-permute-start.10) | collective-permute-done | bytes 131104 | tf_op jit(solution)/shard_map/ppermute | solution.py:167
  158.7 0.7 fusion.54
  (82 shorter events, 2.3 us)
Async XLA Ops:
  0.0 117.0 %copy-start = (bf16[1,384,4096]{2,1,0:T(8,128)(2,1)S(1)}, bf16[1,384,4096]{2,1,0:T(8,128)(2,1)}, u32[]{:S(2)}) copy-start(bf16[1,384,4096]{2,1,0:T(8,128)(2,1)} %param.17) | copy-start | bytes 9437188
  0.0 6.9 %copy-start.4 = (bf16[1,256,256]{2,1,0:T(8,128)(2,1)S(1)}, bf16[1,256,256]{2,1,0:T(8,128)(2,1)}, u32[]{:S(2)}) copy-start(bf16[1,256,256]{2,1,0:T(8,128)(2,1)} %param.11) | copy-start | bytes 393220
  2.5 14.0 %all-to-all-start = ((bf16[4,256,256]{2,1,0:T(8,128)(2,1)}), bf16[4,256,256]{2,1,0:T(8,128)(2,1)}, u32[]{:S(2)}, u32[]{:S(2)}) async-start(bf16[4,256,256]{2,1,0:T(8,128)(2,1)} %pad_maximum_fusion.3), calls=%async_computation | async-start | bytes 1048576 | tf_op jit(solution)/shard_map/all_to_all | solution.py:56
  7.1 13.4 %collective-permute-start.1 = (bf16[2,256,128]{2,1,0:T(8,128)(2,1)S(1)}, bf16[2,256,128]{2,1,0:T(8,128)(2,1)S(1)}, u32[]{:S(2)}, u32[]{:S(2)}) collective-permute-start(bf16[2,256,128]{2,1,0:T(8,128)(2,1)S(1)} %bitcast.238), channel_id=1, source_target_pairs={{0,2},{2,0},{1,3},{3,1},{4,6},{6,4},{5,7},{7,5},{8,10},{10,8},{9,1... | collective-permute-start | bytes 393224 | tf_op jit(solution)/shard_map/ppermute | solution.py:26
  16.5 2.1 %collective-permute-start = (bf16[4,256,256]{2,1,0:T(8,128)(2,1)}, bf16[4,256,256]{2,1,0:T(8,128)(2,1)S(1)}, u32[]{:S(2)}, u32[]{:S(2)}) collective-permute-start(bf16[4,256,256]{2,1,0:T(8,128)(2,1)} %all-to-all-done), channel_id=1, source_target_pairs={{0,1},{1,0},{2,3},{3,2},{4,5},{5,4},{6,7},{7,6},{8,9},{9,8},{10,11... | collective-permute-start | bytes 1572872 | tf_op jit(solution)/shard_map/ppermute | solution.py:26
  23.2 8.0 %collective-permute-start.2 = (f32[2,256,2]{1,0,2:T(2,128)S(1)}, f32[2,256,2]{1,0,2:T(2,128)S(1)}, u32[]{:S(2)}, u32[]{:S(2)}) collective-permute-start(f32[2,256,2]{1,0,2:T(2,128)S(1)} %pad_maximum_fusion.5), channel_id=1, source_target_pairs={{0,2},{2,0},{1,3},{3,1},{4,6},{6,4},{5,7},{7,5},{8,10},{10,8},{9,1... | collective-permute-start | bytes 12296 | tf_op jit(solution)/shard_map/ppermute | solution.py:26
  30.6 12.1 %collective-permute-start.3 = (bf16[2,256,128]{1,2,0:T(8,128)(2,1)S(1)}, bf16[2,256,128]{1,2,0:T(8,128)(2,1)S(1)}, u32[]{:S(2)}, u32[]{:S(2)}) collective-permute-start(bf16[2,256,128]{1,2,0:T(8,128)(2,1)S(1)} %fusion.32), channel_id=1, source_target_pairs={{0,2},{2,0},{1,3},{3,1},{4,6},{6,4},{5,7},{7,5},{8,10},{10,8},{9,1... | collective-permute-start | bytes 393224 | tf_op jit(solution)/shard_map/ppermute | solution.py:26
  42.7 1.6 copy-start.2
  45.0 8.8 %copy-start.3 = (bf16[1,16,4096]{2,1,0:T(8,128)(2,1)S(1)}, bf16[1,16,4096]{2,1,0:T(8,128)(2,1)}, u32[]{:S(2)}) copy-start(bf16[1,16,4096]{2,1,0:T(8,128)(2,1)} %param.10) | copy-start | bytes 393220
  45.0 9.3 %copy-start.16 = (s32[1,256,2]{1,2,0:T(2,128)S(1)}, s32[1,256,2]{1,2,0:T(2,128)}, u32[]{:S(2)}) copy-start(s32[1,256,2]{1,2,0:T(2,128)} %param.18) | copy-start | bytes 6148
  45.1 2.7 %collective-permute-start.4 = (bf16[4,2,16,4096]{3,2,1,0:T(8,128)(2,1)S(1)}, bf16[4,2,16,4096]{3,2,1,0:T(8,128)(2,1)S(1)}, u32[]{:S(2)}, u32[]{:S(2)}) collective-permute-start(bf16[4,2,16,4096]{3,2,1,0:T(8,128)(2,1)S(1)} %fusion.35), channel_id=1, source_target_pairs={{0,1},{1,0},{2,3},{3,2},{4,5},{5,4},{6,7},{7,6},{8,9},{9,8},{10,11... | collective-permute-start | bytes 3145736 | tf_op jit(solution)/shard_map/ppermute | solution.py:26
  49.4 41.1 %copy-start.5 = (f32[1,4096]{1,0:T(1,128)S(1)}, f32[1,4096]{1,0:T(1,128)}, u32[]{:S(2)}) copy-start(f32[1,4096]{1,0:T(1,128)} %param.14) | copy-start | bytes 49156
  49.4 20.1 %all-to-all-start.1 = ((bf16[4,2,16,4096]{3,2,1,0:T(8,128)(2,1)}), bf16[4,2,16,4096]{3,2,1,0:T(8,128)(2,1)}, u32[]{:S(2)}, u32[]{:S(2)}) async-start(bf16[4,2,16,4096]{3,2,1,0:T(8,128)(2,1)} %fusion.21), calls=%async_computation.1 | async-start | bytes 2097152 | tf_op jit(solution)/shard_map/all_to_all | solution.py:99
  53.8 35.4 %collective-permute-start.6 = (bf16[16,4096]{1,0:T(8,128)(2,1)S(1)}, bf16[16,4096]{1,0:T(8,128)(2,1)}, u32[]{:S(2)}, u32[]{:S(2)}) collective-permute-start(bf16[16,4096]{1,0:T(8,128)(2,1)S(1)} %bitcast.226), channel_id=1, source_target_pairs={{0,2},{2,0},{1,3},{3,1},{4,6},{6,4},{5,7},{7,5},{8,10},{10,8},{9,1... | collective-permute-start | bytes 393224 | tf_op jit(solution)/shard_map/ppermute | solution.py:26
  54.3 0.6 copy-start.8
  54.3 0.6 copy-start.10
  54.8 0.6 copy-start.13
  71.6 16.5 %collective-permute-start.5 = (bf16[2,16,4096]{2,1,0:T(8,128)(2,1)}, bf16[2,16,4096]{2,1,0:T(8,128)(2,1)}, u32[]{:S(2)}, u32[]{:S(2)}) collective-permute-start(bf16[2,16,4096]{2,1,0:T(8,128)(2,1)} %pad_maximum_fusion.4), channel_id=1, source_target_pairs={{0,2},{2,0},{1,3},{3,1},{4,6},{6,4},{5,7},{7,5},{8,10},{10,8},{9,1... | collective-permute-start | bytes 786440 | tf_op jit(solution)/shard_map/ppermute | solution.py:26
  89.1 2.4 %copy-start.1 = (f32[2,16,4096]{2,1,0:T(8,128)}, f32[2,16,4096]{2,1,0:T(8,128)S(1)}, u32[]{:S(2)}) copy-start(f32[2,16,4096]{2,1,0:T(8,128)S(1)} %convert_element_type.138) | copy-start | bytes 1572868
  92.9 21.2 %copy-start.17 = (bf16[1,4096,384]{2,1,0:T(8,128)(2,1)S(1)}, bf16[1,4096,384]{2,1,0:T(8,128)(2,1)}, u32[]{:S(2)}) copy-start(bf16[1,4096,384]{2,1,0:T(8,128)(2,1)} %param.15) | copy-start | bytes 9437188
  111.2 2.7 %collective-permute-start.7 = (bf16[4,2,16,4096]{3,2,1,0:T(8,128)(2,1)S(1)}, bf16[4,2,16,4096]{3,2,1,0:T(8,128)(2,1)S(1)}, u32[]{:S(2)}, u32[]{:S(2)}) collective-permute-start(bf16[4,2,16,4096]{3,2,1,0:T(8,128)(2,1)S(1)} %all_to_all.20), channel_id=1, source_target_pairs={{0,1},{1,0},{2,3},{3,2},{4,5},{5,4},{6,7},{7,6},{8,9},{9,8},{10,11... | collective-permute-start | bytes 3145736 | tf_op jit(solution)/shard_map/ppermute | solution.py:26
  113.9 1.9 %copy-start.18 = (bf16[1,4096,384]{2,1,0:T(8,128)(2,1)S(1)}, bf16[1,4096,384]{2,1,0:T(8,128)(2,1)}, u32[]{:S(2)}) copy-start(bf16[1,4096,384]{2,1,0:T(8,128)(2,1)} %param.16) | copy-start | bytes 9437188
  117.1 1.8 %copy-start.15 = (f32[1,256,2]{1,2,0:T(2,128)S(1)}, f32[1,256,2]{1,2,0:T(2,128)}, u32[]{:S(2)}) copy-start(f32[1,256,2]{1,2,0:T(2,128)} %param.19) | copy-start | bytes 6148
  118.4 8.5 %copy-start.9 = (s32[16,2]{0,1:T(2,128)S(1)}, s32[16,2]{0,1:T(2,128)}, u32[]{:S(2)}) copy-start(s32[16,2]{0,1:T(2,128)} %copy-done.8) | copy-start | bytes 388
  118.4 8.5 %copy-start.11 = (s32[16,2]{0,1:T(2,128)S(1)}, s32[16,2]{0,1:T(2,128)}, u32[]{:S(2)}) copy-start(s32[16,2]{0,1:T(2,128)} %copy-done.10) | copy-start | bytes 388
  118.4 9.1 %copy-start.6 = (s32[4,16]{1,0:T(4,128)S(1)}, s32[4,16]{1,0:T(4,128)}, u32[]{:S(2)}) copy-start(s32[4,16]{1,0:T(4,128)} %copy.103) | copy-start | bytes 772
  118.4 9.1 %copy-start.7 = (s32[4,16]{1,0:T(4,128)S(1)}, s32[4,16]{1,0:T(4,128)}, u32[]{:S(2)}) copy-start(s32[4,16]{1,0:T(4,128)} %copy.107) | copy-start | bytes 772
  118.4 9.2 %copy-start.14 = (pred[16,4]{0,1:T(4,128)(4,1)S(1)}, pred[16,4]{0,1:T(4,128)(4,1)}, u32[]{:S(2)}) copy-start(pred[16,4]{0,1:T(4,128)(4,1)} %copy-done.13) | copy-start | bytes 196
  118.4 9.3 %copy-start.12 = (pred[16,4]{0,1:T(4,128)(4,1)S(1)}, pred[16,4]{0,1:T(4,128)(4,1)}, u32[]{:S(2)}) copy-start(pred[16,4]{0,1:T(4,128)(4,1)} %get-tuple-element.33) | copy-start | bytes 196
  118.6 2.7 %collective-permute-start.8 = (bf16[4,2,16,4096]{3,2,1,0:T(8,128)(2,1)S(1)}, bf16[4,2,16,4096]{3,2,1,0:T(8,128)(2,1)S(1)}, u32[]{:S(2)}, u32[]{:S(2)}) collective-permute-start(bf16[4,2,16,4096]{3,2,1,0:T(8,128)(2,1)S(1)} %bitcast.231), channel_id=1, source_target_pairs={{0,1},{1,0},{2,3},{3,2},{4,5},{5,4},{6,7},{7,6},{8,9},{9,8},{10,11... | collective-permute-start | bytes 3145736 | tf_op jit(solution)/shard_map/ppermute | solution.py:26
  122.6 20.0 %all-to-all-start.3 = ((bf16[4,2,16,4096]{3,2,1,0:T(8,128)(2,1)}), bf16[4,2,16,4096]{3,2,1,0:T(8,128)(2,1)}, u32[]{:S(2)}, u32[]{:S(2)}) async-start(bf16[4,2,16,4096]{3,2,1,0:T(8,128)(2,1)} %fusion.20), calls=%async_computation.3 | async-start | bytes 2097152 | tf_op jit(solution)/shard_map/all_to_all | solution.py:156
  144.4 5.0 %collective-permute-start.9 = (bf16[16,4096]{1,0:T(8,128)(2,1)S(1)}, bf16[16,4096]{1,0:T(8,128)(2,1)S(1)}, u32[]{:S(2)}, u32[]{:S(2)}) collective-permute-start(bf16[16,4096]{1,0:T(8,128)(2,1)S(1)} %fusion.3), channel_id=1, source_target_pairs={{240,0},{0,16},{16,32},{32,48},{48,64},{64,80},{80,96},{96,112},{1... | collective-permute-start | bytes 393224 | tf_op jit(solution)/shard_map/ppermute | solution.py:22
  147.3 11.4 %collective-permute-start.10 = (bf16[16,4096]{1,0:T(8,128)(2,1)S(1)}, bf16[16,4096]{1,0:T(8,128)(2,1)S(1)}, u32[]{:S(2)}, u32[]{:S(2)}) collective-permute-start(bf16[16,4096]{1,0:T(8,128)(2,1)S(1)} %fusion.4), channel_id=1, source_target_pairs={{0,18},{2,16},{16,34},{18,32},{32,50},{34,48},{48,66},{50,64},{64,... | collective-permute-start | bytes 393224 | tf_op jit(solution)/shard_map/ppermute | solution.py:167
